TPU v7x, 32 devices: a whole 2x2x4 slice. The times are simulated.
32 devices in a mesh: row: 8 (over z, x), col: 4 (over y, core).
Axes of the slice: x: 2, y: 2, z: 4, core: 2. Of those that a mesh axis runs over, the one named last changes fastest.
Arguments:
- centers: float32 [3, 9472], P(None, ('row', 'col')), may hold values from -1 to 1
- panel_areas: float32 [9472], P(('row', 'col')), may hold values from 0.006164962 to 0.024659848
- jump_term: float32 [9472], P(('row', 'col')), may hold values from 1.5 to 3
- displacement: float32 [3, 9472], P(None, ('row', 'col')), may hold values from -0.3 to 0.3
- design_ids: int32 [9472], P(('row', 'col')), may hold values from 0 to 127
- primal_field: float32 [2, 9472], P(None, ('row', 'col')), may hold values from -6 to 6
- adjoint_start: float32 [9472, 8], P(('row', 'col')), may hold values from -6 to 6
- mic_panels: int32 [4, 4], replicated, may hold values from 0 to 9471
- wavenumber: float32 [1], replicated, may hold values from 10 to 20
Outputs:
- adjoint_field: float32 [9472, 8], P(('row', 'col'))
- sensitivity: float32 [4, 128], replicated
All inputs are finite; a program needn't handle non-finite values.
Results may differ from a plain program's by a relative error of at most 0.0003.
Values sent between devices are 32-bit elements; how exact they have to be, the bound alone decides.
No kernel may reach another device: no remote copies, remote signals or barrier semaphores. Data moves between devices by JAX's collectives and lax.ppermute only.
A program may use at most 64 MiB of HBM per device.

v0:
```python
import functools
import math

import jax
import jax.numpy as jnp
from jax import lax
from jax.experimental import pallas as pl
from jax.experimental.pallas import tpu as pltpu
from jax.sharding import PartitionSpec as P

DESIGN = 128


highest = lax.Precision.HIGHEST
four_pi = 4.0 * math.pi


def distances(rows_xyz, rows_area, cols_xyz, cols_area):
    diff_x = rows_xyz[0][:, None] - cols_xyz[0][None, :]
    diff_y = rows_xyz[1][:, None] - cols_xyz[1][None, :]
    diff_z = rows_xyz[2][:, None] - cols_xyz[2][None, :]
    square = (
        diff_x * diff_x
        + diff_y * diff_y
        + diff_z * diff_z
        + 0.5 * (rows_area[:, None] + cols_area[None, :])
    )
    return (diff_x, diff_y, diff_z, jnp.sqrt(square))


def kernel_parts(rows_xyz, rows_area, cols_xyz, cols_area, wave_value):
    radius = distances(rows_xyz, rows_area, cols_xyz, cols_area)[3]
    phase = wave_value * radius
    factor = 1.0 / (four_pi * radius)
    return (jnp.cos(phase) * factor, jnp.sin(phase) * factor)


def slope_parts(rows_xyz, rows_area, cols_xyz, cols_area, cols_move, wave_value):
    diff_x, diff_y, diff_z, radius = distances(rows_xyz, rows_area, cols_xyz, cols_area)
    along_move = (
        diff_x * cols_move[0][None, :]
        + diff_y * cols_move[1][None, :]
        + diff_z * cols_move[2][None, :]
    )
    phase = wave_value * radius
    cosine_part = jnp.cos(phase)
    sine_part = jnp.sin(phase)
    factor = along_move / (four_pi * radius * radius * radius)
    return ((-cosine_part - phase * sine_part) * factor, (phase * cosine_part - sine_part) * factor)


def contract_first(matrix, vector):
    return lax.dot_general(matrix, vector, (((0,), (0,)), ((), ())), precision=highest)


def conj_columns(real_part, imag_part, vector, zone_count):
    left_part = contract_first(real_part, vector)
    right_part = contract_first(imag_part, vector)
    return jnp.concatenate(
        [
            left_part[:, :zone_count] + right_part[:, zone_count:],
            left_part[:, zone_count:] - right_part[:, :zone_count],
        ],
        1,
    )


def inner_parts(left_part, right_part, zone_count):
    left_re, left_im = (left_part[:, :zone_count], left_part[:, zone_count:])
    right_re, right_im = (right_part[:, :zone_count], right_part[:, zone_count:])
    return (
        jnp.sum(left_re * right_re + left_im * right_im, 0),
        jnp.sum(left_re * right_im - left_im * right_re, 0),
    )


def square_sum(vector):
    return jnp.sum(vector * vector, 0).reshape(2, -1).sum(0)


def complex_scale(scale_re, scale_im, vector, zone_count):
    vec_re, vec_im = (vector[:, :zone_count], vector[:, zone_count:])
    return jnp.concatenate(
        [scale_re * vec_re - scale_im * vec_im, scale_re * vec_im + scale_im * vec_re], 1
    )


def least_squares(
    start_norm,
    first_re,
    first_im,
    first_norm,
    cross_re,
    cross_im,
    second_re,
    second_im,
    second_norm,
):
    gram_one = first_re * first_re + first_im * first_im + first_norm * first_norm
    gram_off_re = first_re * cross_re + first_im * cross_im + first_norm * second_re
    gram_off_im = first_re * cross_im - first_im * cross_re + first_norm * second_im
    gram_two = (
        cross_re * cross_re
        + cross_im * cross_im
        + second_re * second_re
        + second_im * second_im
        + second_norm * second_norm
    )
    rhs_one_re = start_norm * first_re
    rhs_one_im = -start_norm * first_im
    rhs_two_re = start_norm * cross_re
    rhs_two_im = -start_norm * cross_im
    determinant = gram_one * gram_two - gram_off_re * gram_off_re - gram_off_im * gram_off_im
    coef_one_re = (
        gram_two * rhs_one_re - (gram_off_re * rhs_two_re - gram_off_im * rhs_two_im)
    ) / determinant
    coef_one_im = (
        gram_two * rhs_one_im - (gram_off_re * rhs_two_im + gram_off_im * rhs_two_re)
    ) / determinant
    coef_two_re = (
        gram_one * rhs_two_re - (gram_off_re * rhs_one_re + gram_off_im * rhs_one_im)
    ) / determinant
    coef_two_im = (
        gram_one * rhs_two_im - (gram_off_re * rhs_one_im - gram_off_im * rhs_one_re)
    ) / determinant
    return (coef_one_re, coef_one_im, coef_two_re, coef_two_im)


def slope_parts_t(own_xyz, own_area, own_move, all_xyz, all_area, wave_value):
    diff_x = all_xyz[0][None, :] - own_xyz[0][:, None]
    diff_y = all_xyz[1][None, :] - own_xyz[1][:, None]
    diff_z = all_xyz[2][None, :] - own_xyz[2][:, None]
    square = (
        diff_x * diff_x
        + diff_y * diff_y
        + diff_z * diff_z
        + 0.5 * (all_area[None, :] + own_area[:, None])
    )
    radius = jnp.sqrt(square)
    along_move = (
        diff_x * own_move[0][:, None]
        + diff_y * own_move[1][:, None]
        + diff_z * own_move[2][:, None]
    )
    phase = wave_value * radius
    cosine_part = jnp.cos(phase)
    sine_part = jnp.sin(phase)
    factor = along_move / (four_pi * radius * radius * radius)
    return ((-cosine_part - phase * sine_part) * factor, (phase * cosine_part - sine_part) * factor)


LANES = 256


def panel_kernel(slope_mode, wave_ref, own_ref, all_ref, vec_ref, out_ref):
    wave_value = wave_ref[0]
    own_total = own_ref.shape[0]
    panel_total = all_ref.shape[1]
    width = LANES if panel_total % LANES == 0 else 128
    chunk_count = panel_total // width

    def row_block(block, carry):
        first = pl.multiple_of(block * 8, 8)
        own = own_ref[pl.ds(first, 8), :]
        own_x = jnp.broadcast_to(own[:, 0:1], (8, width))
        own_y = jnp.broadcast_to(own[:, 1:2], (8, width))
        own_z = jnp.broadcast_to(own[:, 2:3], (8, width))
        own_a = jnp.broadcast_to(own[:, 3:4], (8, width))
        if slope_mode:
            move_x = jnp.broadcast_to(own[:, 4:5], (8, width))
            move_y = jnp.broadcast_to(own[:, 5:6], (8, width))
            move_z = jnp.broadcast_to(own[:, 6:7], (8, width))

        def lane_block(chunk, sums):
            start = pl.multiple_of(chunk * width, width)
            span = pl.ds(start, width)
            diff_x = all_ref[0:1, span] - own_x
            diff_y = all_ref[1:2, span] - own_y
            diff_z = all_ref[2:3, span] - own_z
            square = (
                diff_x * diff_x
                + diff_y * diff_y
                + diff_z * diff_z
                + 0.5 * (all_ref[3:4, span] + own_a)
            )
            radius = jnp.sqrt(square)
            phase = wave_value * radius
            cosine_part = jnp.cos(phase)
            sine_part = jnp.sin(phase)
            if slope_mode:
                along_move = diff_x * move_x + diff_y * move_y + diff_z * move_z
                factor = along_move / (four_pi * radius * radius * radius)
                first_part = (-cosine_part - phase * sine_part) * factor
                second_part = (phase * cosine_part - sine_part) * factor
            else:
                factor = 1.0 / (four_pi * radius)
                first_part = cosine_part * factor
                second_part = sine_part * factor
            zone_count = len(sums) // 2
            new_re = []
            new_im = []
            for zone in range(zone_count):
                vec_re = vec_ref[zone:zone + 1, span]
                vec_im = vec_ref[zone_count + zone:zone_count + zone + 1, span]
                new_re.append(sums[zone] + first_part * vec_re + second_part * vec_im)
                if slope_mode:
                    new_im.append(sums[zone_count + zone] + second_part * vec_re - first_part * vec_im)
                else:
                    new_im.append(sums[zone_count + zone] + first_part * vec_im - second_part * vec_re)
            return tuple(new_re + new_im)

        columns = vec_ref.shape[0]
        zeros = tuple(jnp.zeros((8, width), jnp.float32) for _ in range(columns))
        sums = lax.fori_loop(0, chunk_count, lane_block, zeros)
        lane = lax.broadcasted_iota(jnp.int32, (8, columns), 1)
        result = jnp.zeros((8, columns), jnp.float32)
        for column in range(columns):
            total = jnp.sum(sums[column], axis=1, keepdims=True)
            result = jnp.where(lane == column, total, result)
        out_ref[pl.ds(first, 8), :] = result
        return carry

    lax.fori_loop(0, own_total // 8, row_block, 0)


def panel_contract(slope_mode, wavenumber, own_table, all_table, vector_rows):
    own_total = own_table.shape[0]
    columns = vector_rows.shape[0]
    panel_total = all_table.shape[1]
    elements = own_total * panel_total
    return pl.pallas_call(
        functools.partial(panel_kernel, slope_mode),
        out_shape=jax.ShapeDtypeStruct((own_total, columns), jnp.float32),
        in_specs=[
            pl.BlockSpec(memory_space=pltpu.SMEM),
            pl.BlockSpec(memory_space=pltpu.VMEM),
            pl.BlockSpec(memory_space=pltpu.VMEM),
            pl.BlockSpec(memory_space=pltpu.VMEM),
        ],
        out_specs=pl.BlockSpec(memory_space=pltpu.VMEM),
        cost_estimate=pl.CostEstimate(
            flops=150 * elements,
            transcendentals=4 * elements,
            bytes_accessed=4 * (own_table.size + all_table.size + vector_rows.size + own_total * columns),
        ),
    )(wavenumber, own_table, all_table, vector_rows)


def chunk_size_of(count, limit):
    return math.gcd(count, limit)


def rows_sum(block_fn, count, limit):
    size = chunk_size_of(count, limit)
    starts = jnp.arange(count // size, dtype=jnp.int32) * size
    return jnp.sum(lax.map(lambda start: block_fn(start, size), starts), 0)


def local(
    centers,
    panel_areas,
    jump_term,
    displacement,
    design_ids,
    primal_field,
    adjoint_start,
    mic_panels,
    wavenumber,
):
    zone_count = adjoint_start.shape[1] // 2
    owned_count = centers.shape[1]
    axes = ("row", "col")
    wave_value = wavenumber[0]
    packed = jnp.concatenate([centers.T, panel_areas[:, None], adjoint_start], 1)
    gathered = lax.all_gather(packed, axes, axis=0, tiled=True)
    panel_total = gathered.shape[0]
    all_xyz = gathered[:, :3].T
    all_area = gathered[:, 3]
    start_full = gathered[:, 4:]
    all_table = gathered[:, :4].T
    own_table = jnp.concatenate(
        [centers.T, panel_areas[:, None], displacement.T, jnp.zeros((owned_count, 1), jnp.float32)], 1
    )

    def apply_adjoint(vector_full, vector_own):
        summed = panel_contract(False, wavenumber, own_table, all_table, vector_full.T)
        return panel_areas[:, None] * summed + jump_term[:, None] * vector_own

    first_panel = (
        lax.axis_index("row") * lax.axis_size("col") + lax.axis_index("col")
    ) * owned_count
    panel_ids = first_panel + jnp.arange(owned_count, dtype=jnp.int32)
    mic_hits = jnp.sum(
        (panel_ids[:, None, None] == mic_panels[None, :, :]).astype(jnp.float32), axis=2
    )
    right_side = jnp.concatenate(
        [mic_hits * primal_field[0][:, None], mic_hits * primal_field[1][:, None]], 1
    )
    residual = right_side - apply_adjoint(start_full, adjoint_start)
    residual_full = lax.all_gather(residual, axes, axis=0, tiled=True)
    start_norm = jnp.sqrt(square_sum(residual_full))
    start_scale = jnp.concatenate([start_norm, start_norm])[None, :]
    basis_one = residual / start_scale
    basis_one_full = residual_full / start_scale
    image_one = apply_adjoint(basis_one_full, basis_one)
    image_one_full = lax.all_gather(image_one, axes, axis=0, tiled=True)
    first_re, first_im = inner_parts(basis_one_full, image_one_full, zone_count)
    lean_one_full = image_one_full - complex_scale(first_re, first_im, basis_one_full, zone_count)
    lean_one = image_one - complex_scale(first_re, first_im, basis_one, zone_count)
    first_norm = jnp.sqrt(square_sum(lean_one_full))
    first_scale = jnp.concatenate([first_norm, first_norm])[None, :]
    basis_two = lean_one / first_scale
    basis_two_full = lean_one_full / first_scale
    image_two = apply_adjoint(basis_two_full, basis_two)
    image_two_full = lax.all_gather(image_two, axes, axis=0, tiled=True)
    cross_re, cross_im = inner_parts(basis_one_full, image_two_full, zone_count)
    second_re, second_im = inner_parts(basis_two_full, image_two_full, zone_count)
    lean_two_full = (
        image_two_full
        - complex_scale(cross_re, cross_im, basis_one_full, zone_count)
        - complex_scale(second_re, second_im, basis_two_full, zone_count)
    )
    second_norm = jnp.sqrt(square_sum(lean_two_full))
    coef_one_re, coef_one_im, coef_two_re, coef_two_im = least_squares(
        start_norm,
        first_re,
        first_im,
        first_norm,
        cross_re,
        cross_im,
        second_re,
        second_im,
        second_norm,
    )
    adjoint_field = (
        adjoint_start
        + complex_scale(coef_one_re, coef_one_im, basis_one, zone_count)
        + complex_scale(coef_two_re, coef_two_im, basis_two, zone_count)
    )
    field_full = (
        start_full
        + complex_scale(coef_one_re, coef_one_im, basis_one_full, zone_count)
        + complex_scale(coef_two_re, coef_two_im, basis_two_full, zone_count)
    )

    contracted = panel_contract(True, wavenumber, own_table, all_table, field_full.T)
    contrib = panel_areas[:, None] * (
        primal_field[0][:, None] * contracted[:, :zone_count]
        - primal_field[1][:, None] * contracted[:, zone_count:]
    )
    onehot = (design_ids[:, None] == jnp.arange(DESIGN, dtype=jnp.int32)[None, :]).astype(
        jnp.float32
    )
    local_sums = contract_first(contrib, onehot)
    sensitivity = lax.psum(local_sums, axes)
    return (adjoint_field, sensitivity)


def solution(mesh):
    return jax.shard_map(
        local,
        mesh=mesh,
        in_specs=(
            P(None, ("row", "col")),
            P(("row", "col")),
            P(("row", "col")),
            P(None, ("row", "col")),
            P(("row", "col")),
            P(None, ("row", "col")),
            P(("row", "col"), None),
            P(),
            P(),
        ),
        out_specs=(P(("row", "col"), None), P()),
        check_vma=False,
    )
```

profile of v0, /device:TPU:0, one launch (start us, length us, event | category | flops | bytes accessed | tf_op | source)
XLA Modules:
  0.0 647.0 jit_solution(9464304466326948958)
XLA Ops:
  2.0 0.7 copy-done.9
  3.4 0.7 copy-done.5
  4.1 0.6 copy-done.3
  4.8 0.8 copy.98.own_ref
  6.0 45.4 %all-gather = f32[32,296,12]{1,2,0:T(8,128)S(1)} all-gather(f32[1,296,12]{1,2,0:T(8,128)S(1)} %maximum_bitcast_fusion), channel_id=1, replica_groups=mesh['row'=8,'col'=4] {'row','col'}, dimensions={0}, use_global_device_ids=true | all-gather | bytes 468864 | tf_op jit(solution)/shard_map/all_gather | solution.py:275
  52.0 0.7 slice_bitcast_fusion.1.all_ref
  52.6 0.7 slice_bitcast_fusion.vec_ref
  53.4 106.2 %shard_map.104 = f32[296,8]{1,0:T(8,128)} custom-call(f32[1]{0:T(128)S(6)} %copy.144.wave_ref, f32[296,8]{1,0:T(8,128)} %copy.98.own_ref, f32[4,9472]{1,0:T(4,128)} %slice_bitcast_fusion.1.all_ref, f32[8,9472]{1,0:T(8,128)} %slice_bitcast_fusion.vec_ref), custom_call_target="tpu_custom_call" | custom-call | flops 420556800 | bytes 473600 | tf_op jit(solution)/shard_map/pallas_call | solution.py:231
  159.6 1.1 maximum_subtract_fusion.2
  160.7 37.7 %all-gather.1 = f32[32,296,8]{1,2,0:T(8,128)S(1)} all-gather(f32[1,296,8]{1,2,0:T(8,128)S(1)} %copy.101), channel_id=1, replica_groups=mesh['row'=8,'col'=4] {'row','col'}, dimensions={0}, use_global_device_ids=true | all-gather | bytes 312576 | tf_op jit(solution)/shard_map/all_gather | solution.py:300
  199.3 0.8 fusion.15.vec_ref
  200.1 106.2 %shard_map.105 = f32[296,8]{1,0:T(8,128)} custom-call(f32[1]{0:T(128)S(6)} %copy.144.wave_ref, f32[296,8]{1,0:T(8,128)} %copy.98.own_ref, f32[4,9472]{1,0:T(4,128)} %slice_bitcast_fusion.1.all_ref, f32[8,9472]{1,0:T(8,128)} %fusion.15.vec_ref), custom_call_target="tpu_custom_call" | custom-call | flops 420556800 | bytes 473600 | tf_op jit(solution)/shard_map/pallas_call | solution.py:231
  306.3 1.1 fusion.14
  307.4 39.0 %all-gather.2 = f32[32,296,8]{1,2,0:T(8,128)S(1)} all-gather(f32[1,296,8]{1,2,0:T(8,128)S(1)} %copy.104), channel_id=1, replica_groups=mesh['row'=8,'col'=4] {'row','col'}, dimensions={0}, use_global_device_ids=true | all-gather | bytes 312576 | tf_op jit(solution)/shard_map/all_gather | solution.py:306
  347.7 0.8 broadcast_divide_fusion
  348.5 106.2 %shard_map.106 = f32[296,8]{1,0:T(8,128)} custom-call(f32[1]{0:T(128)S(6)} %copy.144.wave_ref, f32[296,8]{1,0:T(8,128)} %copy.98.own_ref, f32[4,9472]{1,0:T(4,128)} %slice_bitcast_fusion.1.all_ref, f32[8,9472]{1,0:T(8,128)} %bitcast.27), custom_call_target="tpu_custom_call" | custom-call | flops 420556800 | bytes 473600 | tf_op jit(solution)/shard_map/pallas_call | solution.py:231
  455.4 0.6 copy-done.1
  456.4 37.7 %all-gather.3 = f32[32,296,8]{1,2,0:T(8,128)S(1)} all-gather(f32[1,296,8]{1,2,0:T(8,128)S(1)} %copy.116), channel_id=1, replica_groups=mesh['row'=8,'col'=4] {'row','col'}, dimensions={0}, use_global_device_ids=true | all-gather | bytes 312576 | tf_op jit(solution)/shard_map/all_gather | solution.py:315
  494.4 0.7 copy-done
  496.6 0.9 fusion.4.vec_ref
  497.5 109.3 %shard_map.107 = f32[296,8]{1,0:T(8,128)} custom-call(f32[1]{0:T(128)S(6)} %copy.144.wave_ref, f32[296,8]{1,0:T(8,128)} %copy.98.own_ref, f32[4,9472]{1,0:T(4,128)} %slice_bitcast_fusion.1.all_ref, f32[8,9472]{1,0:T(8,128)} %fusion.4.vec_ref), custom_call_target="tpu_custom_call" | custom-call | flops 420556800 | bytes 473600 | tf_op jit(solution)/shard_map/pallas_call | solution.py:231
  606.8 1.5 fusion.7
  608.3 37.0 %psum.7 = f32[4,128]{1,0:T(4,128)} all-reduce(f32[4,128]{1,0:T(4,128)S(1)} %fusion.7), channel_id=1, replica_groups=mesh['row'=8,'col'=4] {'row','col'}, use_global_device_ids=true, to_apply=%region_13.0 | all-reduce | flops 512 | bytes 4096 | tf_op jit(solution)/shard_map/psum | solution.py:355
  646.4 0.6 fusion.13
  (86 shorter events, 8.5 us)
Async XLA Ops:
  1.3 0.7 copy-start.4
  2.0 0.7 copy-start.9
  2.6 0.7 copy-start.8
  3.4 0.7 copy-start.5
  3.4 0.7 copy-start.7
  4.1 0.7 copy-start.3
  4.1 0.7 copy-start.6
  455.1 0.9 copy-start.1
  455.2 1.0 copy-start.2
  494.2 1.0 copy-start
  497.5 109.3 %copy-start.10 = (s32[296]{0:T(512)S(1)}, s32[296]{0:T(512)}, u32[]{:S(2)}) copy-start(s32[296]{0:T(512)} %param.13) | copy-start | bytes 3556
where the time goes:
time: 649 us; the launch traced here: 647 us
  Pallas kernels  428 us (66%)
  blocking collectives  197 us (30%)
  local copies, waits for them, and re-layouts  10.7 us (2%)
  other arithmetic  8.57 us (1%)
    pallas_call x4, Pallas kernels, panel_contract(): pl.pallas_call(functools.partial(panel_kernel, slope_mode), out_shape=jax...  428 us
    all_gather x1, blocking collectives, local(): gathered = lax.all_gather(packed, axes, axis=0, tiled=True)  45.4 us
    all_gather x1, blocking collectives, local(): image_one_full = lax.all_gather(image_one, axes, axis=0, tiled=True)  39 us
    all_gather x1, blocking collectives, local(): residual_full = lax.all_gather(residual, axes, axis=0, tiled=True)  37.7 us
    all_gather x1, blocking collectives, local(): image_two_full = lax.all_gather(image_two, axes, axis=0, tiled=True)  37.7 us
    psum x1, blocking collectives, local(): sensitivity = lax.psum(local_sums, axes)  37 us

commit v1 on v0

--- a/solution.py
+++ b/solution.py
@@ -150,18 +150,27 @@
 
 
 LANES = 256
-
-
-def panel_kernel(slope_mode, wave_ref, own_ref, all_ref, vec_ref, out_ref):
+STORE_LIMIT = 24 * 1024 * 1024
+
+
+def panel_kernel(slope_mode, stored_in, store_out, wave_ref, own_ref, all_ref, vec_ref, *refs):
+    if stored_in:
+        real_ref, imag_ref, out_ref = refs
+    elif store_out:
+        out_ref, real_ref, imag_ref = refs
+    else:
+        (out_ref,) = refs
     wave_value = wave_ref[0]
     own_total = own_ref.shape[0]
     panel_total = all_ref.shape[1]
     width = LANES if panel_total % LANES == 0 else 128
     chunk_count = panel_total // width
+    needs_geometry = slope_mode or not stored_in
 
     def row_block(block, carry):
         first = pl.multiple_of(block * 8, 8)
-        own = own_ref[pl.ds(first, 8), :]
+        rows = pl.ds(first, 8)
+        own = own_ref[rows, :]
         own_x = jnp.broadcast_to(own[:, 0:1], (8, width))
         own_y = jnp.broadcast_to(own[:, 1:2], (8, width))
         own_z = jnp.broadcast_to(own[:, 2:3], (8, width))
@@ -174,28 +183,44 @@
         def lane_block(chunk, sums):
             start = pl.multiple_of(chunk * width, width)
             span = pl.ds(start, width)
-            diff_x = all_ref[0:1, span] - own_x
-            diff_y = all_ref[1:2, span] - own_y
-            diff_z = all_ref[2:3, span] - own_z
-            square = (
-                diff_x * diff_x
-                + diff_y * diff_y
-                + diff_z * diff_z
-                + 0.5 * (all_ref[3:4, span] + own_a)
-            )
-            radius = jnp.sqrt(square)
-            phase = wave_value * radius
-            cosine_part = jnp.cos(phase)
-            sine_part = jnp.sin(phase)
-            if slope_mode:
-                along_move = diff_x * move_x + diff_y * move_y + diff_z * move_z
-                factor = along_move / (four_pi * radius * radius * radius)
-                first_part = (-cosine_part - phase * sine_part) * factor
-                second_part = (phase * cosine_part - sine_part) * factor
+            if needs_geometry:
+                diff_x = all_ref[0:1, span] - own_x
+                diff_y = all_ref[1:2, span] - own_y
+                diff_z = all_ref[2:3, span] - own_z
+                square = (
+                    diff_x * diff_x
+                    + diff_y * diff_y
+                    + diff_z * diff_z
+                    + 0.5 * (all_ref[3:4, span] + own_a)
+                )
+                radius = jnp.sqrt(square)
+                phase = wave_value * radius
+            if stored_in:
+                real_part = real_ref[rows, span]
+                imag_part = imag_ref[rows, span]
+                if slope_mode:
+                    along_move = diff_x * move_x + diff_y * move_y + diff_z * move_z
+                    factor = along_move / square
+                    first_part = (-real_part - phase * imag_part) * factor
+                    second_part = (phase * real_part - imag_part) * factor
+                else:
+                    first_part = real_part
+                    second_part = imag_part
             else:
-                factor = 1.0 / (four_pi * radius)
-                first_part = cosine_part * factor
-                second_part = sine_part * factor
+                cosine_part = jnp.cos(phase)
+                sine_part = jnp.sin(phase)
+                if slope_mode:
+                    along_move = diff_x * move_x + diff_y * move_y + diff_z * move_z
+                    factor = along_move / (four_pi * radius * radius * radius)
+                    first_part = (-cosine_part - phase * sine_part) * factor
+                    second_part = (phase * cosine_part - sine_part) * factor
+                else:
+                    factor = 1.0 / (four_pi * radius)
+                    first_part = cosine_part * factor
+                    second_part = sine_part * factor
+                if store_out:
+                    real_ref[rows, span] = first_part
+                    imag_ref[rows, span] = second_part
             zone_count = len(sums) // 2
             new_re = []
             new_im = []
@@ -217,33 +242,49 @@
         for column in range(columns):
             total = jnp.sum(sums[column], axis=1, keepdims=True)
             result = jnp.where(lane == column, total, result)
-        out_ref[pl.ds(first, 8), :] = result
+        out_ref[rows, :] = result
         return carry
 
     lax.fori_loop(0, own_total // 8, row_block, 0)
 
 
-def panel_contract(slope_mode, wavenumber, own_table, all_table, vector_rows):
+def panel_contract(slope_mode, wavenumber, own_table, all_table, vector_rows, stored=None, store_out=False):
     own_total = own_table.shape[0]
     columns = vector_rows.shape[0]
     panel_total = all_table.shape[1]
     elements = own_total * panel_total
+    stored_in = stored is not None
+    operands = [wavenumber, own_table, all_table, vector_rows]
+    out_shape = [jax.ShapeDtypeStruct((own_total, columns), jnp.float32)]
+    matrix_bytes = 0
+    if stored_in:
+        operands += list(stored)
+        matrix_bytes = 8 * elements
+    if store_out:
+        out_shape += [jax.ShapeDtypeStruct((own_total, panel_total), jnp.float32)] * 2
+        matrix_bytes = 8 * elements
+    vmem = pl.BlockSpec(memory_space=pltpu.VMEM)
+    params = {}
+    if matrix_bytes:
+        params["compiler_params"] = pltpu.CompilerParams(vmem_limit_bytes=matrix_bytes + 16 * 1024 * 1024)
+    if stored_in and not slope_mode:
+        flops, transcendentals = 32 * elements, 0
+    elif stored_in:
+        flops, transcendentals = 60 * elements, 2 * elements
+    else:
+        flops, transcendentals = 150 * elements, 4 * elements
     return pl.pallas_call(
-        functools.partial(panel_kernel, slope_mode),
-        out_shape=jax.ShapeDtypeStruct((own_total, columns), jnp.float32),
-        in_specs=[
-            pl.BlockSpec(memory_space=pltpu.SMEM),
-            pl.BlockSpec(memory_space=pltpu.VMEM),
-            pl.BlockSpec(memory_space=pltpu.VMEM),
-            pl.BlockSpec(memory_space=pltpu.VMEM),
-        ],
-        out_specs=pl.BlockSpec(memory_space=pltpu.VMEM),
+        functools.partial(panel_kernel, slope_mode, stored_in, store_out),
+        out_shape=tuple(out_shape) if store_out else out_shape[0],
+        in_specs=[pl.BlockSpec(memory_space=pltpu.SMEM)] + [vmem] * (len(operands) - 1),
+        out_specs=tuple([vmem] * len(out_shape)) if store_out else vmem,
         cost_estimate=pl.CostEstimate(
-            flops=150 * elements,
-            transcendentals=4 * elements,
-            bytes_accessed=4 * (own_table.size + all_table.size + vector_rows.size + own_total * columns),
+            flops=flops,
+            transcendentals=transcendentals,
+            bytes_accessed=4 * (own_table.size + all_table.size + vector_rows.size + own_total * columns) + matrix_bytes,
         ),
-    )(wavenumber, own_table, all_table, vector_rows)
+        **params,
+    )(*operands)
 
 
 def chunk_size_of(count, limit):
@@ -282,8 +323,19 @@
         [centers.T, panel_areas[:, None], displacement.T, jnp.zeros((owned_count, 1), jnp.float32)], 1
     )
 
+    store = 8 * owned_count * panel_total <= STORE_LIMIT
+    saved = []
+
     def apply_adjoint(vector_full, vector_own):
-        summed = panel_contract(False, wavenumber, own_table, all_table, vector_full.T)
+        if store and saved:
+            summed = panel_contract(False, wavenumber, own_table, all_table, vector_full.T, stored=saved)
+        elif store:
+            summed, real_part, imag_part = panel_contract(
+                False, wavenumber, own_table, all_table, vector_full.T, store_out=True
+            )
+            saved.extend([real_part, imag_part])
+        else:
+            summed = panel_contract(False, wavenumber, own_table, all_table, vector_full.T)
         return panel_areas[:, None] * summed + jump_term[:, None] * vector_own
 
     first_panel = (
@@ -343,7 +395,7 @@
         + complex_scale(coef_two_re, coef_two_im, basis_two_full, zone_count)
     )
 
-    contracted = panel_contract(True, wavenumber, own_table, all_table, field_full.T)
+    contracted = panel_contract(True, wavenumber, own_table, all_table, field_full.T, stored=saved or None)
     contrib = panel_areas[:, None] * (
         primal_field[0][:, None] * contracted[:, :zone_count]
         - primal_field[1][:, None] * contracted[:, zone_count:]

time: 649 us -> 445 us (0.69)
  Pallas kernels: 428 us -> 216 us
  local copies, waits for them, and re-layouts: 10.7 us -> 22.3 us
    pallas_call x4, Pallas kernels: 428 us -> 216 us  [panel_contract(): pl.pallas_call(functools.partial(panel_kernel, slope_mode, stored_in, sto...]
    unnamed x29 -> x23, local copies, waits for them, and re-layouts: 5.93 us -> 18 us
where the time goes in v1:
time: 445 us; the launch traced here: 444 us
  Pallas kernels  216 us (49%)
  blocking collectives  197 us (44%)
  local copies, waits for them, and re-layouts  22.3 us (5%)
  other arithmetic  6.86 us (2%)
    pallas_call x4, Pallas kernels, panel_contract(): pl.pallas_call(functools.partial(panel_kernel, slope_mode, stored_in, sto...  216 us
    all_gather x1, blocking collectives, local(): gathered = lax.all_gather(packed, axes, axis=0, tiled=True)  45.4 us
    all_gather x1, blocking collectives, local(): image_one_full = lax.all_gather(image_one, axes, axis=0, tiled=True)  39 us
    all_gather x1, blocking collectives, local(): residual_full = lax.all_gather(residual, axes, axis=0, tiled=True)  37.7 us
    all_gather x1, blocking collectives, local(): image_two_full = lax.all_gather(image_two, axes, axis=0, tiled=True)  37.7 us
    psum x1, blocking collectives, local(): sensitivity = lax.psum(local_sums, axes)  36.9 us
    unnamed x23, local copies, waits for them, and re-layouts  18 us

profile of v1, /device:TPU:0, one launch (start us, length us, event | category | flops | bytes accessed | tf_op | source)
XLA Modules:
  0.0 443.7 jit_solution(9035498118566063158)
XLA Ops:
  1.4 0.7 broadcast_in_dim.4
  2.0 0.8 convert_reduce_fusion
  2.8 0.8 slice_reduce_fusion.1
  3.6 0.8 maximum_maximum_fusion
  4.4 0.7 maximum_bitcast_fusion
  5.5 45.4 %all-gather = f32[32,296,12]{1,2,0:T(8,128)S(1)} all-gather(f32[1,296,12]{1,2,0:T(8,128)S(1)} %maximum_bitcast_fusion), channel_id=1, replica_groups=mesh['row'=8,'col'=4] {'row','col'}, dimensions={0}, use_global_device_ids=true | all-gather | bytes 468864 | tf_op jit(solution)/shard_map/all_gather | solution.py:316
  51.1 0.4 reshape.168
  51.6 108.6 %shard_map.104 = (f32[296,8]{1,0:T(8,128)S(1)}, f32[296,9472]{1,0:T(8,128)S(1)}, f32[296,9472]{1,0:T(8,128)}) custom-call(f32[1]{0:T(128)S(6)} %copy.149.wave_ref, f32[296,8]{1,0:T(8,128)S(1)} %copy.102.own_ref, f32[4,9472]{1,0:T(4,128)S(1)} %slice_bitcast_fusion.1.all_ref, f32[8,9472]{1,0:T(8,128)S(1)} %slice_bitcast_fusion.vec_ref), custom_call_target="tpu_custom_call" | custom-call | flops 420556800 | bytes 22903296 | tf_op jit(solution)/shard_map/pallas_call | solution.py:276
  160.2 4.1 copy-done
  164.9 37.7 %all-gather.1 = f32[32,296,8]{1,2,0:T(8,128)S(1)} all-gather(f32[1,296,8]{1,2,0:T(8,128)S(1)} %copy.106), channel_id=1, replica_groups=mesh['row'=8,'col'=4] {'row','col'}, dimensions={0}, use_global_device_ids=true | all-gather | bytes 312576 | tf_op jit(solution)/shard_map/all_gather | solution.py:352
  203.5 4.2 copy-done.1
  207.7 28.0 %shard_map.105 = f32[296,8]{1,0:T(8,128)S(1)} custom-call(f32[1]{0:T(128)S(6)} %copy.149.wave_ref, f32[296,8]{1,0:T(8,128)S(1)} %copy.102.own_ref, f32[4,9472]{1,0:T(4,128)S(1)} %slice_bitcast_fusion.1.all_ref, f32[8,9472]{1,0:T(8,128)S(1)} %fusion.16.vec_ref, f32[296,9472]{1,0:T(8,128)S(1)} %copy-done.1, f32[296,9472]{1,0:T(8,128)} %get-tuple-element.7.refs_1_), custom_call_target="tpu_custom_call" | custom-call | flops 89718784 | bytes 22903296 | tf_op jit(solution)/shard_map/pallas_call | solution.py:276
  236.0 39.0 %all-gather.2 = f32[32,296,8]{1,2,0:T(8,128)S(1)} all-gather(f32[1,296,8]{1,2,0:T(8,128)S(1)} %copy.109), channel_id=1, replica_groups=mesh['row'=8,'col'=4] {'row','col'}, dimensions={0}, use_global_device_ids=true | all-gather | bytes 312576 | tf_op jit(solution)/shard_map/all_gather | solution.py:358
  275.3 0.3 subtract_reduce_fusion.2
  276.3 4.2 copy-done.2
  280.5 28.0 %shard_map.106 = f32[296,8]{1,0:T(8,128)S(1)} custom-call(f32[1]{0:T(128)S(6)} %copy.149.wave_ref, f32[296,8]{1,0:T(8,128)S(1)} %copy.102.own_ref, f32[4,9472]{1,0:T(4,128)S(1)} %slice_bitcast_fusion.1.all_ref, f32[8,9472]{1,0:T(8,128)S(1)} %bitcast.28, f32[296,9472]{1,0:T(8,128)S(1)} %copy-done.2, f32[296,9472]{1,0:T(8,128)} %get-tuple-element.7.refs_1_), custom_call_target="tpu_custom_call" | custom-call | flops 89718784 | bytes 22903296 | tf_op jit(solution)/shard_map/pallas_call | solution.py:276
  309.5 37.7 %all-gather.3 = f32[32,296,8]{1,2,0:T(8,128)S(1)} all-gather(f32[1,296,8]{1,2,0:T(8,128)S(1)} %copy.121), channel_id=1, replica_groups=mesh['row'=8,'col'=4] {'row','col'}, dimensions={0}, use_global_device_ids=true | all-gather | bytes 312576 | tf_op jit(solution)/shard_map/all_gather | solution.py:367
  347.5 0.5 add_reduce_fusion
  348.3 0.3 fusion.2
  349.2 4.2 copy-done.3
  353.3 51.1 %shard_map.107 = f32[296,8]{1,0:T(8,128)S(1)} custom-call(f32[1]{0:T(128)S(6)} %copy.149.wave_ref, f32[296,8]{1,0:T(8,128)S(1)} %copy.102.own_ref, f32[4,9472]{1,0:T(4,128)S(1)} %slice_bitcast_fusion.1.all_ref, f32[8,9472]{1,0:T(8,128)S(1)} %fusion.4.vec_ref, f32[296,9472]{1,0:T(8,128)S(1)} %copy-done.3, f32[296,9472]{1,0:T(8,128)} %get-tuple-element.7.refs_1_), custom_call_target="tpu_custom_call" | custom-call | flops 168222720 | bytes 22903296 | tf_op jit(solution)/shard_map/pallas_call | solution.py:276
  404.4 0.5 fusion.7
  404.9 36.9 %psum.7 = f32[4,128]{1,0:T(4,128)} all-reduce(f32[4,128]{1,0:T(4,128)S(1)} %fusion.7), channel_id=1, replica_groups=mesh['row'=8,'col'=4] {'row','col'}, use_global_device_ids=true, to_apply=%region_13.0 | all-reduce | flops 512 | bytes 4096 | tf_op jit(solution)/shard_map/psum | solution.py:407
  443.0 0.6 fusion.13
  (82 shorter events, 6.6 us)
Async XLA Ops:
  51.5 112.8 %copy-start.5 = (f32[296]{0:T(512)S(1)}, f32[296]{0:T(512)}, u32[]{:S(2)}) copy-start(f32[296]{0:T(512)} %param.10) | copy-start | bytes 3556
  51.5 113.0 %copy-start.4 = (f32[296,8]{0,1:T(8,128)S(1)}, f32[296,8]{0,1:T(8,128)}, u32[]{:S(2)}) copy-start(f32[296,8]{0,1:T(8,128)} %param.15) | copy-start | bytes 28420
  51.5 113.0 %copy-start.6 = (f32[296]{0:T(512)S(1)}, f32[296]{0:T(512)}, u32[]{:S(2)}) copy-start(f32[296]{0:T(512)} %param.11) | copy-start | bytes 3556
  160.2 4.1 copy-start
  203.5 4.2 copy-start.1
  276.3 4.2 copy-start.2
  349.2 4.2 copy-start.3
  353.3 51.1 %copy-start.7 = (s32[296]{0:T(512)S(1)}, s32[296]{0:T(512)}, u32[]{:S(2)}) copy-start(s32[296]{0:T(512)} %param.13) | copy-start | bytes 3556

commit v2 on v1

--- a/solution.py
+++ b/solution.py
@@ -287,6 +287,23 @@
     )(*operands)
 
 
+def gather_axis(vector, name):
+    count = lax.axis_size(name)
+    if count > 8:
+        return lax.all_gather(vector, name, axis=0, tiled=True)
+    index = lax.axis_index(name)
+    parts = [vector]
+    for shift in range(1, count):
+        parts.append(lax.ppermute(vector, name, [(i, (i + shift) % count) for i in range(count)]))
+    stacked = jnp.stack([parts[(-offset) % count] for offset in range(count)])
+    ordered = jnp.roll(stacked, index, axis=0)
+    return ordered.reshape((count * vector.shape[0],) + vector.shape[1:])
+
+
+def gather_panels(vector):
+    return gather_axis(gather_axis(vector, "col"), "row")
+
+
 def chunk_size_of(count, limit):
     return math.gcd(count, limit)
 
@@ -313,7 +330,7 @@
     axes = ("row", "col")
     wave_value = wavenumber[0]
     packed = jnp.concatenate([centers.T, panel_areas[:, None], adjoint_start], 1)
-    gathered = lax.all_gather(packed, axes, axis=0, tiled=True)
+    gathered = gather_panels(packed)
     panel_total = gathered.shape[0]
     all_xyz = gathered[:, :3].T
     all_area = gathered[:, 3]
@@ -349,13 +366,13 @@
         [mic_hits * primal_field[0][:, None], mic_hits * primal_field[1][:, None]], 1
     )
     residual = right_side - apply_adjoint(start_full, adjoint_start)
-    residual_full = lax.all_gather(residual, axes, axis=0, tiled=True)
+    residual_full = gather_panels(residual)
     start_norm = jnp.sqrt(square_sum(residual_full))
     start_scale = jnp.concatenate([start_norm, start_norm])[None, :]
     basis_one = residual / start_scale
     basis_one_full = residual_full / start_scale
     image_one = apply_adjoint(basis_one_full, basis_one)
-    image_one_full = lax.all_gather(image_one, axes, axis=0, tiled=True)
+    image_one_full = gather_panels(image_one)
     first_re, first_im = inner_parts(basis_one_full, image_one_full, zone_count)
     lean_one_full = image_one_full - complex_scale(first_re, first_im, basis_one_full, zone_count)
     lean_one = image_one - complex_scale(first_re, first_im, basis_one, zone_count)
@@ -364,7 +381,7 @@
     basis_two = lean_one / first_scale
     basis_two_full = lean_one_full / first_scale
     image_two = apply_adjoint(basis_two_full, basis_two)
-    image_two_full = lax.all_gather(image_two, axes, axis=0, tiled=True)
+    image_two_full = gather_panels(image_two)
     cross_re, cross_im = inner_parts(basis_one_full, image_two_full, zone_count)
     second_re, second_im = inner_parts(basis_two_full, image_two_full, zone_count)
     lean_two_full = (
@@ -404,7 +421,7 @@
         jnp.float32
     )
     local_sums = contract_first(contrib, onehot)
-    sensitivity = lax.psum(local_sums, axes)
+    sensitivity = lax.psum(lax.psum(local_sums, "col"), "row")
     return (adjoint_field, sensitivity)
 
 

time: 445 us -> 402 us (0.903)
  blocking collectives: 197 us -> 30.5 us
  starting transfers between devices: 0 us -> 77 us
  waiting for transfers between devices: 0 us -> 41.5 us
    all_gather x4 -> x0, blocking collectives: 160 us -> none  [the longest x1 45.4 us: local(): gathered = lax.all_gather(packed, axes, axis=0, tiled=True)]
    ppermute x0 -> x40, starting transfers between devices: none -> 77 us  [gather_axis(): lax.ppermute(vector, name, [(i, (i + shift) % count) for i in range(count)])]
    ppermute x0 -> x40, waiting for transfers between devices: none -> 41.5 us  [gather_axis(): lax.ppermute(vector, name, [(i, (i + shift) % count) for i in range(count)])]
    psum x1 -> x2, blocking collectives: 36.9 us -> 30.5 us  [local(): sensitivity = lax.psum(lax.psum(local_sums, 'col'), 'row')]
    unnamed x23 -> x57, local copies, waits for them, and re-layouts: 18 us -> 16.9 us
  transfers between devices with their start and end apart: 0 -> 40, of which waited for: 0 -> 21; matrix products, arithmetic and copies ran while one was open for 0% -> 1% of each run, Pallas kernels for 0% -> 0%
where the time goes in v2:
time: 402 us; the launch traced here: 401 us
  Pallas kernels  216 us (54%)
  starting transfers between devices  77 us (19%)
  waiting for transfers between devices  41.5 us (10%)
  blocking collectives  30.5 us (8%)
  local copies, waits for them, and re-layouts  25.2 us (6%)
  other arithmetic  8.76 us (2%)
    pallas_call x4, Pallas kernels, panel_contract(): pl.pallas_call(functools.partial(panel_kernel, slope_mode, stored_in, sto...  216 us
    ppermute x40, starting transfers between devices, gather_axis(): lax.ppermute(vector, name, [(i, (i + shift) % count) for i in range(count)])  77 us
    ppermute x40, waiting for transfers between devices, gather_axis(): lax.ppermute(vector, name, [(i, (i + shift) % count) for i in range(count)])  41.5 us
    psum x2, blocking collectives, local(): sensitivity = lax.psum(lax.psum(local_sums, 'col'), 'row')  30.5 us
    unnamed x57, local copies, waits for them, and re-layouts  16.9 us
  transfers between devices with their start and end apart: 40, of which 21 were waited for; matrix products, arithmetic and copies ran while one was open for 1% of the time, Pallas kernels for 0%

profile of v2, /device:TPU:0, one launch (start us, length us, event | category | flops | bytes accessed | tf_op | source)
XLA Modules:
  0.0 401.4 jit_solution(4174513619566899120)
XLA Ops:
  2.0 3.0 collective-permute-start.1
  27.5 4.4 %collective-permute-start.5 = (f32[1184,12]{0,1:T(8,128)S(1)}, f32[1184,12]{0,1:T(8,128)S(1)}, u32[]{:S(2)}, u32[]{:S(2)}) collective-permute-start(f32[1184,12]{0,1:T(8,128)S(1)} %reshape.194), channel_id=1, source_target_pairs={{0,20},{4,24},{8,28},{12,0},{16,4},{20,8},{24,12},{28,16},{1,21},{... | collective-permute-start | bytes 170504 | tf_op jit(solution)/shard_map/ppermute | solution.py:297
  31.9 3.4 collective-permute-done.5
  36.3 108.6 %shard_map.104 = (f32[296,8]{1,0:T(8,128)S(1)}, f32[296,9472]{1,0:T(8,128)S(1)}, f32[296,9472]{1,0:T(8,128)}) custom-call(f32[1]{0:T(128)S(6)} %copy.301.wave_ref, f32[296,8]{1,0:T(8,128)S(1)} %copy.190.own_ref, f32[4,9472]{1,0:T(4,128)S(1)} %slice_bitcast_fusion.1.all_ref, f32[8,9472]{1,0:T(8,128)S(1)} %slice_bitcast_fusion.vec_ref), custom_call_target="tpu_custom_call" | custom-call | flops 420556800 | bytes 22903296 | tf_op jit(solution)/shard_map/pallas_call | solution.py:276
  144.9 4.1 %copy-done = f32[296,9472]{1,0:T(8,128)} copy-done((f32[296,9472]{1,0:T(8,128)}, f32[296,9472]{1,0:T(8,128)S(1)}, u32[]{:S(2)}) %copy-start) | copy-done | bytes 11214872
  151.9 3.3 collective-permute-done.12
  164.3 3.8 collective-permute-start.13
  170.8 3.0 collective-permute-done.14
  173.7 3.6 collective-permute-start.15
  179.9 4.2 %copy-done.1 = f32[296,9472]{1,0:T(8,128)S(1)} copy-done((f32[296,9472]{1,0:T(8,128)S(1)}, f32[296,9472]{1,0:T(8,128)}, u32[]{:S(2)}) %copy-start.1) | copy-done | bytes 11214872
  184.0 28.0 %shard_map.105 = f32[296,8]{1,0:T(8,128)S(1)} custom-call(f32[1]{0:T(128)S(6)} %copy.301.wave_ref, f32[296,8]{1,0:T(8,128)S(1)} %copy.190.own_ref, f32[4,9472]{1,0:T(4,128)S(1)} %slice_bitcast_fusion.1.all_ref, f32[8,9472]{1,0:T(8,128)S(1)} %fusion.42.vec_ref, f32[296,9472]{1,0:T(8,128)S(1)} %copy-done.1, f32[296,9472]{1,0:T(8,128)} %get-tuple-element.9.refs_1_), custom_call_target="tpu_custom_call" | custom-call | flops 89718784 | bytes 22903296 | tf_op jit(solution)/shard_map/pallas_call | solution.py:276
  220.7 4.1 %collective-permute-start.29 = (f32[1184,8]{0,1:T(8,128)S(1)}, f32[1184,8]{0,1:T(8,128)S(1)}, u32[]{:S(2)}, u32[]{:S(2)}) collective-permute-start(f32[1184,8]{0,1:T(8,128)S(1)} %reshape.199), channel_id=1, source_target_pairs={{0,4},{4,8},{8,12},{12,16},{16,20},{20,24},{24,28},{28,0},{1,5},{5... | collective-permute-start | bytes 113672 | tf_op jit(solution)/shard_map/ppermute | solution.py:297
  226.9 3.3 collective-permute-start.26
  238.6 3.8 collective-permute-start.25
  246.1 4.2 %copy-done.2 = f32[296,9472]{1,0:T(8,128)S(1)} copy-done((f32[296,9472]{1,0:T(8,128)S(1)}, f32[296,9472]{1,0:T(8,128)}, u32[]{:S(2)}) %copy-start.2) | copy-done | bytes 11214872
  250.3 28.0 %shard_map.106 = f32[296,8]{1,0:T(8,128)S(1)} custom-call(f32[1]{0:T(128)S(6)} %copy.301.wave_ref, f32[296,8]{1,0:T(8,128)S(1)} %copy.190.own_ref, f32[4,9472]{1,0:T(4,128)S(1)} %slice_bitcast_fusion.1.all_ref, f32[8,9472]{1,0:T(8,128)S(1)} %bitcast.135, f32[296,9472]{1,0:T(8,128)S(1)} %copy-done.2, f32[296,9472]{1,0:T(8,128)} %get-tuple-element.9.refs_1_), custom_call_target="tpu_custom_call" | custom-call | flops 89718784 | bytes 22903296 | tf_op jit(solution)/shard_map/pallas_call | solution.py:276
  281.4 3.4 collective-permute-done.32
  287.3 3.9 collective-permute-start.39
  291.2 3.1 collective-permute-start.37
  304.8 3.7 collective-permute-start.35
  313.4 4.2 %copy-done.3 = f32[296,9472]{1,0:T(8,128)S(1)} copy-done((f32[296,9472]{1,0:T(8,128)S(1)}, f32[296,9472]{1,0:T(8,128)}, u32[]{:S(2)}) %copy-start.3) | copy-done | bytes 11214872
  317.6 51.1 %shard_map.107 = f32[296,8]{1,0:T(8,128)S(1)} custom-call(f32[1]{0:T(128)S(6)} %copy.301.wave_ref, f32[296,8]{1,0:T(8,128)S(1)} %copy.190.own_ref, f32[4,9472]{1,0:T(4,128)S(1)} %slice_bitcast_fusion.1.all_ref, f32[8,9472]{1,0:T(8,128)S(1)} %fusion.10.vec_ref, f32[296,9472]{1,0:T(8,128)S(1)} %copy-done.3, f32[296,9472]{1,0:T(8,128)} %get-tuple-element.9.refs_1_), custom_call_target="tpu_custom_call" | custom-call | flops 168222720 | bytes 22903296 | tf_op jit(solution)/shard_map/pallas_call | solution.py:276
  369.2 5.7 %psum.14 = f32[4,128]{1,0:T(4,128)S(1)} all-reduce(f32[4,128]{1,0:T(4,128)S(1)} %fusion.13), channel_id=1, replica_groups=mesh['row'=8,'col'=4] {'col'}, use_global_device_ids=true, to_apply=%region_13.16 | all-reduce | flops 512 | bytes 4096 | tf_op jit(solution)/shard_map/psum | solution.py:424
  374.8 24.8 %psum.15 = f32[4,128]{1,0:T(4,128)} all-reduce(f32[4,128]{1,0:T(4,128)S(1)} %psum.14), channel_id=1, replica_groups=mesh['row'=8,'col'=4] {'row'}, use_global_device_ids=true, to_apply=%region_14.17 | all-reduce | flops 512 | bytes 4096 | tf_op jit(solution)/shard_map/psum | solution.py:424
  (247 shorter events, 86.5 us)
Async XLA Ops:
  2.0 7.8 %collective-permute-start.1 = (f32[296,12]{0,1:T(8,128)S(1)}, f32[296,12]{0,1:T(8,128)S(1)}, u32[]{:S(2)}, u32[]{:S(2)}) collective-permute-start(f32[296,12]{0,1:T(8,128)S(1)} %pad_maximum_fusion), channel_id=1, source_target_pairs={{0,2},{1,3},{2,0},{3,1},{4,6},{5,7},{6,4},{7,5},{8,10},{9,11},{10,... | collective-permute-start | bytes 42632 | tf_op jit(solution)/shard_map/ppermute | solution.py:297
  11.0 24.5 %collective-permute-start.9 = (f32[1184,12]{0,1:T(8,128)S(1)}, f32[1184,12]{0,1:T(8,128)S(1)}, u32[]{:S(2)}, u32[]{:S(2)}) collective-permute-start(f32[1184,12]{0,1:T(8,128)S(1)} %reshape.194), channel_id=1, source_target_pairs={{0,4},{4,8},{8,12},{12,16},{16,20},{20,24},{24,28},{28,0},{1,5},{5... | collective-permute-start | bytes 170504 | tf_op jit(solution)/shard_map/ppermute | solution.py:297
  12.5 22.9 %collective-permute-start.8 = (f32[1184,12]{0,1:T(8,128)S(1)}, f32[1184,12]{0,1:T(8,128)S(1)}, u32[]{:S(2)}, u32[]{:S(2)}) collective-permute-start(f32[1184,12]{0,1:T(8,128)S(1)} %reshape.194), channel_id=1, source_target_pairs={{0,8},{4,12},{8,16},{12,20},{16,24},{20,28},{24,0},{28,4},{1,9},{5... | collective-permute-start | bytes 170504 | tf_op jit(solution)/shard_map/ppermute | solution.py:297
  14.1 21.3 %collective-permute-start.7 = (f32[1184,12]{0,1:T(8,128)S(1)}, f32[1184,12]{0,1:T(8,128)S(1)}, u32[]{:S(2)}, u32[]{:S(2)}) collective-permute-start(f32[1184,12]{0,1:T(8,128)S(1)} %reshape.194), channel_id=1, source_target_pairs={{0,12},{4,16},{8,20},{12,24},{16,28},{20,0},{24,4},{28,8},{1,13},{... | collective-permute-start | bytes 170504 | tf_op jit(solution)/shard_map/ppermute | solution.py:297
  16.6 18.7 %collective-permute-start.6 = (f32[1184,12]{0,1:T(8,128)S(1)}, f32[1184,12]{0,1:T(8,128)S(1)}, u32[]{:S(2)}, u32[]{:S(2)}) collective-permute-start(f32[1184,12]{0,1:T(8,128)S(1)} %reshape.194), channel_id=1, source_target_pairs={{0,16},{4,20},{8,24},{12,28},{16,0},{20,4},{24,8},{28,12},{1,17},{... | collective-permute-start | bytes 170504 | tf_op jit(solution)/shard_map/ppermute | solution.py:297
  27.5 7.9 %collective-permute-start.5 = (f32[1184,12]{0,1:T(8,128)S(1)}, f32[1184,12]{0,1:T(8,128)S(1)}, u32[]{:S(2)}, u32[]{:S(2)}) collective-permute-start(f32[1184,12]{0,1:T(8,128)S(1)} %reshape.194), channel_id=1, source_target_pairs={{0,20},{4,24},{8,28},{12,0},{16,4},{20,8},{24,12},{28,16},{1,21},{... | collective-permute-start | bytes 170504 | tf_op jit(solution)/shard_map/ppermute | solution.py:297
  149.6 6.8 %collective-permute-start.11 = (f32[296,8]{1,0:T(8,128)S(1)}, f32[296,8]{1,0:T(8,128)S(1)}, u32[]{:S(2)}, u32[]{:S(2)}) collective-permute-start(f32[296,8]{1,0:T(8,128)S(1)} %maximum_subtract_fusion.3), channel_id=1, source_target_pairs={{0,2},{1,3},{2,0},{3,1},{4,6},{5,7},{6,4},{7,5},{8,10},{9,11},{10,... | collective-permute-start | bytes 28424 | tf_op jit(solution)/shard_map/ppermute | solution.py:297
  150.4 6.9 %collective-permute-start.10 = (f32[296,8]{1,0:T(8,128)S(1)}, f32[296,8]{1,0:T(8,128)S(1)}, u32[]{:S(2)}, u32[]{:S(2)}) collective-permute-start(f32[296,8]{1,0:T(8,128)S(1)} %maximum_subtract_fusion.3), channel_id=1, source_target_pairs={{0,3},{1,0},{2,1},{3,2},{4,7},{5,4},{6,5},{7,6},{8,11},{9,8},{10,9... | collective-permute-start | bytes 28424 | tf_op jit(solution)/shard_map/ppermute | solution.py:297
  157.7 21.4 %collective-permute-start.19 = (f32[1184,8]{0,1:T(8,128)S(1)}, f32[1184,8]{0,1:T(8,128)S(1)}, u32[]{:S(2)}, u32[]{:S(2)}) collective-permute-start(f32[1184,8]{0,1:T(8,128)S(1)} %reshape.196), channel_id=1, source_target_pairs={{0,4},{4,8},{8,12},{12,16},{16,20},{20,24},{24,28},{28,0},{1,5},{5... | collective-permute-start | bytes 113672 | tf_op jit(solution)/shard_map/ppermute | solution.py:297
  160.4 18.6 %collective-permute-start.18 = (f32[1184,8]{0,1:T(8,128)S(1)}, f32[1184,8]{0,1:T(8,128)S(1)}, u32[]{:S(2)}, u32[]{:S(2)}) collective-permute-start(f32[1184,8]{0,1:T(8,128)S(1)} %reshape.196), channel_id=1, source_target_pairs={{0,8},{4,12},{8,16},{12,20},{16,24},{20,28},{24,0},{28,4},{1,9},{5... | collective-permute-start | bytes 113672 | tf_op jit(solution)/shard_map/ppermute | solution.py:297
  162.1 16.9 %collective-permute-start.17 = (f32[1184,8]{0,1:T(8,128)S(1)}, f32[1184,8]{0,1:T(8,128)S(1)}, u32[]{:S(2)}, u32[]{:S(2)}) collective-permute-start(f32[1184,8]{0,1:T(8,128)S(1)} %reshape.196), channel_id=1, source_target_pairs={{0,12},{4,16},{8,20},{12,24},{16,28},{20,0},{24,4},{28,8},{1,13},{... | collective-permute-start | bytes 113672 | tf_op jit(solution)/shard_map/ppermute | solution.py:297
  162.4 16.5 %collective-permute-start.16 = (f32[1184,8]{0,1:T(8,128)S(1)}, f32[1184,8]{0,1:T(8,128)S(1)}, u32[]{:S(2)}, u32[]{:S(2)}) collective-permute-start(f32[1184,8]{0,1:T(8,128)S(1)} %reshape.196), channel_id=1, source_target_pairs={{0,16},{4,20},{8,24},{12,28},{16,0},{20,4},{24,8},{28,12},{1,17},{... | collective-permute-start | bytes 113672 | tf_op jit(solution)/shard_map/ppermute | solution.py:297
  212.3 6.8 %collective-permute-start.21 = (f32[296,8]{1,0:T(8,128)S(1)}, f32[296,8]{1,0:T(8,128)S(1)}, u32[]{:S(2)}, u32[]{:S(2)}) collective-permute-start(f32[296,8]{1,0:T(8,128)S(1)} %get-tuple-element.28), channel_id=1, source_target_pairs={{0,2},{1,3},{2,0},{3,1},{4,6},{5,7},{6,4},{7,5},{8,10},{9,11},{10,... | collective-permute-start | bytes 28424 | tf_op jit(solution)/shard_map/ppermute | solution.py:297
  213.4 6.9 %collective-permute-start.20 = (f32[296,8]{1,0:T(8,128)S(1)}, f32[296,8]{1,0:T(8,128)S(1)}, u32[]{:S(2)}, u32[]{:S(2)}) collective-permute-start(f32[296,8]{1,0:T(8,128)S(1)} %get-tuple-element.28), channel_id=1, source_target_pairs={{0,3},{1,0},{2,1},{3,2},{4,7},{5,4},{6,5},{7,6},{8,11},{9,8},{10,9... | collective-permute-start | bytes 28424 | tf_op jit(solution)/shard_map/ppermute | solution.py:297
  220.7 23.4 %collective-permute-start.29 = (f32[1184,8]{0,1:T(8,128)S(1)}, f32[1184,8]{0,1:T(8,128)S(1)}, u32[]{:S(2)}, u32[]{:S(2)}) collective-permute-start(f32[1184,8]{0,1:T(8,128)S(1)} %reshape.199), channel_id=1, source_target_pairs={{0,4},{4,8},{8,12},{12,16},{16,20},{20,24},{24,28},{28,0},{1,5},{5... | collective-permute-start | bytes 113672 | tf_op jit(solution)/shard_map/ppermute | solution.py:297
  224.8 19.3 %collective-permute-start.28 = (f32[1184,8]{0,1:T(8,128)S(1)}, f32[1184,8]{0,1:T(8,128)S(1)}, u32[]{:S(2)}, u32[]{:S(2)}) collective-permute-start(f32[1184,8]{0,1:T(8,128)S(1)} %reshape.199), channel_id=1, source_target_pairs={{0,8},{4,12},{8,16},{12,20},{16,24},{20,28},{24,0},{28,4},{1,9},{5... | collective-permute-start | bytes 113672 | tf_op jit(solution)/shard_map/ppermute | solution.py:297
  225.1 19.1 %collective-permute-start.27 = (f32[1184,8]{0,1:T(8,128)S(1)}, f32[1184,8]{0,1:T(8,128)S(1)}, u32[]{:S(2)}, u32[]{:S(2)}) collective-permute-start(f32[1184,8]{0,1:T(8,128)S(1)} %reshape.199), channel_id=1, source_target_pairs={{0,12},{4,16},{8,20},{12,24},{16,28},{20,0},{24,4},{28,8},{1,13},{... | collective-permute-start | bytes 113672 | tf_op jit(solution)/shard_map/ppermute | solution.py:297
  226.9 17.2 %collective-permute-start.26 = (f32[1184,8]{0,1:T(8,128)S(1)}, f32[1184,8]{0,1:T(8,128)S(1)}, u32[]{:S(2)}, u32[]{:S(2)}) collective-permute-start(f32[1184,8]{0,1:T(8,128)S(1)} %reshape.199), channel_id=1, source_target_pairs={{0,16},{4,20},{8,24},{12,28},{16,0},{20,4},{24,8},{28,12},{1,17},{... | collective-permute-start | bytes 113672 | tf_op jit(solution)/shard_map/ppermute | solution.py:297
  279.2 6.8 %collective-permute-start.31 = (f32[296,8]{1,0:T(8,128)S(1)}, f32[296,8]{1,0:T(8,128)S(1)}, u32[]{:S(2)}, u32[]{:S(2)}) collective-permute-start(f32[296,8]{1,0:T(8,128)S(1)} %get-tuple-element.26), channel_id=1, source_target_pairs={{0,2},{1,3},{2,0},{3,1},{4,6},{5,7},{6,4},{7,5},{8,10},{9,11},{10,... | collective-permute-start | bytes 28424 | tf_op jit(solution)/shard_map/ppermute | solution.py:297
  280.0 6.9 %collective-permute-start.30 = (f32[296,8]{1,0:T(8,128)S(1)}, f32[296,8]{1,0:T(8,128)S(1)}, u32[]{:S(2)}, u32[]{:S(2)}) collective-permute-start(f32[296,8]{1,0:T(8,128)S(1)} %get-tuple-element.26), channel_id=1, source_target_pairs={{0,3},{1,0},{2,1},{3,2},{4,7},{5,4},{6,5},{7,6},{8,11},{9,8},{10,9... | collective-permute-start | bytes 28424 | tf_op jit(solution)/shard_map/ppermute | solution.py:297
  287.3 23.0 %collective-permute-start.39 = (f32[1184,8]{0,1:T(8,128)S(1)}, f32[1184,8]{0,1:T(8,128)S(1)}, u32[]{:S(2)}, u32[]{:S(2)}) collective-permute-start(f32[1184,8]{0,1:T(8,128)S(1)} %reshape.202), channel_id=1, source_target_pairs={{0,4},{4,8},{8,12},{12,16},{16,20},{20,24},{24,28},{28,0},{1,5},{5... | collective-permute-start | bytes 113672 | tf_op jit(solution)/shard_map/ppermute | solution.py:297
  291.1 19.1 %collective-permute-start.38 = (f32[1184,8]{0,1:T(8,128)S(1)}, f32[1184,8]{0,1:T(8,128)S(1)}, u32[]{:S(2)}, u32[]{:S(2)}) collective-permute-start(f32[1184,8]{0,1:T(8,128)S(1)} %reshape.202), channel_id=1, source_target_pairs={{0,8},{4,12},{8,16},{12,20},{16,24},{20,28},{24,0},{28,4},{1,9},{5... | collective-permute-start | bytes 113672 | tf_op jit(solution)/shard_map/ppermute | solution.py:297
  291.2 19.1 %collective-permute-start.37 = (f32[1184,8]{0,1:T(8,128)S(1)}, f32[1184,8]{0,1:T(8,128)S(1)}, u32[]{:S(2)}, u32[]{:S(2)}) collective-permute-start(f32[1184,8]{0,1:T(8,128)S(1)} %reshape.202), channel_id=1, source_target_pairs={{0,12},{4,16},{8,20},{12,24},{16,28},{20,0},{24,4},{28,8},{1,13},{... | collective-permute-start | bytes 113672 | tf_op jit(solution)/shard_map/ppermute | solution.py:297
  294.3 16.0 %collective-permute-start.36 = (f32[1184,8]{0,1:T(8,128)S(1)}, f32[1184,8]{0,1:T(8,128)S(1)}, u32[]{:S(2)}, u32[]{:S(2)}) collective-permute-start(f32[1184,8]{0,1:T(8,128)S(1)} %reshape.202), channel_id=1, source_target_pairs={{0,16},{4,20},{8,24},{12,28},{16,0},{20,4},{24,8},{28,12},{1,17},{... | collective-permute-start | bytes 113672 | tf_op jit(solution)/shard_map/ppermute | solution.py:297
  (24 other events, 484.9 us)

commit v3 on v2

--- a/solution.py
+++ b/solution.py
@@ -149,6 +149,33 @@
     return ((-cosine_part - phase * sine_part) * factor, (phase * cosine_part - sine_part) * factor)
 
 
+TWO_OVER_PI = 0.6366197723675814
+HALF_PI_HI = 1.5703125
+HALF_PI_MID = 4.837512969970703125e-4
+HALF_PI_LO = 7.54978995489188216e-8
+
+
+def sin_cos(angle):
+    turns = jnp.floor(angle * TWO_OVER_PI + 0.5)
+    rest = angle - turns * HALF_PI_HI
+    rest = rest - turns * HALF_PI_MID
+    rest = rest - turns * HALF_PI_LO
+    rest2 = rest * rest
+    sine = rest + rest * rest2 * (
+        -1.6666654611e-1 + rest2 * (8.3321608736e-3 + rest2 * (-1.9515295891e-4))
+    )
+    cosine = 1.0 - 0.5 * rest2 + rest2 * rest2 * (
+        4.166664568298827e-2 + rest2 * (-1.388731625493765e-3 + rest2 * 2.443315711809948e-5)
+    )
+    quarter = turns.astype(jnp.int32)
+    swap = (quarter & 1) == 1
+    sine_out = jnp.where(swap, cosine, sine)
+    cosine_out = jnp.where(swap, sine, cosine)
+    sine_out = jnp.where((quarter & 2) == 2, -sine_out, sine_out)
+    cosine_out = jnp.where(((quarter + 1) & 2) == 2, -cosine_out, cosine_out)
+    return sine_out, cosine_out
+
+
 LANES = 256
 STORE_LIMIT = 24 * 1024 * 1024
 
@@ -193,29 +220,29 @@
                     + diff_z * diff_z
                     + 0.5 * (all_ref[3:4, span] + own_a)
                 )
-                radius = jnp.sqrt(square)
+                inverse = lax.rsqrt(square)
+                radius = square * inverse
                 phase = wave_value * radius
             if stored_in:
                 real_part = real_ref[rows, span]
                 imag_part = imag_ref[rows, span]
                 if slope_mode:
                     along_move = diff_x * move_x + diff_y * move_y + diff_z * move_z
-                    factor = along_move / square
+                    factor = along_move * (inverse * inverse)
                     first_part = (-real_part - phase * imag_part) * factor
                     second_part = (phase * real_part - imag_part) * factor
                 else:
                     first_part = real_part
                     second_part = imag_part
             else:
-                cosine_part = jnp.cos(phase)
-                sine_part = jnp.sin(phase)
+                sine_part, cosine_part = sin_cos(phase)
                 if slope_mode:
                     along_move = diff_x * move_x + diff_y * move_y + diff_z * move_z
-                    factor = along_move / (four_pi * radius * radius * radius)
+                    factor = along_move * (inverse * inverse * inverse) * (1.0 / four_pi)
                     first_part = (-cosine_part - phase * sine_part) * factor
                     second_part = (phase * cosine_part - sine_part) * factor
                 else:
-                    factor = 1.0 / (four_pi * radius)
+                    factor = inverse * (1.0 / four_pi)
                     first_part = cosine_part * factor
                     second_part = sine_part * factor
                 if store_out:

time: 402 us -> 362 us (0.900)
  Pallas kernels: 216 us -> 175 us
    pallas_call x4, Pallas kernels: 216 us -> 175 us  [panel_contract(): pl.pallas_call(functools.partial(panel_kernel, slope_mode, stored_in, sto...]
where the time goes in v3:
time: 362 us; the launch traced here: 361 us
  Pallas kernels  175 us (48%)
  starting transfers between devices  77 us (21%)
  waiting for transfers between devices  41.5 us (11%)
  blocking collectives  30.5 us (8%)
  local copies, waits for them, and re-layouts  25.2 us (7%)
  other arithmetic  8.76 us (2%)
    pallas_call x4, Pallas kernels, panel_contract(): pl.pallas_call(functools.partial(panel_kernel, slope_mode, stored_in, sto...  175 us
    ppermute x40, starting transfers between devices, gather_axis(): lax.ppermute(vector, name, [(i, (i + shift) % count) for i in range(count)])  77 us
    ppermute x40, waiting for transfers between devices, gather_axis(): lax.ppermute(vector, name, [(i, (i + shift) % count) for i in range(count)])  41.5 us
    psum x2, blocking collectives, local(): sensitivity = lax.psum(lax.psum(local_sums, 'col'), 'row')  30.5 us
    unnamed x57, local copies, waits for them, and re-layouts  16.9 us
  transfers between devices with their start and end apart: 40, of which 21 were waited for; matrix products, arithmetic and copies ran while one was open for 1% of the time, Pallas kernels for 0%

profile of v3, /device:TPU:0, one launch (start us, length us, event | category | flops | bytes accessed | tf_op | source)
XLA Modules:
  0.0 361.1 jit_solution(17680658142737687075)
XLA Ops:
  2.0 3.0 collective-permute-start.1
  27.5 4.4 %collective-permute-start.5 = (f32[1184,12]{0,1:T(8,128)S(1)}, f32[1184,12]{0,1:T(8,128)S(1)}, u32[]{:S(2)}, u32[]{:S(2)}) collective-permute-start(f32[1184,12]{0,1:T(8,128)S(1)} %reshape.194), channel_id=1, source_target_pairs={{0,20},{4,24},{8,28},{12,0},{16,4},{20,8},{24,12},{28,16},{1,21},{... | collective-permute-start | bytes 170504 | tf_op jit(solution)/shard_map/ppermute | solution.py:324
  31.9 3.4 collective-permute-done.5
  36.3 69.7 %shard_map.104 = (f32[296,8]{1,0:T(8,128)S(1)}, f32[296,9472]{1,0:T(8,128)S(1)}, f32[296,9472]{1,0:T(8,128)}) custom-call(f32[1]{0:T(128)S(6)} %copy.301.wave_ref, f32[296,8]{1,0:T(8,128)S(1)} %copy.190.own_ref, f32[4,9472]{1,0:T(4,128)S(1)} %slice_bitcast_fusion.1.all_ref, f32[8,9472]{1,0:T(8,128)S(1)} %slice_bitcast_fusion.vec_ref), custom_call_target="tpu_custom_call" | custom-call | flops 420556800 | bytes 22903296 | tf_op jit(solution)/shard_map/pallas_call | solution.py:303
  106.0 4.1 %copy-done = f32[296,9472]{1,0:T(8,128)} copy-done((f32[296,9472]{1,0:T(8,128)}, f32[296,9472]{1,0:T(8,128)S(1)}, u32[]{:S(2)}) %copy-start) | copy-done | bytes 11214872
  113.0 3.3 collective-permute-done.12
  125.4 3.8 %collective-permute-start.13 = (f32[1184,8]{0,1:T(8,128)S(1)}, f32[1184,8]{0,1:T(8,128)S(1)}, u32[]{:S(2)}, u32[]{:S(2)}) collective-permute-start(f32[1184,8]{0,1:T(8,128)S(1)} %reshape.196), channel_id=1, source_target_pairs={{0,28},{4,0},{8,4},{12,8},{16,12},{20,16},{24,20},{28,24},{1,29},{... | collective-permute-start | bytes 113672 | tf_op jit(solution)/shard_map/ppermute | solution.py:324
  131.8 3.0 collective-permute-done.14
  134.8 3.6 collective-permute-start.15
  141.0 4.2 %copy-done.1 = f32[296,9472]{1,0:T(8,128)S(1)} copy-done((f32[296,9472]{1,0:T(8,128)S(1)}, f32[296,9472]{1,0:T(8,128)}, u32[]{:S(2)}) %copy-start.1) | copy-done | bytes 11214872
  145.1 28.0 %shard_map.105 = f32[296,8]{1,0:T(8,128)S(1)} custom-call(f32[1]{0:T(128)S(6)} %copy.301.wave_ref, f32[296,8]{1,0:T(8,128)S(1)} %copy.190.own_ref, f32[4,9472]{1,0:T(4,128)S(1)} %slice_bitcast_fusion.1.all_ref, f32[8,9472]{1,0:T(8,128)S(1)} %fusion.42.vec_ref, f32[296,9472]{1,0:T(8,128)S(1)} %copy-done.1, f32[296,9472]{1,0:T(8,128)} %get-tuple-element.9.refs_1_), custom_call_target="tpu_custom_call" | custom-call | flops 89718784 | bytes 22903296 | tf_op jit(solution)/shard_map/pallas_call | solution.py:303
  181.8 4.1 %collective-permute-start.29 = (f32[1184,8]{0,1:T(8,128)S(1)}, f32[1184,8]{0,1:T(8,128)S(1)}, u32[]{:S(2)}, u32[]{:S(2)}) collective-permute-start(f32[1184,8]{0,1:T(8,128)S(1)} %reshape.199), channel_id=1, source_target_pairs={{0,4},{4,8},{8,12},{12,16},{16,20},{20,24},{24,28},{28,0},{1,5},{5... | collective-permute-start | bytes 113672 | tf_op jit(solution)/shard_map/ppermute | solution.py:324
  188.0 3.3 collective-permute-start.26
  199.7 3.8 %collective-permute-start.25 = (f32[1184,8]{0,1:T(8,128)S(1)}, f32[1184,8]{0,1:T(8,128)S(1)}, u32[]{:S(2)}, u32[]{:S(2)}) collective-permute-start(f32[1184,8]{0,1:T(8,128)S(1)} %reshape.199), channel_id=1, source_target_pairs={{0,20},{4,24},{8,28},{12,0},{16,4},{20,8},{24,12},{28,16},{1,21},{... | collective-permute-start | bytes 113672 | tf_op jit(solution)/shard_map/ppermute | solution.py:324
  207.2 4.2 %copy-done.2 = f32[296,9472]{1,0:T(8,128)S(1)} copy-done((f32[296,9472]{1,0:T(8,128)S(1)}, f32[296,9472]{1,0:T(8,128)}, u32[]{:S(2)}) %copy-start.2) | copy-done | bytes 11214872
  211.4 28.0 %shard_map.106 = f32[296,8]{1,0:T(8,128)S(1)} custom-call(f32[1]{0:T(128)S(6)} %copy.301.wave_ref, f32[296,8]{1,0:T(8,128)S(1)} %copy.190.own_ref, f32[4,9472]{1,0:T(4,128)S(1)} %slice_bitcast_fusion.1.all_ref, f32[8,9472]{1,0:T(8,128)S(1)} %bitcast.135, f32[296,9472]{1,0:T(8,128)S(1)} %copy-done.2, f32[296,9472]{1,0:T(8,128)} %get-tuple-element.9.refs_1_), custom_call_target="tpu_custom_call" | custom-call | flops 89718784 | bytes 22903296 | tf_op jit(solution)/shard_map/pallas_call | solution.py:303
  242.5 3.4 collective-permute-done.32
  248.4 3.9 %collective-permute-start.39 = (f32[1184,8]{0,1:T(8,128)S(1)}, f32[1184,8]{0,1:T(8,128)S(1)}, u32[]{:S(2)}, u32[]{:S(2)}) collective-permute-start(f32[1184,8]{0,1:T(8,128)S(1)} %reshape.202), channel_id=1, source_target_pairs={{0,4},{4,8},{8,12},{12,16},{16,20},{20,24},{24,28},{28,0},{1,5},{5... | collective-permute-start | bytes 113672 | tf_op jit(solution)/shard_map/ppermute | solution.py:324
  252.3 3.1 collective-permute-start.37
  265.9 3.7 %collective-permute-start.35 = (f32[1184,8]{0,1:T(8,128)S(1)}, f32[1184,8]{0,1:T(8,128)S(1)}, u32[]{:S(2)}, u32[]{:S(2)}) collective-permute-start(f32[1184,8]{0,1:T(8,128)S(1)} %reshape.202), channel_id=1, source_target_pairs={{0,20},{4,24},{8,28},{12,0},{16,4},{20,8},{24,12},{28,16},{1,21},{... | collective-permute-start | bytes 113672 | tf_op jit(solution)/shard_map/ppermute | solution.py:324
  274.5 4.2 %copy-done.3 = f32[296,9472]{1,0:T(8,128)S(1)} copy-done((f32[296,9472]{1,0:T(8,128)S(1)}, f32[296,9472]{1,0:T(8,128)}, u32[]{:S(2)}) %copy-start.3) | copy-done | bytes 11214872
  278.7 49.7 %shard_map.107 = f32[296,8]{1,0:T(8,128)S(1)} custom-call(f32[1]{0:T(128)S(6)} %copy.301.wave_ref, f32[296,8]{1,0:T(8,128)S(1)} %copy.190.own_ref, f32[4,9472]{1,0:T(4,128)S(1)} %slice_bitcast_fusion.1.all_ref, f32[8,9472]{1,0:T(8,128)S(1)} %fusion.10.vec_ref, f32[296,9472]{1,0:T(8,128)S(1)} %copy-done.3, f32[296,9472]{1,0:T(8,128)} %get-tuple-element.9.refs_1_), custom_call_target="tpu_custom_call" | custom-call | flops 168222720 | bytes 22903296 | tf_op jit(solution)/shard_map/pallas_call | solution.py:303
  328.9 5.7 %psum.14 = f32[4,128]{1,0:T(4,128)S(1)} all-reduce(f32[4,128]{1,0:T(4,128)S(1)} %fusion.13), channel_id=1, replica_groups=mesh['row'=8,'col'=4] {'col'}, use_global_device_ids=true, to_apply=%region_13.16 | all-reduce | flops 512 | bytes 4096 | tf_op jit(solution)/shard_map/psum | solution.py:451
  334.6 24.8 %psum.15 = f32[4,128]{1,0:T(4,128)} all-reduce(f32[4,128]{1,0:T(4,128)S(1)} %psum.14), channel_id=1, replica_groups=mesh['row'=8,'col'=4] {'row'}, use_global_device_ids=true, to_apply=%region_14.17 | all-reduce | flops 512 | bytes 4096 | tf_op jit(solution)/shard_map/psum | solution.py:451
  (247 shorter events, 86.5 us)
Async XLA Ops:
  2.0 7.8 %collective-permute-start.1 = (f32[296,12]{0,1:T(8,128)S(1)}, f32[296,12]{0,1:T(8,128)S(1)}, u32[]{:S(2)}, u32[]{:S(2)}) collective-permute-start(f32[296,12]{0,1:T(8,128)S(1)} %pad_maximum_fusion), channel_id=1, source_target_pairs={{0,2},{1,3},{2,0},{3,1},{4,6},{5,7},{6,4},{7,5},{8,10},{9,11},{10,... | collective-permute-start | bytes 42632 | tf_op jit(solution)/shard_map/ppermute | solution.py:324
  11.0 24.5 %collective-permute-start.9 = (f32[1184,12]{0,1:T(8,128)S(1)}, f32[1184,12]{0,1:T(8,128)S(1)}, u32[]{:S(2)}, u32[]{:S(2)}) collective-permute-start(f32[1184,12]{0,1:T(8,128)S(1)} %reshape.194), channel_id=1, source_target_pairs={{0,4},{4,8},{8,12},{12,16},{16,20},{20,24},{24,28},{28,0},{1,5},{5... | collective-permute-start | bytes 170504 | tf_op jit(solution)/shard_map/ppermute | solution.py:324
  12.5 22.9 %collective-permute-start.8 = (f32[1184,12]{0,1:T(8,128)S(1)}, f32[1184,12]{0,1:T(8,128)S(1)}, u32[]{:S(2)}, u32[]{:S(2)}) collective-permute-start(f32[1184,12]{0,1:T(8,128)S(1)} %reshape.194), channel_id=1, source_target_pairs={{0,8},{4,12},{8,16},{12,20},{16,24},{20,28},{24,0},{28,4},{1,9},{5... | collective-permute-start | bytes 170504 | tf_op jit(solution)/shard_map/ppermute | solution.py:324
  14.1 21.3 %collective-permute-start.7 = (f32[1184,12]{0,1:T(8,128)S(1)}, f32[1184,12]{0,1:T(8,128)S(1)}, u32[]{:S(2)}, u32[]{:S(2)}) collective-permute-start(f32[1184,12]{0,1:T(8,128)S(1)} %reshape.194), channel_id=1, source_target_pairs={{0,12},{4,16},{8,20},{12,24},{16,28},{20,0},{24,4},{28,8},{1,13},{... | collective-permute-start | bytes 170504 | tf_op jit(solution)/shard_map/ppermute | solution.py:324
  16.6 18.7 %collective-permute-start.6 = (f32[1184,12]{0,1:T(8,128)S(1)}, f32[1184,12]{0,1:T(8,128)S(1)}, u32[]{:S(2)}, u32[]{:S(2)}) collective-permute-start(f32[1184,12]{0,1:T(8,128)S(1)} %reshape.194), channel_id=1, source_target_pairs={{0,16},{4,20},{8,24},{12,28},{16,0},{20,4},{24,8},{28,12},{1,17},{... | collective-permute-start | bytes 170504 | tf_op jit(solution)/shard_map/ppermute | solution.py:324
  27.5 7.9 %collective-permute-start.5 = (f32[1184,12]{0,1:T(8,128)S(1)}, f32[1184,12]{0,1:T(8,128)S(1)}, u32[]{:S(2)}, u32[]{:S(2)}) collective-permute-start(f32[1184,12]{0,1:T(8,128)S(1)} %reshape.194), channel_id=1, source_target_pairs={{0,20},{4,24},{8,28},{12,0},{16,4},{20,8},{24,12},{28,16},{1,21},{... | collective-permute-start | bytes 170504 | tf_op jit(solution)/shard_map/ppermute | solution.py:324
  110.7 6.8 %collective-permute-start.11 = (f32[296,8]{1,0:T(8,128)S(1)}, f32[296,8]{1,0:T(8,128)S(1)}, u32[]{:S(2)}, u32[]{:S(2)}) collective-permute-start(f32[296,8]{1,0:T(8,128)S(1)} %maximum_subtract_fusion.3), channel_id=1, source_target_pairs={{0,2},{1,3},{2,0},{3,1},{4,6},{5,7},{6,4},{7,5},{8,10},{9,11},{10,... | collective-permute-start | bytes 28424 | tf_op jit(solution)/shard_map/ppermute | solution.py:324
  111.5 6.9 %collective-permute-start.10 = (f32[296,8]{1,0:T(8,128)S(1)}, f32[296,8]{1,0:T(8,128)S(1)}, u32[]{:S(2)}, u32[]{:S(2)}) collective-permute-start(f32[296,8]{1,0:T(8,128)S(1)} %maximum_subtract_fusion.3), channel_id=1, source_target_pairs={{0,3},{1,0},{2,1},{3,2},{4,7},{5,4},{6,5},{7,6},{8,11},{9,8},{10,9... | collective-permute-start | bytes 28424 | tf_op jit(solution)/shard_map/ppermute | solution.py:324
  118.8 21.4 %collective-permute-start.19 = (f32[1184,8]{0,1:T(8,128)S(1)}, f32[1184,8]{0,1:T(8,128)S(1)}, u32[]{:S(2)}, u32[]{:S(2)}) collective-permute-start(f32[1184,8]{0,1:T(8,128)S(1)} %reshape.196), channel_id=1, source_target_pairs={{0,4},{4,8},{8,12},{12,16},{16,20},{20,24},{24,28},{28,0},{1,5},{5... | collective-permute-start | bytes 113672 | tf_op jit(solution)/shard_map/ppermute | solution.py:324
  121.5 18.6 %collective-permute-start.18 = (f32[1184,8]{0,1:T(8,128)S(1)}, f32[1184,8]{0,1:T(8,128)S(1)}, u32[]{:S(2)}, u32[]{:S(2)}) collective-permute-start(f32[1184,8]{0,1:T(8,128)S(1)} %reshape.196), channel_id=1, source_target_pairs={{0,8},{4,12},{8,16},{12,20},{16,24},{20,28},{24,0},{28,4},{1,9},{5... | collective-permute-start | bytes 113672 | tf_op jit(solution)/shard_map/ppermute | solution.py:324
  123.2 16.9 %collective-permute-start.17 = (f32[1184,8]{0,1:T(8,128)S(1)}, f32[1184,8]{0,1:T(8,128)S(1)}, u32[]{:S(2)}, u32[]{:S(2)}) collective-permute-start(f32[1184,8]{0,1:T(8,128)S(1)} %reshape.196), channel_id=1, source_target_pairs={{0,12},{4,16},{8,20},{12,24},{16,28},{20,0},{24,4},{28,8},{1,13},{... | collective-permute-start | bytes 113672 | tf_op jit(solution)/shard_map/ppermute | solution.py:324
  123.5 16.5 %collective-permute-start.16 = (f32[1184,8]{0,1:T(8,128)S(1)}, f32[1184,8]{0,1:T(8,128)S(1)}, u32[]{:S(2)}, u32[]{:S(2)}) collective-permute-start(f32[1184,8]{0,1:T(8,128)S(1)} %reshape.196), channel_id=1, source_target_pairs={{0,16},{4,20},{8,24},{12,28},{16,0},{20,4},{24,8},{28,12},{1,17},{... | collective-permute-start | bytes 113672 | tf_op jit(solution)/shard_map/ppermute | solution.py:324
  173.3 6.8 %collective-permute-start.21 = (f32[296,8]{1,0:T(8,128)S(1)}, f32[296,8]{1,0:T(8,128)S(1)}, u32[]{:S(2)}, u32[]{:S(2)}) collective-permute-start(f32[296,8]{1,0:T(8,128)S(1)} %get-tuple-element.28), channel_id=1, source_target_pairs={{0,2},{1,3},{2,0},{3,1},{4,6},{5,7},{6,4},{7,5},{8,10},{9,11},{10,... | collective-permute-start | bytes 28424 | tf_op jit(solution)/shard_map/ppermute | solution.py:324
  174.5 6.9 %collective-permute-start.20 = (f32[296,8]{1,0:T(8,128)S(1)}, f32[296,8]{1,0:T(8,128)S(1)}, u32[]{:S(2)}, u32[]{:S(2)}) collective-permute-start(f32[296,8]{1,0:T(8,128)S(1)} %get-tuple-element.28), channel_id=1, source_target_pairs={{0,3},{1,0},{2,1},{3,2},{4,7},{5,4},{6,5},{7,6},{8,11},{9,8},{10,9... | collective-permute-start | bytes 28424 | tf_op jit(solution)/shard_map/ppermute | solution.py:324
  181.8 23.4 %collective-permute-start.29 = (f32[1184,8]{0,1:T(8,128)S(1)}, f32[1184,8]{0,1:T(8,128)S(1)}, u32[]{:S(2)}, u32[]{:S(2)}) collective-permute-start(f32[1184,8]{0,1:T(8,128)S(1)} %reshape.199), channel_id=1, source_target_pairs={{0,4},{4,8},{8,12},{12,16},{16,20},{20,24},{24,28},{28,0},{1,5},{5... | collective-permute-start | bytes 113672 | tf_op jit(solution)/shard_map/ppermute | solution.py:324
  185.9 19.3 %collective-permute-start.28 = (f32[1184,8]{0,1:T(8,128)S(1)}, f32[1184,8]{0,1:T(8,128)S(1)}, u32[]{:S(2)}, u32[]{:S(2)}) collective-permute-start(f32[1184,8]{0,1:T(8,128)S(1)} %reshape.199), channel_id=1, source_target_pairs={{0,8},{4,12},{8,16},{12,20},{16,24},{20,28},{24,0},{28,4},{1,9},{5... | collective-permute-start | bytes 113672 | tf_op jit(solution)/shard_map/ppermute | solution.py:324
  186.1 19.1 %collective-permute-start.27 = (f32[1184,8]{0,1:T(8,128)S(1)}, f32[1184,8]{0,1:T(8,128)S(1)}, u32[]{:S(2)}, u32[]{:S(2)}) collective-permute-start(f32[1184,8]{0,1:T(8,128)S(1)} %reshape.199), channel_id=1, source_target_pairs={{0,12},{4,16},{8,20},{12,24},{16,28},{20,0},{24,4},{28,8},{1,13},{... | collective-permute-start | bytes 113672 | tf_op jit(solution)/shard_map/ppermute | solution.py:324
  188.0 17.2 %collective-permute-start.26 = (f32[1184,8]{0,1:T(8,128)S(1)}, f32[1184,8]{0,1:T(8,128)S(1)}, u32[]{:S(2)}, u32[]{:S(2)}) collective-permute-start(f32[1184,8]{0,1:T(8,128)S(1)} %reshape.199), channel_id=1, source_target_pairs={{0,16},{4,20},{8,24},{12,28},{16,0},{20,4},{24,8},{28,12},{1,17},{... | collective-permute-start | bytes 113672 | tf_op jit(solution)/shard_map/ppermute | solution.py:324
  240.3 6.8 %collective-permute-start.31 = (f32[296,8]{1,0:T(8,128)S(1)}, f32[296,8]{1,0:T(8,128)S(1)}, u32[]{:S(2)}, u32[]{:S(2)}) collective-permute-start(f32[296,8]{1,0:T(8,128)S(1)} %get-tuple-element.26), channel_id=1, source_target_pairs={{0,2},{1,3},{2,0},{3,1},{4,6},{5,7},{6,4},{7,5},{8,10},{9,11},{10,... | collective-permute-start | bytes 28424 | tf_op jit(solution)/shard_map/ppermute | solution.py:324
  241.1 6.9 %collective-permute-start.30 = (f32[296,8]{1,0:T(8,128)S(1)}, f32[296,8]{1,0:T(8,128)S(1)}, u32[]{:S(2)}, u32[]{:S(2)}) collective-permute-start(f32[296,8]{1,0:T(8,128)S(1)} %get-tuple-element.26), channel_id=1, source_target_pairs={{0,3},{1,0},{2,1},{3,2},{4,7},{5,4},{6,5},{7,6},{8,11},{9,8},{10,9... | collective-permute-start | bytes 28424 | tf_op jit(solution)/shard_map/ppermute | solution.py:324
  248.4 23.0 %collective-permute-start.39 = (f32[1184,8]{0,1:T(8,128)S(1)}, f32[1184,8]{0,1:T(8,128)S(1)}, u32[]{:S(2)}, u32[]{:S(2)}) collective-permute-start(f32[1184,8]{0,1:T(8,128)S(1)} %reshape.202), channel_id=1, source_target_pairs={{0,4},{4,8},{8,12},{12,16},{16,20},{20,24},{24,28},{28,0},{1,5},{5... | collective-permute-start | bytes 113672 | tf_op jit(solution)/shard_map/ppermute | solution.py:324
  252.2 19.1 %collective-permute-start.38 = (f32[1184,8]{0,1:T(8,128)S(1)}, f32[1184,8]{0,1:T(8,128)S(1)}, u32[]{:S(2)}, u32[]{:S(2)}) collective-permute-start(f32[1184,8]{0,1:T(8,128)S(1)} %reshape.202), channel_id=1, source_target_pairs={{0,8},{4,12},{8,16},{12,20},{16,24},{20,28},{24,0},{28,4},{1,9},{5... | collective-permute-start | bytes 113672 | tf_op jit(solution)/shard_map/ppermute | solution.py:324
  252.3 19.1 %collective-permute-start.37 = (f32[1184,8]{0,1:T(8,128)S(1)}, f32[1184,8]{0,1:T(8,128)S(1)}, u32[]{:S(2)}, u32[]{:S(2)}) collective-permute-start(f32[1184,8]{0,1:T(8,128)S(1)} %reshape.202), channel_id=1, source_target_pairs={{0,12},{4,16},{8,20},{12,24},{16,28},{20,0},{24,4},{28,8},{1,13},{... | collective-permute-start | bytes 113672 | tf_op jit(solution)/shard_map/ppermute | solution.py:324
  255.4 16.0 %collective-permute-start.36 = (f32[1184,8]{0,1:T(8,128)S(1)}, f32[1184,8]{0,1:T(8,128)S(1)}, u32[]{:S(2)}, u32[]{:S(2)}) collective-permute-start(f32[1184,8]{0,1:T(8,128)S(1)} %reshape.202), channel_id=1, source_target_pairs={{0,16},{4,20},{8,24},{12,28},{16,0},{20,4},{24,8},{28,12},{1,17},{... | collective-permute-start | bytes 113672 | tf_op jit(solution)/shard_map/ppermute | solution.py:324
  (24 other events, 366.8 us)

commit v4 on v3

--- a/solution.py
+++ b/solution.py
@@ -248,18 +248,16 @@
                 if store_out:
                     real_ref[rows, span] = first_part
                     imag_ref[rows, span] = second_part
-            zone_count = len(sums) // 2
-            new_re = []
-            new_im = []
+            zone_count = len(sums) // 3
+            both_parts = first_part + second_part
+            new_sums = []
             for zone in range(zone_count):
-                vec_re = vec_ref[zone:zone + 1, span]
-                vec_im = vec_ref[zone_count + zone:zone_count + zone + 1, span]
-                new_re.append(sums[zone] + first_part * vec_re + second_part * vec_im)
-                if slope_mode:
-                    new_im.append(sums[zone_count + zone] + second_part * vec_re - first_part * vec_im)
-                else:
-                    new_im.append(sums[zone_count + zone] + first_part * vec_im - second_part * vec_re)
-            return tuple(new_re + new_im)
+                new_sums.append(sums[zone] + first_part * vec_ref[zone:zone + 1, span])
+            for zone in range(zone_count, 2 * zone_count):
+                new_sums.append(sums[zone] + second_part * vec_ref[zone:zone + 1, span])
+            for zone in range(2 * zone_count, 3 * zone_count):
+                new_sums.append(sums[zone] + both_parts * vec_ref[zone:zone + 1, span])
+            return tuple(new_sums)
 
         columns = vec_ref.shape[0]
         zeros = tuple(jnp.zeros((8, width), jnp.float32) for _ in range(columns))
@@ -275,7 +273,27 @@
     lax.fori_loop(0, own_total // 8, row_block, 0)
 
 
-def panel_contract(slope_mode, wavenumber, own_table, all_table, vector_rows, stored=None, store_out=False):
+def panel_contract(slope_mode, wavenumber, own_table, all_table, vector_full, stored=None, store_out=False):
+    zone_count = vector_full.shape[1] // 2
+    vector_rows = jnp.concatenate(
+        [vector_full.T, (vector_full[:, :zone_count] - vector_full[:, zone_count:]).T], 0
+    )
+    outs = panel_call(slope_mode, wavenumber, own_table, all_table, vector_rows, stored, store_out)
+    sums = outs[0] if store_out else outs
+    first_sum = sums[:, :zone_count]
+    second_sum = sums[:, zone_count:2 * zone_count]
+    both_sum = sums[:, 2 * zone_count:]
+    if slope_mode:
+        imag_sum = both_sum - first_sum + second_sum
+    else:
+        imag_sum = first_sum - second_sum - both_sum
+    combined = jnp.concatenate([first_sum + second_sum, imag_sum], 1)
+    if store_out:
+        return (combined,) + tuple(outs[1:])
+    return combined
+
+
+def panel_call(slope_mode, wavenumber, own_table, all_table, vector_rows, stored, store_out):
     own_total = own_table.shape[0]
     columns = vector_rows.shape[0]
     panel_total = all_table.shape[1]
@@ -372,14 +390,14 @@
 
     def apply_adjoint(vector_full, vector_own):
         if store and saved:
-            summed = panel_contract(False, wavenumber, own_table, all_table, vector_full.T, stored=saved)
+            summed = panel_contract(False, wavenumber, own_table, all_table, vector_full, stored=saved)
         elif store:
             summed, real_part, imag_part = panel_contract(
-                False, wavenumber, own_table, all_table, vector_full.T, store_out=True
+                False, wavenumber, own_table, all_table, vector_full, store_out=True
             )
             saved.extend([real_part, imag_part])
         else:
-            summed = panel_contract(False, wavenumber, own_table, all_table, vector_full.T)
+            summed = panel_contract(False, wavenumber, own_table, all_table, vector_full)
         return panel_areas[:, None] * summed + jump_term[:, None] * vector_own
 
     first_panel = (
@@ -439,7 +457,7 @@
         + complex_scale(coef_two_re, coef_two_im, basis_two_full, zone_count)
     )
 
-    contracted = panel_contract(True, wavenumber, own_table, all_table, field_full.T, stored=saved or None)
+    contracted = panel_contract(True, wavenumber, own_table, all_table, field_full, stored=saved or None)
     contrib = panel_areas[:, None] * (
         primal_field[0][:, None] * contracted[:, :zone_count]
         - primal_field[1][:, None] * contracted[:, zone_count:]

time: 362 us -> 353 us (0.975)
  waiting for transfers between devices: 41.5 us -> 29.9 us
  Pallas kernels: 175 us -> 179 us
    ppermute x40, waiting for transfers between devices: 41.5 us -> 29.9 us  [gather_axis(): lax.ppermute(vector, name, [(i, (i + shift) % count) for i in range(count)])]
    pallas_call x4, Pallas kernels: 175 us -> 179 us  [panel_call(): pl.pallas_call(functools.partial(panel_kernel, slope_mode, stored_in, sto...]
  transfers between devices with their start and end apart: 40 -> 40, of which waited for: 21 -> 20; matrix products, arithmetic and copies ran while one was open for 1% -> 1% of each run, Pallas kernels for 0% -> 0%
where the time goes in v4:
time: 353 us; the launch traced here: 352 us
  Pallas kernels  179 us (51%)
  starting transfers between devices  77.1 us (22%)
  blocking collectives  30.5 us (9%)
  waiting for transfers between devices  29.9 us (8%)
  local copies, waits for them, and re-layouts  23.5 us (7%)
  other arithmetic  8.89 us (3%)
    pallas_call x4, Pallas kernels, panel_call(): pl.pallas_call(functools.partial(panel_kernel, slope_mode, stored_in, sto...  179 us
    ppermute x40, starting transfers between devices, gather_axis(): lax.ppermute(vector, name, [(i, (i + shift) % count) for i in range(count)])  77.1 us
    psum x2, blocking collectives, local(): sensitivity = lax.psum(lax.psum(local_sums, 'col'), 'row')  30.5 us
    ppermute x40, waiting for transfers between devices, gather_axis(): lax.ppermute(vector, name, [(i, (i + shift) % count) for i in range(count)])  29.9 us
    unnamed x57, local copies, waits for them, and re-layouts  17.1 us
  transfers between devices with their start and end apart: 40, of which 20 were waited for; matrix products, arithmetic and copies ran while one was open for 1% of the time, Pallas kernels for 0%

profile of v4, /device:TPU:0, one launch (start us, length us, event | category | flops | bytes accessed | tf_op | source)
XLA Modules:
  0.0 351.7 jit_solution(3716760639014171079)
XLA Ops:
  2.0 3.0 collective-permute-start.1
  24.3 2.9 collective-permute-done.4
  27.2 4.4 %collective-permute-start.5 = (f32[1184,12]{0,1:T(8,128)S(1)}, f32[1184,12]{0,1:T(8,128)S(1)}, u32[]{:S(2)}, u32[]{:S(2)}) collective-permute-start(f32[1184,12]{0,1:T(8,128)S(1)} %reshape.194), channel_id=1, source_target_pairs={{0,20},{4,24},{8,28},{12,0},{16,4},{20,8},{24,12},{28,16},{1,21},{... | collective-permute-start | bytes 170504 | tf_op jit(solution)/shard_map/ppermute | solution.py:342
  31.6 3.4 collective-permute-done.5
  36.1 70.7 %shard_map.104 = (f32[296,12]{1,0:T(8,128)S(1)}, f32[296,9472]{1,0:T(8,128)S(1)}, f32[296,9472]{1,0:T(8,128)}) custom-call(f32[1]{0:T(128)S(6)} %copy.219.wave_ref, f32[296,8]{1,0:T(8,128)S(1)} %copy.147.own_ref, f32[4,9472]{1,0:T(4,128)S(1)} %get-tuple-element.33.all_ref, f32[12,9472]{1,0:T(8,128)S(1)} %pad_maximum_fusion.vec_ref), custom_call_target="tpu_custom_call" | custom-call | flops 420556800 | bytes 23059584 | tf_op jit(solution)/shard_map/pallas_call | solution.py:321
  106.8 4.1 %copy-done = f32[296,9472]{1,0:T(8,128)} copy-done((f32[296,9472]{1,0:T(8,128)}, f32[296,9472]{1,0:T(8,128)S(1)}, u32[]{:S(2)}) %copy-start) | copy-done | bytes 11214872
  122.2 3.8 %collective-permute-start.13 = (f32[1184,8]{0,1:T(8,128)S(1)}, f32[1184,8]{0,1:T(8,128)S(1)}, u32[]{:S(2)}, u32[]{:S(2)}) collective-permute-start(f32[1184,8]{0,1:T(8,128)S(1)} %reshape.196), channel_id=1, source_target_pairs={{0,28},{4,0},{8,4},{12,8},{16,12},{20,16},{24,20},{28,24},{1,29},{... | collective-permute-start | bytes 113672 | tf_op jit(solution)/shard_map/ppermute | solution.py:342
  128.7 2.9 collective-permute-done.14
  131.7 3.6 %collective-permute-start.15 = (f32[1184,8]{0,1:T(8,128)S(1)}, f32[1184,8]{0,1:T(8,128)S(1)}, u32[]{:S(2)}, u32[]{:S(2)}) collective-permute-start(f32[1184,8]{0,1:T(8,128)S(1)} %reshape.196), channel_id=1, source_target_pairs={{0,20},{4,24},{8,28},{12,0},{16,4},{20,8},{24,12},{28,16},{1,21},{... | collective-permute-start | bytes 113672 | tf_op jit(solution)/shard_map/ppermute | solution.py:342
  138.0 4.2 %copy-done.1 = f32[296,9472]{1,0:T(8,128)S(1)} copy-done((f32[296,9472]{1,0:T(8,128)S(1)}, f32[296,9472]{1,0:T(8,128)}, u32[]{:S(2)}) %copy-start.1) | copy-done | bytes 11214872
  142.2 29.0 %shard_map.105 = f32[296,12]{1,0:T(8,128)S(1)} custom-call(f32[1]{0:T(128)S(6)} %copy.219.wave_ref, f32[296,8]{1,0:T(8,128)S(1)} %copy.147.own_ref, f32[4,9472]{1,0:T(4,128)S(1)} %get-tuple-element.33.all_ref, f32[12,9472]{1,0:T(8,128)S(1)} %pad_maximum_fusion.1.vec_ref, f32[296,9472]{1,0:T(8,128)S(1)} %copy-done.1, f32[296,9472]{1,0:T(8,128)} %get-tuple-element.9.refs_1_), custom_call_target="tpu_custom_call" | custom-call | flops 89718784 | bytes 23059584 | tf_op jit(solution)/shard_map/pallas_call | solution.py:321
  175.7 4.0 %collective-permute-start.29 = (f32[1184,8]{0,1:T(8,128)S(1)}, f32[1184,8]{0,1:T(8,128)S(1)}, u32[]{:S(2)}, u32[]{:S(2)}) collective-permute-start(f32[1184,8]{0,1:T(8,128)S(1)} %reshape.199), channel_id=1, source_target_pairs={{0,4},{4,8},{8,12},{12,16},{16,20},{20,24},{24,28},{28,0},{1,5},{5... | collective-permute-start | bytes 113672 | tf_op jit(solution)/shard_map/ppermute | solution.py:342
  182.1 3.1 collective-permute-start.26
  193.5 3.8 %collective-permute-start.25 = (f32[1184,8]{0,1:T(8,128)S(1)}, f32[1184,8]{0,1:T(8,128)S(1)}, u32[]{:S(2)}, u32[]{:S(2)}) collective-permute-start(f32[1184,8]{0,1:T(8,128)S(1)} %reshape.199), channel_id=1, source_target_pairs={{0,20},{4,24},{8,28},{12,0},{16,4},{20,8},{24,12},{28,16},{1,21},{... | collective-permute-start | bytes 113672 | tf_op jit(solution)/shard_map/ppermute | solution.py:342
  201.2 4.2 %copy-done.2 = f32[296,9472]{1,0:T(8,128)S(1)} copy-done((f32[296,9472]{1,0:T(8,128)S(1)}, f32[296,9472]{1,0:T(8,128)}, u32[]{:S(2)}) %copy-start.2) | copy-done | bytes 11214872
  205.3 29.0 %shard_map.106 = f32[296,12]{1,0:T(8,128)S(1)} custom-call(f32[1]{0:T(128)S(6)} %copy.219.wave_ref, f32[296,8]{1,0:T(8,128)S(1)} %copy.147.own_ref, f32[4,9472]{1,0:T(4,128)S(1)} %get-tuple-element.33.all_ref, f32[12,9472]{1,0:T(8,128)S(1)} %pad_maximum_fusion.2.vec_ref, f32[296,9472]{1,0:T(8,128)S(1)} %copy-done.2, f32[296,9472]{1,0:T(8,128)} %get-tuple-element.9.refs_1_), custom_call_target="tpu_custom_call" | custom-call | flops 89718784 | bytes 23059584 | tf_op jit(solution)/shard_map/pallas_call | solution.py:321
  239.0 3.6 %collective-permute-start.39 = (f32[1184,8]{0,1:T(8,128)S(1)}, f32[1184,8]{0,1:T(8,128)S(1)}, u32[]{:S(2)}, u32[]{:S(2)}) collective-permute-start(f32[1184,8]{0,1:T(8,128)S(1)} %reshape.202), channel_id=1, source_target_pairs={{0,4},{4,8},{8,12},{12,16},{16,20},{20,24},{24,28},{28,0},{1,5},{5... | collective-permute-start | bytes 113672 | tf_op jit(solution)/shard_map/ppermute | solution.py:342
  242.8 3.3 collective-permute-start.37
  248.1 2.7 collective-permute-start.33
  256.4 3.8 %collective-permute-start.35 = (f32[1184,8]{0,1:T(8,128)S(1)}, f32[1184,8]{0,1:T(8,128)S(1)}, u32[]{:S(2)}, u32[]{:S(2)}) collective-permute-start(f32[1184,8]{0,1:T(8,128)S(1)} %reshape.202), channel_id=1, source_target_pairs={{0,20},{4,24},{8,28},{12,0},{16,4},{20,8},{24,12},{28,16},{1,21},{... | collective-permute-start | bytes 113672 | tf_op jit(solution)/shard_map/ppermute | solution.py:342
  265.3 4.2 %copy-done.3 = f32[296,9472]{1,0:T(8,128)S(1)} copy-done((f32[296,9472]{1,0:T(8,128)S(1)}, f32[296,9472]{1,0:T(8,128)}, u32[]{:S(2)}) %copy-start.3) | copy-done | bytes 11214872
  269.5 50.6 %shard_map.107 = f32[296,12]{1,0:T(8,128)S(1)} custom-call(f32[1]{0:T(128)S(6)} %copy.219.wave_ref, f32[296,8]{1,0:T(8,128)S(1)} %copy.147.own_ref, f32[4,9472]{1,0:T(4,128)S(1)} %get-tuple-element.33.all_ref, f32[12,9472]{1,0:T(8,128)S(1)} %pad_maximum_fusion.3.vec_ref, f32[296,9472]{1,0:T(8,128)S(1)} %copy-done.3, f32[296,9472]{1,0:T(8,128)} %get-tuple-element.9.refs_1_), custom_call_target="tpu_custom_call" | custom-call | flops 168222720 | bytes 23059584 | tf_op jit(solution)/shard_map/pallas_call | solution.py:321
  320.6 5.6 %psum.14 = f32[4,128]{1,0:T(4,128)S(1)} all-reduce(f32[4,128]{1,0:T(4,128)S(1)} %fusion.14), channel_id=1, replica_groups=mesh['row'=8,'col'=4] {'col'}, use_global_device_ids=true, to_apply=%region_13.16 | all-reduce | flops 512 | bytes 4096 | tf_op jit(solution)/shard_map/psum | solution.py:469
  326.3 24.8 %psum.15 = f32[4,128]{1,0:T(4,128)} all-reduce(f32[4,128]{1,0:T(4,128)S(1)} %psum.14), channel_id=1, replica_groups=mesh['row'=8,'col'=4] {'row'}, use_global_device_ids=true, to_apply=%region_14.17 | all-reduce | flops 512 | bytes 4096 | tf_op jit(solution)/shard_map/psum | solution.py:469
  (227 shorter events, 74.8 us)
Async XLA Ops:
  2.0 7.5 %collective-permute-start.1 = (f32[296,12]{0,1:T(8,128)S(1)}, f32[296,12]{0,1:T(8,128)S(1)}, u32[]{:S(2)}, u32[]{:S(2)}) collective-permute-start(f32[296,12]{0,1:T(8,128)S(1)} %pad_maximum_fusion.4), channel_id=1, source_target_pairs={{0,2},{1,3},{2,0},{3,1},{4,6},{5,7},{6,4},{7,5},{8,10},{9,11},{10,... | collective-permute-start | bytes 42632 | tf_op jit(solution)/shard_map/ppermute | solution.py:342
  5.1 4.5 %collective-permute-start.2 = (f32[296,12]{0,1:T(8,128)S(1)}, f32[296,12]{0,1:T(8,128)S(1)}, u32[]{:S(2)}, u32[]{:S(2)}) collective-permute-start(f32[296,12]{0,1:T(8,128)S(1)} %pad_maximum_fusion.4), channel_id=1, source_target_pairs={{0,1},{1,2},{2,3},{3,0},{4,5},{5,6},{6,7},{7,4},{8,9},{9,10},{10,1... | collective-permute-start | bytes 42632 | tf_op jit(solution)/shard_map/ppermute | solution.py:342
  10.7 24.5 %collective-permute-start.9 = (f32[1184,12]{0,1:T(8,128)S(1)}, f32[1184,12]{0,1:T(8,128)S(1)}, u32[]{:S(2)}, u32[]{:S(2)}) collective-permute-start(f32[1184,12]{0,1:T(8,128)S(1)} %reshape.194), channel_id=1, source_target_pairs={{0,4},{4,8},{8,12},{12,16},{16,20},{20,24},{24,28},{28,0},{1,5},{5... | collective-permute-start | bytes 170504 | tf_op jit(solution)/shard_map/ppermute | solution.py:342
  12.2 22.9 %collective-permute-start.8 = (f32[1184,12]{0,1:T(8,128)S(1)}, f32[1184,12]{0,1:T(8,128)S(1)}, u32[]{:S(2)}, u32[]{:S(2)}) collective-permute-start(f32[1184,12]{0,1:T(8,128)S(1)} %reshape.194), channel_id=1, source_target_pairs={{0,8},{4,12},{8,16},{12,20},{16,24},{20,28},{24,0},{28,4},{1,9},{5... | collective-permute-start | bytes 170504 | tf_op jit(solution)/shard_map/ppermute | solution.py:342
  13.8 21.3 %collective-permute-start.7 = (f32[1184,12]{0,1:T(8,128)S(1)}, f32[1184,12]{0,1:T(8,128)S(1)}, u32[]{:S(2)}, u32[]{:S(2)}) collective-permute-start(f32[1184,12]{0,1:T(8,128)S(1)} %reshape.194), channel_id=1, source_target_pairs={{0,12},{4,16},{8,20},{12,24},{16,28},{20,0},{24,4},{28,8},{1,13},{... | collective-permute-start | bytes 170504 | tf_op jit(solution)/shard_map/ppermute | solution.py:342
  16.3 18.7 %collective-permute-start.6 = (f32[1184,12]{0,1:T(8,128)S(1)}, f32[1184,12]{0,1:T(8,128)S(1)}, u32[]{:S(2)}, u32[]{:S(2)}) collective-permute-start(f32[1184,12]{0,1:T(8,128)S(1)} %reshape.194), channel_id=1, source_target_pairs={{0,16},{4,20},{8,24},{12,28},{16,0},{20,4},{24,8},{28,12},{1,17},{... | collective-permute-start | bytes 170504 | tf_op jit(solution)/shard_map/ppermute | solution.py:342
  22.0 5.2 %collective-permute-start.4 = (f32[1184,12]{0,1:T(8,128)S(1)}, f32[1184,12]{0,1:T(8,128)S(1)}, u32[]{:S(2)}, u32[]{:S(2)}) collective-permute-start(f32[1184,12]{0,1:T(8,128)S(1)} %reshape.194), channel_id=1, source_target_pairs={{0,24},{4,28},{8,0},{12,4},{16,8},{20,12},{24,16},{28,20},{1,25},{... | collective-permute-start | bytes 170504 | tf_op jit(solution)/shard_map/ppermute | solution.py:342
  27.2 7.9 %collective-permute-start.5 = (f32[1184,12]{0,1:T(8,128)S(1)}, f32[1184,12]{0,1:T(8,128)S(1)}, u32[]{:S(2)}, u32[]{:S(2)}) collective-permute-start(f32[1184,12]{0,1:T(8,128)S(1)} %reshape.194), channel_id=1, source_target_pairs={{0,20},{4,24},{8,28},{12,0},{16,4},{20,8},{24,12},{28,16},{1,21},{... | collective-permute-start | bytes 170504 | tf_op jit(solution)/shard_map/ppermute | solution.py:342
  115.7 21.3 %collective-permute-start.19 = (f32[1184,8]{0,1:T(8,128)S(1)}, f32[1184,8]{0,1:T(8,128)S(1)}, u32[]{:S(2)}, u32[]{:S(2)}) collective-permute-start(f32[1184,8]{0,1:T(8,128)S(1)} %reshape.196), channel_id=1, source_target_pairs={{0,4},{4,8},{8,12},{12,16},{16,20},{20,24},{24,28},{28,0},{1,5},{5... | collective-permute-start | bytes 113672 | tf_op jit(solution)/shard_map/ppermute | solution.py:342
  118.3 18.6 %collective-permute-start.18 = (f32[1184,8]{0,1:T(8,128)S(1)}, f32[1184,8]{0,1:T(8,128)S(1)}, u32[]{:S(2)}, u32[]{:S(2)}) collective-permute-start(f32[1184,8]{0,1:T(8,128)S(1)} %reshape.196), channel_id=1, source_target_pairs={{0,8},{4,12},{8,16},{12,20},{16,24},{20,28},{24,0},{28,4},{1,9},{5... | collective-permute-start | bytes 113672 | tf_op jit(solution)/shard_map/ppermute | solution.py:342
  120.1 16.8 %collective-permute-start.17 = (f32[1184,8]{0,1:T(8,128)S(1)}, f32[1184,8]{0,1:T(8,128)S(1)}, u32[]{:S(2)}, u32[]{:S(2)}) collective-permute-start(f32[1184,8]{0,1:T(8,128)S(1)} %reshape.196), channel_id=1, source_target_pairs={{0,12},{4,16},{8,20},{12,24},{16,28},{20,0},{24,4},{28,8},{1,13},{... | collective-permute-start | bytes 113672 | tf_op jit(solution)/shard_map/ppermute | solution.py:342
  120.4 16.5 %collective-permute-start.16 = (f32[1184,8]{0,1:T(8,128)S(1)}, f32[1184,8]{0,1:T(8,128)S(1)}, u32[]{:S(2)}, u32[]{:S(2)}) collective-permute-start(f32[1184,8]{0,1:T(8,128)S(1)} %reshape.196), channel_id=1, source_target_pairs={{0,16},{4,20},{8,24},{12,28},{16,0},{20,4},{24,8},{28,12},{1,17},{... | collective-permute-start | bytes 113672 | tf_op jit(solution)/shard_map/ppermute | solution.py:342
  122.2 5.4 %collective-permute-start.13 = (f32[1184,8]{0,1:T(8,128)S(1)}, f32[1184,8]{0,1:T(8,128)S(1)}, u32[]{:S(2)}, u32[]{:S(2)}) collective-permute-start(f32[1184,8]{0,1:T(8,128)S(1)} %reshape.196), channel_id=1, source_target_pairs={{0,28},{4,0},{8,4},{12,8},{16,12},{20,16},{24,20},{28,24},{1,29},{... | collective-permute-start | bytes 113672 | tf_op jit(solution)/shard_map/ppermute | solution.py:342
  131.7 5.2 %collective-permute-start.15 = (f32[1184,8]{0,1:T(8,128)S(1)}, f32[1184,8]{0,1:T(8,128)S(1)}, u32[]{:S(2)}, u32[]{:S(2)}) collective-permute-start(f32[1184,8]{0,1:T(8,128)S(1)} %reshape.196), channel_id=1, source_target_pairs={{0,20},{4,24},{8,28},{12,0},{16,4},{20,8},{24,12},{28,16},{1,21},{... | collective-permute-start | bytes 113672 | tf_op jit(solution)/shard_map/ppermute | solution.py:342
  175.7 23.3 %collective-permute-start.29 = (f32[1184,8]{0,1:T(8,128)S(1)}, f32[1184,8]{0,1:T(8,128)S(1)}, u32[]{:S(2)}, u32[]{:S(2)}) collective-permute-start(f32[1184,8]{0,1:T(8,128)S(1)} %reshape.199), channel_id=1, source_target_pairs={{0,4},{4,8},{8,12},{12,16},{16,20},{20,24},{24,28},{28,0},{1,5},{5... | collective-permute-start | bytes 113672 | tf_op jit(solution)/shard_map/ppermute | solution.py:342
  179.8 19.3 %collective-permute-start.28 = (f32[1184,8]{0,1:T(8,128)S(1)}, f32[1184,8]{0,1:T(8,128)S(1)}, u32[]{:S(2)}, u32[]{:S(2)}) collective-permute-start(f32[1184,8]{0,1:T(8,128)S(1)} %reshape.199), channel_id=1, source_target_pairs={{0,8},{4,12},{8,16},{12,20},{16,24},{20,28},{24,0},{28,4},{1,9},{5... | collective-permute-start | bytes 113672 | tf_op jit(solution)/shard_map/ppermute | solution.py:342
  180.0 19.1 %collective-permute-start.27 = (f32[1184,8]{0,1:T(8,128)S(1)}, f32[1184,8]{0,1:T(8,128)S(1)}, u32[]{:S(2)}, u32[]{:S(2)}) collective-permute-start(f32[1184,8]{0,1:T(8,128)S(1)} %reshape.199), channel_id=1, source_target_pairs={{0,12},{4,16},{8,20},{12,24},{16,28},{20,0},{24,4},{28,8},{1,13},{... | collective-permute-start | bytes 113672 | tf_op jit(solution)/shard_map/ppermute | solution.py:342
  182.1 16.9 %collective-permute-start.26 = (f32[1184,8]{0,1:T(8,128)S(1)}, f32[1184,8]{0,1:T(8,128)S(1)}, u32[]{:S(2)}, u32[]{:S(2)}) collective-permute-start(f32[1184,8]{0,1:T(8,128)S(1)} %reshape.199), channel_id=1, source_target_pairs={{0,16},{4,20},{8,24},{12,28},{16,0},{20,4},{24,8},{28,12},{1,17},{... | collective-permute-start | bytes 113672 | tf_op jit(solution)/shard_map/ppermute | solution.py:342
  193.5 5.5 %collective-permute-start.25 = (f32[1184,8]{0,1:T(8,128)S(1)}, f32[1184,8]{0,1:T(8,128)S(1)}, u32[]{:S(2)}, u32[]{:S(2)}) collective-permute-start(f32[1184,8]{0,1:T(8,128)S(1)} %reshape.199), channel_id=1, source_target_pairs={{0,20},{4,24},{8,28},{12,0},{16,4},{20,8},{24,12},{28,16},{1,21},{... | collective-permute-start | bytes 113672 | tf_op jit(solution)/shard_map/ppermute | solution.py:342
  239.0 22.9 %collective-permute-start.39 = (f32[1184,8]{0,1:T(8,128)S(1)}, f32[1184,8]{0,1:T(8,128)S(1)}, u32[]{:S(2)}, u32[]{:S(2)}) collective-permute-start(f32[1184,8]{0,1:T(8,128)S(1)} %reshape.202), channel_id=1, source_target_pairs={{0,4},{4,8},{8,12},{12,16},{16,20},{20,24},{24,28},{28,0},{1,5},{5... | collective-permute-start | bytes 113672 | tf_op jit(solution)/shard_map/ppermute | solution.py:342
  242.6 19.3 %collective-permute-start.38 = (f32[1184,8]{0,1:T(8,128)S(1)}, f32[1184,8]{0,1:T(8,128)S(1)}, u32[]{:S(2)}, u32[]{:S(2)}) collective-permute-start(f32[1184,8]{0,1:T(8,128)S(1)} %reshape.202), channel_id=1, source_target_pairs={{0,8},{4,12},{8,16},{12,20},{16,24},{20,28},{24,0},{28,4},{1,9},{5... | collective-permute-start | bytes 113672 | tf_op jit(solution)/shard_map/ppermute | solution.py:342
  242.8 19.1 %collective-permute-start.37 = (f32[1184,8]{0,1:T(8,128)S(1)}, f32[1184,8]{0,1:T(8,128)S(1)}, u32[]{:S(2)}, u32[]{:S(2)}) collective-permute-start(f32[1184,8]{0,1:T(8,128)S(1)} %reshape.202), channel_id=1, source_target_pairs={{0,12},{4,16},{8,20},{12,24},{16,28},{20,0},{24,4},{28,8},{1,13},{... | collective-permute-start | bytes 113672 | tf_op jit(solution)/shard_map/ppermute | solution.py:342
  246.1 15.7 %collective-permute-start.36 = (f32[1184,8]{0,1:T(8,128)S(1)}, f32[1184,8]{0,1:T(8,128)S(1)}, u32[]{:S(2)}, u32[]{:S(2)}) collective-permute-start(f32[1184,8]{0,1:T(8,128)S(1)} %reshape.202), channel_id=1, source_target_pairs={{0,16},{4,20},{8,24},{12,28},{16,0},{20,4},{24,8},{28,12},{1,17},{... | collective-permute-start | bytes 113672 | tf_op jit(solution)/shard_map/ppermute | solution.py:342
  256.4 5.5 %collective-permute-start.35 = (f32[1184,8]{0,1:T(8,128)S(1)}, f32[1184,8]{0,1:T(8,128)S(1)}, u32[]{:S(2)}, u32[]{:S(2)}) collective-permute-start(f32[1184,8]{0,1:T(8,128)S(1)} %reshape.202), channel_id=1, source_target_pairs={{0,20},{4,24},{8,28},{12,0},{16,4},{20,8},{24,12},{28,16},{1,21},{... | collective-permute-start | bytes 113672 | tf_op jit(solution)/shard_map/ppermute | solution.py:342
  (24 other events, 128.4 us)

commit v5 on v4

--- a/solution.py
+++ b/solution.py
@@ -261,7 +261,7 @@
 
         columns = vec_ref.shape[0]
         zeros = tuple(jnp.zeros((8, width), jnp.float32) for _ in range(columns))
-        sums = lax.fori_loop(0, chunk_count, lane_block, zeros)
+        sums = lax.fori_loop(0, chunk_count, lane_block, zeros, unroll=2)
         lane = lax.broadcasted_iota(jnp.int32, (8, columns), 1)
         result = jnp.zeros((8, columns), jnp.float32)
         for column in range(columns):

time: 353 us -> 315 us (0.89)
  Pallas kernels: 179 us -> 142 us
    pallas_call x4, Pallas kernels: 179 us -> 142 us  [panel_call(): pl.pallas_call(functools.partial(panel_kernel, slope_mode, stored_in, sto...]
where the time goes in v5:
time: 315 us
  Pallas kernels  142 us (45%)
  starting transfers between devices  77.1 us (24%)
  blocking collectives  30.5 us (10%)
  waiting for transfers between devices  29.9 us (9%)
  local copies, waits for them, and re-layouts  23.5 us (7%)
  other arithmetic  8.89 us (3%)
    pallas_call x4, Pallas kernels, panel_call(): pl.pallas_call(functools.partial(panel_kernel, slope_mode, stored_in, sto...  142 us
    ppermute x40, starting transfers between devices, gather_axis(): lax.ppermute(vector, name, [(i, (i + shift) % count) for i in range(count)])  77.1 us
    psum x2, blocking collectives, local(): sensitivity = lax.psum(lax.psum(local_sums, 'col'), 'row')  30.5 us
    ppermute x40, waiting for transfers between devices, gather_axis(): lax.ppermute(vector, name, [(i, (i + shift) % count) for i in range(count)])  29.9 us
    unnamed x57, local copies, waits for them, and re-layouts  17.1 us
  transfers between devices with their start and end apart: 40, of which 20 were waited for; matrix products, arithmetic and copies ran while one was open for 1% of the time, Pallas kernels for 0%

profile of v5, /device:TPU:0, one launch (start us, length us, event | category | flops | bytes accessed | tf_op | source)
XLA Modules:
  0.0 314.6 jit_solution(2153395295314553038)
XLA Ops:
  2.0 3.0 collective-permute-start.1
  24.3 2.9 collective-permute-done.4
  27.2 4.4 %collective-permute-start.5 = (f32[1184,12]{0,1:T(8,128)S(1)}, f32[1184,12]{0,1:T(8,128)S(1)}, u32[]{:S(2)}, u32[]{:S(2)}) collective-permute-start(f32[1184,12]{0,1:T(8,128)S(1)} %reshape.194), channel_id=1, source_target_pairs={{0,20},{4,24},{8,28},{12,0},{16,4},{20,8},{24,12},{28,16},{1,21},{... | collective-permute-start | bytes 170504 | tf_op jit(solution)/shard_map/ppermute | solution.py:342
  31.6 3.4 %collective-permute-done.5 = f32[1184,12]{0,1:T(8,128)S(1)} collective-permute-done((f32[1184,12]{0,1:T(8,128)S(1)}, f32[1184,12]{0,1:T(8,128)S(1)}, u32[]{:S(2)}, u32[]{:S(2)}) %collective-permute-start.5) | collective-permute-done | bytes 56864 | tf_op jit(solution)/shard_map/ppermute | solution.py:342
  36.1 53.1 %shard_map.104 = (f32[296,12]{1,0:T(8,128)S(1)}, f32[296,9472]{1,0:T(8,128)S(1)}, f32[296,9472]{1,0:T(8,128)}) custom-call(f32[1]{0:T(128)S(6)} %copy.219.wave_ref, f32[296,8]{1,0:T(8,128)S(1)} %copy.147.own_ref, f32[4,9472]{1,0:T(4,128)S(1)} %get-tuple-element.33.all_ref, f32[12,9472]{1,0:T(8,128)S(1)} %pad_maximum_fusion.vec_ref), custom_call_target="tpu_custom_call" | custom-call | flops 420556800 | bytes 23059584 | tf_op jit(solution)/shard_map/pallas_call | solution.py:321
  89.2 4.1 %copy-done = f32[296,9472]{1,0:T(8,128)} copy-done((f32[296,9472]{1,0:T(8,128)}, f32[296,9472]{1,0:T(8,128)S(1)}, u32[]{:S(2)}) %copy-start) | copy-done | bytes 11214872
  104.7 3.8 %collective-permute-start.13 = (f32[1184,8]{0,1:T(8,128)S(1)}, f32[1184,8]{0,1:T(8,128)S(1)}, u32[]{:S(2)}, u32[]{:S(2)}) collective-permute-start(f32[1184,8]{0,1:T(8,128)S(1)} %reshape.196), channel_id=1, source_target_pairs={{0,28},{4,0},{8,4},{12,8},{16,12},{20,16},{24,20},{28,24},{1,29},{... | collective-permute-start | bytes 113672 | tf_op jit(solution)/shard_map/ppermute | solution.py:342
  111.2 2.9 collective-permute-done.14
  114.1 3.6 %collective-permute-start.15 = (f32[1184,8]{0,1:T(8,128)S(1)}, f32[1184,8]{0,1:T(8,128)S(1)}, u32[]{:S(2)}, u32[]{:S(2)}) collective-permute-start(f32[1184,8]{0,1:T(8,128)S(1)} %reshape.196), channel_id=1, source_target_pairs={{0,20},{4,24},{8,28},{12,0},{16,4},{20,8},{24,12},{28,16},{1,21},{... | collective-permute-start | bytes 113672 | tf_op jit(solution)/shard_map/ppermute | solution.py:342
  120.5 4.2 %copy-done.1 = f32[296,9472]{1,0:T(8,128)S(1)} copy-done((f32[296,9472]{1,0:T(8,128)S(1)}, f32[296,9472]{1,0:T(8,128)}, u32[]{:S(2)}) %copy-start.1) | copy-done | bytes 11214872
  124.6 22.9 %shard_map.105 = f32[296,12]{1,0:T(8,128)S(1)} custom-call(f32[1]{0:T(128)S(6)} %copy.219.wave_ref, f32[296,8]{1,0:T(8,128)S(1)} %copy.147.own_ref, f32[4,9472]{1,0:T(4,128)S(1)} %get-tuple-element.33.all_ref, f32[12,9472]{1,0:T(8,128)S(1)} %pad_maximum_fusion.1.vec_ref, f32[296,9472]{1,0:T(8,128)S(1)} %copy-done.1, f32[296,9472]{1,0:T(8,128)} %get-tuple-element.9.refs_1_), custom_call_target="tpu_custom_call" | custom-call | flops 89718784 | bytes 23059584 | tf_op jit(solution)/shard_map/pallas_call | solution.py:321
  152.2 4.0 %collective-permute-start.29 = (f32[1184,8]{0,1:T(8,128)S(1)}, f32[1184,8]{0,1:T(8,128)S(1)}, u32[]{:S(2)}, u32[]{:S(2)}) collective-permute-start(f32[1184,8]{0,1:T(8,128)S(1)} %reshape.199), channel_id=1, source_target_pairs={{0,4},{4,8},{8,12},{12,16},{16,20},{20,24},{24,28},{28,0},{1,5},{5... | collective-permute-start | bytes 113672 | tf_op jit(solution)/shard_map/ppermute | solution.py:342
  158.6 3.1 collective-permute-start.26
  170.0 3.8 %collective-permute-start.25 = (f32[1184,8]{0,1:T(8,128)S(1)}, f32[1184,8]{0,1:T(8,128)S(1)}, u32[]{:S(2)}, u32[]{:S(2)}) collective-permute-start(f32[1184,8]{0,1:T(8,128)S(1)} %reshape.199), channel_id=1, source_target_pairs={{0,20},{4,24},{8,28},{12,0},{16,4},{20,8},{24,12},{28,16},{1,21},{... | collective-permute-start | bytes 113672 | tf_op jit(solution)/shard_map/ppermute | solution.py:342
  177.6 4.2 %copy-done.2 = f32[296,9472]{1,0:T(8,128)S(1)} copy-done((f32[296,9472]{1,0:T(8,128)S(1)}, f32[296,9472]{1,0:T(8,128)}, u32[]{:S(2)}) %copy-start.2) | copy-done | bytes 11214872
  181.8 22.9 %shard_map.106 = f32[296,12]{1,0:T(8,128)S(1)} custom-call(f32[1]{0:T(128)S(6)} %copy.219.wave_ref, f32[296,8]{1,0:T(8,128)S(1)} %copy.147.own_ref, f32[4,9472]{1,0:T(4,128)S(1)} %get-tuple-element.33.all_ref, f32[12,9472]{1,0:T(8,128)S(1)} %pad_maximum_fusion.2.vec_ref, f32[296,9472]{1,0:T(8,128)S(1)} %copy-done.2, f32[296,9472]{1,0:T(8,128)} %get-tuple-element.9.refs_1_), custom_call_target="tpu_custom_call" | custom-call | flops 89718784 | bytes 23059584 | tf_op jit(solution)/shard_map/pallas_call | solution.py:321
  209.4 3.6 %collective-permute-start.39 = (f32[1184,8]{0,1:T(8,128)S(1)}, f32[1184,8]{0,1:T(8,128)S(1)}, u32[]{:S(2)}, u32[]{:S(2)}) collective-permute-start(f32[1184,8]{0,1:T(8,128)S(1)} %reshape.202), channel_id=1, source_target_pairs={{0,4},{4,8},{8,12},{12,16},{16,20},{20,24},{24,28},{28,0},{1,5},{5... | collective-permute-start | bytes 113672 | tf_op jit(solution)/shard_map/ppermute | solution.py:342
  213.2 3.3 %collective-permute-start.37 = (f32[1184,8]{0,1:T(8,128)S(1)}, f32[1184,8]{0,1:T(8,128)S(1)}, u32[]{:S(2)}, u32[]{:S(2)}) collective-permute-start(f32[1184,8]{0,1:T(8,128)S(1)} %reshape.202), channel_id=1, source_target_pairs={{0,12},{4,16},{8,20},{12,24},{16,28},{20,0},{24,4},{28,8},{1,13},{... | collective-permute-start | bytes 113672 | tf_op jit(solution)/shard_map/ppermute | solution.py:342
  218.5 2.7 collective-permute-start.33
  226.8 3.8 %collective-permute-start.35 = (f32[1184,8]{0,1:T(8,128)S(1)}, f32[1184,8]{0,1:T(8,128)S(1)}, u32[]{:S(2)}, u32[]{:S(2)}) collective-permute-start(f32[1184,8]{0,1:T(8,128)S(1)} %reshape.202), channel_id=1, source_target_pairs={{0,20},{4,24},{8,28},{12,0},{16,4},{20,8},{24,12},{28,16},{1,21},{... | collective-permute-start | bytes 113672 | tf_op jit(solution)/shard_map/ppermute | solution.py:342
  235.7 4.2 %copy-done.3 = f32[296,9472]{1,0:T(8,128)S(1)} copy-done((f32[296,9472]{1,0:T(8,128)S(1)}, f32[296,9472]{1,0:T(8,128)}, u32[]{:S(2)}) %copy-start.3) | copy-done | bytes 11214872
  239.9 43.1 %shard_map.107 = f32[296,12]{1,0:T(8,128)S(1)} custom-call(f32[1]{0:T(128)S(6)} %copy.219.wave_ref, f32[296,8]{1,0:T(8,128)S(1)} %copy.147.own_ref, f32[4,9472]{1,0:T(4,128)S(1)} %get-tuple-element.33.all_ref, f32[12,9472]{1,0:T(8,128)S(1)} %pad_maximum_fusion.3.vec_ref, f32[296,9472]{1,0:T(8,128)S(1)} %copy-done.3, f32[296,9472]{1,0:T(8,128)} %get-tuple-element.9.refs_1_), custom_call_target="tpu_custom_call" | custom-call | flops 168222720 | bytes 23059584 | tf_op jit(solution)/shard_map/pallas_call | solution.py:321
  283.5 5.6 %psum.14 = f32[4,128]{1,0:T(4,128)S(1)} all-reduce(f32[4,128]{1,0:T(4,128)S(1)} %fusion.14), channel_id=1, replica_groups=mesh['row'=8,'col'=4] {'col'}, use_global_device_ids=true, to_apply=%region_13.16 | all-reduce | flops 512 | bytes 4096 | tf_op jit(solution)/shard_map/psum | solution.py:469
  289.1 24.8 %psum.15 = f32[4,128]{1,0:T(4,128)} all-reduce(f32[4,128]{1,0:T(4,128)S(1)} %psum.14), channel_id=1, replica_groups=mesh['row'=8,'col'=4] {'row'}, use_global_device_ids=true, to_apply=%region_14.17 | all-reduce | flops 512 | bytes 4096 | tf_op jit(solution)/shard_map/psum | solution.py:469
  (227 shorter events, 74.8 us)
Async XLA Ops:
  2.0 7.5 %collective-permute-start.1 = (f32[296,12]{0,1:T(8,128)S(1)}, f32[296,12]{0,1:T(8,128)S(1)}, u32[]{:S(2)}, u32[]{:S(2)}) collective-permute-start(f32[296,12]{0,1:T(8,128)S(1)} %pad_maximum_fusion.4), channel_id=1, source_target_pairs={{0,2},{1,3},{2,0},{3,1},{4,6},{5,7},{6,4},{7,5},{8,10},{9,11},{10,... | collective-permute-start | bytes 42632 | tf_op jit(solution)/shard_map/ppermute | solution.py:342
  5.1 4.5 %collective-permute-start.2 = (f32[296,12]{0,1:T(8,128)S(1)}, f32[296,12]{0,1:T(8,128)S(1)}, u32[]{:S(2)}, u32[]{:S(2)}) collective-permute-start(f32[296,12]{0,1:T(8,128)S(1)} %pad_maximum_fusion.4), channel_id=1, source_target_pairs={{0,1},{1,2},{2,3},{3,0},{4,5},{5,6},{6,7},{7,4},{8,9},{9,10},{10,1... | collective-permute-start | bytes 42632 | tf_op jit(solution)/shard_map/ppermute | solution.py:342
  10.7 24.5 %collective-permute-start.9 = (f32[1184,12]{0,1:T(8,128)S(1)}, f32[1184,12]{0,1:T(8,128)S(1)}, u32[]{:S(2)}, u32[]{:S(2)}) collective-permute-start(f32[1184,12]{0,1:T(8,128)S(1)} %reshape.194), channel_id=1, source_target_pairs={{0,4},{4,8},{8,12},{12,16},{16,20},{20,24},{24,28},{28,0},{1,5},{5... | collective-permute-start | bytes 170504 | tf_op jit(solution)/shard_map/ppermute | solution.py:342
  12.2 22.9 %collective-permute-start.8 = (f32[1184,12]{0,1:T(8,128)S(1)}, f32[1184,12]{0,1:T(8,128)S(1)}, u32[]{:S(2)}, u32[]{:S(2)}) collective-permute-start(f32[1184,12]{0,1:T(8,128)S(1)} %reshape.194), channel_id=1, source_target_pairs={{0,8},{4,12},{8,16},{12,20},{16,24},{20,28},{24,0},{28,4},{1,9},{5... | collective-permute-start | bytes 170504 | tf_op jit(solution)/shard_map/ppermute | solution.py:342
  13.8 21.3 %collective-permute-start.7 = (f32[1184,12]{0,1:T(8,128)S(1)}, f32[1184,12]{0,1:T(8,128)S(1)}, u32[]{:S(2)}, u32[]{:S(2)}) collective-permute-start(f32[1184,12]{0,1:T(8,128)S(1)} %reshape.194), channel_id=1, source_target_pairs={{0,12},{4,16},{8,20},{12,24},{16,28},{20,0},{24,4},{28,8},{1,13},{... | collective-permute-start | bytes 170504 | tf_op jit(solution)/shard_map/ppermute | solution.py:342
  16.3 18.7 %collective-permute-start.6 = (f32[1184,12]{0,1:T(8,128)S(1)}, f32[1184,12]{0,1:T(8,128)S(1)}, u32[]{:S(2)}, u32[]{:S(2)}) collective-permute-start(f32[1184,12]{0,1:T(8,128)S(1)} %reshape.194), channel_id=1, source_target_pairs={{0,16},{4,20},{8,24},{12,28},{16,0},{20,4},{24,8},{28,12},{1,17},{... | collective-permute-start | bytes 170504 | tf_op jit(solution)/shard_map/ppermute | solution.py:342
  22.0 5.2 %collective-permute-start.4 = (f32[1184,12]{0,1:T(8,128)S(1)}, f32[1184,12]{0,1:T(8,128)S(1)}, u32[]{:S(2)}, u32[]{:S(2)}) collective-permute-start(f32[1184,12]{0,1:T(8,128)S(1)} %reshape.194), channel_id=1, source_target_pairs={{0,24},{4,28},{8,0},{12,4},{16,8},{20,12},{24,16},{28,20},{1,25},{... | collective-permute-start | bytes 170504 | tf_op jit(solution)/shard_map/ppermute | solution.py:342
  27.2 7.9 %collective-permute-start.5 = (f32[1184,12]{0,1:T(8,128)S(1)}, f32[1184,12]{0,1:T(8,128)S(1)}, u32[]{:S(2)}, u32[]{:S(2)}) collective-permute-start(f32[1184,12]{0,1:T(8,128)S(1)} %reshape.194), channel_id=1, source_target_pairs={{0,20},{4,24},{8,28},{12,0},{16,4},{20,8},{24,12},{28,16},{1,21},{... | collective-permute-start | bytes 170504 | tf_op jit(solution)/shard_map/ppermute | solution.py:342
  98.1 21.3 %collective-permute-start.19 = (f32[1184,8]{0,1:T(8,128)S(1)}, f32[1184,8]{0,1:T(8,128)S(1)}, u32[]{:S(2)}, u32[]{:S(2)}) collective-permute-start(f32[1184,8]{0,1:T(8,128)S(1)} %reshape.196), channel_id=1, source_target_pairs={{0,4},{4,8},{8,12},{12,16},{16,20},{20,24},{24,28},{28,0},{1,5},{5... | collective-permute-start | bytes 113672 | tf_op jit(solution)/shard_map/ppermute | solution.py:342
  100.8 18.6 %collective-permute-start.18 = (f32[1184,8]{0,1:T(8,128)S(1)}, f32[1184,8]{0,1:T(8,128)S(1)}, u32[]{:S(2)}, u32[]{:S(2)}) collective-permute-start(f32[1184,8]{0,1:T(8,128)S(1)} %reshape.196), channel_id=1, source_target_pairs={{0,8},{4,12},{8,16},{12,20},{16,24},{20,28},{24,0},{28,4},{1,9},{5... | collective-permute-start | bytes 113672 | tf_op jit(solution)/shard_map/ppermute | solution.py:342
  102.6 16.8 %collective-permute-start.17 = (f32[1184,8]{0,1:T(8,128)S(1)}, f32[1184,8]{0,1:T(8,128)S(1)}, u32[]{:S(2)}, u32[]{:S(2)}) collective-permute-start(f32[1184,8]{0,1:T(8,128)S(1)} %reshape.196), channel_id=1, source_target_pairs={{0,12},{4,16},{8,20},{12,24},{16,28},{20,0},{24,4},{28,8},{1,13},{... | collective-permute-start | bytes 113672 | tf_op jit(solution)/shard_map/ppermute | solution.py:342
  102.8 16.5 %collective-permute-start.16 = (f32[1184,8]{0,1:T(8,128)S(1)}, f32[1184,8]{0,1:T(8,128)S(1)}, u32[]{:S(2)}, u32[]{:S(2)}) collective-permute-start(f32[1184,8]{0,1:T(8,128)S(1)} %reshape.196), channel_id=1, source_target_pairs={{0,16},{4,20},{8,24},{12,28},{16,0},{20,4},{24,8},{28,12},{1,17},{... | collective-permute-start | bytes 113672 | tf_op jit(solution)/shard_map/ppermute | solution.py:342
  104.7 5.4 %collective-permute-start.13 = (f32[1184,8]{0,1:T(8,128)S(1)}, f32[1184,8]{0,1:T(8,128)S(1)}, u32[]{:S(2)}, u32[]{:S(2)}) collective-permute-start(f32[1184,8]{0,1:T(8,128)S(1)} %reshape.196), channel_id=1, source_target_pairs={{0,28},{4,0},{8,4},{12,8},{16,12},{20,16},{24,20},{28,24},{1,29},{... | collective-permute-start | bytes 113672 | tf_op jit(solution)/shard_map/ppermute | solution.py:342
  114.1 5.2 %collective-permute-start.15 = (f32[1184,8]{0,1:T(8,128)S(1)}, f32[1184,8]{0,1:T(8,128)S(1)}, u32[]{:S(2)}, u32[]{:S(2)}) collective-permute-start(f32[1184,8]{0,1:T(8,128)S(1)} %reshape.196), channel_id=1, source_target_pairs={{0,20},{4,24},{8,28},{12,0},{16,4},{20,8},{24,12},{28,16},{1,21},{... | collective-permute-start | bytes 113672 | tf_op jit(solution)/shard_map/ppermute | solution.py:342
  152.2 23.3 %collective-permute-start.29 = (f32[1184,8]{0,1:T(8,128)S(1)}, f32[1184,8]{0,1:T(8,128)S(1)}, u32[]{:S(2)}, u32[]{:S(2)}) collective-permute-start(f32[1184,8]{0,1:T(8,128)S(1)} %reshape.199), channel_id=1, source_target_pairs={{0,4},{4,8},{8,12},{12,16},{16,20},{20,24},{24,28},{28,0},{1,5},{5... | collective-permute-start | bytes 113672 | tf_op jit(solution)/shard_map/ppermute | solution.py:342
  156.2 19.3 %collective-permute-start.28 = (f32[1184,8]{0,1:T(8,128)S(1)}, f32[1184,8]{0,1:T(8,128)S(1)}, u32[]{:S(2)}, u32[]{:S(2)}) collective-permute-start(f32[1184,8]{0,1:T(8,128)S(1)} %reshape.199), channel_id=1, source_target_pairs={{0,8},{4,12},{8,16},{12,20},{16,24},{20,28},{24,0},{28,4},{1,9},{5... | collective-permute-start | bytes 113672 | tf_op jit(solution)/shard_map/ppermute | solution.py:342
  156.4 19.1 %collective-permute-start.27 = (f32[1184,8]{0,1:T(8,128)S(1)}, f32[1184,8]{0,1:T(8,128)S(1)}, u32[]{:S(2)}, u32[]{:S(2)}) collective-permute-start(f32[1184,8]{0,1:T(8,128)S(1)} %reshape.199), channel_id=1, source_target_pairs={{0,12},{4,16},{8,20},{12,24},{16,28},{20,0},{24,4},{28,8},{1,13},{... | collective-permute-start | bytes 113672 | tf_op jit(solution)/shard_map/ppermute | solution.py:342
  158.6 16.9 %collective-permute-start.26 = (f32[1184,8]{0,1:T(8,128)S(1)}, f32[1184,8]{0,1:T(8,128)S(1)}, u32[]{:S(2)}, u32[]{:S(2)}) collective-permute-start(f32[1184,8]{0,1:T(8,128)S(1)} %reshape.199), channel_id=1, source_target_pairs={{0,16},{4,20},{8,24},{12,28},{16,0},{20,4},{24,8},{28,12},{1,17},{... | collective-permute-start | bytes 113672 | tf_op jit(solution)/shard_map/ppermute | solution.py:342
  170.0 5.5 %collective-permute-start.25 = (f32[1184,8]{0,1:T(8,128)S(1)}, f32[1184,8]{0,1:T(8,128)S(1)}, u32[]{:S(2)}, u32[]{:S(2)}) collective-permute-start(f32[1184,8]{0,1:T(8,128)S(1)} %reshape.199), channel_id=1, source_target_pairs={{0,20},{4,24},{8,28},{12,0},{16,4},{20,8},{24,12},{28,16},{1,21},{... | collective-permute-start | bytes 113672 | tf_op jit(solution)/shard_map/ppermute | solution.py:342
  209.4 22.9 %collective-permute-start.39 = (f32[1184,8]{0,1:T(8,128)S(1)}, f32[1184,8]{0,1:T(8,128)S(1)}, u32[]{:S(2)}, u32[]{:S(2)}) collective-permute-start(f32[1184,8]{0,1:T(8,128)S(1)} %reshape.202), channel_id=1, source_target_pairs={{0,4},{4,8},{8,12},{12,16},{16,20},{20,24},{24,28},{28,0},{1,5},{5... | collective-permute-start | bytes 113672 | tf_op jit(solution)/shard_map/ppermute | solution.py:342
  213.0 19.3 %collective-permute-start.38 = (f32[1184,8]{0,1:T(8,128)S(1)}, f32[1184,8]{0,1:T(8,128)S(1)}, u32[]{:S(2)}, u32[]{:S(2)}) collective-permute-start(f32[1184,8]{0,1:T(8,128)S(1)} %reshape.202), channel_id=1, source_target_pairs={{0,8},{4,12},{8,16},{12,20},{16,24},{20,28},{24,0},{28,4},{1,9},{5... | collective-permute-start | bytes 113672 | tf_op jit(solution)/shard_map/ppermute | solution.py:342
  213.2 19.1 %collective-permute-start.37 = (f32[1184,8]{0,1:T(8,128)S(1)}, f32[1184,8]{0,1:T(8,128)S(1)}, u32[]{:S(2)}, u32[]{:S(2)}) collective-permute-start(f32[1184,8]{0,1:T(8,128)S(1)} %reshape.202), channel_id=1, source_target_pairs={{0,12},{4,16},{8,20},{12,24},{16,28},{20,0},{24,4},{28,8},{1,13},{... | collective-permute-start | bytes 113672 | tf_op jit(solution)/shard_map/ppermute | solution.py:342
  216.5 15.7 %collective-permute-start.36 = (f32[1184,8]{0,1:T(8,128)S(1)}, f32[1184,8]{0,1:T(8,128)S(1)}, u32[]{:S(2)}, u32[]{:S(2)}) collective-permute-start(f32[1184,8]{0,1:T(8,128)S(1)} %reshape.202), channel_id=1, source_target_pairs={{0,16},{4,20},{8,24},{12,28},{16,0},{20,4},{24,8},{28,12},{1,17},{... | collective-permute-start | bytes 113672 | tf_op jit(solution)/shard_map/ppermute | solution.py:342
  226.8 5.5 %collective-permute-start.35 = (f32[1184,8]{0,1:T(8,128)S(1)}, f32[1184,8]{0,1:T(8,128)S(1)}, u32[]{:S(2)}, u32[]{:S(2)}) collective-permute-start(f32[1184,8]{0,1:T(8,128)S(1)} %reshape.202), channel_id=1, source_target_pairs={{0,20},{4,24},{8,28},{12,0},{16,4},{20,8},{24,12},{28,16},{1,21},{... | collective-permute-start | bytes 113672 | tf_op jit(solution)/shard_map/ppermute | solution.py:342
  (24 other events, 120.8 us)

commit v6 on v5

--- a/solution.py
+++ b/solution.py
@@ -261,7 +261,7 @@
 
         columns = vec_ref.shape[0]
         zeros = tuple(jnp.zeros((8, width), jnp.float32) for _ in range(columns))
-        sums = lax.fori_loop(0, chunk_count, lane_block, zeros, unroll=2)
+        sums = lax.fori_loop(0, chunk_count, lane_block, zeros, unroll=4 if stored_in and not slope_mode else 3)
         lane = lax.broadcasted_iota(jnp.int32, (8, columns), 1)
         result = jnp.zeros((8, columns), jnp.float32)
         for column in range(columns):

time: 315 us -> 300 us (0.952)
  Pallas kernels: 142 us -> 127 us
    pallas_call x4, Pallas kernels: 142 us -> 127 us  [panel_call(): pl.pallas_call(functools.partial(panel_kernel, slope_mode, stored_in, sto...]
where the time goes in v6:
time: 300 us; the launch traced here: 299 us
  Pallas kernels  127 us (42%)
  starting transfers between devices  77.1 us (26%)
  blocking collectives  30.5 us (10%)
  waiting for transfers between devices  29.9 us (10%)
  local copies, waits for them, and re-layouts  23.5 us (8%)
  other arithmetic  8.89 us (3%)
    pallas_call x4, Pallas kernels, panel_call(): pl.pallas_call(functools.partial(panel_kernel, slope_mode, stored_in, sto...  127 us
    ppermute x40, starting transfers between devices, gather_axis(): lax.ppermute(vector, name, [(i, (i + shift) % count) for i in range(count)])  77.1 us
    psum x2, blocking collectives, local(): sensitivity = lax.psum(lax.psum(local_sums, 'col'), 'row')  30.5 us
    ppermute x40, waiting for transfers between devices, gather_axis(): lax.ppermute(vector, name, [(i, (i + shift) % count) for i in range(count)])  29.9 us
    unnamed x57, local copies, waits for them, and re-layouts  17.1 us
  transfers between devices with their start and end apart: 40, of which 20 were waited for; matrix products, arithmetic and copies ran while one was open for 1% of the time, Pallas kernels for 0%

profile of v6, /device:TPU:0, one launch (start us, length us, event | category | flops | bytes accessed | tf_op | source)
XLA Modules:
  0.0 299.1 jit_solution(9295809220527426705)
XLA Ops:
  2.0 3.0 %collective-permute-start.1 = (f32[296,12]{0,1:T(8,128)S(1)}, f32[296,12]{0,1:T(8,128)S(1)}, u32[]{:S(2)}, u32[]{:S(2)}) collective-permute-start(f32[296,12]{0,1:T(8,128)S(1)} %pad_maximum_fusion.4), channel_id=1, source_target_pairs={{0,2},{1,3},{2,0},{3,1},{4,6},{5,7},{6,4},{7,5},{8,10},{9,11},{10,... | collective-permute-start | bytes 42632 | tf_op jit(solution)/shard_map/ppermute | solution.py:342
  24.3 2.9 collective-permute-done.4
  27.2 4.4 %collective-permute-start.5 = (f32[1184,12]{0,1:T(8,128)S(1)}, f32[1184,12]{0,1:T(8,128)S(1)}, u32[]{:S(2)}, u32[]{:S(2)}) collective-permute-start(f32[1184,12]{0,1:T(8,128)S(1)} %reshape.194), channel_id=1, source_target_pairs={{0,20},{4,24},{8,28},{12,0},{16,4},{20,8},{24,12},{28,16},{1,21},{... | collective-permute-start | bytes 170504 | tf_op jit(solution)/shard_map/ppermute | solution.py:342
  31.6 3.4 %collective-permute-done.5 = f32[1184,12]{0,1:T(8,128)S(1)} collective-permute-done((f32[1184,12]{0,1:T(8,128)S(1)}, f32[1184,12]{0,1:T(8,128)S(1)}, u32[]{:S(2)}, u32[]{:S(2)}) %collective-permute-start.5) | collective-permute-done | bytes 56864 | tf_op jit(solution)/shard_map/ppermute | solution.py:342
  36.1 48.5 %shard_map.104 = (f32[296,12]{1,0:T(8,128)S(1)}, f32[296,9472]{1,0:T(8,128)S(1)}, f32[296,9472]{1,0:T(8,128)}) custom-call(f32[1]{0:T(128)S(6)} %copy.219.wave_ref, f32[296,8]{1,0:T(8,128)S(1)} %copy.147.own_ref, f32[4,9472]{1,0:T(4,128)S(1)} %get-tuple-element.33.all_ref, f32[12,9472]{1,0:T(8,128)S(1)} %pad_maximum_fusion.vec_ref), custom_call_target="tpu_custom_call" | custom-call | flops 420556800 | bytes 23059584 | tf_op jit(solution)/shard_map/pallas_call | solution.py:321
  84.6 4.1 %copy-done = f32[296,9472]{1,0:T(8,128)} copy-done((f32[296,9472]{1,0:T(8,128)}, f32[296,9472]{1,0:T(8,128)S(1)}, u32[]{:S(2)}) %copy-start) | copy-done | bytes 11214872
  100.1 3.8 %collective-permute-start.13 = (f32[1184,8]{0,1:T(8,128)S(1)}, f32[1184,8]{0,1:T(8,128)S(1)}, u32[]{:S(2)}, u32[]{:S(2)}) collective-permute-start(f32[1184,8]{0,1:T(8,128)S(1)} %reshape.196), channel_id=1, source_target_pairs={{0,28},{4,0},{8,4},{12,8},{16,12},{20,16},{24,20},{28,24},{1,29},{... | collective-permute-start | bytes 113672 | tf_op jit(solution)/shard_map/ppermute | solution.py:342
  106.6 2.9 collective-permute-done.14
  109.5 3.6 %collective-permute-start.15 = (f32[1184,8]{0,1:T(8,128)S(1)}, f32[1184,8]{0,1:T(8,128)S(1)}, u32[]{:S(2)}, u32[]{:S(2)}) collective-permute-start(f32[1184,8]{0,1:T(8,128)S(1)} %reshape.196), channel_id=1, source_target_pairs={{0,20},{4,24},{8,28},{12,0},{16,4},{20,8},{24,12},{28,16},{1,21},{... | collective-permute-start | bytes 113672 | tf_op jit(solution)/shard_map/ppermute | solution.py:342
  115.9 4.2 %copy-done.1 = f32[296,9472]{1,0:T(8,128)S(1)} copy-done((f32[296,9472]{1,0:T(8,128)S(1)}, f32[296,9472]{1,0:T(8,128)}, u32[]{:S(2)}) %copy-start.1) | copy-done | bytes 11214872
  120.0 19.8 %shard_map.105 = f32[296,12]{1,0:T(8,128)S(1)} custom-call(f32[1]{0:T(128)S(6)} %copy.219.wave_ref, f32[296,8]{1,0:T(8,128)S(1)} %copy.147.own_ref, f32[4,9472]{1,0:T(4,128)S(1)} %get-tuple-element.33.all_ref, f32[12,9472]{1,0:T(8,128)S(1)} %pad_maximum_fusion.1.vec_ref, f32[296,9472]{1,0:T(8,128)S(1)} %copy-done.1, f32[296,9472]{1,0:T(8,128)} %get-tuple-element.9.refs_1_), custom_call_target="tpu_custom_call" | custom-call | flops 89718784 | bytes 23059584 | tf_op jit(solution)/shard_map/pallas_call | solution.py:321
  144.4 4.0 %collective-permute-start.29 = (f32[1184,8]{0,1:T(8,128)S(1)}, f32[1184,8]{0,1:T(8,128)S(1)}, u32[]{:S(2)}, u32[]{:S(2)}) collective-permute-start(f32[1184,8]{0,1:T(8,128)S(1)} %reshape.199), channel_id=1, source_target_pairs={{0,4},{4,8},{8,12},{12,16},{16,20},{20,24},{24,28},{28,0},{1,5},{5... | collective-permute-start | bytes 113672 | tf_op jit(solution)/shard_map/ppermute | solution.py:342
  150.8 3.1 %collective-permute-start.26 = (f32[1184,8]{0,1:T(8,128)S(1)}, f32[1184,8]{0,1:T(8,128)S(1)}, u32[]{:S(2)}, u32[]{:S(2)}) collective-permute-start(f32[1184,8]{0,1:T(8,128)S(1)} %reshape.199), channel_id=1, source_target_pairs={{0,16},{4,20},{8,24},{12,28},{16,0},{20,4},{24,8},{28,12},{1,17},{... | collective-permute-start | bytes 113672 | tf_op jit(solution)/shard_map/ppermute | solution.py:342
  162.2 3.8 %collective-permute-start.25 = (f32[1184,8]{0,1:T(8,128)S(1)}, f32[1184,8]{0,1:T(8,128)S(1)}, u32[]{:S(2)}, u32[]{:S(2)}) collective-permute-start(f32[1184,8]{0,1:T(8,128)S(1)} %reshape.199), channel_id=1, source_target_pairs={{0,20},{4,24},{8,28},{12,0},{16,4},{20,8},{24,12},{28,16},{1,21},{... | collective-permute-start | bytes 113672 | tf_op jit(solution)/shard_map/ppermute | solution.py:342
  169.8 4.2 %copy-done.2 = f32[296,9472]{1,0:T(8,128)S(1)} copy-done((f32[296,9472]{1,0:T(8,128)S(1)}, f32[296,9472]{1,0:T(8,128)}, u32[]{:S(2)}) %copy-start.2) | copy-done | bytes 11214872
  174.0 19.8 %shard_map.106 = f32[296,12]{1,0:T(8,128)S(1)} custom-call(f32[1]{0:T(128)S(6)} %copy.219.wave_ref, f32[296,8]{1,0:T(8,128)S(1)} %copy.147.own_ref, f32[4,9472]{1,0:T(4,128)S(1)} %get-tuple-element.33.all_ref, f32[12,9472]{1,0:T(8,128)S(1)} %pad_maximum_fusion.2.vec_ref, f32[296,9472]{1,0:T(8,128)S(1)} %copy-done.2, f32[296,9472]{1,0:T(8,128)} %get-tuple-element.9.refs_1_), custom_call_target="tpu_custom_call" | custom-call | flops 89718784 | bytes 23059584 | tf_op jit(solution)/shard_map/pallas_call | solution.py:321
  198.5 3.6 %collective-permute-start.39 = (f32[1184,8]{0,1:T(8,128)S(1)}, f32[1184,8]{0,1:T(8,128)S(1)}, u32[]{:S(2)}, u32[]{:S(2)}) collective-permute-start(f32[1184,8]{0,1:T(8,128)S(1)} %reshape.202), channel_id=1, source_target_pairs={{0,4},{4,8},{8,12},{12,16},{16,20},{20,24},{24,28},{28,0},{1,5},{5... | collective-permute-start | bytes 113672 | tf_op jit(solution)/shard_map/ppermute | solution.py:342
  202.3 3.3 %collective-permute-start.37 = (f32[1184,8]{0,1:T(8,128)S(1)}, f32[1184,8]{0,1:T(8,128)S(1)}, u32[]{:S(2)}, u32[]{:S(2)}) collective-permute-start(f32[1184,8]{0,1:T(8,128)S(1)} %reshape.202), channel_id=1, source_target_pairs={{0,12},{4,16},{8,20},{12,24},{16,28},{20,0},{24,4},{28,8},{1,13},{... | collective-permute-start | bytes 113672 | tf_op jit(solution)/shard_map/ppermute | solution.py:342
  207.5 2.7 collective-permute-start.33
  215.9 3.8 %collective-permute-start.35 = (f32[1184,8]{0,1:T(8,128)S(1)}, f32[1184,8]{0,1:T(8,128)S(1)}, u32[]{:S(2)}, u32[]{:S(2)}) collective-permute-start(f32[1184,8]{0,1:T(8,128)S(1)} %reshape.202), channel_id=1, source_target_pairs={{0,20},{4,24},{8,28},{12,0},{16,4},{20,8},{24,12},{28,16},{1,21},{... | collective-permute-start | bytes 113672 | tf_op jit(solution)/shard_map/ppermute | solution.py:342
  224.8 4.2 %copy-done.3 = f32[296,9472]{1,0:T(8,128)S(1)} copy-done((f32[296,9472]{1,0:T(8,128)S(1)}, f32[296,9472]{1,0:T(8,128)}, u32[]{:S(2)}) %copy-start.3) | copy-done | bytes 11214872
  228.9 38.5 %shard_map.107 = f32[296,12]{1,0:T(8,128)S(1)} custom-call(f32[1]{0:T(128)S(6)} %copy.219.wave_ref, f32[296,8]{1,0:T(8,128)S(1)} %copy.147.own_ref, f32[4,9472]{1,0:T(4,128)S(1)} %get-tuple-element.33.all_ref, f32[12,9472]{1,0:T(8,128)S(1)} %pad_maximum_fusion.3.vec_ref, f32[296,9472]{1,0:T(8,128)S(1)} %copy-done.3, f32[296,9472]{1,0:T(8,128)} %get-tuple-element.9.refs_1_), custom_call_target="tpu_custom_call" | custom-call | flops 168222720 | bytes 23059584 | tf_op jit(solution)/shard_map/pallas_call | solution.py:321
  268.0 5.6 %psum.14 = f32[4,128]{1,0:T(4,128)S(1)} all-reduce(f32[4,128]{1,0:T(4,128)S(1)} %fusion.14), channel_id=1, replica_groups=mesh['row'=8,'col'=4] {'col'}, use_global_device_ids=true, to_apply=%region_13.16 | all-reduce | flops 512 | bytes 4096 | tf_op jit(solution)/shard_map/psum | solution.py:469
  273.6 24.8 %psum.15 = f32[4,128]{1,0:T(4,128)} all-reduce(f32[4,128]{1,0:T(4,128)S(1)} %psum.14), channel_id=1, replica_groups=mesh['row'=8,'col'=4] {'row'}, use_global_device_ids=true, to_apply=%region_14.17 | all-reduce | flops 512 | bytes 4096 | tf_op jit(solution)/shard_map/psum | solution.py:469
  (227 shorter events, 74.8 us)
Async XLA Ops:
  2.0 7.5 %collective-permute-start.1 = (f32[296,12]{0,1:T(8,128)S(1)}, f32[296,12]{0,1:T(8,128)S(1)}, u32[]{:S(2)}, u32[]{:S(2)}) collective-permute-start(f32[296,12]{0,1:T(8,128)S(1)} %pad_maximum_fusion.4), channel_id=1, source_target_pairs={{0,2},{1,3},{2,0},{3,1},{4,6},{5,7},{6,4},{7,5},{8,10},{9,11},{10,... | collective-permute-start | bytes 42632 | tf_op jit(solution)/shard_map/ppermute | solution.py:342
  5.1 4.5 %collective-permute-start.2 = (f32[296,12]{0,1:T(8,128)S(1)}, f32[296,12]{0,1:T(8,128)S(1)}, u32[]{:S(2)}, u32[]{:S(2)}) collective-permute-start(f32[296,12]{0,1:T(8,128)S(1)} %pad_maximum_fusion.4), channel_id=1, source_target_pairs={{0,1},{1,2},{2,3},{3,0},{4,5},{5,6},{6,7},{7,4},{8,9},{9,10},{10,1... | collective-permute-start | bytes 42632 | tf_op jit(solution)/shard_map/ppermute | solution.py:342
  10.7 24.5 %collective-permute-start.9 = (f32[1184,12]{0,1:T(8,128)S(1)}, f32[1184,12]{0,1:T(8,128)S(1)}, u32[]{:S(2)}, u32[]{:S(2)}) collective-permute-start(f32[1184,12]{0,1:T(8,128)S(1)} %reshape.194), channel_id=1, source_target_pairs={{0,4},{4,8},{8,12},{12,16},{16,20},{20,24},{24,28},{28,0},{1,5},{5... | collective-permute-start | bytes 170504 | tf_op jit(solution)/shard_map/ppermute | solution.py:342
  12.2 22.9 %collective-permute-start.8 = (f32[1184,12]{0,1:T(8,128)S(1)}, f32[1184,12]{0,1:T(8,128)S(1)}, u32[]{:S(2)}, u32[]{:S(2)}) collective-permute-start(f32[1184,12]{0,1:T(8,128)S(1)} %reshape.194), channel_id=1, source_target_pairs={{0,8},{4,12},{8,16},{12,20},{16,24},{20,28},{24,0},{28,4},{1,9},{5... | collective-permute-start | bytes 170504 | tf_op jit(solution)/shard_map/ppermute | solution.py:342
  13.8 21.3 %collective-permute-start.7 = (f32[1184,12]{0,1:T(8,128)S(1)}, f32[1184,12]{0,1:T(8,128)S(1)}, u32[]{:S(2)}, u32[]{:S(2)}) collective-permute-start(f32[1184,12]{0,1:T(8,128)S(1)} %reshape.194), channel_id=1, source_target_pairs={{0,12},{4,16},{8,20},{12,24},{16,28},{20,0},{24,4},{28,8},{1,13},{... | collective-permute-start | bytes 170504 | tf_op jit(solution)/shard_map/ppermute | solution.py:342
  16.3 18.7 %collective-permute-start.6 = (f32[1184,12]{0,1:T(8,128)S(1)}, f32[1184,12]{0,1:T(8,128)S(1)}, u32[]{:S(2)}, u32[]{:S(2)}) collective-permute-start(f32[1184,12]{0,1:T(8,128)S(1)} %reshape.194), channel_id=1, source_target_pairs={{0,16},{4,20},{8,24},{12,28},{16,0},{20,4},{24,8},{28,12},{1,17},{... | collective-permute-start | bytes 170504 | tf_op jit(solution)/shard_map/ppermute | solution.py:342
  22.0 5.2 %collective-permute-start.4 = (f32[1184,12]{0,1:T(8,128)S(1)}, f32[1184,12]{0,1:T(8,128)S(1)}, u32[]{:S(2)}, u32[]{:S(2)}) collective-permute-start(f32[1184,12]{0,1:T(8,128)S(1)} %reshape.194), channel_id=1, source_target_pairs={{0,24},{4,28},{8,0},{12,4},{16,8},{20,12},{24,16},{28,20},{1,25},{... | collective-permute-start | bytes 170504 | tf_op jit(solution)/shard_map/ppermute | solution.py:342
  27.2 7.9 %collective-permute-start.5 = (f32[1184,12]{0,1:T(8,128)S(1)}, f32[1184,12]{0,1:T(8,128)S(1)}, u32[]{:S(2)}, u32[]{:S(2)}) collective-permute-start(f32[1184,12]{0,1:T(8,128)S(1)} %reshape.194), channel_id=1, source_target_pairs={{0,20},{4,24},{8,28},{12,0},{16,4},{20,8},{24,12},{28,16},{1,21},{... | collective-permute-start | bytes 170504 | tf_op jit(solution)/shard_map/ppermute | solution.py:342
  93.5 21.3 %collective-permute-start.19 = (f32[1184,8]{0,1:T(8,128)S(1)}, f32[1184,8]{0,1:T(8,128)S(1)}, u32[]{:S(2)}, u32[]{:S(2)}) collective-permute-start(f32[1184,8]{0,1:T(8,128)S(1)} %reshape.196), channel_id=1, source_target_pairs={{0,4},{4,8},{8,12},{12,16},{16,20},{20,24},{24,28},{28,0},{1,5},{5... | collective-permute-start | bytes 113672 | tf_op jit(solution)/shard_map/ppermute | solution.py:342
  96.2 18.6 %collective-permute-start.18 = (f32[1184,8]{0,1:T(8,128)S(1)}, f32[1184,8]{0,1:T(8,128)S(1)}, u32[]{:S(2)}, u32[]{:S(2)}) collective-permute-start(f32[1184,8]{0,1:T(8,128)S(1)} %reshape.196), channel_id=1, source_target_pairs={{0,8},{4,12},{8,16},{12,20},{16,24},{20,28},{24,0},{28,4},{1,9},{5... | collective-permute-start | bytes 113672 | tf_op jit(solution)/shard_map/ppermute | solution.py:342
  98.0 16.8 %collective-permute-start.17 = (f32[1184,8]{0,1:T(8,128)S(1)}, f32[1184,8]{0,1:T(8,128)S(1)}, u32[]{:S(2)}, u32[]{:S(2)}) collective-permute-start(f32[1184,8]{0,1:T(8,128)S(1)} %reshape.196), channel_id=1, source_target_pairs={{0,12},{4,16},{8,20},{12,24},{16,28},{20,0},{24,4},{28,8},{1,13},{... | collective-permute-start | bytes 113672 | tf_op jit(solution)/shard_map/ppermute | solution.py:342
  98.2 16.5 %collective-permute-start.16 = (f32[1184,8]{0,1:T(8,128)S(1)}, f32[1184,8]{0,1:T(8,128)S(1)}, u32[]{:S(2)}, u32[]{:S(2)}) collective-permute-start(f32[1184,8]{0,1:T(8,128)S(1)} %reshape.196), channel_id=1, source_target_pairs={{0,16},{4,20},{8,24},{12,28},{16,0},{20,4},{24,8},{28,12},{1,17},{... | collective-permute-start | bytes 113672 | tf_op jit(solution)/shard_map/ppermute | solution.py:342
  100.1 5.4 %collective-permute-start.13 = (f32[1184,8]{0,1:T(8,128)S(1)}, f32[1184,8]{0,1:T(8,128)S(1)}, u32[]{:S(2)}, u32[]{:S(2)}) collective-permute-start(f32[1184,8]{0,1:T(8,128)S(1)} %reshape.196), channel_id=1, source_target_pairs={{0,28},{4,0},{8,4},{12,8},{16,12},{20,16},{24,20},{28,24},{1,29},{... | collective-permute-start | bytes 113672 | tf_op jit(solution)/shard_map/ppermute | solution.py:342
  109.5 5.2 %collective-permute-start.15 = (f32[1184,8]{0,1:T(8,128)S(1)}, f32[1184,8]{0,1:T(8,128)S(1)}, u32[]{:S(2)}, u32[]{:S(2)}) collective-permute-start(f32[1184,8]{0,1:T(8,128)S(1)} %reshape.196), channel_id=1, source_target_pairs={{0,20},{4,24},{8,28},{12,0},{16,4},{20,8},{24,12},{28,16},{1,21},{... | collective-permute-start | bytes 113672 | tf_op jit(solution)/shard_map/ppermute | solution.py:342
  144.4 23.3 %collective-permute-start.29 = (f32[1184,8]{0,1:T(8,128)S(1)}, f32[1184,8]{0,1:T(8,128)S(1)}, u32[]{:S(2)}, u32[]{:S(2)}) collective-permute-start(f32[1184,8]{0,1:T(8,128)S(1)} %reshape.199), channel_id=1, source_target_pairs={{0,4},{4,8},{8,12},{12,16},{16,20},{20,24},{24,28},{28,0},{1,5},{5... | collective-permute-start | bytes 113672 | tf_op jit(solution)/shard_map/ppermute | solution.py:342
  148.4 19.3 %collective-permute-start.28 = (f32[1184,8]{0,1:T(8,128)S(1)}, f32[1184,8]{0,1:T(8,128)S(1)}, u32[]{:S(2)}, u32[]{:S(2)}) collective-permute-start(f32[1184,8]{0,1:T(8,128)S(1)} %reshape.199), channel_id=1, source_target_pairs={{0,8},{4,12},{8,16},{12,20},{16,24},{20,28},{24,0},{28,4},{1,9},{5... | collective-permute-start | bytes 113672 | tf_op jit(solution)/shard_map/ppermute | solution.py:342
  148.6 19.1 %collective-permute-start.27 = (f32[1184,8]{0,1:T(8,128)S(1)}, f32[1184,8]{0,1:T(8,128)S(1)}, u32[]{:S(2)}, u32[]{:S(2)}) collective-permute-start(f32[1184,8]{0,1:T(8,128)S(1)} %reshape.199), channel_id=1, source_target_pairs={{0,12},{4,16},{8,20},{12,24},{16,28},{20,0},{24,4},{28,8},{1,13},{... | collective-permute-start | bytes 113672 | tf_op jit(solution)/shard_map/ppermute | solution.py:342
  150.8 16.9 %collective-permute-start.26 = (f32[1184,8]{0,1:T(8,128)S(1)}, f32[1184,8]{0,1:T(8,128)S(1)}, u32[]{:S(2)}, u32[]{:S(2)}) collective-permute-start(f32[1184,8]{0,1:T(8,128)S(1)} %reshape.199), channel_id=1, source_target_pairs={{0,16},{4,20},{8,24},{12,28},{16,0},{20,4},{24,8},{28,12},{1,17},{... | collective-permute-start | bytes 113672 | tf_op jit(solution)/shard_map/ppermute | solution.py:342
  162.2 5.5 %collective-permute-start.25 = (f32[1184,8]{0,1:T(8,128)S(1)}, f32[1184,8]{0,1:T(8,128)S(1)}, u32[]{:S(2)}, u32[]{:S(2)}) collective-permute-start(f32[1184,8]{0,1:T(8,128)S(1)} %reshape.199), channel_id=1, source_target_pairs={{0,20},{4,24},{8,28},{12,0},{16,4},{20,8},{24,12},{28,16},{1,21},{... | collective-permute-start | bytes 113672 | tf_op jit(solution)/shard_map/ppermute | solution.py:342
  198.5 22.9 %collective-permute-start.39 = (f32[1184,8]{0,1:T(8,128)S(1)}, f32[1184,8]{0,1:T(8,128)S(1)}, u32[]{:S(2)}, u32[]{:S(2)}) collective-permute-start(f32[1184,8]{0,1:T(8,128)S(1)} %reshape.202), channel_id=1, source_target_pairs={{0,4},{4,8},{8,12},{12,16},{16,20},{20,24},{24,28},{28,0},{1,5},{5... | collective-permute-start | bytes 113672 | tf_op jit(solution)/shard_map/ppermute | solution.py:342
  202.1 19.3 %collective-permute-start.38 = (f32[1184,8]{0,1:T(8,128)S(1)}, f32[1184,8]{0,1:T(8,128)S(1)}, u32[]{:S(2)}, u32[]{:S(2)}) collective-permute-start(f32[1184,8]{0,1:T(8,128)S(1)} %reshape.202), channel_id=1, source_target_pairs={{0,8},{4,12},{8,16},{12,20},{16,24},{20,28},{24,0},{28,4},{1,9},{5... | collective-permute-start | bytes 113672 | tf_op jit(solution)/shard_map/ppermute | solution.py:342
  202.3 19.1 %collective-permute-start.37 = (f32[1184,8]{0,1:T(8,128)S(1)}, f32[1184,8]{0,1:T(8,128)S(1)}, u32[]{:S(2)}, u32[]{:S(2)}) collective-permute-start(f32[1184,8]{0,1:T(8,128)S(1)} %reshape.202), channel_id=1, source_target_pairs={{0,12},{4,16},{8,20},{12,24},{16,28},{20,0},{24,4},{28,8},{1,13},{... | collective-permute-start | bytes 113672 | tf_op jit(solution)/shard_map/ppermute | solution.py:342
  205.6 15.7 %collective-permute-start.36 = (f32[1184,8]{0,1:T(8,128)S(1)}, f32[1184,8]{0,1:T(8,128)S(1)}, u32[]{:S(2)}, u32[]{:S(2)}) collective-permute-start(f32[1184,8]{0,1:T(8,128)S(1)} %reshape.202), channel_id=1, source_target_pairs={{0,16},{4,20},{8,24},{12,28},{16,0},{20,4},{24,8},{28,12},{1,17},{... | collective-permute-start | bytes 113672 | tf_op jit(solution)/shard_map/ppermute | solution.py:342
  215.9 5.5 %collective-permute-start.35 = (f32[1184,8]{0,1:T(8,128)S(1)}, f32[1184,8]{0,1:T(8,128)S(1)}, u32[]{:S(2)}, u32[]{:S(2)}) collective-permute-start(f32[1184,8]{0,1:T(8,128)S(1)} %reshape.202), channel_id=1, source_target_pairs={{0,20},{4,24},{8,28},{12,0},{16,4},{20,8},{24,12},{28,16},{1,21},{... | collective-permute-start | bytes 113672 | tf_op jit(solution)/shard_map/ppermute | solution.py:342
  (24 other events, 116.3 us)

commit v7 on v6

--- a/solution.py
+++ b/solution.py
@@ -182,11 +182,19 @@
 
 def panel_kernel(slope_mode, stored_in, store_out, wave_ref, own_ref, all_ref, vec_ref, *refs):
     if stored_in:
-        real_ref, imag_ref, out_ref = refs
+        real_hbm, imag_hbm, out_ref, real_buf, imag_buf, sems = refs
     elif store_out:
-        out_ref, real_ref, imag_ref = refs
+        out_ref, real_hbm, imag_hbm, real_buf, imag_buf, sems = refs
     else:
         (out_ref,) = refs
+    block_count = own_ref.shape[0] // 8
+
+    def copies(block, slot):
+        rows = pl.ds(pl.multiple_of(block * 8, 8), 8)
+        pairs = [(real_hbm, real_buf), (imag_hbm, imag_buf)]
+        if stored_in:
+            return [pltpu.make_async_copy(hbm.at[rows], buf.at[slot], sems.at[k, slot]) for k, (hbm, buf) in enumerate(pairs)]
+        return [pltpu.make_async_copy(buf.at[slot], hbm.at[rows], sems.at[k, slot]) for k, (hbm, buf) in enumerate(pairs)]
     wave_value = wave_ref[0]
     own_total = own_ref.shape[0]
     panel_total = all_ref.shape[1]
@@ -197,6 +205,23 @@
     def row_block(block, carry):
         first = pl.multiple_of(block * 8, 8)
         rows = pl.ds(first, 8)
+        slot = lax.rem(block, 2)
+        if stored_in:
+            for copy in copies(block, slot):
+                copy.wait()
+
+            @pl.when(block + 1 < block_count)
+            def _():
+                for copy in copies(block + 1, 1 - slot):
+                    copy.start()
+
+        if store_out:
+
+            @pl.when(block >= 2)
+            def _():
+                for copy in copies(block - 2, slot):
+                    copy.wait()
+
         own = own_ref[rows, :]
         own_x = jnp.broadcast_to(own[:, 0:1], (8, width))
         own_y = jnp.broadcast_to(own[:, 1:2], (8, width))
@@ -224,8 +249,8 @@
                 radius = square * inverse
                 phase = wave_value * radius
             if stored_in:
-                real_part = real_ref[rows, span]
-                imag_part = imag_ref[rows, span]
+                real_part = real_buf[slot, :, span]
+                imag_part = imag_buf[slot, :, span]
                 if slope_mode:
                     along_move = diff_x * move_x + diff_y * move_y + diff_z * move_z
                     factor = along_move * (inverse * inverse)
@@ -246,8 +271,8 @@
                     first_part = cosine_part * factor
                     second_part = sine_part * factor
                 if store_out:
-                    real_ref[rows, span] = first_part
-                    imag_ref[rows, span] = second_part
+                    real_buf[slot, :, span] = first_part
+                    imag_buf[slot, :, span] = second_part
             zone_count = len(sums) // 3
             both_parts = first_part + second_part
             new_sums = []
@@ -268,9 +293,19 @@
             total = jnp.sum(sums[column], axis=1, keepdims=True)
             result = jnp.where(lane == column, total, result)
         out_ref[rows, :] = result
+        if store_out:
+            for copy in copies(block, slot):
+                copy.start()
         return carry
 
-    lax.fori_loop(0, own_total // 8, row_block, 0)
+    if stored_in:
+        for copy in copies(0, 0):
+            copy.start()
+    lax.fori_loop(0, block_count, row_block, 0)
+    if store_out:
+        for block in range(max(0, block_count - 2), block_count):
+            for copy in copies(block, block % 2):
+                copy.wait()
 
 
 def panel_contract(slope_mode, wavenumber, own_table, all_table, vector_full, stored=None, store_out=False):
@@ -309,9 +344,14 @@
         out_shape += [jax.ShapeDtypeStruct((own_total, panel_total), jnp.float32)] * 2
         matrix_bytes = 8 * elements
     vmem = pl.BlockSpec(memory_space=pltpu.VMEM)
+    hbm = pl.BlockSpec(memory_space=pl.ANY)
     params = {}
     if matrix_bytes:
-        params["compiler_params"] = pltpu.CompilerParams(vmem_limit_bytes=matrix_bytes + 16 * 1024 * 1024)
+        params["scratch_shapes"] = [
+            pltpu.VMEM((2, 8, panel_total), jnp.float32),
+            pltpu.VMEM((2, 8, panel_total), jnp.float32),
+            pltpu.SemaphoreType.DMA((2, 2)),
+        ]
     if stored_in and not slope_mode:
         flops, transcendentals = 32 * elements, 0
     elif stored_in:
@@ -321,8 +361,8 @@
     return pl.pallas_call(
         functools.partial(panel_kernel, slope_mode, stored_in, store_out),
         out_shape=tuple(out_shape) if store_out else out_shape[0],
-        in_specs=[pl.BlockSpec(memory_space=pltpu.SMEM)] + [vmem] * (len(operands) - 1),
-        out_specs=tuple([vmem] * len(out_shape)) if store_out else vmem,
+        in_specs=[pl.BlockSpec(memory_space=pltpu.SMEM)] + [vmem] * 3 + [hbm] * (len(operands) - 4),
+        out_specs=tuple([vmem] + [hbm] * (len(out_shape) - 1)) if store_out else vmem,
         cost_estimate=pl.CostEstimate(
             flops=flops,
             transcendentals=transcendentals,

time: 300 us -> 339 us (1.13)
  Pallas kernels: 127 us -> 172 us
  local copies, waits for them, and re-layouts: 23.5 us -> 8.39 us
  other arithmetic: 8.89 us -> 15 us
    pallas_call x4, Pallas kernels: 127 us -> 172 us  [panel_call(): pl.pallas_call(functools.partial(panel_kernel, slope_mode, stored_in, sto...]
    unnamed x57 -> x49, local copies, waits for them, and re-layouts: 17.1 us -> 0.26 us
where the time goes in v7:
time: 339 us; the launch traced here: 337 us
  Pallas kernels  172 us (51%)
  starting transfers between devices  77.1 us (23%)
  blocking collectives  30.5 us (9%)
  waiting for transfers between devices  29.9 us (9%)
  other arithmetic  15 us (4%)
  local copies, waits for them, and re-layouts  8.39 us (2%)
    pallas_call x4, Pallas kernels, panel_call(): pl.pallas_call(functools.partial(panel_kernel, slope_mode, stored_in, sto...  172 us
    ppermute x40, starting transfers between devices, gather_axis(): lax.ppermute(vector, name, [(i, (i + shift) % count) for i in range(count)])  77.1 us
    psum x2, blocking collectives, local(): sensitivity = lax.psum(lax.psum(local_sums, 'col'), 'row')  30.5 us
    ppermute x40, waiting for transfers between devices, gather_axis(): lax.ppermute(vector, name, [(i, (i + shift) % count) for i in range(count)])  29.9 us
  transfers between devices with their start and end apart: 40, of which 20 were waited for; matrix products, arithmetic and copies ran while one was open for 1% of the time, Pallas kernels for 0%

profile of v7, /device:TPU:0, one launch (start us, length us, event | category | flops | bytes accessed | tf_op | source)
XLA Modules:
  0.0 336.5 jit_solution(17900768785456056398)
XLA Ops:
  2.0 3.0 collective-permute-start.1
  14.4 2.6 collective-permute-start.7
  18.2 2.3 collective-permute-start.3
  24.9 2.9 collective-permute-done.4
  27.8 4.4 %collective-permute-start.5 = (f32[1184,12]{0,1:T(8,128)S(1)}, f32[1184,12]{0,1:T(8,128)S(1)}, u32[]{:S(2)}, u32[]{:S(2)}) collective-permute-start(f32[1184,12]{0,1:T(8,128)S(1)} %reshape.194), channel_id=1, source_target_pairs={{0,20},{4,24},{8,28},{12,0},{16,4},{20,8},{24,12},{28,16},{1,21},{... | collective-permute-start | bytes 170504 | tf_op jit(solution)/shard_map/ppermute | solution.py:382
  32.3 3.4 %collective-permute-done.5 = f32[1184,12]{0,1:T(8,128)S(1)} collective-permute-done((f32[1184,12]{0,1:T(8,128)S(1)}, f32[1184,12]{0,1:T(8,128)S(1)}, u32[]{:S(2)}, u32[]{:S(2)}) %collective-permute-start.5) | collective-permute-done | bytes 56864 | tf_op jit(solution)/shard_map/ppermute | solution.py:382
  38.2 47.1 %shard_map.104 = (f32[296,12]{1,0:T(8,128)}, f32[296,9472]{1,0:T(8,128)}, f32[296,9472]{1,0:T(8,128)}) custom-call(f32[1]{0:T(128)S(6)} %copy.219.wave_ref, f32[296,8]{1,0:T(8,128)} %copy.147.own_ref, f32[4,9472]{1,0:T(4,128)} %get-tuple-element.33.all_ref, f32[12,9472]{1,0:T(8,128)} %pad_maximum_fusion.vec_ref), custom_call_target="tpu_custom_call" | custom-call | flops 420556800 | bytes 23059584 | tf_op jit(solution)/shard_map/pallas_call | solution.py:361
  91.0 2.7 collective-permute-start.19
  97.6 3.8 %collective-permute-start.13 = (f32[1184,8]{0,1:T(8,128)S(1)}, f32[1184,8]{0,1:T(8,128)S(1)}, u32[]{:S(2)}, u32[]{:S(2)}) collective-permute-start(f32[1184,8]{0,1:T(8,128)S(1)} %reshape.196), channel_id=1, source_target_pairs={{0,28},{4,0},{8,4},{12,8},{16,12},{20,16},{24,20},{28,24},{1,29},{... | collective-permute-start | bytes 113672 | tf_op jit(solution)/shard_map/ppermute | solution.py:382
  104.1 2.9 collective-permute-done.14
  107.0 3.6 %collective-permute-start.15 = (f32[1184,8]{0,1:T(8,128)S(1)}, f32[1184,8]{0,1:T(8,128)S(1)}, u32[]{:S(2)}, u32[]{:S(2)}) collective-permute-start(f32[1184,8]{0,1:T(8,128)S(1)} %reshape.196), channel_id=1, source_target_pairs={{0,20},{4,24},{8,28},{12,0},{16,4},{20,8},{24,12},{28,16},{1,21},{... | collective-permute-start | bytes 113672 | tf_op jit(solution)/shard_map/ppermute | solution.py:382
  114.2 41.4 %shard_map.105 = f32[296,12]{1,0:T(8,128)} custom-call(f32[1]{0:T(128)S(6)} %copy.219.wave_ref, f32[296,8]{1,0:T(8,128)} %copy.147.own_ref, f32[4,9472]{1,0:T(4,128)} %get-tuple-element.33.all_ref, f32[12,9472]{1,0:T(8,128)} %pad_maximum_fusion.1.vec_ref, f32[296,9472]{1,0:T(8,128)} %get-tuple-element.8.refs_0_, f32[296,9472]{1,0:T(8,128)} %get-tuple-element.9.refs_1_), custom_call_target="tpu_custom_call" | custom-call | flops 89718784 | bytes 23059584 | tf_op jit(solution)/shard_map/pallas_call | solution.py:361
  161.3 4.0 %collective-permute-start.29 = (f32[1184,8]{0,1:T(8,128)S(1)}, f32[1184,8]{0,1:T(8,128)S(1)}, u32[]{:S(2)}, u32[]{:S(2)}) collective-permute-start(f32[1184,8]{0,1:T(8,128)S(1)} %reshape.199), channel_id=1, source_target_pairs={{0,4},{4,8},{8,12},{12,16},{16,20},{20,24},{24,28},{28,0},{1,5},{5... | collective-permute-start | bytes 113672 | tf_op jit(solution)/shard_map/ppermute | solution.py:382
  167.7 3.1 collective-permute-start.26
  170.8 2.7 collective-permute-start.23
  179.1 3.8 %collective-permute-start.25 = (f32[1184,8]{0,1:T(8,128)S(1)}, f32[1184,8]{0,1:T(8,128)S(1)}, u32[]{:S(2)}, u32[]{:S(2)}) collective-permute-start(f32[1184,8]{0,1:T(8,128)S(1)} %reshape.199), channel_id=1, source_target_pairs={{0,20},{4,24},{8,28},{12,0},{16,4},{20,8},{24,12},{28,16},{1,21},{... | collective-permute-start | bytes 113672 | tf_op jit(solution)/shard_map/ppermute | solution.py:382
  187.5 41.4 %shard_map.106 = f32[296,12]{1,0:T(8,128)} custom-call(f32[1]{0:T(128)S(6)} %copy.219.wave_ref, f32[296,8]{1,0:T(8,128)} %copy.147.own_ref, f32[4,9472]{1,0:T(4,128)} %get-tuple-element.33.all_ref, f32[12,9472]{1,0:T(8,128)} %pad_maximum_fusion.2.vec_ref, f32[296,9472]{1,0:T(8,128)} %get-tuple-element.8.refs_0_, f32[296,9472]{1,0:T(8,128)} %get-tuple-element.9.refs_1_), custom_call_target="tpu_custom_call" | custom-call | flops 89718784 | bytes 23059584 | tf_op jit(solution)/shard_map/pallas_call | solution.py:361
  234.7 3.6 %collective-permute-start.39 = (f32[1184,8]{0,1:T(8,128)S(1)}, f32[1184,8]{0,1:T(8,128)S(1)}, u32[]{:S(2)}, u32[]{:S(2)}) collective-permute-start(f32[1184,8]{0,1:T(8,128)S(1)} %reshape.202), channel_id=1, source_target_pairs={{0,4},{4,8},{8,12},{12,16},{16,20},{20,24},{24,28},{28,0},{1,5},{5... | collective-permute-start | bytes 113672 | tf_op jit(solution)/shard_map/ppermute | solution.py:382
  238.6 3.3 collective-permute-start.37
  243.8 2.7 collective-permute-start.33
  252.2 3.8 %collective-permute-start.35 = (f32[1184,8]{0,1:T(8,128)S(1)}, f32[1184,8]{0,1:T(8,128)S(1)}, u32[]{:S(2)}, u32[]{:S(2)}) collective-permute-start(f32[1184,8]{0,1:T(8,128)S(1)} %reshape.202), channel_id=1, source_target_pairs={{0,20},{4,24},{8,28},{12,0},{16,4},{20,8},{24,12},{28,16},{1,21},{... | collective-permute-start | bytes 113672 | tf_op jit(solution)/shard_map/ppermute | solution.py:382
  261.9 42.0 %shard_map.107 = f32[296,12]{1,0:T(8,128)} custom-call(f32[1]{0:T(128)S(6)} %copy.219.wave_ref, f32[296,8]{1,0:T(8,128)} %copy.147.own_ref, f32[4,9472]{1,0:T(4,128)} %get-tuple-element.33.all_ref, f32[12,9472]{1,0:T(8,128)} %pad_maximum_fusion.3.vec_ref, f32[296,9472]{1,0:T(8,128)} %get-tuple-element.8.refs_0_, f32[296,9472]{1,0:T(8,128)} %get-tuple-element.9.refs_1_), custom_call_target="tpu_custom_call" | custom-call | flops 168222720 | bytes 23059584 | tf_op jit(solution)/shard_map/pallas_call | solution.py:361
  305.4 5.6 %psum.14 = f32[4,128]{1,0:T(4,128)S(1)} all-reduce(f32[4,128]{1,0:T(4,128)S(1)} %fusion.14), channel_id=1, replica_groups=mesh['row'=8,'col'=4] {'col'}, use_global_device_ids=true, to_apply=%region_13.16 | all-reduce | flops 512 | bytes 4096 | tf_op jit(solution)/shard_map/psum | solution.py:509
  311.1 24.8 %psum.15 = f32[4,128]{1,0:T(4,128)} all-reduce(f32[4,128]{1,0:T(4,128)S(1)} %psum.14), channel_id=1, replica_groups=mesh['row'=8,'col'=4] {'row'}, use_global_device_ids=true, to_apply=%region_14.17 | all-reduce | flops 512 | bytes 4096 | tf_op jit(solution)/shard_map/psum | solution.py:509
  (219 shorter events, 73.4 us)
Async XLA Ops:
  2.0 8.2 %collective-permute-start.1 = (f32[296,12]{0,1:T(8,128)S(1)}, f32[296,12]{0,1:T(8,128)S(1)}, u32[]{:S(2)}, u32[]{:S(2)}) collective-permute-start(f32[296,12]{0,1:T(8,128)S(1)} %pad_maximum_fusion.4), channel_id=1, source_target_pairs={{0,2},{1,3},{2,0},{3,1},{4,6},{5,7},{6,4},{7,5},{8,10},{9,11},{10,... | collective-permute-start | bytes 42632 | tf_op jit(solution)/shard_map/ppermute | solution.py:382
  5.1 5.2 %collective-permute-start.2 = (f32[296,12]{0,1:T(8,128)S(1)}, f32[296,12]{0,1:T(8,128)S(1)}, u32[]{:S(2)}, u32[]{:S(2)}) collective-permute-start(f32[296,12]{0,1:T(8,128)S(1)} %pad_maximum_fusion.4), channel_id=1, source_target_pairs={{0,1},{1,2},{2,3},{3,0},{4,5},{5,6},{6,7},{7,4},{8,9},{9,10},{10,1... | collective-permute-start | bytes 42632 | tf_op jit(solution)/shard_map/ppermute | solution.py:382
  11.3 24.5 %collective-permute-start.9 = (f32[1184,12]{0,1:T(8,128)S(1)}, f32[1184,12]{0,1:T(8,128)S(1)}, u32[]{:S(2)}, u32[]{:S(2)}) collective-permute-start(f32[1184,12]{0,1:T(8,128)S(1)} %reshape.194), channel_id=1, source_target_pairs={{0,4},{4,8},{8,12},{12,16},{16,20},{20,24},{24,28},{28,0},{1,5},{5... | collective-permute-start | bytes 170504 | tf_op jit(solution)/shard_map/ppermute | solution.py:382
  12.8 22.9 %collective-permute-start.8 = (f32[1184,12]{0,1:T(8,128)S(1)}, f32[1184,12]{0,1:T(8,128)S(1)}, u32[]{:S(2)}, u32[]{:S(2)}) collective-permute-start(f32[1184,12]{0,1:T(8,128)S(1)} %reshape.194), channel_id=1, source_target_pairs={{0,8},{4,12},{8,16},{12,20},{16,24},{20,28},{24,0},{28,4},{1,9},{5... | collective-permute-start | bytes 170504 | tf_op jit(solution)/shard_map/ppermute | solution.py:382
  14.4 21.3 %collective-permute-start.7 = (f32[1184,12]{0,1:T(8,128)S(1)}, f32[1184,12]{0,1:T(8,128)S(1)}, u32[]{:S(2)}, u32[]{:S(2)}) collective-permute-start(f32[1184,12]{0,1:T(8,128)S(1)} %reshape.194), channel_id=1, source_target_pairs={{0,12},{4,16},{8,20},{12,24},{16,28},{20,0},{24,4},{28,8},{1,13},{... | collective-permute-start | bytes 170504 | tf_op jit(solution)/shard_map/ppermute | solution.py:382
  17.0 18.7 %collective-permute-start.6 = (f32[1184,12]{0,1:T(8,128)S(1)}, f32[1184,12]{0,1:T(8,128)S(1)}, u32[]{:S(2)}, u32[]{:S(2)}) collective-permute-start(f32[1184,12]{0,1:T(8,128)S(1)} %reshape.194), channel_id=1, source_target_pairs={{0,16},{4,20},{8,24},{12,28},{16,0},{20,4},{24,8},{28,12},{1,17},{... | collective-permute-start | bytes 170504 | tf_op jit(solution)/shard_map/ppermute | solution.py:382
  22.7 5.2 %collective-permute-start.4 = (f32[1184,12]{0,1:T(8,128)S(1)}, f32[1184,12]{0,1:T(8,128)S(1)}, u32[]{:S(2)}, u32[]{:S(2)}) collective-permute-start(f32[1184,12]{0,1:T(8,128)S(1)} %reshape.194), channel_id=1, source_target_pairs={{0,24},{4,28},{8,0},{12,4},{16,8},{20,12},{24,16},{28,20},{1,25},{... | collective-permute-start | bytes 170504 | tf_op jit(solution)/shard_map/ppermute | solution.py:382
  27.8 7.9 %collective-permute-start.5 = (f32[1184,12]{0,1:T(8,128)S(1)}, f32[1184,12]{0,1:T(8,128)S(1)}, u32[]{:S(2)}, u32[]{:S(2)}) collective-permute-start(f32[1184,12]{0,1:T(8,128)S(1)} %reshape.194), channel_id=1, source_target_pairs={{0,20},{4,24},{8,28},{12,0},{16,4},{20,8},{24,12},{28,16},{1,21},{... | collective-permute-start | bytes 170504 | tf_op jit(solution)/shard_map/ppermute | solution.py:382
  91.0 21.3 %collective-permute-start.19 = (f32[1184,8]{0,1:T(8,128)S(1)}, f32[1184,8]{0,1:T(8,128)S(1)}, u32[]{:S(2)}, u32[]{:S(2)}) collective-permute-start(f32[1184,8]{0,1:T(8,128)S(1)} %reshape.196), channel_id=1, source_target_pairs={{0,4},{4,8},{8,12},{12,16},{16,20},{20,24},{24,28},{28,0},{1,5},{5... | collective-permute-start | bytes 113672 | tf_op jit(solution)/shard_map/ppermute | solution.py:382
  93.7 18.6 %collective-permute-start.18 = (f32[1184,8]{0,1:T(8,128)S(1)}, f32[1184,8]{0,1:T(8,128)S(1)}, u32[]{:S(2)}, u32[]{:S(2)}) collective-permute-start(f32[1184,8]{0,1:T(8,128)S(1)} %reshape.196), channel_id=1, source_target_pairs={{0,8},{4,12},{8,16},{12,20},{16,24},{20,28},{24,0},{28,4},{1,9},{5... | collective-permute-start | bytes 113672 | tf_op jit(solution)/shard_map/ppermute | solution.py:382
  95.5 16.8 %collective-permute-start.17 = (f32[1184,8]{0,1:T(8,128)S(1)}, f32[1184,8]{0,1:T(8,128)S(1)}, u32[]{:S(2)}, u32[]{:S(2)}) collective-permute-start(f32[1184,8]{0,1:T(8,128)S(1)} %reshape.196), channel_id=1, source_target_pairs={{0,12},{4,16},{8,20},{12,24},{16,28},{20,0},{24,4},{28,8},{1,13},{... | collective-permute-start | bytes 113672 | tf_op jit(solution)/shard_map/ppermute | solution.py:382
  95.7 16.5 %collective-permute-start.16 = (f32[1184,8]{0,1:T(8,128)S(1)}, f32[1184,8]{0,1:T(8,128)S(1)}, u32[]{:S(2)}, u32[]{:S(2)}) collective-permute-start(f32[1184,8]{0,1:T(8,128)S(1)} %reshape.196), channel_id=1, source_target_pairs={{0,16},{4,20},{8,24},{12,28},{16,0},{20,4},{24,8},{28,12},{1,17},{... | collective-permute-start | bytes 113672 | tf_op jit(solution)/shard_map/ppermute | solution.py:382
  97.6 5.4 %collective-permute-start.13 = (f32[1184,8]{0,1:T(8,128)S(1)}, f32[1184,8]{0,1:T(8,128)S(1)}, u32[]{:S(2)}, u32[]{:S(2)}) collective-permute-start(f32[1184,8]{0,1:T(8,128)S(1)} %reshape.196), channel_id=1, source_target_pairs={{0,28},{4,0},{8,4},{12,8},{16,12},{20,16},{24,20},{28,24},{1,29},{... | collective-permute-start | bytes 113672 | tf_op jit(solution)/shard_map/ppermute | solution.py:382
  107.0 5.2 %collective-permute-start.15 = (f32[1184,8]{0,1:T(8,128)S(1)}, f32[1184,8]{0,1:T(8,128)S(1)}, u32[]{:S(2)}, u32[]{:S(2)}) collective-permute-start(f32[1184,8]{0,1:T(8,128)S(1)} %reshape.196), channel_id=1, source_target_pairs={{0,20},{4,24},{8,28},{12,0},{16,4},{20,8},{24,12},{28,16},{1,21},{... | collective-permute-start | bytes 113672 | tf_op jit(solution)/shard_map/ppermute | solution.py:382
  161.3 23.3 %collective-permute-start.29 = (f32[1184,8]{0,1:T(8,128)S(1)}, f32[1184,8]{0,1:T(8,128)S(1)}, u32[]{:S(2)}, u32[]{:S(2)}) collective-permute-start(f32[1184,8]{0,1:T(8,128)S(1)} %reshape.199), channel_id=1, source_target_pairs={{0,4},{4,8},{8,12},{12,16},{16,20},{20,24},{24,28},{28,0},{1,5},{5... | collective-permute-start | bytes 113672 | tf_op jit(solution)/shard_map/ppermute | solution.py:382
  165.3 19.3 %collective-permute-start.28 = (f32[1184,8]{0,1:T(8,128)S(1)}, f32[1184,8]{0,1:T(8,128)S(1)}, u32[]{:S(2)}, u32[]{:S(2)}) collective-permute-start(f32[1184,8]{0,1:T(8,128)S(1)} %reshape.199), channel_id=1, source_target_pairs={{0,8},{4,12},{8,16},{12,20},{16,24},{20,28},{24,0},{28,4},{1,9},{5... | collective-permute-start | bytes 113672 | tf_op jit(solution)/shard_map/ppermute | solution.py:382
  165.5 19.1 %collective-permute-start.27 = (f32[1184,8]{0,1:T(8,128)S(1)}, f32[1184,8]{0,1:T(8,128)S(1)}, u32[]{:S(2)}, u32[]{:S(2)}) collective-permute-start(f32[1184,8]{0,1:T(8,128)S(1)} %reshape.199), channel_id=1, source_target_pairs={{0,12},{4,16},{8,20},{12,24},{16,28},{20,0},{24,4},{28,8},{1,13},{... | collective-permute-start | bytes 113672 | tf_op jit(solution)/shard_map/ppermute | solution.py:382
  167.7 16.9 %collective-permute-start.26 = (f32[1184,8]{0,1:T(8,128)S(1)}, f32[1184,8]{0,1:T(8,128)S(1)}, u32[]{:S(2)}, u32[]{:S(2)}) collective-permute-start(f32[1184,8]{0,1:T(8,128)S(1)} %reshape.199), channel_id=1, source_target_pairs={{0,16},{4,20},{8,24},{12,28},{16,0},{20,4},{24,8},{28,12},{1,17},{... | collective-permute-start | bytes 113672 | tf_op jit(solution)/shard_map/ppermute | solution.py:382
  179.1 5.5 %collective-permute-start.25 = (f32[1184,8]{0,1:T(8,128)S(1)}, f32[1184,8]{0,1:T(8,128)S(1)}, u32[]{:S(2)}, u32[]{:S(2)}) collective-permute-start(f32[1184,8]{0,1:T(8,128)S(1)} %reshape.199), channel_id=1, source_target_pairs={{0,20},{4,24},{8,28},{12,0},{16,4},{20,8},{24,12},{28,16},{1,21},{... | collective-permute-start | bytes 113672 | tf_op jit(solution)/shard_map/ppermute | solution.py:382
  234.7 22.9 %collective-permute-start.39 = (f32[1184,8]{0,1:T(8,128)S(1)}, f32[1184,8]{0,1:T(8,128)S(1)}, u32[]{:S(2)}, u32[]{:S(2)}) collective-permute-start(f32[1184,8]{0,1:T(8,128)S(1)} %reshape.202), channel_id=1, source_target_pairs={{0,4},{4,8},{8,12},{12,16},{16,20},{20,24},{24,28},{28,0},{1,5},{5... | collective-permute-start | bytes 113672 | tf_op jit(solution)/shard_map/ppermute | solution.py:382
  238.4 19.3 %collective-permute-start.38 = (f32[1184,8]{0,1:T(8,128)S(1)}, f32[1184,8]{0,1:T(8,128)S(1)}, u32[]{:S(2)}, u32[]{:S(2)}) collective-permute-start(f32[1184,8]{0,1:T(8,128)S(1)} %reshape.202), channel_id=1, source_target_pairs={{0,8},{4,12},{8,16},{12,20},{16,24},{20,28},{24,0},{28,4},{1,9},{5... | collective-permute-start | bytes 113672 | tf_op jit(solution)/shard_map/ppermute | solution.py:382
  238.6 19.1 %collective-permute-start.37 = (f32[1184,8]{0,1:T(8,128)S(1)}, f32[1184,8]{0,1:T(8,128)S(1)}, u32[]{:S(2)}, u32[]{:S(2)}) collective-permute-start(f32[1184,8]{0,1:T(8,128)S(1)} %reshape.202), channel_id=1, source_target_pairs={{0,12},{4,16},{8,20},{12,24},{16,28},{20,0},{24,4},{28,8},{1,13},{... | collective-permute-start | bytes 113672 | tf_op jit(solution)/shard_map/ppermute | solution.py:382
  241.9 15.8 %collective-permute-start.36 = (f32[1184,8]{0,1:T(8,128)S(1)}, f32[1184,8]{0,1:T(8,128)S(1)}, u32[]{:S(2)}, u32[]{:S(2)}) collective-permute-start(f32[1184,8]{0,1:T(8,128)S(1)} %reshape.202), channel_id=1, source_target_pairs={{0,16},{4,20},{8,24},{12,28},{16,0},{20,4},{24,8},{28,12},{1,17},{... | collective-permute-start | bytes 113672 | tf_op jit(solution)/shard_map/ppermute | solution.py:382
  252.2 5.5 %collective-permute-start.35 = (f32[1184,8]{0,1:T(8,128)S(1)}, f32[1184,8]{0,1:T(8,128)S(1)}, u32[]{:S(2)}, u32[]{:S(2)}) collective-permute-start(f32[1184,8]{0,1:T(8,128)S(1)} %reshape.202), channel_id=1, source_target_pairs={{0,20},{4,24},{8,28},{12,0},{16,4},{20,8},{24,12},{28,16},{1,21},{... | collective-permute-start | bytes 113672 | tf_op jit(solution)/shard_map/ppermute | solution.py:382
  (20 other events, 106.4 us)

commit v8 on v7

--- a/solution.py
+++ b/solution.py
@@ -193,7 +193,7 @@
         rows = pl.ds(pl.multiple_of(block * 8, 8), 8)
         pairs = [(real_hbm, real_buf), (imag_hbm, imag_buf)]
         if stored_in:
-            return [pltpu.make_async_copy(hbm.at[rows], buf.at[slot], sems.at[k, slot]) for k, (hbm, buf) in enumerate(pairs)]
+            return [pltpu.make_async_copy(hbm.at[rows], buf.at[rows], sems.at[k, block]) for k, (hbm, buf) in enumerate(pairs)]
         return [pltpu.make_async_copy(buf.at[slot], hbm.at[rows], sems.at[k, slot]) for k, (hbm, buf) in enumerate(pairs)]
     wave_value = wave_ref[0]
     own_total = own_ref.shape[0]
@@ -209,11 +209,6 @@
         if stored_in:
             for copy in copies(block, slot):
                 copy.wait()
-
-            @pl.when(block + 1 < block_count)
-            def _():
-                for copy in copies(block + 1, 1 - slot):
-                    copy.start()
 
         if store_out:
 
@@ -249,8 +244,8 @@
                 radius = square * inverse
                 phase = wave_value * radius
             if stored_in:
-                real_part = real_buf[slot, :, span]
-                imag_part = imag_buf[slot, :, span]
+                real_part = real_buf[rows, span]
+                imag_part = imag_buf[rows, span]
                 if slope_mode:
                     along_move = diff_x * move_x + diff_y * move_y + diff_z * move_z
                     factor = along_move * (inverse * inverse)
@@ -299,8 +294,9 @@
         return carry
 
     if stored_in:
-        for copy in copies(0, 0):
-            copy.start()
+        for block in range(block_count):
+            for copy in copies(block, 0):
+                copy.start()
     lax.fori_loop(0, block_count, row_block, 0)
     if store_out:
         for block in range(max(0, block_count - 2), block_count):
@@ -346,7 +342,14 @@
     vmem = pl.BlockSpec(memory_space=pltpu.VMEM)
     hbm = pl.BlockSpec(memory_space=pl.ANY)
     params = {}
-    if matrix_bytes:
+    if stored_in:
+        params["scratch_shapes"] = [
+            pltpu.VMEM((own_total, panel_total), jnp.float32),
+            pltpu.VMEM((own_total, panel_total), jnp.float32),
+            pltpu.SemaphoreType.DMA((2, own_total // 8)),
+        ]
+        params["compiler_params"] = pltpu.CompilerParams(vmem_limit_bytes=matrix_bytes + 16 * 1024 * 1024)
+    elif store_out:
         params["scratch_shapes"] = [
             pltpu.VMEM((2, 8, panel_total), jnp.float32),
             pltpu.VMEM((2, 8, panel_total), jnp.float32),

time: 339 us -> 296 us (0.87)
  Pallas kernels: 172 us -> 123 us
  local copies, waits for them, and re-layouts: 8.39 us -> 21.6 us
  other arithmetic: 15 us -> 10.4 us
    pallas_call x4, Pallas kernels: 172 us -> 123 us  [panel_call(): pl.pallas_call(functools.partial(panel_kernel, slope_mode, stored_in, sto...]
    unnamed x49 -> x59, local copies, waits for them, and re-layouts: 0.26 us -> 13.5 us
where the time goes in v8:
time: 296 us; the launch traced here: 295 us
  Pallas kernels  123 us (42%)
  starting transfers between devices  77.1 us (26%)
  blocking collectives  30.5 us (10%)
  waiting for transfers between devices  29.9 us (10%)
  local copies, waits for them, and re-layouts  21.6 us (7%)
  other arithmetic  10.4 us (4%)
    pallas_call x4, Pallas kernels, panel_call(): pl.pallas_call(functools.partial(panel_kernel, slope_mode, stored_in, sto...  123 us
    ppermute x40, starting transfers between devices, gather_axis(): lax.ppermute(vector, name, [(i, (i + shift) % count) for i in range(count)])  77.1 us
    psum x2, blocking collectives, local(): sensitivity = lax.psum(lax.psum(local_sums, 'col'), 'row')  30.5 us
    ppermute x40, waiting for transfers between devices, gather_axis(): lax.ppermute(vector, name, [(i, (i + shift) % count) for i in range(count)])  29.9 us
    unnamed x59, local copies, waits for them, and re-layouts  13.5 us
  transfers between devices with their start and end apart: 40, of which 20 were waited for; matrix products, arithmetic and copies ran while one was open for 1% of the time, Pallas kernels for 0%

profile of v8, /device:TPU:0, one launch (start us, length us, event | category | flops | bytes accessed | tf_op | source)
XLA Modules:
  0.0 295.2 jit_solution(15701770386517284276)
XLA Ops:
  2.1 3.0 %collective-permute-start.1 = (f32[296,12]{0,1:T(8,128)S(1)}, f32[296,12]{0,1:T(8,128)S(1)}, u32[]{:S(2)}, u32[]{:S(2)}) collective-permute-start(f32[296,12]{0,1:T(8,128)S(1)} %pad_maximum_fusion.4), channel_id=1, source_target_pairs={{0,2},{1,3},{2,0},{3,1},{4,6},{5,7},{6,4},{7,5},{8,10},{9,11},{10,... | collective-permute-start | bytes 42632 | tf_op jit(solution)/shard_map/ppermute | solution.py:385
  24.9 2.9 collective-permute-done.4
  27.9 4.4 %collective-permute-start.5 = (f32[1184,12]{0,1:T(8,128)S(1)}, f32[1184,12]{0,1:T(8,128)S(1)}, u32[]{:S(2)}, u32[]{:S(2)}) collective-permute-start(f32[1184,12]{0,1:T(8,128)S(1)} %reshape.194), channel_id=1, source_target_pairs={{0,20},{4,24},{8,28},{12,0},{16,4},{20,8},{24,12},{28,16},{1,21},{... | collective-permute-start | bytes 170504 | tf_op jit(solution)/shard_map/ppermute | solution.py:385
  32.3 3.4 %collective-permute-done.5 = f32[1184,12]{0,1:T(8,128)S(1)} collective-permute-done((f32[1184,12]{0,1:T(8,128)S(1)}, f32[1184,12]{0,1:T(8,128)S(1)}, u32[]{:S(2)}, u32[]{:S(2)}) %collective-permute-start.5) | collective-permute-done | bytes 56864 | tf_op jit(solution)/shard_map/ppermute | solution.py:385
  38.2 47.1 %shard_map.104 = (f32[296,12]{1,0:T(8,128)}, f32[296,9472]{1,0:T(8,128)}, f32[296,9472]{1,0:T(8,128)}) custom-call(f32[1]{0:T(128)S(6)} %copy.219.wave_ref, f32[296,8]{1,0:T(8,128)} %copy.147.own_ref, f32[4,9472]{1,0:T(4,128)} %get-tuple-element.33.all_ref, f32[12,9472]{1,0:T(8,128)} %pad_maximum_fusion.vec_ref), custom_call_target="tpu_custom_call" | custom-call | flops 420556800 | bytes 23059584 | tf_op jit(solution)/shard_map/pallas_call | solution.py:364
  97.7 3.8 %collective-permute-start.13 = (f32[1184,8]{0,1:T(8,128)S(1)}, f32[1184,8]{0,1:T(8,128)S(1)}, u32[]{:S(2)}, u32[]{:S(2)}) collective-permute-start(f32[1184,8]{0,1:T(8,128)S(1)} %reshape.196), channel_id=1, source_target_pairs={{0,28},{4,0},{8,4},{12,8},{16,12},{20,16},{24,20},{28,24},{1,29},{... | collective-permute-start | bytes 113672 | tf_op jit(solution)/shard_map/ppermute | solution.py:385
  104.2 2.9 collective-permute-done.14
  107.1 3.6 %collective-permute-start.15 = (f32[1184,8]{0,1:T(8,128)S(1)}, f32[1184,8]{0,1:T(8,128)S(1)}, u32[]{:S(2)}, u32[]{:S(2)}) collective-permute-start(f32[1184,8]{0,1:T(8,128)S(1)} %reshape.196), channel_id=1, source_target_pairs={{0,20},{4,24},{8,28},{12,0},{16,4},{20,8},{24,12},{28,16},{1,21},{... | collective-permute-start | bytes 113672 | tf_op jit(solution)/shard_map/ppermute | solution.py:385
  114.1 4.2 %copy-done = f32[296,9472]{1,0:T(8,128)S(1)} copy-done((f32[296,9472]{1,0:T(8,128)S(1)}, f32[296,9472]{1,0:T(8,128)}, u32[]{:S(2)}) %copy-start) | copy-done | bytes 11214872
  118.3 19.2 %shard_map.105 = f32[296,12]{1,0:T(8,128)S(1)} custom-call(f32[1]{0:T(128)S(6)} %copy.219.wave_ref, f32[296,8]{1,0:T(8,128)S(1)} %copy-done.3, f32[4,9472]{1,0:T(4,128)S(1)} %copy-done.4, f32[12,9472]{1,0:T(8,128)S(1)} %pad_maximum_fusion.1.vec_ref, f32[296,9472]{1,0:T(8,128)S(1)} %copy-done, f32[296,9472]{1,0:T(8,128)} %get-tuple-element.9.refs_1_), custom_call_target="tpu_custom_call" | custom-call | flops 89718784 | bytes 23059584 | tf_op jit(solution)/shard_map/pallas_call | solution.py:364
  142.2 4.0 %collective-permute-start.29 = (f32[1184,8]{0,1:T(8,128)S(1)}, f32[1184,8]{0,1:T(8,128)S(1)}, u32[]{:S(2)}, u32[]{:S(2)}) collective-permute-start(f32[1184,8]{0,1:T(8,128)S(1)} %reshape.199), channel_id=1, source_target_pairs={{0,4},{4,8},{8,12},{12,16},{16,20},{20,24},{24,28},{28,0},{1,5},{5... | collective-permute-start | bytes 113672 | tf_op jit(solution)/shard_map/ppermute | solution.py:385
  148.6 3.1 %collective-permute-start.26 = (f32[1184,8]{0,1:T(8,128)S(1)}, f32[1184,8]{0,1:T(8,128)S(1)}, u32[]{:S(2)}, u32[]{:S(2)}) collective-permute-start(f32[1184,8]{0,1:T(8,128)S(1)} %reshape.199), channel_id=1, source_target_pairs={{0,16},{4,20},{8,24},{12,28},{16,0},{20,4},{24,8},{28,12},{1,17},{... | collective-permute-start | bytes 113672 | tf_op jit(solution)/shard_map/ppermute | solution.py:385
  151.6 2.7 collective-permute-start.23
  160.0 3.8 %collective-permute-start.25 = (f32[1184,8]{0,1:T(8,128)S(1)}, f32[1184,8]{0,1:T(8,128)S(1)}, u32[]{:S(2)}, u32[]{:S(2)}) collective-permute-start(f32[1184,8]{0,1:T(8,128)S(1)} %reshape.199), channel_id=1, source_target_pairs={{0,20},{4,24},{8,28},{12,0},{16,4},{20,8},{24,12},{28,16},{1,21},{... | collective-permute-start | bytes 113672 | tf_op jit(solution)/shard_map/ppermute | solution.py:385
  167.6 4.2 %copy-done.1 = f32[296,9472]{1,0:T(8,128)S(1)} copy-done((f32[296,9472]{1,0:T(8,128)S(1)}, f32[296,9472]{1,0:T(8,128)}, u32[]{:S(2)}) %copy-start.1) | copy-done | bytes 11214872
  171.8 19.2 %shard_map.106 = f32[296,12]{1,0:T(8,128)S(1)} custom-call(f32[1]{0:T(128)S(6)} %copy.219.wave_ref, f32[296,8]{1,0:T(8,128)S(1)} %copy-done.3, f32[4,9472]{1,0:T(4,128)S(1)} %copy-done.4, f32[12,9472]{1,0:T(8,128)S(1)} %pad_maximum_fusion.2.vec_ref, f32[296,9472]{1,0:T(8,128)S(1)} %copy-done.1, f32[296,9472]{1,0:T(8,128)} %get-tuple-element.9.refs_1_), custom_call_target="tpu_custom_call" | custom-call | flops 89718784 | bytes 23059584 | tf_op jit(solution)/shard_map/pallas_call | solution.py:364
  195.7 3.6 %collective-permute-start.39 = (f32[1184,8]{0,1:T(8,128)S(1)}, f32[1184,8]{0,1:T(8,128)S(1)}, u32[]{:S(2)}, u32[]{:S(2)}) collective-permute-start(f32[1184,8]{0,1:T(8,128)S(1)} %reshape.202), channel_id=1, source_target_pairs={{0,4},{4,8},{8,12},{12,16},{16,20},{20,24},{24,28},{28,0},{1,5},{5... | collective-permute-start | bytes 113672 | tf_op jit(solution)/shard_map/ppermute | solution.py:385
  199.6 3.3 %collective-permute-start.37 = (f32[1184,8]{0,1:T(8,128)S(1)}, f32[1184,8]{0,1:T(8,128)S(1)}, u32[]{:S(2)}, u32[]{:S(2)}) collective-permute-start(f32[1184,8]{0,1:T(8,128)S(1)} %reshape.202), channel_id=1, source_target_pairs={{0,12},{4,16},{8,20},{12,24},{16,28},{20,0},{24,4},{28,8},{1,13},{... | collective-permute-start | bytes 113672 | tf_op jit(solution)/shard_map/ppermute | solution.py:385
  204.8 2.7 collective-permute-start.33
  213.1 3.8 %collective-permute-start.35 = (f32[1184,8]{0,1:T(8,128)S(1)}, f32[1184,8]{0,1:T(8,128)S(1)}, u32[]{:S(2)}, u32[]{:S(2)}) collective-permute-start(f32[1184,8]{0,1:T(8,128)S(1)} %reshape.202), channel_id=1, source_target_pairs={{0,20},{4,24},{8,28},{12,0},{16,4},{20,8},{24,12},{28,16},{1,21},{... | collective-permute-start | bytes 113672 | tf_op jit(solution)/shard_map/ppermute | solution.py:385
  222.0 4.2 %copy-done.2 = f32[296,9472]{1,0:T(8,128)S(1)} copy-done((f32[296,9472]{1,0:T(8,128)S(1)}, f32[296,9472]{1,0:T(8,128)}, u32[]{:S(2)}) %copy-start.2) | copy-done | bytes 11214872
  226.2 37.4 %shard_map.107 = f32[296,12]{1,0:T(8,128)S(1)} custom-call(f32[1]{0:T(128)S(6)} %copy.219.wave_ref, f32[296,8]{1,0:T(8,128)S(1)} %copy-done.3, f32[4,9472]{1,0:T(4,128)S(1)} %copy-done.4, f32[12,9472]{1,0:T(8,128)S(1)} %pad_maximum_fusion.3.vec_ref, f32[296,9472]{1,0:T(8,128)S(1)} %copy-done.2, f32[296,9472]{1,0:T(8,128)} %get-tuple-element.9.refs_1_), custom_call_target="tpu_custom_call" | custom-call | flops 168222720 | bytes 23059584 | tf_op jit(solution)/shard_map/pallas_call | solution.py:364
  264.1 5.6 %psum.14 = f32[4,128]{1,0:T(4,128)S(1)} all-reduce(f32[4,128]{1,0:T(4,128)S(1)} %fusion.14), channel_id=1, replica_groups=mesh['row'=8,'col'=4] {'col'}, use_global_device_ids=true, to_apply=%region_13.16 | all-reduce | flops 512 | bytes 4096 | tf_op jit(solution)/shard_map/psum | solution.py:512
  269.7 24.8 %psum.15 = f32[4,128]{1,0:T(4,128)} all-reduce(f32[4,128]{1,0:T(4,128)S(1)} %psum.14), channel_id=1, replica_groups=mesh['row'=8,'col'=4] {'row'}, use_global_device_ids=true, to_apply=%region_14.17 | all-reduce | flops 512 | bytes 4096 | tf_op jit(solution)/shard_map/psum | solution.py:512
  (229 shorter events, 75.9 us)
Async XLA Ops:
  2.1 8.2 %collective-permute-start.1 = (f32[296,12]{0,1:T(8,128)S(1)}, f32[296,12]{0,1:T(8,128)S(1)}, u32[]{:S(2)}, u32[]{:S(2)}) collective-permute-start(f32[296,12]{0,1:T(8,128)S(1)} %pad_maximum_fusion.4), channel_id=1, source_target_pairs={{0,2},{1,3},{2,0},{3,1},{4,6},{5,7},{6,4},{7,5},{8,10},{9,11},{10,... | collective-permute-start | bytes 42632 | tf_op jit(solution)/shard_map/ppermute | solution.py:385
  5.1 5.2 %collective-permute-start.2 = (f32[296,12]{0,1:T(8,128)S(1)}, f32[296,12]{0,1:T(8,128)S(1)}, u32[]{:S(2)}, u32[]{:S(2)}) collective-permute-start(f32[296,12]{0,1:T(8,128)S(1)} %pad_maximum_fusion.4), channel_id=1, source_target_pairs={{0,1},{1,2},{2,3},{3,0},{4,5},{5,6},{6,7},{7,4},{8,9},{9,10},{10,1... | collective-permute-start | bytes 42632 | tf_op jit(solution)/shard_map/ppermute | solution.py:385
  11.3 24.5 %collective-permute-start.9 = (f32[1184,12]{0,1:T(8,128)S(1)}, f32[1184,12]{0,1:T(8,128)S(1)}, u32[]{:S(2)}, u32[]{:S(2)}) collective-permute-start(f32[1184,12]{0,1:T(8,128)S(1)} %reshape.194), channel_id=1, source_target_pairs={{0,4},{4,8},{8,12},{12,16},{16,20},{20,24},{24,28},{28,0},{1,5},{5... | collective-permute-start | bytes 170504 | tf_op jit(solution)/shard_map/ppermute | solution.py:385
  12.9 22.9 %collective-permute-start.8 = (f32[1184,12]{0,1:T(8,128)S(1)}, f32[1184,12]{0,1:T(8,128)S(1)}, u32[]{:S(2)}, u32[]{:S(2)}) collective-permute-start(f32[1184,12]{0,1:T(8,128)S(1)} %reshape.194), channel_id=1, source_target_pairs={{0,8},{4,12},{8,16},{12,20},{16,24},{20,28},{24,0},{28,4},{1,9},{5... | collective-permute-start | bytes 170504 | tf_op jit(solution)/shard_map/ppermute | solution.py:385
  14.5 21.3 %collective-permute-start.7 = (f32[1184,12]{0,1:T(8,128)S(1)}, f32[1184,12]{0,1:T(8,128)S(1)}, u32[]{:S(2)}, u32[]{:S(2)}) collective-permute-start(f32[1184,12]{0,1:T(8,128)S(1)} %reshape.194), channel_id=1, source_target_pairs={{0,12},{4,16},{8,20},{12,24},{16,28},{20,0},{24,4},{28,8},{1,13},{... | collective-permute-start | bytes 170504 | tf_op jit(solution)/shard_map/ppermute | solution.py:385
  17.0 18.7 %collective-permute-start.6 = (f32[1184,12]{0,1:T(8,128)S(1)}, f32[1184,12]{0,1:T(8,128)S(1)}, u32[]{:S(2)}, u32[]{:S(2)}) collective-permute-start(f32[1184,12]{0,1:T(8,128)S(1)} %reshape.194), channel_id=1, source_target_pairs={{0,16},{4,20},{8,24},{12,28},{16,0},{20,4},{24,8},{28,12},{1,17},{... | collective-permute-start | bytes 170504 | tf_op jit(solution)/shard_map/ppermute | solution.py:385
  22.7 5.2 %collective-permute-start.4 = (f32[1184,12]{0,1:T(8,128)S(1)}, f32[1184,12]{0,1:T(8,128)S(1)}, u32[]{:S(2)}, u32[]{:S(2)}) collective-permute-start(f32[1184,12]{0,1:T(8,128)S(1)} %reshape.194), channel_id=1, source_target_pairs={{0,24},{4,28},{8,0},{12,4},{16,8},{20,12},{24,16},{28,20},{1,25},{... | collective-permute-start | bytes 170504 | tf_op jit(solution)/shard_map/ppermute | solution.py:385
  27.9 7.9 %collective-permute-start.5 = (f32[1184,12]{0,1:T(8,128)S(1)}, f32[1184,12]{0,1:T(8,128)S(1)}, u32[]{:S(2)}, u32[]{:S(2)}) collective-permute-start(f32[1184,12]{0,1:T(8,128)S(1)} %reshape.194), channel_id=1, source_target_pairs={{0,20},{4,24},{8,28},{12,0},{16,4},{20,8},{24,12},{28,16},{1,21},{... | collective-permute-start | bytes 170504 | tf_op jit(solution)/shard_map/ppermute | solution.py:385
  91.1 21.3 %collective-permute-start.19 = (f32[1184,8]{0,1:T(8,128)S(1)}, f32[1184,8]{0,1:T(8,128)S(1)}, u32[]{:S(2)}, u32[]{:S(2)}) collective-permute-start(f32[1184,8]{0,1:T(8,128)S(1)} %reshape.196), channel_id=1, source_target_pairs={{0,4},{4,8},{8,12},{12,16},{16,20},{20,24},{24,28},{28,0},{1,5},{5... | collective-permute-start | bytes 113672 | tf_op jit(solution)/shard_map/ppermute | solution.py:385
  93.8 18.6 %collective-permute-start.18 = (f32[1184,8]{0,1:T(8,128)S(1)}, f32[1184,8]{0,1:T(8,128)S(1)}, u32[]{:S(2)}, u32[]{:S(2)}) collective-permute-start(f32[1184,8]{0,1:T(8,128)S(1)} %reshape.196), channel_id=1, source_target_pairs={{0,8},{4,12},{8,16},{12,20},{16,24},{20,28},{24,0},{28,4},{1,9},{5... | collective-permute-start | bytes 113672 | tf_op jit(solution)/shard_map/ppermute | solution.py:385
  95.5 16.8 %collective-permute-start.17 = (f32[1184,8]{0,1:T(8,128)S(1)}, f32[1184,8]{0,1:T(8,128)S(1)}, u32[]{:S(2)}, u32[]{:S(2)}) collective-permute-start(f32[1184,8]{0,1:T(8,128)S(1)} %reshape.196), channel_id=1, source_target_pairs={{0,12},{4,16},{8,20},{12,24},{16,28},{20,0},{24,4},{28,8},{1,13},{... | collective-permute-start | bytes 113672 | tf_op jit(solution)/shard_map/ppermute | solution.py:385
  95.8 16.5 %collective-permute-start.16 = (f32[1184,8]{0,1:T(8,128)S(1)}, f32[1184,8]{0,1:T(8,128)S(1)}, u32[]{:S(2)}, u32[]{:S(2)}) collective-permute-start(f32[1184,8]{0,1:T(8,128)S(1)} %reshape.196), channel_id=1, source_target_pairs={{0,16},{4,20},{8,24},{12,28},{16,0},{20,4},{24,8},{28,12},{1,17},{... | collective-permute-start | bytes 113672 | tf_op jit(solution)/shard_map/ppermute | solution.py:385
  97.7 5.4 %collective-permute-start.13 = (f32[1184,8]{0,1:T(8,128)S(1)}, f32[1184,8]{0,1:T(8,128)S(1)}, u32[]{:S(2)}, u32[]{:S(2)}) collective-permute-start(f32[1184,8]{0,1:T(8,128)S(1)} %reshape.196), channel_id=1, source_target_pairs={{0,28},{4,0},{8,4},{12,8},{16,12},{20,16},{24,20},{28,24},{1,29},{... | collective-permute-start | bytes 113672 | tf_op jit(solution)/shard_map/ppermute | solution.py:385
  107.1 5.2 %collective-permute-start.15 = (f32[1184,8]{0,1:T(8,128)S(1)}, f32[1184,8]{0,1:T(8,128)S(1)}, u32[]{:S(2)}, u32[]{:S(2)}) collective-permute-start(f32[1184,8]{0,1:T(8,128)S(1)} %reshape.196), channel_id=1, source_target_pairs={{0,20},{4,24},{8,28},{12,0},{16,4},{20,8},{24,12},{28,16},{1,21},{... | collective-permute-start | bytes 113672 | tf_op jit(solution)/shard_map/ppermute | solution.py:385
  142.2 23.3 %collective-permute-start.29 = (f32[1184,8]{0,1:T(8,128)S(1)}, f32[1184,8]{0,1:T(8,128)S(1)}, u32[]{:S(2)}, u32[]{:S(2)}) collective-permute-start(f32[1184,8]{0,1:T(8,128)S(1)} %reshape.199), channel_id=1, source_target_pairs={{0,4},{4,8},{8,12},{12,16},{16,20},{20,24},{24,28},{28,0},{1,5},{5... | collective-permute-start | bytes 113672 | tf_op jit(solution)/shard_map/ppermute | solution.py:385
  146.2 19.3 %collective-permute-start.28 = (f32[1184,8]{0,1:T(8,128)S(1)}, f32[1184,8]{0,1:T(8,128)S(1)}, u32[]{:S(2)}, u32[]{:S(2)}) collective-permute-start(f32[1184,8]{0,1:T(8,128)S(1)} %reshape.199), channel_id=1, source_target_pairs={{0,8},{4,12},{8,16},{12,20},{16,24},{20,28},{24,0},{28,4},{1,9},{5... | collective-permute-start | bytes 113672 | tf_op jit(solution)/shard_map/ppermute | solution.py:385
  146.4 19.1 %collective-permute-start.27 = (f32[1184,8]{0,1:T(8,128)S(1)}, f32[1184,8]{0,1:T(8,128)S(1)}, u32[]{:S(2)}, u32[]{:S(2)}) collective-permute-start(f32[1184,8]{0,1:T(8,128)S(1)} %reshape.199), channel_id=1, source_target_pairs={{0,12},{4,16},{8,20},{12,24},{16,28},{20,0},{24,4},{28,8},{1,13},{... | collective-permute-start | bytes 113672 | tf_op jit(solution)/shard_map/ppermute | solution.py:385
  148.6 16.9 %collective-permute-start.26 = (f32[1184,8]{0,1:T(8,128)S(1)}, f32[1184,8]{0,1:T(8,128)S(1)}, u32[]{:S(2)}, u32[]{:S(2)}) collective-permute-start(f32[1184,8]{0,1:T(8,128)S(1)} %reshape.199), channel_id=1, source_target_pairs={{0,16},{4,20},{8,24},{12,28},{16,0},{20,4},{24,8},{28,12},{1,17},{... | collective-permute-start | bytes 113672 | tf_op jit(solution)/shard_map/ppermute | solution.py:385
  160.0 5.5 %collective-permute-start.25 = (f32[1184,8]{0,1:T(8,128)S(1)}, f32[1184,8]{0,1:T(8,128)S(1)}, u32[]{:S(2)}, u32[]{:S(2)}) collective-permute-start(f32[1184,8]{0,1:T(8,128)S(1)} %reshape.199), channel_id=1, source_target_pairs={{0,20},{4,24},{8,28},{12,0},{16,4},{20,8},{24,12},{28,16},{1,21},{... | collective-permute-start | bytes 113672 | tf_op jit(solution)/shard_map/ppermute | solution.py:385
  195.7 22.9 %collective-permute-start.39 = (f32[1184,8]{0,1:T(8,128)S(1)}, f32[1184,8]{0,1:T(8,128)S(1)}, u32[]{:S(2)}, u32[]{:S(2)}) collective-permute-start(f32[1184,8]{0,1:T(8,128)S(1)} %reshape.202), channel_id=1, source_target_pairs={{0,4},{4,8},{8,12},{12,16},{16,20},{20,24},{24,28},{28,0},{1,5},{5... | collective-permute-start | bytes 113672 | tf_op jit(solution)/shard_map/ppermute | solution.py:385
  199.4 19.3 %collective-permute-start.38 = (f32[1184,8]{0,1:T(8,128)S(1)}, f32[1184,8]{0,1:T(8,128)S(1)}, u32[]{:S(2)}, u32[]{:S(2)}) collective-permute-start(f32[1184,8]{0,1:T(8,128)S(1)} %reshape.202), channel_id=1, source_target_pairs={{0,8},{4,12},{8,16},{12,20},{16,24},{20,28},{24,0},{28,4},{1,9},{5... | collective-permute-start | bytes 113672 | tf_op jit(solution)/shard_map/ppermute | solution.py:385
  199.6 19.1 %collective-permute-start.37 = (f32[1184,8]{0,1:T(8,128)S(1)}, f32[1184,8]{0,1:T(8,128)S(1)}, u32[]{:S(2)}, u32[]{:S(2)}) collective-permute-start(f32[1184,8]{0,1:T(8,128)S(1)} %reshape.202), channel_id=1, source_target_pairs={{0,12},{4,16},{8,20},{12,24},{16,28},{20,0},{24,4},{28,8},{1,13},{... | collective-permute-start | bytes 113672 | tf_op jit(solution)/shard_map/ppermute | solution.py:385
  202.9 15.7 %collective-permute-start.36 = (f32[1184,8]{0,1:T(8,128)S(1)}, f32[1184,8]{0,1:T(8,128)S(1)}, u32[]{:S(2)}, u32[]{:S(2)}) collective-permute-start(f32[1184,8]{0,1:T(8,128)S(1)} %reshape.202), channel_id=1, source_target_pairs={{0,16},{4,20},{8,24},{12,28},{16,0},{20,4},{24,8},{28,12},{1,17},{... | collective-permute-start | bytes 113672 | tf_op jit(solution)/shard_map/ppermute | solution.py:385
  213.1 5.5 %collective-permute-start.35 = (f32[1184,8]{0,1:T(8,128)S(1)}, f32[1184,8]{0,1:T(8,128)S(1)}, u32[]{:S(2)}, u32[]{:S(2)}) collective-permute-start(f32[1184,8]{0,1:T(8,128)S(1)} %reshape.202), channel_id=1, source_target_pairs={{0,20},{4,24},{8,28},{12,0},{16,4},{20,8},{24,12},{28,16},{1,21},{... | collective-permute-start | bytes 113672 | tf_op jit(solution)/shard_map/ppermute | solution.py:385
  (25 other events, 116.3 us)

commit v9 on v8

--- a/solution.py
+++ b/solution.py
@@ -340,7 +340,7 @@
         out_shape += [jax.ShapeDtypeStruct((own_total, panel_total), jnp.float32)] * 2
         matrix_bytes = 8 * elements
     vmem = pl.BlockSpec(memory_space=pltpu.VMEM)
-    hbm = pl.BlockSpec(memory_space=pl.ANY)
+    hbm = pl.BlockSpec(memory_space=pltpu.HBM)
     params = {}
     if stored_in:
         params["scratch_shapes"] = [
@@ -348,7 +348,7 @@
             pltpu.VMEM((own_total, panel_total), jnp.float32),
             pltpu.SemaphoreType.DMA((2, own_total // 8)),
         ]
-        params["compiler_params"] = pltpu.CompilerParams(vmem_limit_bytes=matrix_bytes + 16 * 1024 * 1024)
+        params["compiler_params"] = pltpu.CompilerParams(vmem_limit_bytes=60 * 1024 * 1024)
     elif store_out:
         params["scratch_shapes"] = [
             pltpu.VMEM((2, 8, panel_total), jnp.float32),

time: 296 us -> 289 us (0.976)
  local copies, waits for them, and re-layouts: 21.6 us -> 8.39 us
  other arithmetic: 10.4 us -> 15 us
    unnamed x59 -> x49, local copies, waits for them, and re-layouts: 13.5 us -> 0.26 us
where the time goes in v9:
time: 289 us; the launch traced here: 288 us
  Pallas kernels  124 us (43%)
  starting transfers between devices  77.1 us (27%)
  blocking collectives  30.5 us (11%)
  waiting for transfers between devices  29.9 us (10%)
  other arithmetic  15 us (5%)
  local copies, waits for them, and re-layouts  8.39 us (3%)
    pallas_call x4, Pallas kernels, panel_call(): pl.pallas_call(functools.partial(panel_kernel, slope_mode, stored_in, sto...  124 us
    ppermute x40, starting transfers between devices, gather_axis(): lax.ppermute(vector, name, [(i, (i + shift) % count) for i in range(count)])  77.1 us
    psum x2, blocking collectives, local(): sensitivity = lax.psum(lax.psum(local_sums, 'col'), 'row')  30.5 us
    ppermute x40, waiting for transfers between devices, gather_axis(): lax.ppermute(vector, name, [(i, (i + shift) % count) for i in range(count)])  29.9 us
  transfers between devices with their start and end apart: 40, of which 20 were waited for; matrix products, arithmetic and copies ran while one was open for 1% of the time, Pallas kernels for 0%

profile of v9, /device:TPU:0, one launch (start us, length us, event | category | flops | bytes accessed | tf_op | source)
XLA Modules:
  0.0 288.5 jit_solution(14317706891951157717)
XLA Ops:
  2.1 3.0 %collective-permute-start.1 = (f32[296,12]{0,1:T(8,128)S(1)}, f32[296,12]{0,1:T(8,128)S(1)}, u32[]{:S(2)}, u32[]{:S(2)}) collective-permute-start(f32[296,12]{0,1:T(8,128)S(1)} %pad_maximum_fusion.4), channel_id=1, source_target_pairs={{0,2},{1,3},{2,0},{3,1},{4,6},{5,7},{6,4},{7,5},{8,10},{9,11},{10,... | collective-permute-start | bytes 42632 | tf_op jit(solution)/shard_map/ppermute | solution.py:385
  14.5 2.6 collective-permute-start.7
  18.3 2.3 collective-permute-start.3
  24.9 2.9 %collective-permute-done.4 = f32[1184,12]{0,1:T(8,128)S(1)} collective-permute-done((f32[1184,12]{0,1:T(8,128)S(1)}, f32[1184,12]{0,1:T(8,128)S(1)}, u32[]{:S(2)}, u32[]{:S(2)}) %collective-permute-start.4) | collective-permute-done | bytes 56864 | tf_op jit(solution)/shard_map/ppermute | solution.py:385
  27.9 4.4 %collective-permute-start.5 = (f32[1184,12]{0,1:T(8,128)S(1)}, f32[1184,12]{0,1:T(8,128)S(1)}, u32[]{:S(2)}, u32[]{:S(2)}) collective-permute-start(f32[1184,12]{0,1:T(8,128)S(1)} %reshape.194), channel_id=1, source_target_pairs={{0,20},{4,24},{8,28},{12,0},{16,4},{20,8},{24,12},{28,16},{1,21},{... | collective-permute-start | bytes 170504 | tf_op jit(solution)/shard_map/ppermute | solution.py:385
  32.3 3.4 %collective-permute-done.5 = f32[1184,12]{0,1:T(8,128)S(1)} collective-permute-done((f32[1184,12]{0,1:T(8,128)S(1)}, f32[1184,12]{0,1:T(8,128)S(1)}, u32[]{:S(2)}, u32[]{:S(2)}) %collective-permute-start.5) | collective-permute-done | bytes 56864 | tf_op jit(solution)/shard_map/ppermute | solution.py:385
  38.2 47.1 %shard_map.104 = (f32[296,12]{1,0:T(8,128)}, f32[296,9472]{1,0:T(8,128)}, f32[296,9472]{1,0:T(8,128)}) custom-call(f32[1]{0:T(128)S(6)} %copy.219.wave_ref, f32[296,8]{1,0:T(8,128)} %copy.147.own_ref, f32[4,9472]{1,0:T(4,128)} %get-tuple-element.33.all_ref, f32[12,9472]{1,0:T(8,128)} %pad_maximum_fusion.vec_ref), custom_call_target="tpu_custom_call" | custom-call | flops 420556800 | bytes 23059584 | tf_op jit(solution)/shard_map/pallas_call | solution.py:364
  91.1 2.7 collective-permute-start.19
  97.6 3.8 %collective-permute-start.13 = (f32[1184,8]{0,1:T(8,128)S(1)}, f32[1184,8]{0,1:T(8,128)S(1)}, u32[]{:S(2)}, u32[]{:S(2)}) collective-permute-start(f32[1184,8]{0,1:T(8,128)S(1)} %reshape.196), channel_id=1, source_target_pairs={{0,28},{4,0},{8,4},{12,8},{16,12},{20,16},{24,20},{28,24},{1,29},{... | collective-permute-start | bytes 113672 | tf_op jit(solution)/shard_map/ppermute | solution.py:385
  104.1 2.9 %collective-permute-done.14 = f32[1184,8]{0,1:T(8,128)S(1)} collective-permute-done((f32[1184,8]{0,1:T(8,128)S(1)}, f32[1184,8]{0,1:T(8,128)S(1)}, u32[]{:S(2)}, u32[]{:S(2)}) %collective-permute-start.14) | collective-permute-done | bytes 37920 | tf_op jit(solution)/shard_map/ppermute | solution.py:385
  107.1 3.6 %collective-permute-start.15 = (f32[1184,8]{0,1:T(8,128)S(1)}, f32[1184,8]{0,1:T(8,128)S(1)}, u32[]{:S(2)}, u32[]{:S(2)}) collective-permute-start(f32[1184,8]{0,1:T(8,128)S(1)} %reshape.196), channel_id=1, source_target_pairs={{0,20},{4,24},{8,28},{12,0},{16,4},{20,8},{24,12},{28,16},{1,21},{... | collective-permute-start | bytes 113672 | tf_op jit(solution)/shard_map/ppermute | solution.py:385
  114.2 19.5 %shard_map.105 = f32[296,12]{1,0:T(8,128)} custom-call(f32[1]{0:T(128)S(6)} %copy.219.wave_ref, f32[296,8]{1,0:T(8,128)} %copy.147.own_ref, f32[4,9472]{1,0:T(4,128)} %get-tuple-element.33.all_ref, f32[12,9472]{1,0:T(8,128)} %pad_maximum_fusion.1.vec_ref, f32[296,9472]{1,0:T(8,128)} %get-tuple-element.8.refs_0_, f32[296,9472]{1,0:T(8,128)} %get-tuple-element.9.refs_1_), custom_call_target="tpu_custom_call" | custom-call | flops 89718784 | bytes 23059584 | tf_op jit(solution)/shard_map/pallas_call | solution.py:364
  139.4 4.0 %collective-permute-start.29 = (f32[1184,8]{0,1:T(8,128)S(1)}, f32[1184,8]{0,1:T(8,128)S(1)}, u32[]{:S(2)}, u32[]{:S(2)}) collective-permute-start(f32[1184,8]{0,1:T(8,128)S(1)} %reshape.199), channel_id=1, source_target_pairs={{0,4},{4,8},{8,12},{12,16},{16,20},{20,24},{24,28},{28,0},{1,5},{5... | collective-permute-start | bytes 113672 | tf_op jit(solution)/shard_map/ppermute | solution.py:385
  145.8 3.1 %collective-permute-start.26 = (f32[1184,8]{0,1:T(8,128)S(1)}, f32[1184,8]{0,1:T(8,128)S(1)}, u32[]{:S(2)}, u32[]{:S(2)}) collective-permute-start(f32[1184,8]{0,1:T(8,128)S(1)} %reshape.199), channel_id=1, source_target_pairs={{0,16},{4,20},{8,24},{12,28},{16,0},{20,4},{24,8},{28,12},{1,17},{... | collective-permute-start | bytes 113672 | tf_op jit(solution)/shard_map/ppermute | solution.py:385
  148.9 2.7 collective-permute-start.23
  157.2 3.8 %collective-permute-start.25 = (f32[1184,8]{0,1:T(8,128)S(1)}, f32[1184,8]{0,1:T(8,128)S(1)}, u32[]{:S(2)}, u32[]{:S(2)}) collective-permute-start(f32[1184,8]{0,1:T(8,128)S(1)} %reshape.199), channel_id=1, source_target_pairs={{0,20},{4,24},{8,28},{12,0},{16,4},{20,8},{24,12},{28,16},{1,21},{... | collective-permute-start | bytes 113672 | tf_op jit(solution)/shard_map/ppermute | solution.py:385
  165.6 19.5 %shard_map.106 = f32[296,12]{1,0:T(8,128)} custom-call(f32[1]{0:T(128)S(6)} %copy.219.wave_ref, f32[296,8]{1,0:T(8,128)} %copy.147.own_ref, f32[4,9472]{1,0:T(4,128)} %get-tuple-element.33.all_ref, f32[12,9472]{1,0:T(8,128)} %pad_maximum_fusion.2.vec_ref, f32[296,9472]{1,0:T(8,128)} %get-tuple-element.8.refs_0_, f32[296,9472]{1,0:T(8,128)} %get-tuple-element.9.refs_1_), custom_call_target="tpu_custom_call" | custom-call | flops 89718784 | bytes 23059584 | tf_op jit(solution)/shard_map/pallas_call | solution.py:364
  190.9 3.6 %collective-permute-start.39 = (f32[1184,8]{0,1:T(8,128)S(1)}, f32[1184,8]{0,1:T(8,128)S(1)}, u32[]{:S(2)}, u32[]{:S(2)}) collective-permute-start(f32[1184,8]{0,1:T(8,128)S(1)} %reshape.202), channel_id=1, source_target_pairs={{0,4},{4,8},{8,12},{12,16},{16,20},{20,24},{24,28},{28,0},{1,5},{5... | collective-permute-start | bytes 113672 | tf_op jit(solution)/shard_map/ppermute | solution.py:385
  194.8 3.3 %collective-permute-start.37 = (f32[1184,8]{0,1:T(8,128)S(1)}, f32[1184,8]{0,1:T(8,128)S(1)}, u32[]{:S(2)}, u32[]{:S(2)}) collective-permute-start(f32[1184,8]{0,1:T(8,128)S(1)} %reshape.202), channel_id=1, source_target_pairs={{0,12},{4,16},{8,20},{12,24},{16,28},{20,0},{24,4},{28,8},{1,13},{... | collective-permute-start | bytes 113672 | tf_op jit(solution)/shard_map/ppermute | solution.py:385
  200.0 2.7 collective-permute-start.33
  208.4 3.8 %collective-permute-start.35 = (f32[1184,8]{0,1:T(8,128)S(1)}, f32[1184,8]{0,1:T(8,128)S(1)}, u32[]{:S(2)}, u32[]{:S(2)}) collective-permute-start(f32[1184,8]{0,1:T(8,128)S(1)} %reshape.202), channel_id=1, source_target_pairs={{0,20},{4,24},{8,28},{12,0},{16,4},{20,8},{24,12},{28,16},{1,21},{... | collective-permute-start | bytes 113672 | tf_op jit(solution)/shard_map/ppermute | solution.py:385
  218.1 37.7 %shard_map.107 = f32[296,12]{1,0:T(8,128)} custom-call(f32[1]{0:T(128)S(6)} %copy.219.wave_ref, f32[296,8]{1,0:T(8,128)} %copy.147.own_ref, f32[4,9472]{1,0:T(4,128)} %get-tuple-element.33.all_ref, f32[12,9472]{1,0:T(8,128)} %pad_maximum_fusion.3.vec_ref, f32[296,9472]{1,0:T(8,128)} %get-tuple-element.8.refs_0_, f32[296,9472]{1,0:T(8,128)} %get-tuple-element.9.refs_1_), custom_call_target="tpu_custom_call" | custom-call | flops 168222720 | bytes 23059584 | tf_op jit(solution)/shard_map/pallas_call | solution.py:364
  257.4 5.6 %psum.14 = f32[4,128]{1,0:T(4,128)S(1)} all-reduce(f32[4,128]{1,0:T(4,128)S(1)} %fusion.14), channel_id=1, replica_groups=mesh['row'=8,'col'=4] {'col'}, use_global_device_ids=true, to_apply=%region_13.16 | all-reduce | flops 512 | bytes 4096 | tf_op jit(solution)/shard_map/psum | solution.py:512
  263.0 24.8 %psum.15 = f32[4,128]{1,0:T(4,128)} all-reduce(f32[4,128]{1,0:T(4,128)S(1)} %psum.14), channel_id=1, replica_groups=mesh['row'=8,'col'=4] {'row'}, use_global_device_ids=true, to_apply=%region_14.17 | all-reduce | flops 512 | bytes 4096 | tf_op jit(solution)/shard_map/psum | solution.py:512
  (219 shorter events, 73.4 us)
Async XLA Ops:
  2.1 8.2 %collective-permute-start.1 = (f32[296,12]{0,1:T(8,128)S(1)}, f32[296,12]{0,1:T(8,128)S(1)}, u32[]{:S(2)}, u32[]{:S(2)}) collective-permute-start(f32[296,12]{0,1:T(8,128)S(1)} %pad_maximum_fusion.4), channel_id=1, source_target_pairs={{0,2},{1,3},{2,0},{3,1},{4,6},{5,7},{6,4},{7,5},{8,10},{9,11},{10,... | collective-permute-start | bytes 42632 | tf_op jit(solution)/shard_map/ppermute | solution.py:385
  5.1 5.2 %collective-permute-start.2 = (f32[296,12]{0,1:T(8,128)S(1)}, f32[296,12]{0,1:T(8,128)S(1)}, u32[]{:S(2)}, u32[]{:S(2)}) collective-permute-start(f32[296,12]{0,1:T(8,128)S(1)} %pad_maximum_fusion.4), channel_id=1, source_target_pairs={{0,1},{1,2},{2,3},{3,0},{4,5},{5,6},{6,7},{7,4},{8,9},{9,10},{10,1... | collective-permute-start | bytes 42632 | tf_op jit(solution)/shard_map/ppermute | solution.py:385
  11.3 24.5 %collective-permute-start.9 = (f32[1184,12]{0,1:T(8,128)S(1)}, f32[1184,12]{0,1:T(8,128)S(1)}, u32[]{:S(2)}, u32[]{:S(2)}) collective-permute-start(f32[1184,12]{0,1:T(8,128)S(1)} %reshape.194), channel_id=1, source_target_pairs={{0,4},{4,8},{8,12},{12,16},{16,20},{20,24},{24,28},{28,0},{1,5},{5... | collective-permute-start | bytes 170504 | tf_op jit(solution)/shard_map/ppermute | solution.py:385
  12.9 22.9 %collective-permute-start.8 = (f32[1184,12]{0,1:T(8,128)S(1)}, f32[1184,12]{0,1:T(8,128)S(1)}, u32[]{:S(2)}, u32[]{:S(2)}) collective-permute-start(f32[1184,12]{0,1:T(8,128)S(1)} %reshape.194), channel_id=1, source_target_pairs={{0,8},{4,12},{8,16},{12,20},{16,24},{20,28},{24,0},{28,4},{1,9},{5... | collective-permute-start | bytes 170504 | tf_op jit(solution)/shard_map/ppermute | solution.py:385
  14.5 21.3 %collective-permute-start.7 = (f32[1184,12]{0,1:T(8,128)S(1)}, f32[1184,12]{0,1:T(8,128)S(1)}, u32[]{:S(2)}, u32[]{:S(2)}) collective-permute-start(f32[1184,12]{0,1:T(8,128)S(1)} %reshape.194), channel_id=1, source_target_pairs={{0,12},{4,16},{8,20},{12,24},{16,28},{20,0},{24,4},{28,8},{1,13},{... | collective-permute-start | bytes 170504 | tf_op jit(solution)/shard_map/ppermute | solution.py:385
  17.0 18.7 %collective-permute-start.6 = (f32[1184,12]{0,1:T(8,128)S(1)}, f32[1184,12]{0,1:T(8,128)S(1)}, u32[]{:S(2)}, u32[]{:S(2)}) collective-permute-start(f32[1184,12]{0,1:T(8,128)S(1)} %reshape.194), channel_id=1, source_target_pairs={{0,16},{4,20},{8,24},{12,28},{16,0},{20,4},{24,8},{28,12},{1,17},{... | collective-permute-start | bytes 170504 | tf_op jit(solution)/shard_map/ppermute | solution.py:385
  22.7 5.2 %collective-permute-start.4 = (f32[1184,12]{0,1:T(8,128)S(1)}, f32[1184,12]{0,1:T(8,128)S(1)}, u32[]{:S(2)}, u32[]{:S(2)}) collective-permute-start(f32[1184,12]{0,1:T(8,128)S(1)} %reshape.194), channel_id=1, source_target_pairs={{0,24},{4,28},{8,0},{12,4},{16,8},{20,12},{24,16},{28,20},{1,25},{... | collective-permute-start | bytes 170504 | tf_op jit(solution)/shard_map/ppermute | solution.py:385
  27.9 7.9 %collective-permute-start.5 = (f32[1184,12]{0,1:T(8,128)S(1)}, f32[1184,12]{0,1:T(8,128)S(1)}, u32[]{:S(2)}, u32[]{:S(2)}) collective-permute-start(f32[1184,12]{0,1:T(8,128)S(1)} %reshape.194), channel_id=1, source_target_pairs={{0,20},{4,24},{8,28},{12,0},{16,4},{20,8},{24,12},{28,16},{1,21},{... | collective-permute-start | bytes 170504 | tf_op jit(solution)/shard_map/ppermute | solution.py:385
  91.1 21.3 %collective-permute-start.19 = (f32[1184,8]{0,1:T(8,128)S(1)}, f32[1184,8]{0,1:T(8,128)S(1)}, u32[]{:S(2)}, u32[]{:S(2)}) collective-permute-start(f32[1184,8]{0,1:T(8,128)S(1)} %reshape.196), channel_id=1, source_target_pairs={{0,4},{4,8},{8,12},{12,16},{16,20},{20,24},{24,28},{28,0},{1,5},{5... | collective-permute-start | bytes 113672 | tf_op jit(solution)/shard_map/ppermute | solution.py:385
  93.8 18.6 %collective-permute-start.18 = (f32[1184,8]{0,1:T(8,128)S(1)}, f32[1184,8]{0,1:T(8,128)S(1)}, u32[]{:S(2)}, u32[]{:S(2)}) collective-permute-start(f32[1184,8]{0,1:T(8,128)S(1)} %reshape.196), channel_id=1, source_target_pairs={{0,8},{4,12},{8,16},{12,20},{16,24},{20,28},{24,0},{28,4},{1,9},{5... | collective-permute-start | bytes 113672 | tf_op jit(solution)/shard_map/ppermute | solution.py:385
  95.5 16.8 %collective-permute-start.17 = (f32[1184,8]{0,1:T(8,128)S(1)}, f32[1184,8]{0,1:T(8,128)S(1)}, u32[]{:S(2)}, u32[]{:S(2)}) collective-permute-start(f32[1184,8]{0,1:T(8,128)S(1)} %reshape.196), channel_id=1, source_target_pairs={{0,12},{4,16},{8,20},{12,24},{16,28},{20,0},{24,4},{28,8},{1,13},{... | collective-permute-start | bytes 113672 | tf_op jit(solution)/shard_map/ppermute | solution.py:385
  95.8 16.5 %collective-permute-start.16 = (f32[1184,8]{0,1:T(8,128)S(1)}, f32[1184,8]{0,1:T(8,128)S(1)}, u32[]{:S(2)}, u32[]{:S(2)}) collective-permute-start(f32[1184,8]{0,1:T(8,128)S(1)} %reshape.196), channel_id=1, source_target_pairs={{0,16},{4,20},{8,24},{12,28},{16,0},{20,4},{24,8},{28,12},{1,17},{... | collective-permute-start | bytes 113672 | tf_op jit(solution)/shard_map/ppermute | solution.py:385
  97.6 5.4 %collective-permute-start.13 = (f32[1184,8]{0,1:T(8,128)S(1)}, f32[1184,8]{0,1:T(8,128)S(1)}, u32[]{:S(2)}, u32[]{:S(2)}) collective-permute-start(f32[1184,8]{0,1:T(8,128)S(1)} %reshape.196), channel_id=1, source_target_pairs={{0,28},{4,0},{8,4},{12,8},{16,12},{20,16},{24,20},{28,24},{1,29},{... | collective-permute-start | bytes 113672 | tf_op jit(solution)/shard_map/ppermute | solution.py:385
  107.1 5.2 %collective-permute-start.15 = (f32[1184,8]{0,1:T(8,128)S(1)}, f32[1184,8]{0,1:T(8,128)S(1)}, u32[]{:S(2)}, u32[]{:S(2)}) collective-permute-start(f32[1184,8]{0,1:T(8,128)S(1)} %reshape.196), channel_id=1, source_target_pairs={{0,20},{4,24},{8,28},{12,0},{16,4},{20,8},{24,12},{28,16},{1,21},{... | collective-permute-start | bytes 113672 | tf_op jit(solution)/shard_map/ppermute | solution.py:385
  139.4 23.3 %collective-permute-start.29 = (f32[1184,8]{0,1:T(8,128)S(1)}, f32[1184,8]{0,1:T(8,128)S(1)}, u32[]{:S(2)}, u32[]{:S(2)}) collective-permute-start(f32[1184,8]{0,1:T(8,128)S(1)} %reshape.199), channel_id=1, source_target_pairs={{0,4},{4,8},{8,12},{12,16},{16,20},{20,24},{24,28},{28,0},{1,5},{5... | collective-permute-start | bytes 113672 | tf_op jit(solution)/shard_map/ppermute | solution.py:385
  143.5 19.3 %collective-permute-start.28 = (f32[1184,8]{0,1:T(8,128)S(1)}, f32[1184,8]{0,1:T(8,128)S(1)}, u32[]{:S(2)}, u32[]{:S(2)}) collective-permute-start(f32[1184,8]{0,1:T(8,128)S(1)} %reshape.199), channel_id=1, source_target_pairs={{0,8},{4,12},{8,16},{12,20},{16,24},{20,28},{24,0},{28,4},{1,9},{5... | collective-permute-start | bytes 113672 | tf_op jit(solution)/shard_map/ppermute | solution.py:385
  143.6 19.1 %collective-permute-start.27 = (f32[1184,8]{0,1:T(8,128)S(1)}, f32[1184,8]{0,1:T(8,128)S(1)}, u32[]{:S(2)}, u32[]{:S(2)}) collective-permute-start(f32[1184,8]{0,1:T(8,128)S(1)} %reshape.199), channel_id=1, source_target_pairs={{0,12},{4,16},{8,20},{12,24},{16,28},{20,0},{24,4},{28,8},{1,13},{... | collective-permute-start | bytes 113672 | tf_op jit(solution)/shard_map/ppermute | solution.py:385
  145.8 16.9 %collective-permute-start.26 = (f32[1184,8]{0,1:T(8,128)S(1)}, f32[1184,8]{0,1:T(8,128)S(1)}, u32[]{:S(2)}, u32[]{:S(2)}) collective-permute-start(f32[1184,8]{0,1:T(8,128)S(1)} %reshape.199), channel_id=1, source_target_pairs={{0,16},{4,20},{8,24},{12,28},{16,0},{20,4},{24,8},{28,12},{1,17},{... | collective-permute-start | bytes 113672 | tf_op jit(solution)/shard_map/ppermute | solution.py:385
  157.2 5.5 %collective-permute-start.25 = (f32[1184,8]{0,1:T(8,128)S(1)}, f32[1184,8]{0,1:T(8,128)S(1)}, u32[]{:S(2)}, u32[]{:S(2)}) collective-permute-start(f32[1184,8]{0,1:T(8,128)S(1)} %reshape.199), channel_id=1, source_target_pairs={{0,20},{4,24},{8,28},{12,0},{16,4},{20,8},{24,12},{28,16},{1,21},{... | collective-permute-start | bytes 113672 | tf_op jit(solution)/shard_map/ppermute | solution.py:385
  190.9 22.9 %collective-permute-start.39 = (f32[1184,8]{0,1:T(8,128)S(1)}, f32[1184,8]{0,1:T(8,128)S(1)}, u32[]{:S(2)}, u32[]{:S(2)}) collective-permute-start(f32[1184,8]{0,1:T(8,128)S(1)} %reshape.202), channel_id=1, source_target_pairs={{0,4},{4,8},{8,12},{12,16},{16,20},{20,24},{24,28},{28,0},{1,5},{5... | collective-permute-start | bytes 113672 | tf_op jit(solution)/shard_map/ppermute | solution.py:385
  194.6 19.3 %collective-permute-start.38 = (f32[1184,8]{0,1:T(8,128)S(1)}, f32[1184,8]{0,1:T(8,128)S(1)}, u32[]{:S(2)}, u32[]{:S(2)}) collective-permute-start(f32[1184,8]{0,1:T(8,128)S(1)} %reshape.202), channel_id=1, source_target_pairs={{0,8},{4,12},{8,16},{12,20},{16,24},{20,28},{24,0},{28,4},{1,9},{5... | collective-permute-start | bytes 113672 | tf_op jit(solution)/shard_map/ppermute | solution.py:385
  194.8 19.1 %collective-permute-start.37 = (f32[1184,8]{0,1:T(8,128)S(1)}, f32[1184,8]{0,1:T(8,128)S(1)}, u32[]{:S(2)}, u32[]{:S(2)}) collective-permute-start(f32[1184,8]{0,1:T(8,128)S(1)} %reshape.202), channel_id=1, source_target_pairs={{0,12},{4,16},{8,20},{12,24},{16,28},{20,0},{24,4},{28,8},{1,13},{... | collective-permute-start | bytes 113672 | tf_op jit(solution)/shard_map/ppermute | solution.py:385
  198.1 15.8 %collective-permute-start.36 = (f32[1184,8]{0,1:T(8,128)S(1)}, f32[1184,8]{0,1:T(8,128)S(1)}, u32[]{:S(2)}, u32[]{:S(2)}) collective-permute-start(f32[1184,8]{0,1:T(8,128)S(1)} %reshape.202), channel_id=1, source_target_pairs={{0,16},{4,20},{8,24},{12,28},{16,0},{20,4},{24,8},{28,12},{1,17},{... | collective-permute-start | bytes 113672 | tf_op jit(solution)/shard_map/ppermute | solution.py:385
  208.4 5.5 %collective-permute-start.35 = (f32[1184,8]{0,1:T(8,128)S(1)}, f32[1184,8]{0,1:T(8,128)S(1)}, u32[]{:S(2)}, u32[]{:S(2)}) collective-permute-start(f32[1184,8]{0,1:T(8,128)S(1)} %reshape.202), channel_id=1, source_target_pairs={{0,20},{4,24},{8,28},{12,0},{16,4},{20,8},{24,12},{28,16},{1,21},{... | collective-permute-start | bytes 113672 | tf_op jit(solution)/shard_map/ppermute | solution.py:385
  (20 other events, 102.2 us)

commit v10 on v9

--- a/solution.py
+++ b/solution.py
@@ -509,7 +509,10 @@
         jnp.float32
     )
     local_sums = contract_first(contrib, onehot)
-    sensitivity = lax.psum(lax.psum(local_sums, "col"), "row")
+    if lax.axis_size("row") > 8:
+        sensitivity = lax.psum(lax.psum(local_sums, "col"), "row")
+    else:
+        sensitivity = jnp.sum(gather_axis(lax.psum(local_sums, "col")[None], "row"), 0)
     return (adjoint_field, sensitivity)
 
 

time: 289 us -> 287 us (level)
  blocking collectives: 30.5 us -> 5.65 us
  starting transfers between devices: 77.1 us -> 94.5 us
  waiting for transfers between devices: 29.9 us -> 33.3 us
    psum x2 -> x1, blocking collectives: 30.5 us -> 5.65 us  [local(): lax.psum(local_sums, 'col')[None]]
    ppermute x40 -> x47, starting transfers between devices: 77.1 us -> 94.5 us  [gather_axis(): lax.ppermute(vector, name, [(i, (i + shift) % count) for i in range(count)])]
    ppermute x40 -> x47, waiting for transfers between devices: 29.9 us -> 33.3 us  [gather_axis(): lax.ppermute(vector, name, [(i, (i + shift) % count) for i in range(count)])]
  transfers between devices with their start and end apart: 40 -> 47, of which waited for: 20 -> 23; matrix products, arithmetic and copies ran while one was open for 1% -> 2% of each run, Pallas kernels for 0% -> 0%
where the time goes in v10:
time: 287 us; the launch traced here: 285 us
  Pallas kernels  124 us (43%)
  starting transfers between devices  94.5 us (33%)
  waiting for transfers between devices  33.3 us (12%)
  other arithmetic  15.7 us (5%)
  local copies, waits for them, and re-layouts  8.53 us (3%)
  blocking collectives  5.65 us (2%)
    pallas_call x4, Pallas kernels, panel_call(): pl.pallas_call(functools.partial(panel_kernel, slope_mode, stored_in, sto...  124 us
    ppermute x47, starting transfers between devices, gather_axis(): lax.ppermute(vector, name, [(i, (i + shift) % count) for i in range(count)])  94.5 us
    ppermute x47, waiting for transfers between devices, gather_axis(): lax.ppermute(vector, name, [(i, (i + shift) % count) for i in range(count)])  33.3 us
  transfers between devices with their start and end apart: 47, of which 23 were waited for; matrix products, arithmetic and copies ran while one was open for 2% of the time, Pallas kernels for 0%

profile of v10, /device:TPU:0, one launch (start us, length us, event | category | flops | bytes accessed | tf_op | source)
XLA Modules:
  0.0 285.5 jit_solution(1518428937331669401)
XLA Ops:
  2.1 3.0 %collective-permute-start.1 = (f32[296,12]{0,1:T(8,128)S(1)}, f32[296,12]{0,1:T(8,128)S(1)}, u32[]{:S(2)}, u32[]{:S(2)}) collective-permute-start(f32[296,12]{0,1:T(8,128)S(1)} %pad_maximum_fusion.4), channel_id=1, source_target_pairs={{0,2},{1,3},{2,0},{3,1},{4,6},{5,7},{6,4},{7,5},{8,10},{9,11},{10,... | collective-permute-start | bytes 42632 | tf_op jit(solution)/shard_map/ppermute | solution.py:385
  24.9 2.9 %collective-permute-done.4 = f32[1184,12]{0,1:T(8,128)S(1)} collective-permute-done((f32[1184,12]{0,1:T(8,128)S(1)}, f32[1184,12]{0,1:T(8,128)S(1)}, u32[]{:S(2)}, u32[]{:S(2)}) %collective-permute-start.4) | collective-permute-done | bytes 56864 | tf_op jit(solution)/shard_map/ppermute | solution.py:385
  27.9 4.4 %collective-permute-start.5 = (f32[1184,12]{0,1:T(8,128)S(1)}, f32[1184,12]{0,1:T(8,128)S(1)}, u32[]{:S(2)}, u32[]{:S(2)}) collective-permute-start(f32[1184,12]{0,1:T(8,128)S(1)} %reshape.195), channel_id=1, source_target_pairs={{0,20},{4,24},{8,28},{12,0},{16,4},{20,8},{24,12},{28,16},{1,21},{... | collective-permute-start | bytes 170504 | tf_op jit(solution)/shard_map/ppermute | solution.py:385
  32.3 3.4 %collective-permute-done.5 = f32[1184,12]{0,1:T(8,128)S(1)} collective-permute-done((f32[1184,12]{0,1:T(8,128)S(1)}, f32[1184,12]{0,1:T(8,128)S(1)}, u32[]{:S(2)}, u32[]{:S(2)}) %collective-permute-start.5) | collective-permute-done | bytes 56864 | tf_op jit(solution)/shard_map/ppermute | solution.py:385
  38.2 47.1 %shard_map.104 = (f32[296,12]{1,0:T(8,128)}, f32[296,9472]{1,0:T(8,128)}, f32[296,9472]{1,0:T(8,128)}) custom-call(f32[1]{0:T(128)S(6)} %copy.234.wave_ref, f32[296,8]{1,0:T(8,128)} %copy.147.own_ref, f32[4,9472]{1,0:T(4,128)} %get-tuple-element.33.all_ref, f32[12,9472]{1,0:T(8,128)} %pad_maximum_fusion.vec_ref), custom_call_target="tpu_custom_call" | custom-call | flops 420556800 | bytes 23059584 | tf_op jit(solution)/shard_map/pallas_call | solution.py:364
  97.7 3.8 %collective-permute-start.13 = (f32[1184,8]{0,1:T(8,128)S(1)}, f32[1184,8]{0,1:T(8,128)S(1)}, u32[]{:S(2)}, u32[]{:S(2)}) collective-permute-start(f32[1184,8]{0,1:T(8,128)S(1)} %reshape.197), channel_id=1, source_target_pairs={{0,28},{4,0},{8,4},{12,8},{16,12},{20,16},{24,20},{28,24},{1,29},{... | collective-permute-start | bytes 113672 | tf_op jit(solution)/shard_map/ppermute | solution.py:385
  104.2 2.9 %collective-permute-done.14 = f32[1184,8]{0,1:T(8,128)S(1)} collective-permute-done((f32[1184,8]{0,1:T(8,128)S(1)}, f32[1184,8]{0,1:T(8,128)S(1)}, u32[]{:S(2)}, u32[]{:S(2)}) %collective-permute-start.14) | collective-permute-done | bytes 37920 | tf_op jit(solution)/shard_map/ppermute | solution.py:385
  107.1 3.6 %collective-permute-start.15 = (f32[1184,8]{0,1:T(8,128)S(1)}, f32[1184,8]{0,1:T(8,128)S(1)}, u32[]{:S(2)}, u32[]{:S(2)}) collective-permute-start(f32[1184,8]{0,1:T(8,128)S(1)} %reshape.197), channel_id=1, source_target_pairs={{0,20},{4,24},{8,28},{12,0},{16,4},{20,8},{24,12},{28,16},{1,21},{... | collective-permute-start | bytes 113672 | tf_op jit(solution)/shard_map/ppermute | solution.py:385
  114.3 19.5 %shard_map.105 = f32[296,12]{1,0:T(8,128)} custom-call(f32[1]{0:T(128)S(6)} %copy.234.wave_ref, f32[296,8]{1,0:T(8,128)} %copy.147.own_ref, f32[4,9472]{1,0:T(4,128)} %get-tuple-element.33.all_ref, f32[12,9472]{1,0:T(8,128)} %pad_maximum_fusion.1.vec_ref, f32[296,9472]{1,0:T(8,128)} %get-tuple-element.8.refs_0_, f32[296,9472]{1,0:T(8,128)} %get-tuple-element.9.refs_1_), custom_call_target="tpu_custom_call" | custom-call | flops 89718784 | bytes 23059584 | tf_op jit(solution)/shard_map/pallas_call | solution.py:364
  139.5 4.0 %collective-permute-start.29 = (f32[1184,8]{0,1:T(8,128)S(1)}, f32[1184,8]{0,1:T(8,128)S(1)}, u32[]{:S(2)}, u32[]{:S(2)}) collective-permute-start(f32[1184,8]{0,1:T(8,128)S(1)} %reshape.200), channel_id=1, source_target_pairs={{0,4},{4,8},{8,12},{12,16},{16,20},{20,24},{24,28},{28,0},{1,5},{5... | collective-permute-start | bytes 113672 | tf_op jit(solution)/shard_map/ppermute | solution.py:385
  145.9 3.1 %collective-permute-start.26 = (f32[1184,8]{0,1:T(8,128)S(1)}, f32[1184,8]{0,1:T(8,128)S(1)}, u32[]{:S(2)}, u32[]{:S(2)}) collective-permute-start(f32[1184,8]{0,1:T(8,128)S(1)} %reshape.200), channel_id=1, source_target_pairs={{0,16},{4,20},{8,24},{12,28},{16,0},{20,4},{24,8},{28,12},{1,17},{... | collective-permute-start | bytes 113672 | tf_op jit(solution)/shard_map/ppermute | solution.py:385
  148.9 2.7 collective-permute-start.23
  157.3 3.8 %collective-permute-start.25 = (f32[1184,8]{0,1:T(8,128)S(1)}, f32[1184,8]{0,1:T(8,128)S(1)}, u32[]{:S(2)}, u32[]{:S(2)}) collective-permute-start(f32[1184,8]{0,1:T(8,128)S(1)} %reshape.200), channel_id=1, source_target_pairs={{0,20},{4,24},{8,28},{12,0},{16,4},{20,8},{24,12},{28,16},{1,21},{... | collective-permute-start | bytes 113672 | tf_op jit(solution)/shard_map/ppermute | solution.py:385
  165.7 19.5 %shard_map.106 = f32[296,12]{1,0:T(8,128)} custom-call(f32[1]{0:T(128)S(6)} %copy.234.wave_ref, f32[296,8]{1,0:T(8,128)} %copy.147.own_ref, f32[4,9472]{1,0:T(4,128)} %get-tuple-element.33.all_ref, f32[12,9472]{1,0:T(8,128)} %pad_maximum_fusion.2.vec_ref, f32[296,9472]{1,0:T(8,128)} %get-tuple-element.8.refs_0_, f32[296,9472]{1,0:T(8,128)} %get-tuple-element.9.refs_1_), custom_call_target="tpu_custom_call" | custom-call | flops 89718784 | bytes 23059584 | tf_op jit(solution)/shard_map/pallas_call | solution.py:364
  191.1 3.6 %collective-permute-start.39 = (f32[1184,8]{0,1:T(8,128)S(1)}, f32[1184,8]{0,1:T(8,128)S(1)}, u32[]{:S(2)}, u32[]{:S(2)}) collective-permute-start(f32[1184,8]{0,1:T(8,128)S(1)} %reshape.203), channel_id=1, source_target_pairs={{0,4},{4,8},{8,12},{12,16},{16,20},{20,24},{24,28},{28,0},{1,5},{5... | collective-permute-start | bytes 113672 | tf_op jit(solution)/shard_map/ppermute | solution.py:385
  194.9 3.3 %collective-permute-start.37 = (f32[1184,8]{0,1:T(8,128)S(1)}, f32[1184,8]{0,1:T(8,128)S(1)}, u32[]{:S(2)}, u32[]{:S(2)}) collective-permute-start(f32[1184,8]{0,1:T(8,128)S(1)} %reshape.203), channel_id=1, source_target_pairs={{0,12},{4,16},{8,20},{12,24},{16,28},{20,0},{24,4},{28,8},{1,13},{... | collective-permute-start | bytes 113672 | tf_op jit(solution)/shard_map/ppermute | solution.py:385
  200.1 2.7 collective-permute-start.33
  208.5 3.8 %collective-permute-start.35 = (f32[1184,8]{0,1:T(8,128)S(1)}, f32[1184,8]{0,1:T(8,128)S(1)}, u32[]{:S(2)}, u32[]{:S(2)}) collective-permute-start(f32[1184,8]{0,1:T(8,128)S(1)} %reshape.203), channel_id=1, source_target_pairs={{0,20},{4,24},{8,28},{12,0},{16,4},{20,8},{24,12},{28,16},{1,21},{... | collective-permute-start | bytes 113672 | tf_op jit(solution)/shard_map/ppermute | solution.py:385
  218.1 37.8 %shard_map.107 = f32[296,12]{1,0:T(8,128)} custom-call(f32[1]{0:T(128)S(6)} %copy.234.wave_ref, f32[296,8]{1,0:T(8,128)} %copy.147.own_ref, f32[4,9472]{1,0:T(4,128)} %get-tuple-element.33.all_ref, f32[12,9472]{1,0:T(8,128)} %pad_maximum_fusion.3.vec_ref, f32[296,9472]{1,0:T(8,128)} %get-tuple-element.8.refs_0_, f32[296,9472]{1,0:T(8,128)} %get-tuple-element.9.refs_1_), custom_call_target="tpu_custom_call" | custom-call | flops 168222720 | bytes 23059584 | tf_op jit(solution)/shard_map/pallas_call | solution.py:364
  257.5 5.6 %psum.7 = f32[4,128]{1,0:T(4,128)S(1)} all-reduce(f32[4,128]{1,0:T(4,128)S(1)} %fusion.14), channel_id=1, replica_groups=mesh['row'=8,'col'=4] {'col'}, use_global_device_ids=true, to_apply=%region_13.16 | all-reduce | flops 512 | bytes 4096 | tf_op jit(solution)/shard_map/psum | solution.py:515
  263.2 3.6 %collective-permute-start.46 = (f32[1,4,128]{2,1,0:T(4,128)S(1)}, f32[1,4,128]{2,1,0:T(4,128)S(1)}, u32[]{:S(2)}, u32[]{:S(2)}) collective-permute-start(f32[1,4,128]{2,1,0:T(4,128)S(1)} %bitcast.176), channel_id=1, source_target_pairs={{0,4},{4,8},{8,12},{12,16},{16,20},{20,24},{24,28},{28,0},{1,5},{5... | collective-permute-start | bytes 6152 | tf_op jit(solution)/shard_map/ppermute | solution.py:385
  266.9 3.4 %collective-permute-start.44 = (f32[1,4,128]{2,1,0:T(4,128)S(1)}, f32[1,4,128]{2,1,0:T(4,128)S(1)}, u32[]{:S(2)}, u32[]{:S(2)}) collective-permute-start(f32[1,4,128]{2,1,0:T(4,128)S(1)} %bitcast.178), channel_id=1, source_target_pairs={{0,12},{4,16},{8,20},{12,24},{16,28},{20,0},{24,4},{28,8},{1,13},{... | collective-permute-start | bytes 6152 | tf_op jit(solution)/shard_map/ppermute | solution.py:385
  272.1 2.7 collective-permute-start.40
  279.6 3.7 %collective-permute-start.42 = (f32[1,4,128]{2,1,0:T(4,128)S(1)}, f32[1,4,128]{2,1,0:T(4,128)S(1)}, u32[]{:S(2)}, u32[]{:S(2)}) collective-permute-start(f32[1,4,128]{2,1,0:T(4,128)S(1)} %bitcast.182), channel_id=1, source_target_pairs={{0,20},{4,24},{8,28},{12,0},{16,4},{20,8},{24,12},{28,16},{1,21},{... | collective-permute-start | bytes 6152 | tf_op jit(solution)/shard_map/ppermute | solution.py:385
  (249 shorter events, 89.1 us)
Async XLA Ops:
  2.1 8.2 %collective-permute-start.1 = (f32[296,12]{0,1:T(8,128)S(1)}, f32[296,12]{0,1:T(8,128)S(1)}, u32[]{:S(2)}, u32[]{:S(2)}) collective-permute-start(f32[296,12]{0,1:T(8,128)S(1)} %pad_maximum_fusion.4), channel_id=1, source_target_pairs={{0,2},{1,3},{2,0},{3,1},{4,6},{5,7},{6,4},{7,5},{8,10},{9,11},{10,... | collective-permute-start | bytes 42632 | tf_op jit(solution)/shard_map/ppermute | solution.py:385
  11.3 24.5 %collective-permute-start.9 = (f32[1184,12]{0,1:T(8,128)S(1)}, f32[1184,12]{0,1:T(8,128)S(1)}, u32[]{:S(2)}, u32[]{:S(2)}) collective-permute-start(f32[1184,12]{0,1:T(8,128)S(1)} %reshape.195), channel_id=1, source_target_pairs={{0,4},{4,8},{8,12},{12,16},{16,20},{20,24},{24,28},{28,0},{1,5},{5... | collective-permute-start | bytes 170504 | tf_op jit(solution)/shard_map/ppermute | solution.py:385
  12.9 22.9 %collective-permute-start.8 = (f32[1184,12]{0,1:T(8,128)S(1)}, f32[1184,12]{0,1:T(8,128)S(1)}, u32[]{:S(2)}, u32[]{:S(2)}) collective-permute-start(f32[1184,12]{0,1:T(8,128)S(1)} %reshape.195), channel_id=1, source_target_pairs={{0,8},{4,12},{8,16},{12,20},{16,24},{20,28},{24,0},{28,4},{1,9},{5... | collective-permute-start | bytes 170504 | tf_op jit(solution)/shard_map/ppermute | solution.py:385
  14.5 21.3 %collective-permute-start.7 = (f32[1184,12]{0,1:T(8,128)S(1)}, f32[1184,12]{0,1:T(8,128)S(1)}, u32[]{:S(2)}, u32[]{:S(2)}) collective-permute-start(f32[1184,12]{0,1:T(8,128)S(1)} %reshape.195), channel_id=1, source_target_pairs={{0,12},{4,16},{8,20},{12,24},{16,28},{20,0},{24,4},{28,8},{1,13},{... | collective-permute-start | bytes 170504 | tf_op jit(solution)/shard_map/ppermute | solution.py:385
  17.0 18.7 %collective-permute-start.6 = (f32[1184,12]{0,1:T(8,128)S(1)}, f32[1184,12]{0,1:T(8,128)S(1)}, u32[]{:S(2)}, u32[]{:S(2)}) collective-permute-start(f32[1184,12]{0,1:T(8,128)S(1)} %reshape.195), channel_id=1, source_target_pairs={{0,16},{4,20},{8,24},{12,28},{16,0},{20,4},{24,8},{28,12},{1,17},{... | collective-permute-start | bytes 170504 | tf_op jit(solution)/shard_map/ppermute | solution.py:385
  27.9 7.9 %collective-permute-start.5 = (f32[1184,12]{0,1:T(8,128)S(1)}, f32[1184,12]{0,1:T(8,128)S(1)}, u32[]{:S(2)}, u32[]{:S(2)}) collective-permute-start(f32[1184,12]{0,1:T(8,128)S(1)} %reshape.195), channel_id=1, source_target_pairs={{0,20},{4,24},{8,28},{12,0},{16,4},{20,8},{24,12},{28,16},{1,21},{... | collective-permute-start | bytes 170504 | tf_op jit(solution)/shard_map/ppermute | solution.py:385
  91.1 21.3 %collective-permute-start.19 = (f32[1184,8]{0,1:T(8,128)S(1)}, f32[1184,8]{0,1:T(8,128)S(1)}, u32[]{:S(2)}, u32[]{:S(2)}) collective-permute-start(f32[1184,8]{0,1:T(8,128)S(1)} %reshape.197), channel_id=1, source_target_pairs={{0,4},{4,8},{8,12},{12,16},{16,20},{20,24},{24,28},{28,0},{1,5},{5... | collective-permute-start | bytes 113672 | tf_op jit(solution)/shard_map/ppermute | solution.py:385
  93.8 18.6 %collective-permute-start.18 = (f32[1184,8]{0,1:T(8,128)S(1)}, f32[1184,8]{0,1:T(8,128)S(1)}, u32[]{:S(2)}, u32[]{:S(2)}) collective-permute-start(f32[1184,8]{0,1:T(8,128)S(1)} %reshape.197), channel_id=1, source_target_pairs={{0,8},{4,12},{8,16},{12,20},{16,24},{20,28},{24,0},{28,4},{1,9},{5... | collective-permute-start | bytes 113672 | tf_op jit(solution)/shard_map/ppermute | solution.py:385
  95.5 16.8 %collective-permute-start.17 = (f32[1184,8]{0,1:T(8,128)S(1)}, f32[1184,8]{0,1:T(8,128)S(1)}, u32[]{:S(2)}, u32[]{:S(2)}) collective-permute-start(f32[1184,8]{0,1:T(8,128)S(1)} %reshape.197), channel_id=1, source_target_pairs={{0,12},{4,16},{8,20},{12,24},{16,28},{20,0},{24,4},{28,8},{1,13},{... | collective-permute-start | bytes 113672 | tf_op jit(solution)/shard_map/ppermute | solution.py:385
  95.8 16.5 %collective-permute-start.16 = (f32[1184,8]{0,1:T(8,128)S(1)}, f32[1184,8]{0,1:T(8,128)S(1)}, u32[]{:S(2)}, u32[]{:S(2)}) collective-permute-start(f32[1184,8]{0,1:T(8,128)S(1)} %reshape.197), channel_id=1, source_target_pairs={{0,16},{4,20},{8,24},{12,28},{16,0},{20,4},{24,8},{28,12},{1,17},{... | collective-permute-start | bytes 113672 | tf_op jit(solution)/shard_map/ppermute | solution.py:385
  139.5 23.3 %collective-permute-start.29 = (f32[1184,8]{0,1:T(8,128)S(1)}, f32[1184,8]{0,1:T(8,128)S(1)}, u32[]{:S(2)}, u32[]{:S(2)}) collective-permute-start(f32[1184,8]{0,1:T(8,128)S(1)} %reshape.200), channel_id=1, source_target_pairs={{0,4},{4,8},{8,12},{12,16},{16,20},{20,24},{24,28},{28,0},{1,5},{5... | collective-permute-start | bytes 113672 | tf_op jit(solution)/shard_map/ppermute | solution.py:385
  143.5 19.3 %collective-permute-start.28 = (f32[1184,8]{0,1:T(8,128)S(1)}, f32[1184,8]{0,1:T(8,128)S(1)}, u32[]{:S(2)}, u32[]{:S(2)}) collective-permute-start(f32[1184,8]{0,1:T(8,128)S(1)} %reshape.200), channel_id=1, source_target_pairs={{0,8},{4,12},{8,16},{12,20},{16,24},{20,28},{24,0},{28,4},{1,9},{5... | collective-permute-start | bytes 113672 | tf_op jit(solution)/shard_map/ppermute | solution.py:385
  143.7 19.1 %collective-permute-start.27 = (f32[1184,8]{0,1:T(8,128)S(1)}, f32[1184,8]{0,1:T(8,128)S(1)}, u32[]{:S(2)}, u32[]{:S(2)}) collective-permute-start(f32[1184,8]{0,1:T(8,128)S(1)} %reshape.200), channel_id=1, source_target_pairs={{0,12},{4,16},{8,20},{12,24},{16,28},{20,0},{24,4},{28,8},{1,13},{... | collective-permute-start | bytes 113672 | tf_op jit(solution)/shard_map/ppermute | solution.py:385
  145.9 16.9 %collective-permute-start.26 = (f32[1184,8]{0,1:T(8,128)S(1)}, f32[1184,8]{0,1:T(8,128)S(1)}, u32[]{:S(2)}, u32[]{:S(2)}) collective-permute-start(f32[1184,8]{0,1:T(8,128)S(1)} %reshape.200), channel_id=1, source_target_pairs={{0,16},{4,20},{8,24},{12,28},{16,0},{20,4},{24,8},{28,12},{1,17},{... | collective-permute-start | bytes 113672 | tf_op jit(solution)/shard_map/ppermute | solution.py:385
  157.3 5.5 %collective-permute-start.25 = (f32[1184,8]{0,1:T(8,128)S(1)}, f32[1184,8]{0,1:T(8,128)S(1)}, u32[]{:S(2)}, u32[]{:S(2)}) collective-permute-start(f32[1184,8]{0,1:T(8,128)S(1)} %reshape.200), channel_id=1, source_target_pairs={{0,20},{4,24},{8,28},{12,0},{16,4},{20,8},{24,12},{28,16},{1,21},{... | collective-permute-start | bytes 113672 | tf_op jit(solution)/shard_map/ppermute | solution.py:385
  191.1 22.9 %collective-permute-start.39 = (f32[1184,8]{0,1:T(8,128)S(1)}, f32[1184,8]{0,1:T(8,128)S(1)}, u32[]{:S(2)}, u32[]{:S(2)}) collective-permute-start(f32[1184,8]{0,1:T(8,128)S(1)} %reshape.203), channel_id=1, source_target_pairs={{0,4},{4,8},{8,12},{12,16},{16,20},{20,24},{24,28},{28,0},{1,5},{5... | collective-permute-start | bytes 113672 | tf_op jit(solution)/shard_map/ppermute | solution.py:385
  194.7 19.3 %collective-permute-start.38 = (f32[1184,8]{0,1:T(8,128)S(1)}, f32[1184,8]{0,1:T(8,128)S(1)}, u32[]{:S(2)}, u32[]{:S(2)}) collective-permute-start(f32[1184,8]{0,1:T(8,128)S(1)} %reshape.203), channel_id=1, source_target_pairs={{0,8},{4,12},{8,16},{12,20},{16,24},{20,28},{24,0},{28,4},{1,9},{5... | collective-permute-start | bytes 113672 | tf_op jit(solution)/shard_map/ppermute | solution.py:385
  194.9 19.1 %collective-permute-start.37 = (f32[1184,8]{0,1:T(8,128)S(1)}, f32[1184,8]{0,1:T(8,128)S(1)}, u32[]{:S(2)}, u32[]{:S(2)}) collective-permute-start(f32[1184,8]{0,1:T(8,128)S(1)} %reshape.203), channel_id=1, source_target_pairs={{0,12},{4,16},{8,20},{12,24},{16,28},{20,0},{24,4},{28,8},{1,13},{... | collective-permute-start | bytes 113672 | tf_op jit(solution)/shard_map/ppermute | solution.py:385
  198.2 15.7 %collective-permute-start.36 = (f32[1184,8]{0,1:T(8,128)S(1)}, f32[1184,8]{0,1:T(8,128)S(1)}, u32[]{:S(2)}, u32[]{:S(2)}) collective-permute-start(f32[1184,8]{0,1:T(8,128)S(1)} %reshape.203), channel_id=1, source_target_pairs={{0,16},{4,20},{8,24},{12,28},{16,0},{20,4},{24,8},{28,12},{1,17},{... | collective-permute-start | bytes 113672 | tf_op jit(solution)/shard_map/ppermute | solution.py:385
  208.5 5.5 %collective-permute-start.35 = (f32[1184,8]{0,1:T(8,128)S(1)}, f32[1184,8]{0,1:T(8,128)S(1)}, u32[]{:S(2)}, u32[]{:S(2)}) collective-permute-start(f32[1184,8]{0,1:T(8,128)S(1)} %reshape.203), channel_id=1, source_target_pairs={{0,20},{4,24},{8,28},{12,0},{16,4},{20,8},{24,12},{28,16},{1,21},{... | collective-permute-start | bytes 113672 | tf_op jit(solution)/shard_map/ppermute | solution.py:385
  263.2 21.6 %collective-permute-start.46 = (f32[1,4,128]{2,1,0:T(4,128)S(1)}, f32[1,4,128]{2,1,0:T(4,128)S(1)}, u32[]{:S(2)}, u32[]{:S(2)}) collective-permute-start(f32[1,4,128]{2,1,0:T(4,128)S(1)} %bitcast.176), channel_id=1, source_target_pairs={{0,4},{4,8},{8,12},{12,16},{16,20},{20,24},{24,28},{28,0},{1,5},{5... | collective-permute-start | bytes 6152 | tf_op jit(solution)/shard_map/ppermute | solution.py:385
  266.8 17.9 %collective-permute-start.45 = (f32[1,4,128]{2,1,0:T(4,128)S(1)}, f32[1,4,128]{2,1,0:T(4,128)S(1)}, u32[]{:S(2)}, u32[]{:S(2)}) collective-permute-start(f32[1,4,128]{2,1,0:T(4,128)S(1)} %bitcast.177), channel_id=1, source_target_pairs={{0,8},{4,12},{8,16},{12,20},{16,24},{20,28},{24,0},{28,4},{1,9},{5... | collective-permute-start | bytes 6152 | tf_op jit(solution)/shard_map/ppermute | solution.py:385
  266.9 17.9 %collective-permute-start.44 = (f32[1,4,128]{2,1,0:T(4,128)S(1)}, f32[1,4,128]{2,1,0:T(4,128)S(1)}, u32[]{:S(2)}, u32[]{:S(2)}) collective-permute-start(f32[1,4,128]{2,1,0:T(4,128)S(1)} %bitcast.178), channel_id=1, source_target_pairs={{0,12},{4,16},{8,20},{12,24},{16,28},{20,0},{24,4},{28,8},{1,13},{... | collective-permute-start | bytes 6152 | tf_op jit(solution)/shard_map/ppermute | solution.py:385
  270.3 14.4 %collective-permute-start.43 = (f32[1,4,128]{2,1,0:T(4,128)S(1)}, f32[1,4,128]{2,1,0:T(4,128)S(1)}, u32[]{:S(2)}, u32[]{:S(2)}) collective-permute-start(f32[1,4,128]{2,1,0:T(4,128)S(1)} %bitcast.179), channel_id=1, source_target_pairs={{0,16},{4,20},{8,24},{12,28},{16,0},{20,4},{24,8},{28,12},{1,17},{... | collective-permute-start | bytes 6152 | tf_op jit(solution)/shard_map/ppermute | solution.py:385
  (27 other events, 135.9 us)

commit v11 on v10

--- a/solution.py
+++ b/solution.py
@@ -183,15 +183,19 @@
 def panel_kernel(slope_mode, stored_in, store_out, wave_ref, own_ref, all_ref, vec_ref, *refs):
     if stored_in:
         real_hbm, imag_hbm, out_ref, real_buf, imag_buf, sems = refs
+        hbm_refs, buf_refs = [real_hbm, imag_hbm], [real_buf, imag_buf]
     elif store_out:
-        out_ref, real_hbm, imag_hbm, real_buf, imag_buf, sems = refs
+        out_ref = refs[0]
+        hbm_refs = list(refs[1:1 + store_out])
+        buf_refs = list(refs[1 + store_out:1 + 2 * store_out])
+        sems = refs[-1]
     else:
         (out_ref,) = refs
     block_count = own_ref.shape[0] // 8
 
     def copies(block, slot):
         rows = pl.ds(pl.multiple_of(block * 8, 8), 8)
-        pairs = [(real_hbm, real_buf), (imag_hbm, imag_buf)]
+        pairs = list(zip(hbm_refs, buf_refs))
         if stored_in:
             return [pltpu.make_async_copy(hbm.at[rows], buf.at[rows], sems.at[k, block]) for k, (hbm, buf) in enumerate(pairs)]
         return [pltpu.make_async_copy(buf.at[slot], hbm.at[rows], sems.at[k, slot]) for k, (hbm, buf) in enumerate(pairs)]
@@ -200,7 +204,7 @@
     panel_total = all_ref.shape[1]
     width = LANES if panel_total % LANES == 0 else 128
     chunk_count = panel_total // width
-    needs_geometry = slope_mode or not stored_in
+    needs_geometry = not stored_in or (slope_mode and stored_in == 1)
 
     def row_block(block, carry):
         first = pl.multiple_of(block * 8, 8)
@@ -222,7 +226,7 @@
         own_y = jnp.broadcast_to(own[:, 1:2], (8, width))
         own_z = jnp.broadcast_to(own[:, 2:3], (8, width))
         own_a = jnp.broadcast_to(own[:, 3:4], (8, width))
-        if slope_mode:
+        if slope_mode or store_out == 4:
             move_x = jnp.broadcast_to(own[:, 4:5], (8, width))
             move_y = jnp.broadcast_to(own[:, 5:6], (8, width))
             move_z = jnp.broadcast_to(own[:, 6:7], (8, width))
@@ -246,7 +250,10 @@
             if stored_in:
                 real_part = real_buf[rows, span]
                 imag_part = imag_buf[rows, span]
-                if slope_mode:
+                if stored_in == 2:
+                    first_part = real_part
+                    second_part = imag_part
+                elif slope_mode:
                     along_move = diff_x * move_x + diff_y * move_y + diff_z * move_z
                     factor = along_move * (inverse * inverse)
                     first_part = (-real_part - phase * imag_part) * factor
@@ -266,8 +273,13 @@
                     first_part = cosine_part * factor
                     second_part = sine_part * factor
                 if store_out:
-                    real_buf[slot, :, span] = first_part
-                    imag_buf[slot, :, span] = second_part
+                    buf_refs[0][slot, :, span] = first_part
+                    buf_refs[1][slot, :, span] = second_part
+                if store_out == 4:
+                    along_move = diff_x * move_x + diff_y * move_y + diff_z * move_z
+                    slope_factor = along_move * (inverse * inverse * inverse) * (1.0 / four_pi)
+                    buf_refs[2][slot, :, span] = (-cosine_part - phase * sine_part) * slope_factor
+                    buf_refs[3][slot, :, span] = (phase * cosine_part - sine_part) * slope_factor
             zone_count = len(sums) // 3
             both_parts = first_part + second_part
             new_sums = []
@@ -304,12 +316,12 @@
                 copy.wait()
 
 
-def panel_contract(slope_mode, wavenumber, own_table, all_table, vector_full, stored=None, store_out=False):
+def panel_contract(slope_mode, wavenumber, own_table, all_table, vector_full, stored=None, store_out=0, direct=False):
     zone_count = vector_full.shape[1] // 2
     vector_rows = jnp.concatenate(
         [vector_full.T, (vector_full[:, :zone_count] - vector_full[:, zone_count:]).T], 0
     )
-    outs = panel_call(slope_mode, wavenumber, own_table, all_table, vector_rows, stored, store_out)
+    outs = panel_call(slope_mode, wavenumber, own_table, all_table, vector_rows, stored, store_out, direct)
     sums = outs[0] if store_out else outs
     first_sum = sums[:, :zone_count]
     second_sum = sums[:, zone_count:2 * zone_count]
@@ -324,12 +336,12 @@
     return combined
 
 
-def panel_call(slope_mode, wavenumber, own_table, all_table, vector_rows, stored, store_out):
+def panel_call(slope_mode, wavenumber, own_table, all_table, vector_rows, stored, store_out, direct):
     own_total = own_table.shape[0]
     columns = vector_rows.shape[0]
     panel_total = all_table.shape[1]
     elements = own_total * panel_total
-    stored_in = stored is not None
+    stored_in = 0 if stored is None else (2 if direct else 1)
     operands = [wavenumber, own_table, all_table, vector_rows]
     out_shape = [jax.ShapeDtypeStruct((own_total, columns), jnp.float32)]
     matrix_bytes = 0
@@ -337,8 +349,8 @@
         operands += list(stored)
         matrix_bytes = 8 * elements
     if store_out:
-        out_shape += [jax.ShapeDtypeStruct((own_total, panel_total), jnp.float32)] * 2
-        matrix_bytes = 8 * elements
+        out_shape += [jax.ShapeDtypeStruct((own_total, panel_total), jnp.float32)] * store_out
+        matrix_bytes = 4 * store_out * elements
     vmem = pl.BlockSpec(memory_space=pltpu.VMEM)
     hbm = pl.BlockSpec(memory_space=pltpu.HBM)
     params = {}
@@ -350,12 +362,10 @@
         ]
         params["compiler_params"] = pltpu.CompilerParams(vmem_limit_bytes=60 * 1024 * 1024)
     elif store_out:
-        params["scratch_shapes"] = [
-            pltpu.VMEM((2, 8, panel_total), jnp.float32),
-            pltpu.VMEM((2, 8, panel_total), jnp.float32),
-            pltpu.SemaphoreType.DMA((2, 2)),
+        params["scratch_shapes"] = [pltpu.VMEM((2, 8, panel_total), jnp.float32)] * store_out + [
+            pltpu.SemaphoreType.DMA((store_out, 2))
         ]
-    if stored_in and not slope_mode:
+    if stored_in == 2 or (stored_in and not slope_mode):
         flops, transcendentals = 32 * elements, 0
     elif stored_in:
         flops, transcendentals = 60 * elements, 2 * elements
@@ -429,16 +439,19 @@
     )
 
     store = 8 * owned_count * panel_total <= STORE_LIMIT
+    store_slope = 16 * owned_count * panel_total <= 2 * STORE_LIMIT
     saved = []
+    slope_saved = []
 
     def apply_adjoint(vector_full, vector_own):
         if store and saved:
             summed = panel_contract(False, wavenumber, own_table, all_table, vector_full, stored=saved)
         elif store:
-            summed, real_part, imag_part = panel_contract(
-                False, wavenumber, own_table, all_table, vector_full, store_out=True
+            summed, *parts = panel_contract(
+                False, wavenumber, own_table, all_table, vector_full, store_out=4 if store_slope else 2
             )
-            saved.extend([real_part, imag_part])
+            saved.extend(parts[:2])
+            slope_saved.extend(parts[2:])
         else:
             summed = panel_contract(False, wavenumber, own_table, all_table, vector_full)
         return panel_areas[:, None] * summed + jump_term[:, None] * vector_own
@@ -500,7 +513,10 @@
         + complex_scale(coef_two_re, coef_two_im, basis_two_full, zone_count)
     )
 
-    contracted = panel_contract(True, wavenumber, own_table, all_table, field_full, stored=saved or None)
+    if slope_saved:
+        contracted = panel_contract(True, wavenumber, own_table, all_table, field_full, stored=slope_saved, direct=True)
+    else:
+        contracted = panel_contract(True, wavenumber, own_table, all_table, field_full, stored=saved or None)
     contrib = panel_areas[:, None] * (
         primal_field[0][:, None] * contracted[:, :zone_count]
         - primal_field[1][:, None] * contracted[:, zone_count:]

time: 287 us -> 240 us (0.84)
  starting transfers between devices: 94.5 us -> 52.3 us
  Pallas kernels: 124 us -> 113 us
  waiting for transfers between devices: 33.3 us -> 41.2 us
    ppermute x47, starting transfers between devices: 94.5 us -> 52.3 us  [gather_axis(): lax.ppermute(vector, name, [(i, (i + shift) % count) for i in range(count)])]
    pallas_call x4, Pallas kernels: 124 us -> 113 us  [panel_call(): pl.pallas_call(functools.partial(panel_kernel, slope_mode, stored_in, sto...]
    ppermute x47, waiting for transfers between devices: 33.3 us -> 41.2 us  [gather_axis(): lax.ppermute(vector, name, [(i, (i + shift) % count) for i in range(count)])]
where the time goes in v11:
time: 240 us; the launch traced here: 239 us
  Pallas kernels  113 us (47%)
  starting transfers between devices  52.3 us (22%)
  waiting for transfers between devices  41.2 us (17%)
  other arithmetic  15.6 us (6%)
  local copies, waits for them, and re-layouts  8.48 us (4%)
  blocking collectives  5.65 us (2%)
    pallas_call x4, Pallas kernels, panel_call(): pl.pallas_call(functools.partial(panel_kernel, slope_mode, stored_in, sto...  113 us
    ppermute x47, starting transfers between devices, gather_axis(): lax.ppermute(vector, name, [(i, (i + shift) % count) for i in range(count)])  52.3 us
    ppermute x47, waiting for transfers between devices, gather_axis(): lax.ppermute(vector, name, [(i, (i + shift) % count) for i in range(count)])  41.2 us
    psum x1, blocking collectives, local(): lax.psum(local_sums, 'col')[None]  5.65 us
  transfers between devices with their start and end apart: 47, of which 23 were waited for; matrix products, arithmetic and copies ran while one was open for 2% of the time, Pallas kernels for 0%

profile of v11, /device:TPU:0, one launch (start us, length us, event | category | flops | bytes accessed | tf_op | source)
XLA Modules:
  0.0 239.5 jit_solution(964806803994670306)
XLA Ops:
  2.0 2.5 %collective-permute-start = (f32[296,12]{0,1:T(8,128)S(1)}, f32[296,12]{0,1:T(8,128)S(1)}, u32[]{:S(2)}, u32[]{:S(2)}) collective-permute-start(f32[296,12]{0,1:T(8,128)S(1)} %pad_maximum_fusion.4), channel_id=1, source_target_pairs={{0,3},{1,0},{2,1},{3,2},{4,7},{5,4},{6,5},{7,6},{8,11},{9,8},{10,9... | collective-permute-start | bytes 42632 | tf_op jit(solution)/shard_map/ppermute | solution.py:395
  11.0 4.6 %collective-permute-start.3 = (f32[1184,12]{0,1:T(8,128)S(1)}, f32[1184,12]{0,1:T(8,128)S(1)}, u32[]{:S(2)}, u32[]{:S(2)}) collective-permute-start(f32[1184,12]{0,1:T(8,128)S(1)} %reshape.195), channel_id=1, source_target_pairs={{0,28},{4,0},{8,4},{12,8},{16,12},{20,16},{24,20},{28,24},{1,29},{... | collective-permute-start | bytes 170504 | tf_op jit(solution)/shard_map/ppermute | solution.py:395
  16.0 3.0 %collective-permute-start.6 = (f32[1184,12]{0,1:T(8,128)S(1)}, f32[1184,12]{0,1:T(8,128)S(1)}, u32[]{:S(2)}, u32[]{:S(2)}) collective-permute-start(f32[1184,12]{0,1:T(8,128)S(1)} %reshape.195), channel_id=1, source_target_pairs={{0,16},{4,20},{8,24},{12,28},{16,0},{20,4},{24,8},{28,12},{1,17},{... | collective-permute-start | bytes 170504 | tf_op jit(solution)/shard_map/ppermute | solution.py:395
  22.2 8.8 %collective-permute-done.6 = f32[1184,12]{0,1:T(8,128)S(1)} collective-permute-done((f32[1184,12]{0,1:T(8,128)S(1)}, f32[1184,12]{0,1:T(8,128)S(1)}, u32[]{:S(2)}, u32[]{:S(2)}) %collective-permute-start.6) | collective-permute-done | bytes 56864 | tf_op jit(solution)/shard_map/ppermute | solution.py:395
  31.0 2.6 %collective-permute-done.7 = f32[1184,12]{0,1:T(8,128)S(1)} collective-permute-done((f32[1184,12]{0,1:T(8,128)S(1)}, f32[1184,12]{0,1:T(8,128)S(1)}, u32[]{:S(2)}, u32[]{:S(2)}) %collective-permute-start.7) | collective-permute-done | bytes 56864 | tf_op jit(solution)/shard_map/ppermute | solution.py:395
  36.0 53.0 %shard_map.104 = (f32[296,12]{1,0:T(8,128)}, f32[296,9472]{1,0:T(8,128)}, f32[296,9472]{1,0:T(8,128)}, f32[296,9472]{1,0:T(8,128)}, f32[296,9472]{1,0:T(8,128)}) custom-call(f32[1]{0:T(128)S(6)} %copy.234.wave_ref, f32[296,8]{1,0:T(8,128)} %copy.147.own_ref, f32[4,9472]{1,0:T(4,128)} %get-tuple-element.37.all_ref, f32[12,9472]{1,0:T(8,128)} %pad_maximum_fusion.vec_ref), custom_call_target="tpu_custom_call" | custom-call | flops 420556800 | bytes 45489280 | tf_op jit(solution)/shard_map/pallas_call | solution.py:374
  92.3 2.2 collective-permute-done.11
  100.4 2.4 %collective-permute-start.18 = (f32[1184,8]{0,1:T(8,128)S(1)}, f32[1184,8]{0,1:T(8,128)S(1)}, u32[]{:S(2)}, u32[]{:S(2)}) collective-permute-start(f32[1184,8]{0,1:T(8,128)S(1)} %reshape.197), channel_id=1, source_target_pairs={{0,8},{4,12},{8,16},{12,20},{16,24},{20,28},{24,0},{28,4},{1,9},{5... | collective-permute-start | bytes 113672 | tf_op jit(solution)/shard_map/ppermute | solution.py:395
  102.8 2.0 collective-permute-start.19
  106.4 3.2 %collective-permute-done.19 = f32[1184,8]{0,1:T(8,128)S(1)} collective-permute-done((f32[1184,8]{0,1:T(8,128)S(1)}, f32[1184,8]{0,1:T(8,128)S(1)}, u32[]{:S(2)}, u32[]{:S(2)}) %collective-permute-start.19) | collective-permute-done | bytes 37920 | tf_op jit(solution)/shard_map/ppermute | solution.py:395
  111.4 19.5 %shard_map.105 = f32[296,12]{1,0:T(8,128)} custom-call(f32[1]{0:T(128)S(6)} %copy.234.wave_ref, f32[296,8]{1,0:T(8,128)} %copy.147.own_ref, f32[4,9472]{1,0:T(4,128)} %get-tuple-element.37.all_ref, f32[12,9472]{1,0:T(8,128)} %pad_maximum_fusion.1.vec_ref, f32[296,9472]{1,0:T(8,128)} %get-tuple-element.10.refs_0_, f32[296,9472]{1,0:T(8,128)} %get-tuple-element.11.refs_1_), custom_call_target="tpu_custom_call" | custom-call | flops 89718784 | bytes 23059584 | tf_op jit(solution)/shard_map/pallas_call | solution.py:374
  133.8 2.4 collective-permute-done.21
  138.6 2.6 %collective-permute-start.26 = (f32[1184,8]{0,1:T(8,128)S(1)}, f32[1184,8]{0,1:T(8,128)S(1)}, u32[]{:S(2)}, u32[]{:S(2)}) collective-permute-start(f32[1184,8]{0,1:T(8,128)S(1)} %reshape.200), channel_id=1, source_target_pairs={{0,16},{4,20},{8,24},{12,28},{16,0},{20,4},{24,8},{28,12},{1,17},{... | collective-permute-start | bytes 113672 | tf_op jit(solution)/shard_map/ppermute | solution.py:395
  144.6 2.5 %collective-permute-done.27 = f32[1184,8]{0,1:T(8,128)S(1)} collective-permute-done((f32[1184,8]{0,1:T(8,128)S(1)}, f32[1184,8]{0,1:T(8,128)S(1)}, u32[]{:S(2)}, u32[]{:S(2)}) %collective-permute-start.27) | collective-permute-done | bytes 37920 | tf_op jit(solution)/shard_map/ppermute | solution.py:395
  147.7 2.1 collective-permute-done.29
  152.6 19.5 %shard_map.106 = f32[296,12]{1,0:T(8,128)} custom-call(f32[1]{0:T(128)S(6)} %copy.234.wave_ref, f32[296,8]{1,0:T(8,128)} %copy.147.own_ref, f32[4,9472]{1,0:T(4,128)} %get-tuple-element.37.all_ref, f32[12,9472]{1,0:T(8,128)} %pad_maximum_fusion.2.vec_ref, f32[296,9472]{1,0:T(8,128)} %get-tuple-element.10.refs_0_, f32[296,9472]{1,0:T(8,128)} %get-tuple-element.11.refs_1_), custom_call_target="tpu_custom_call" | custom-call | flops 89718784 | bytes 23059584 | tf_op jit(solution)/shard_map/pallas_call | solution.py:374
  175.3 2.2 collective-permute-done.31
  179.1 2.0 collective-permute-start.34
  181.5 2.3 collective-permute-start.36
  189.8 2.8 %collective-permute-done.39 = f32[1184,8]{0,1:T(8,128)S(1)} collective-permute-done((f32[1184,8]{0,1:T(8,128)S(1)}, f32[1184,8]{0,1:T(8,128)S(1)}, u32[]{:S(2)}, u32[]{:S(2)}) %collective-permute-start.39) | collective-permute-done | bytes 37920 | tf_op jit(solution)/shard_map/ppermute | solution.py:395
  196.8 20.6 %shard_map.107 = f32[296,12]{1,0:T(8,128)} custom-call(f32[1]{0:T(128)S(6)} %copy.234.wave_ref, f32[296,8]{1,0:T(8,128)} %copy.147.own_ref, f32[4,9472]{1,0:T(4,128)} %get-tuple-element.37.all_ref, f32[12,9472]{1,0:T(8,128)} %pad_maximum_fusion.3.vec_ref, f32[296,9472]{1,0:T(8,128)} %get-tuple-element.12.refs_0_, f32[296,9472]{1,0:T(8,128)} %get-tuple-element.13.refs_1_), custom_call_target="tpu_custom_call" | custom-call | flops 89718784 | bytes 23059584 | tf_op jit(solution)/shard_map/pallas_call | solution.py:374
  219.0 5.6 %psum.7 = f32[4,128]{1,0:T(4,128)S(1)} all-reduce(f32[4,128]{1,0:T(4,128)S(1)} %fusion.14), channel_id=1, replica_groups=mesh['row'=8,'col'=4] {'col'}, use_global_device_ids=true, to_apply=%region_13.16 | all-reduce | flops 512 | bytes 4096 | tf_op jit(solution)/shard_map/psum | solution.py:531
  230.3 2.2 collective-permute-start.45
  235.9 2.9 %collective-permute-done.46 = f32[1,4,128]{2,1,0:T(4,128)S(1)} collective-permute-done((f32[1,4,128]{2,1,0:T(4,128)S(1)}, f32[1,4,128]{2,1,0:T(4,128)S(1)}, u32[]{:S(2)}, u32[]{:S(2)}) %collective-permute-start.46) | collective-permute-done | bytes 2080 | tf_op jit(solution)/shard_map/ppermute | solution.py:395
  (249 shorter events, 63.9 us)
Async XLA Ops:
  2.0 7.9 %collective-permute-start = (f32[296,12]{0,1:T(8,128)S(1)}, f32[296,12]{0,1:T(8,128)S(1)}, u32[]{:S(2)}, u32[]{:S(2)}) collective-permute-start(f32[296,12]{0,1:T(8,128)S(1)} %pad_maximum_fusion.4), channel_id=1, source_target_pairs={{0,3},{1,0},{2,1},{3,2},{4,7},{5,4},{6,5},{7,6},{8,11},{9,8},{10,9... | collective-permute-start | bytes 42632 | tf_op jit(solution)/shard_map/ppermute | solution.py:395
  11.0 8.1 %collective-permute-start.3 = (f32[1184,12]{0,1:T(8,128)S(1)}, f32[1184,12]{0,1:T(8,128)S(1)}, u32[]{:S(2)}, u32[]{:S(2)}) collective-permute-start(f32[1184,12]{0,1:T(8,128)S(1)} %reshape.195), channel_id=1, source_target_pairs={{0,28},{4,0},{8,4},{12,8},{16,12},{20,16},{24,20},{28,24},{1,29},{... | collective-permute-start | bytes 170504 | tf_op jit(solution)/shard_map/ppermute | solution.py:395
  15.6 6.0 %collective-permute-start.4 = (f32[1184,12]{0,1:T(8,128)S(1)}, f32[1184,12]{0,1:T(8,128)S(1)}, u32[]{:S(2)}, u32[]{:S(2)}) collective-permute-start(f32[1184,12]{0,1:T(8,128)S(1)} %reshape.195), channel_id=1, source_target_pairs={{0,24},{4,28},{8,0},{12,4},{16,8},{20,12},{24,16},{28,20},{1,25},{... | collective-permute-start | bytes 170504 | tf_op jit(solution)/shard_map/ppermute | solution.py:395
  16.0 6.1 %collective-permute-start.5 = (f32[1184,12]{0,1:T(8,128)S(1)}, f32[1184,12]{0,1:T(8,128)S(1)}, u32[]{:S(2)}, u32[]{:S(2)}) collective-permute-start(f32[1184,12]{0,1:T(8,128)S(1)} %reshape.195), channel_id=1, source_target_pairs={{0,20},{4,24},{8,28},{12,0},{16,4},{20,8},{24,12},{28,16},{1,21},{... | collective-permute-start | bytes 170504 | tf_op jit(solution)/shard_map/ppermute | solution.py:395
  16.0 14.9 %collective-permute-start.6 = (f32[1184,12]{0,1:T(8,128)S(1)}, f32[1184,12]{0,1:T(8,128)S(1)}, u32[]{:S(2)}, u32[]{:S(2)}) collective-permute-start(f32[1184,12]{0,1:T(8,128)S(1)} %reshape.195), channel_id=1, source_target_pairs={{0,16},{4,20},{8,24},{12,28},{16,0},{20,4},{24,8},{28,12},{1,17},{... | collective-permute-start | bytes 170504 | tf_op jit(solution)/shard_map/ppermute | solution.py:395
  19.0 14.6 %collective-permute-start.7 = (f32[1184,12]{0,1:T(8,128)S(1)}, f32[1184,12]{0,1:T(8,128)S(1)}, u32[]{:S(2)}, u32[]{:S(2)}) collective-permute-start(f32[1184,12]{0,1:T(8,128)S(1)} %reshape.195), channel_id=1, source_target_pairs={{0,12},{4,16},{8,20},{12,24},{16,28},{20,0},{24,4},{28,8},{1,13},{... | collective-permute-start | bytes 170504 | tf_op jit(solution)/shard_map/ppermute | solution.py:395
  19.1 14.5 %collective-permute-start.8 = (f32[1184,12]{0,1:T(8,128)S(1)}, f32[1184,12]{0,1:T(8,128)S(1)}, u32[]{:S(2)}, u32[]{:S(2)}) collective-permute-start(f32[1184,12]{0,1:T(8,128)S(1)} %reshape.195), channel_id=1, source_target_pairs={{0,8},{4,12},{8,16},{12,20},{16,24},{20,28},{24,0},{28,4},{1,9},{5... | collective-permute-start | bytes 170504 | tf_op jit(solution)/shard_map/ppermute | solution.py:395
  21.6 12.0 %collective-permute-start.9 = (f32[1184,12]{0,1:T(8,128)S(1)}, f32[1184,12]{0,1:T(8,128)S(1)}, u32[]{:S(2)}, u32[]{:S(2)}) collective-permute-start(f32[1184,12]{0,1:T(8,128)S(1)} %reshape.195), channel_id=1, source_target_pairs={{0,4},{4,8},{8,12},{12,16},{16,20},{20,24},{24,28},{28,0},{1,5},{5... | collective-permute-start | bytes 170504 | tf_op jit(solution)/shard_map/ppermute | solution.py:395
  95.7 7.1 %collective-permute-start.14 = (f32[1184,8]{0,1:T(8,128)S(1)}, f32[1184,8]{0,1:T(8,128)S(1)}, u32[]{:S(2)}, u32[]{:S(2)}) collective-permute-start(f32[1184,8]{0,1:T(8,128)S(1)} %reshape.197), channel_id=1, source_target_pairs={{0,24},{4,28},{8,0},{12,4},{16,8},{20,12},{24,16},{28,20},{1,25},{... | collective-permute-start | bytes 113672 | tf_op jit(solution)/shard_map/ppermute | solution.py:395
  97.0 7.8 %collective-permute-start.15 = (f32[1184,8]{0,1:T(8,128)S(1)}, f32[1184,8]{0,1:T(8,128)S(1)}, u32[]{:S(2)}, u32[]{:S(2)}) collective-permute-start(f32[1184,8]{0,1:T(8,128)S(1)} %reshape.197), channel_id=1, source_target_pairs={{0,20},{4,24},{8,28},{12,0},{16,4},{20,8},{24,12},{28,16},{1,21},{... | collective-permute-start | bytes 113672 | tf_op jit(solution)/shard_map/ppermute | solution.py:395
  98.3 6.5 %collective-permute-start.16 = (f32[1184,8]{0,1:T(8,128)S(1)}, f32[1184,8]{0,1:T(8,128)S(1)}, u32[]{:S(2)}, u32[]{:S(2)}) collective-permute-start(f32[1184,8]{0,1:T(8,128)S(1)} %reshape.197), channel_id=1, source_target_pairs={{0,16},{4,20},{8,24},{12,28},{16,0},{20,4},{24,8},{28,12},{1,17},{... | collective-permute-start | bytes 113672 | tf_op jit(solution)/shard_map/ppermute | solution.py:395
  100.1 6.0 %collective-permute-start.17 = (f32[1184,8]{0,1:T(8,128)S(1)}, f32[1184,8]{0,1:T(8,128)S(1)}, u32[]{:S(2)}, u32[]{:S(2)}) collective-permute-start(f32[1184,8]{0,1:T(8,128)S(1)} %reshape.197), channel_id=1, source_target_pairs={{0,12},{4,16},{8,20},{12,24},{16,28},{20,0},{24,4},{28,8},{1,13},{... | collective-permute-start | bytes 113672 | tf_op jit(solution)/shard_map/ppermute | solution.py:395
  100.4 6.0 %collective-permute-start.18 = (f32[1184,8]{0,1:T(8,128)S(1)}, f32[1184,8]{0,1:T(8,128)S(1)}, u32[]{:S(2)}, u32[]{:S(2)}) collective-permute-start(f32[1184,8]{0,1:T(8,128)S(1)} %reshape.197), channel_id=1, source_target_pairs={{0,8},{4,12},{8,16},{12,20},{16,24},{20,28},{24,0},{28,4},{1,9},{5... | collective-permute-start | bytes 113672 | tf_op jit(solution)/shard_map/ppermute | solution.py:395
  102.8 6.7 %collective-permute-start.19 = (f32[1184,8]{0,1:T(8,128)S(1)}, f32[1184,8]{0,1:T(8,128)S(1)}, u32[]{:S(2)}, u32[]{:S(2)}) collective-permute-start(f32[1184,8]{0,1:T(8,128)S(1)} %reshape.197), channel_id=1, source_target_pairs={{0,4},{4,8},{8,12},{12,16},{16,20},{20,24},{24,28},{28,0},{1,5},{5... | collective-permute-start | bytes 113672 | tf_op jit(solution)/shard_map/ppermute | solution.py:395
  138.5 6.1 %collective-permute-start.25 = (f32[1184,8]{0,1:T(8,128)S(1)}, f32[1184,8]{0,1:T(8,128)S(1)}, u32[]{:S(2)}, u32[]{:S(2)}) collective-permute-start(f32[1184,8]{0,1:T(8,128)S(1)} %reshape.200), channel_id=1, source_target_pairs={{0,20},{4,24},{8,28},{12,0},{16,4},{20,8},{24,12},{28,16},{1,21},{... | collective-permute-start | bytes 113672 | tf_op jit(solution)/shard_map/ppermute | solution.py:395
  141.7 6.0 %collective-permute-start.28 = (f32[1184,8]{0,1:T(8,128)S(1)}, f32[1184,8]{0,1:T(8,128)S(1)}, u32[]{:S(2)}, u32[]{:S(2)}) collective-permute-start(f32[1184,8]{0,1:T(8,128)S(1)} %reshape.200), channel_id=1, source_target_pairs={{0,8},{4,12},{8,16},{12,20},{16,24},{20,28},{24,0},{28,4},{1,9},{5... | collective-permute-start | bytes 113672 | tf_op jit(solution)/shard_map/ppermute | solution.py:395
  143.1 6.7 %collective-permute-start.29 = (f32[1184,8]{0,1:T(8,128)S(1)}, f32[1184,8]{0,1:T(8,128)S(1)}, u32[]{:S(2)}, u32[]{:S(2)}) collective-permute-start(f32[1184,8]{0,1:T(8,128)S(1)} %reshape.200), channel_id=1, source_target_pairs={{0,4},{4,8},{8,12},{12,16},{16,20},{20,24},{24,28},{28,0},{1,5},{5... | collective-permute-start | bytes 113672 | tf_op jit(solution)/shard_map/ppermute | solution.py:395
  179.1 6.7 %collective-permute-start.34 = (f32[1184,8]{0,1:T(8,128)S(1)}, f32[1184,8]{0,1:T(8,128)S(1)}, u32[]{:S(2)}, u32[]{:S(2)}) collective-permute-start(f32[1184,8]{0,1:T(8,128)S(1)} %reshape.203), channel_id=1, source_target_pairs={{0,24},{4,28},{8,0},{12,4},{16,8},{20,12},{24,16},{28,20},{1,25},{... | collective-permute-start | bytes 113672 | tf_op jit(solution)/shard_map/ppermute | solution.py:395
  181.1 6.6 %collective-permute-start.35 = (f32[1184,8]{0,1:T(8,128)S(1)}, f32[1184,8]{0,1:T(8,128)S(1)}, u32[]{:S(2)}, u32[]{:S(2)}) collective-permute-start(f32[1184,8]{0,1:T(8,128)S(1)} %reshape.203), channel_id=1, source_target_pairs={{0,20},{4,24},{8,28},{12,0},{16,4},{20,8},{24,12},{28,16},{1,21},{... | collective-permute-start | bytes 113672 | tf_op jit(solution)/shard_map/ppermute | solution.py:395
  181.5 6.4 %collective-permute-start.36 = (f32[1184,8]{0,1:T(8,128)S(1)}, f32[1184,8]{0,1:T(8,128)S(1)}, u32[]{:S(2)}, u32[]{:S(2)}) collective-permute-start(f32[1184,8]{0,1:T(8,128)S(1)} %reshape.203), channel_id=1, source_target_pairs={{0,16},{4,20},{8,24},{12,28},{16,0},{20,4},{24,8},{28,12},{1,17},{... | collective-permute-start | bytes 113672 | tf_op jit(solution)/shard_map/ppermute | solution.py:395
  185.8 6.9 %collective-permute-start.39 = (f32[1184,8]{0,1:T(8,128)S(1)}, f32[1184,8]{0,1:T(8,128)S(1)}, u32[]{:S(2)}, u32[]{:S(2)}) collective-permute-start(f32[1184,8]{0,1:T(8,128)S(1)} %reshape.203), channel_id=1, source_target_pairs={{0,4},{4,8},{8,12},{12,16},{16,20},{20,24},{24,28},{28,0},{1,5},{5... | collective-permute-start | bytes 113672 | tf_op jit(solution)/shard_map/ppermute | solution.py:395
  225.4 7.1 %collective-permute-start.41 = (f32[1,4,128]{2,1,0:T(4,128)S(1)}, f32[1,4,128]{2,1,0:T(4,128)S(1)}, u32[]{:S(2)}, u32[]{:S(2)}) collective-permute-start(f32[1,4,128]{2,1,0:T(4,128)S(1)} %bitcast.177), channel_id=1, source_target_pairs={{0,24},{4,28},{8,0},{12,4},{16,8},{20,12},{24,16},{28,20},{1,25},{... | collective-permute-start | bytes 6152 | tf_op jit(solution)/shard_map/ppermute | solution.py:395
  227.2 6.4 %collective-permute-start.42 = (f32[1,4,128]{2,1,0:T(4,128)S(1)}, f32[1,4,128]{2,1,0:T(4,128)S(1)}, u32[]{:S(2)}, u32[]{:S(2)}) collective-permute-start(f32[1,4,128]{2,1,0:T(4,128)S(1)} %bitcast.178), channel_id=1, source_target_pairs={{0,20},{4,24},{8,28},{12,0},{16,4},{20,8},{24,12},{28,16},{1,21},{... | collective-permute-start | bytes 6152 | tf_op jit(solution)/shard_map/ppermute | solution.py:395
  232.5 6.3 %collective-permute-start.46 = (f32[1,4,128]{2,1,0:T(4,128)S(1)}, f32[1,4,128]{2,1,0:T(4,128)S(1)}, u32[]{:S(2)}, u32[]{:S(2)}) collective-permute-start(f32[1,4,128]{2,1,0:T(4,128)S(1)} %bitcast.182), channel_id=1, source_target_pairs={{0,4},{4,8},{8,12},{12,16},{16,20},{20,24},{24,28},{28,0},{1,5},{5... | collective-permute-start | bytes 6152 | tf_op jit(solution)/shard_map/ppermute | solution.py:395
  (27 other events, 127.6 us)

commit v12 on v11

--- a/solution.py
+++ b/solution.py
@@ -293,7 +293,7 @@
 
         columns = vec_ref.shape[0]
         zeros = tuple(jnp.zeros((8, width), jnp.float32) for _ in range(columns))
-        sums = lax.fori_loop(0, chunk_count, lane_block, zeros, unroll=4 if stored_in and not slope_mode else 3)
+        sums = lax.fori_loop(0, chunk_count, lane_block, zeros, unroll=4 if stored_in or store_out else 3)
         lane = lax.broadcasted_iota(jnp.int32, (8, columns), 1)
         result = jnp.zeros((8, columns), jnp.float32)
         for column in range(columns):

time: 240 us -> 238 us (level)
  Pallas kernels: 113 us -> 110 us
    pallas_call x4, Pallas kernels: 113 us -> 110 us  [panel_call(): pl.pallas_call(functools.partial(panel_kernel, slope_mode, stored_in, sto...]
where the time goes in v12:
time: 238 us; the launch traced here: 237 us
  Pallas kernels  110 us (46%)
  starting transfers between devices  52.3 us (22%)
  waiting for transfers between devices  41.2 us (17%)
  other arithmetic  15.6 us (7%)
  local copies, waits for them, and re-layouts  8.48 us (4%)
  blocking collectives  5.65 us (2%)
    pallas_call x4, Pallas kernels, panel_call(): pl.pallas_call(functools.partial(panel_kernel, slope_mode, stored_in, sto...  110 us
    ppermute x47, starting transfers between devices, gather_axis(): lax.ppermute(vector, name, [(i, (i + shift) % count) for i in range(count)])  52.3 us
    ppermute x47, waiting for transfers between devices, gather_axis(): lax.ppermute(vector, name, [(i, (i + shift) % count) for i in range(count)])  41.2 us
    psum x1, blocking collectives, local(): lax.psum(local_sums, 'col')[None]  5.65 us
  transfers between devices with their start and end apart: 47, of which 23 were waited for; matrix products, arithmetic and copies ran while one was open for 2% of the time, Pallas kernels for 0%

profile of v12, /device:TPU:0, one launch (start us, length us, event | category | flops | bytes accessed | tf_op | source)
XLA Modules:
  0.0 236.9 jit_solution(10560323438229949912)
XLA Ops:
  2.0 2.5 %collective-permute-start = (f32[296,12]{0,1:T(8,128)S(1)}, f32[296,12]{0,1:T(8,128)S(1)}, u32[]{:S(2)}, u32[]{:S(2)}) collective-permute-start(f32[296,12]{0,1:T(8,128)S(1)} %pad_maximum_fusion.4), channel_id=1, source_target_pairs={{0,3},{1,0},{2,1},{3,2},{4,7},{5,4},{6,5},{7,6},{8,11},{9,8},{10,9... | collective-permute-start | bytes 42632 | tf_op jit(solution)/shard_map/ppermute | solution.py:395
  11.0 4.6 %collective-permute-start.3 = (f32[1184,12]{0,1:T(8,128)S(1)}, f32[1184,12]{0,1:T(8,128)S(1)}, u32[]{:S(2)}, u32[]{:S(2)}) collective-permute-start(f32[1184,12]{0,1:T(8,128)S(1)} %reshape.195), channel_id=1, source_target_pairs={{0,28},{4,0},{8,4},{12,8},{16,12},{20,16},{24,20},{28,24},{1,29},{... | collective-permute-start | bytes 170504 | tf_op jit(solution)/shard_map/ppermute | solution.py:395
  16.0 3.0 %collective-permute-start.6 = (f32[1184,12]{0,1:T(8,128)S(1)}, f32[1184,12]{0,1:T(8,128)S(1)}, u32[]{:S(2)}, u32[]{:S(2)}) collective-permute-start(f32[1184,12]{0,1:T(8,128)S(1)} %reshape.195), channel_id=1, source_target_pairs={{0,16},{4,20},{8,24},{12,28},{16,0},{20,4},{24,8},{28,12},{1,17},{... | collective-permute-start | bytes 170504 | tf_op jit(solution)/shard_map/ppermute | solution.py:395
  22.2 8.8 %collective-permute-done.6 = f32[1184,12]{0,1:T(8,128)S(1)} collective-permute-done((f32[1184,12]{0,1:T(8,128)S(1)}, f32[1184,12]{0,1:T(8,128)S(1)}, u32[]{:S(2)}, u32[]{:S(2)}) %collective-permute-start.6) | collective-permute-done | bytes 56864 | tf_op jit(solution)/shard_map/ppermute | solution.py:395
  31.0 2.6 %collective-permute-done.7 = f32[1184,12]{0,1:T(8,128)S(1)} collective-permute-done((f32[1184,12]{0,1:T(8,128)S(1)}, f32[1184,12]{0,1:T(8,128)S(1)}, u32[]{:S(2)}, u32[]{:S(2)}) %collective-permute-start.7) | collective-permute-done | bytes 56864 | tf_op jit(solution)/shard_map/ppermute | solution.py:395
  36.0 51.5 %shard_map.104 = (f32[296,12]{1,0:T(8,128)}, f32[296,9472]{1,0:T(8,128)}, f32[296,9472]{1,0:T(8,128)}, f32[296,9472]{1,0:T(8,128)}, f32[296,9472]{1,0:T(8,128)}) custom-call(f32[1]{0:T(128)S(6)} %copy.234.wave_ref, f32[296,8]{1,0:T(8,128)} %copy.147.own_ref, f32[4,9472]{1,0:T(4,128)} %get-tuple-element.37.all_ref, f32[12,9472]{1,0:T(8,128)} %pad_maximum_fusion.vec_ref), custom_call_target="tpu_custom_call" | custom-call | flops 420556800 | bytes 45489280 | tf_op jit(solution)/shard_map/pallas_call | solution.py:374
  90.8 2.2 collective-permute-done.11
  98.9 2.4 %collective-permute-start.18 = (f32[1184,8]{0,1:T(8,128)S(1)}, f32[1184,8]{0,1:T(8,128)S(1)}, u32[]{:S(2)}, u32[]{:S(2)}) collective-permute-start(f32[1184,8]{0,1:T(8,128)S(1)} %reshape.197), channel_id=1, source_target_pairs={{0,8},{4,12},{8,16},{12,20},{16,24},{20,28},{24,0},{28,4},{1,9},{5... | collective-permute-start | bytes 113672 | tf_op jit(solution)/shard_map/ppermute | solution.py:395
  101.3 2.0 collective-permute-start.19
  104.9 3.2 %collective-permute-done.19 = f32[1184,8]{0,1:T(8,128)S(1)} collective-permute-done((f32[1184,8]{0,1:T(8,128)S(1)}, f32[1184,8]{0,1:T(8,128)S(1)}, u32[]{:S(2)}, u32[]{:S(2)}) %collective-permute-start.19) | collective-permute-done | bytes 37920 | tf_op jit(solution)/shard_map/ppermute | solution.py:395
  109.9 19.5 %shard_map.105 = f32[296,12]{1,0:T(8,128)} custom-call(f32[1]{0:T(128)S(6)} %copy.234.wave_ref, f32[296,8]{1,0:T(8,128)} %copy.147.own_ref, f32[4,9472]{1,0:T(4,128)} %get-tuple-element.37.all_ref, f32[12,9472]{1,0:T(8,128)} %pad_maximum_fusion.1.vec_ref, f32[296,9472]{1,0:T(8,128)} %get-tuple-element.10.refs_0_, f32[296,9472]{1,0:T(8,128)} %get-tuple-element.11.refs_1_), custom_call_target="tpu_custom_call" | custom-call | flops 89718784 | bytes 23059584 | tf_op jit(solution)/shard_map/pallas_call | solution.py:374
  132.4 2.4 collective-permute-done.21
  137.1 2.6 %collective-permute-start.26 = (f32[1184,8]{0,1:T(8,128)S(1)}, f32[1184,8]{0,1:T(8,128)S(1)}, u32[]{:S(2)}, u32[]{:S(2)}) collective-permute-start(f32[1184,8]{0,1:T(8,128)S(1)} %reshape.200), channel_id=1, source_target_pairs={{0,16},{4,20},{8,24},{12,28},{16,0},{20,4},{24,8},{28,12},{1,17},{... | collective-permute-start | bytes 113672 | tf_op jit(solution)/shard_map/ppermute | solution.py:395
  143.1 2.5 %collective-permute-done.27 = f32[1184,8]{0,1:T(8,128)S(1)} collective-permute-done((f32[1184,8]{0,1:T(8,128)S(1)}, f32[1184,8]{0,1:T(8,128)S(1)}, u32[]{:S(2)}, u32[]{:S(2)}) %collective-permute-start.27) | collective-permute-done | bytes 37920 | tf_op jit(solution)/shard_map/ppermute | solution.py:395
  146.3 2.1 collective-permute-done.29
  151.2 19.5 %shard_map.106 = f32[296,12]{1,0:T(8,128)} custom-call(f32[1]{0:T(128)S(6)} %copy.234.wave_ref, f32[296,8]{1,0:T(8,128)} %copy.147.own_ref, f32[4,9472]{1,0:T(4,128)} %get-tuple-element.37.all_ref, f32[12,9472]{1,0:T(8,128)} %pad_maximum_fusion.2.vec_ref, f32[296,9472]{1,0:T(8,128)} %get-tuple-element.10.refs_0_, f32[296,9472]{1,0:T(8,128)} %get-tuple-element.11.refs_1_), custom_call_target="tpu_custom_call" | custom-call | flops 89718784 | bytes 23059584 | tf_op jit(solution)/shard_map/pallas_call | solution.py:374
  173.8 2.2 collective-permute-done.31
  177.6 2.0 collective-permute-start.34
  180.1 2.3 collective-permute-start.36
  188.4 2.8 %collective-permute-done.39 = f32[1184,8]{0,1:T(8,128)S(1)} collective-permute-done((f32[1184,8]{0,1:T(8,128)S(1)}, f32[1184,8]{0,1:T(8,128)S(1)}, u32[]{:S(2)}, u32[]{:S(2)}) %collective-permute-start.39) | collective-permute-done | bytes 37920 | tf_op jit(solution)/shard_map/ppermute | solution.py:395
  195.3 19.5 %shard_map.107 = f32[296,12]{1,0:T(8,128)} custom-call(f32[1]{0:T(128)S(6)} %copy.234.wave_ref, f32[296,8]{1,0:T(8,128)} %copy.147.own_ref, f32[4,9472]{1,0:T(4,128)} %get-tuple-element.37.all_ref, f32[12,9472]{1,0:T(8,128)} %pad_maximum_fusion.3.vec_ref, f32[296,9472]{1,0:T(8,128)} %get-tuple-element.12.refs_0_, f32[296,9472]{1,0:T(8,128)} %get-tuple-element.13.refs_1_), custom_call_target="tpu_custom_call" | custom-call | flops 89718784 | bytes 23059584 | tf_op jit(solution)/shard_map/pallas_call | solution.py:374
  216.4 5.6 %psum.7 = f32[4,128]{1,0:T(4,128)S(1)} all-reduce(f32[4,128]{1,0:T(4,128)S(1)} %fusion.14), channel_id=1, replica_groups=mesh['row'=8,'col'=4] {'col'}, use_global_device_ids=true, to_apply=%region_13.16 | all-reduce | flops 512 | bytes 4096 | tf_op jit(solution)/shard_map/psum | solution.py:531
  227.7 2.2 collective-permute-start.45
  233.3 2.9 %collective-permute-done.46 = f32[1,4,128]{2,1,0:T(4,128)S(1)} collective-permute-done((f32[1,4,128]{2,1,0:T(4,128)S(1)}, f32[1,4,128]{2,1,0:T(4,128)S(1)}, u32[]{:S(2)}, u32[]{:S(2)}) %collective-permute-start.46) | collective-permute-done | bytes 2080 | tf_op jit(solution)/shard_map/ppermute | solution.py:395
  (249 shorter events, 63.9 us)
Async XLA Ops:
  2.0 7.9 %collective-permute-start = (f32[296,12]{0,1:T(8,128)S(1)}, f32[296,12]{0,1:T(8,128)S(1)}, u32[]{:S(2)}, u32[]{:S(2)}) collective-permute-start(f32[296,12]{0,1:T(8,128)S(1)} %pad_maximum_fusion.4), channel_id=1, source_target_pairs={{0,3},{1,0},{2,1},{3,2},{4,7},{5,4},{6,5},{7,6},{8,11},{9,8},{10,9... | collective-permute-start | bytes 42632 | tf_op jit(solution)/shard_map/ppermute | solution.py:395
  11.0 8.1 %collective-permute-start.3 = (f32[1184,12]{0,1:T(8,128)S(1)}, f32[1184,12]{0,1:T(8,128)S(1)}, u32[]{:S(2)}, u32[]{:S(2)}) collective-permute-start(f32[1184,12]{0,1:T(8,128)S(1)} %reshape.195), channel_id=1, source_target_pairs={{0,28},{4,0},{8,4},{12,8},{16,12},{20,16},{24,20},{28,24},{1,29},{... | collective-permute-start | bytes 170504 | tf_op jit(solution)/shard_map/ppermute | solution.py:395
  15.6 6.0 %collective-permute-start.4 = (f32[1184,12]{0,1:T(8,128)S(1)}, f32[1184,12]{0,1:T(8,128)S(1)}, u32[]{:S(2)}, u32[]{:S(2)}) collective-permute-start(f32[1184,12]{0,1:T(8,128)S(1)} %reshape.195), channel_id=1, source_target_pairs={{0,24},{4,28},{8,0},{12,4},{16,8},{20,12},{24,16},{28,20},{1,25},{... | collective-permute-start | bytes 170504 | tf_op jit(solution)/shard_map/ppermute | solution.py:395
  16.0 6.1 %collective-permute-start.5 = (f32[1184,12]{0,1:T(8,128)S(1)}, f32[1184,12]{0,1:T(8,128)S(1)}, u32[]{:S(2)}, u32[]{:S(2)}) collective-permute-start(f32[1184,12]{0,1:T(8,128)S(1)} %reshape.195), channel_id=1, source_target_pairs={{0,20},{4,24},{8,28},{12,0},{16,4},{20,8},{24,12},{28,16},{1,21},{... | collective-permute-start | bytes 170504 | tf_op jit(solution)/shard_map/ppermute | solution.py:395
  16.0 14.9 %collective-permute-start.6 = (f32[1184,12]{0,1:T(8,128)S(1)}, f32[1184,12]{0,1:T(8,128)S(1)}, u32[]{:S(2)}, u32[]{:S(2)}) collective-permute-start(f32[1184,12]{0,1:T(8,128)S(1)} %reshape.195), channel_id=1, source_target_pairs={{0,16},{4,20},{8,24},{12,28},{16,0},{20,4},{24,8},{28,12},{1,17},{... | collective-permute-start | bytes 170504 | tf_op jit(solution)/shard_map/ppermute | solution.py:395
  19.0 14.6 %collective-permute-start.7 = (f32[1184,12]{0,1:T(8,128)S(1)}, f32[1184,12]{0,1:T(8,128)S(1)}, u32[]{:S(2)}, u32[]{:S(2)}) collective-permute-start(f32[1184,12]{0,1:T(8,128)S(1)} %reshape.195), channel_id=1, source_target_pairs={{0,12},{4,16},{8,20},{12,24},{16,28},{20,0},{24,4},{28,8},{1,13},{... | collective-permute-start | bytes 170504 | tf_op jit(solution)/shard_map/ppermute | solution.py:395
  19.1 14.5 %collective-permute-start.8 = (f32[1184,12]{0,1:T(8,128)S(1)}, f32[1184,12]{0,1:T(8,128)S(1)}, u32[]{:S(2)}, u32[]{:S(2)}) collective-permute-start(f32[1184,12]{0,1:T(8,128)S(1)} %reshape.195), channel_id=1, source_target_pairs={{0,8},{4,12},{8,16},{12,20},{16,24},{20,28},{24,0},{28,4},{1,9},{5... | collective-permute-start | bytes 170504 | tf_op jit(solution)/shard_map/ppermute | solution.py:395
  21.6 12.0 %collective-permute-start.9 = (f32[1184,12]{0,1:T(8,128)S(1)}, f32[1184,12]{0,1:T(8,128)S(1)}, u32[]{:S(2)}, u32[]{:S(2)}) collective-permute-start(f32[1184,12]{0,1:T(8,128)S(1)} %reshape.195), channel_id=1, source_target_pairs={{0,4},{4,8},{8,12},{12,16},{16,20},{20,24},{24,28},{28,0},{1,5},{5... | collective-permute-start | bytes 170504 | tf_op jit(solution)/shard_map/ppermute | solution.py:395
  94.2 7.1 %collective-permute-start.14 = (f32[1184,8]{0,1:T(8,128)S(1)}, f32[1184,8]{0,1:T(8,128)S(1)}, u32[]{:S(2)}, u32[]{:S(2)}) collective-permute-start(f32[1184,8]{0,1:T(8,128)S(1)} %reshape.197), channel_id=1, source_target_pairs={{0,24},{4,28},{8,0},{12,4},{16,8},{20,12},{24,16},{28,20},{1,25},{... | collective-permute-start | bytes 113672 | tf_op jit(solution)/shard_map/ppermute | solution.py:395
  95.5 7.8 %collective-permute-start.15 = (f32[1184,8]{0,1:T(8,128)S(1)}, f32[1184,8]{0,1:T(8,128)S(1)}, u32[]{:S(2)}, u32[]{:S(2)}) collective-permute-start(f32[1184,8]{0,1:T(8,128)S(1)} %reshape.197), channel_id=1, source_target_pairs={{0,20},{4,24},{8,28},{12,0},{16,4},{20,8},{24,12},{28,16},{1,21},{... | collective-permute-start | bytes 113672 | tf_op jit(solution)/shard_map/ppermute | solution.py:395
  96.9 6.5 %collective-permute-start.16 = (f32[1184,8]{0,1:T(8,128)S(1)}, f32[1184,8]{0,1:T(8,128)S(1)}, u32[]{:S(2)}, u32[]{:S(2)}) collective-permute-start(f32[1184,8]{0,1:T(8,128)S(1)} %reshape.197), channel_id=1, source_target_pairs={{0,16},{4,20},{8,24},{12,28},{16,0},{20,4},{24,8},{28,12},{1,17},{... | collective-permute-start | bytes 113672 | tf_op jit(solution)/shard_map/ppermute | solution.py:395
  98.6 6.0 %collective-permute-start.17 = (f32[1184,8]{0,1:T(8,128)S(1)}, f32[1184,8]{0,1:T(8,128)S(1)}, u32[]{:S(2)}, u32[]{:S(2)}) collective-permute-start(f32[1184,8]{0,1:T(8,128)S(1)} %reshape.197), channel_id=1, source_target_pairs={{0,12},{4,16},{8,20},{12,24},{16,28},{20,0},{24,4},{28,8},{1,13},{... | collective-permute-start | bytes 113672 | tf_op jit(solution)/shard_map/ppermute | solution.py:395
  98.9 6.0 %collective-permute-start.18 = (f32[1184,8]{0,1:T(8,128)S(1)}, f32[1184,8]{0,1:T(8,128)S(1)}, u32[]{:S(2)}, u32[]{:S(2)}) collective-permute-start(f32[1184,8]{0,1:T(8,128)S(1)} %reshape.197), channel_id=1, source_target_pairs={{0,8},{4,12},{8,16},{12,20},{16,24},{20,28},{24,0},{28,4},{1,9},{5... | collective-permute-start | bytes 113672 | tf_op jit(solution)/shard_map/ppermute | solution.py:395
  101.3 6.7 %collective-permute-start.19 = (f32[1184,8]{0,1:T(8,128)S(1)}, f32[1184,8]{0,1:T(8,128)S(1)}, u32[]{:S(2)}, u32[]{:S(2)}) collective-permute-start(f32[1184,8]{0,1:T(8,128)S(1)} %reshape.197), channel_id=1, source_target_pairs={{0,4},{4,8},{8,12},{12,16},{16,20},{20,24},{24,28},{28,0},{1,5},{5... | collective-permute-start | bytes 113672 | tf_op jit(solution)/shard_map/ppermute | solution.py:395
  137.0 6.1 %collective-permute-start.25 = (f32[1184,8]{0,1:T(8,128)S(1)}, f32[1184,8]{0,1:T(8,128)S(1)}, u32[]{:S(2)}, u32[]{:S(2)}) collective-permute-start(f32[1184,8]{0,1:T(8,128)S(1)} %reshape.200), channel_id=1, source_target_pairs={{0,20},{4,24},{8,28},{12,0},{16,4},{20,8},{24,12},{28,16},{1,21},{... | collective-permute-start | bytes 113672 | tf_op jit(solution)/shard_map/ppermute | solution.py:395
  140.3 6.0 %collective-permute-start.28 = (f32[1184,8]{0,1:T(8,128)S(1)}, f32[1184,8]{0,1:T(8,128)S(1)}, u32[]{:S(2)}, u32[]{:S(2)}) collective-permute-start(f32[1184,8]{0,1:T(8,128)S(1)} %reshape.200), channel_id=1, source_target_pairs={{0,8},{4,12},{8,16},{12,20},{16,24},{20,28},{24,0},{28,4},{1,9},{5... | collective-permute-start | bytes 113672 | tf_op jit(solution)/shard_map/ppermute | solution.py:395
  141.6 6.7 %collective-permute-start.29 = (f32[1184,8]{0,1:T(8,128)S(1)}, f32[1184,8]{0,1:T(8,128)S(1)}, u32[]{:S(2)}, u32[]{:S(2)}) collective-permute-start(f32[1184,8]{0,1:T(8,128)S(1)} %reshape.200), channel_id=1, source_target_pairs={{0,4},{4,8},{8,12},{12,16},{16,20},{20,24},{24,28},{28,0},{1,5},{5... | collective-permute-start | bytes 113672 | tf_op jit(solution)/shard_map/ppermute | solution.py:395
  177.6 6.7 %collective-permute-start.34 = (f32[1184,8]{0,1:T(8,128)S(1)}, f32[1184,8]{0,1:T(8,128)S(1)}, u32[]{:S(2)}, u32[]{:S(2)}) collective-permute-start(f32[1184,8]{0,1:T(8,128)S(1)} %reshape.203), channel_id=1, source_target_pairs={{0,24},{4,28},{8,0},{12,4},{16,8},{20,12},{24,16},{28,20},{1,25},{... | collective-permute-start | bytes 113672 | tf_op jit(solution)/shard_map/ppermute | solution.py:395
  179.6 6.6 %collective-permute-start.35 = (f32[1184,8]{0,1:T(8,128)S(1)}, f32[1184,8]{0,1:T(8,128)S(1)}, u32[]{:S(2)}, u32[]{:S(2)}) collective-permute-start(f32[1184,8]{0,1:T(8,128)S(1)} %reshape.203), channel_id=1, source_target_pairs={{0,20},{4,24},{8,28},{12,0},{16,4},{20,8},{24,12},{28,16},{1,21},{... | collective-permute-start | bytes 113672 | tf_op jit(solution)/shard_map/ppermute | solution.py:395
  180.1 6.4 %collective-permute-start.36 = (f32[1184,8]{0,1:T(8,128)S(1)}, f32[1184,8]{0,1:T(8,128)S(1)}, u32[]{:S(2)}, u32[]{:S(2)}) collective-permute-start(f32[1184,8]{0,1:T(8,128)S(1)} %reshape.203), channel_id=1, source_target_pairs={{0,16},{4,20},{8,24},{12,28},{16,0},{20,4},{24,8},{28,12},{1,17},{... | collective-permute-start | bytes 113672 | tf_op jit(solution)/shard_map/ppermute | solution.py:395
  184.3 6.9 %collective-permute-start.39 = (f32[1184,8]{0,1:T(8,128)S(1)}, f32[1184,8]{0,1:T(8,128)S(1)}, u32[]{:S(2)}, u32[]{:S(2)}) collective-permute-start(f32[1184,8]{0,1:T(8,128)S(1)} %reshape.203), channel_id=1, source_target_pairs={{0,4},{4,8},{8,12},{12,16},{16,20},{20,24},{24,28},{28,0},{1,5},{5... | collective-permute-start | bytes 113672 | tf_op jit(solution)/shard_map/ppermute | solution.py:395
  222.8 7.1 %collective-permute-start.41 = (f32[1,4,128]{2,1,0:T(4,128)S(1)}, f32[1,4,128]{2,1,0:T(4,128)S(1)}, u32[]{:S(2)}, u32[]{:S(2)}) collective-permute-start(f32[1,4,128]{2,1,0:T(4,128)S(1)} %bitcast.177), channel_id=1, source_target_pairs={{0,24},{4,28},{8,0},{12,4},{16,8},{20,12},{24,16},{28,20},{1,25},{... | collective-permute-start | bytes 6152 | tf_op jit(solution)/shard_map/ppermute | solution.py:395
  224.6 6.4 %collective-permute-start.42 = (f32[1,4,128]{2,1,0:T(4,128)S(1)}, f32[1,4,128]{2,1,0:T(4,128)S(1)}, u32[]{:S(2)}, u32[]{:S(2)}) collective-permute-start(f32[1,4,128]{2,1,0:T(4,128)S(1)} %bitcast.178), channel_id=1, source_target_pairs={{0,20},{4,24},{8,28},{12,0},{16,4},{20,8},{24,12},{28,16},{1,21},{... | collective-permute-start | bytes 6152 | tf_op jit(solution)/shard_map/ppermute | solution.py:395
  229.9 6.3 %collective-permute-start.46 = (f32[1,4,128]{2,1,0:T(4,128)S(1)}, f32[1,4,128]{2,1,0:T(4,128)S(1)}, u32[]{:S(2)}, u32[]{:S(2)}) collective-permute-start(f32[1,4,128]{2,1,0:T(4,128)S(1)} %bitcast.182), channel_id=1, source_target_pairs={{0,4},{4,8},{8,12},{12,16},{16,20},{20,24},{24,28},{28,0},{1,5},{5... | collective-permute-start | bytes 6152 | tf_op jit(solution)/shard_map/ppermute | solution.py:395
  (27 other events, 126.6 us)

commit v13 on v12

--- a/solution.py
+++ b/solution.py
@@ -293,7 +293,7 @@
 
         columns = vec_ref.shape[0]
         zeros = tuple(jnp.zeros((8, width), jnp.float32) for _ in range(columns))
-        sums = lax.fori_loop(0, chunk_count, lane_block, zeros, unroll=4 if stored_in or store_out else 3)
+        sums = lax.fori_loop(0, chunk_count, lane_block, zeros, unroll=6 if stored_in or store_out else 3)
         lane = lax.broadcasted_iota(jnp.int32, (8, columns), 1)
         result = jnp.zeros((8, columns), jnp.float32)
         for column in range(columns):

time: 238 us -> 232 us (0.975)
  Pallas kernels: 110 us -> 104 us
    pallas_call x4, Pallas kernels: 110 us -> 104 us  [panel_call(): pl.pallas_call(functools.partial(panel_kernel, slope_mode, stored_in, sto...]
where the time goes in v13:
time: 232 us; the launch traced here: 231 us
  Pallas kernels  104 us (45%)
  starting transfers between devices  52.3 us (23%)
  waiting for transfers between devices  41.2 us (18%)
  other arithmetic  15.6 us (7%)
  local copies, waits for them, and re-layouts  8.48 us (4%)
  blocking collectives  5.65 us (2%)
    pallas_call x4, Pallas kernels, panel_call(): pl.pallas_call(functools.partial(panel_kernel, slope_mode, stored_in, sto...  104 us
    ppermute x47, starting transfers between devices, gather_axis(): lax.ppermute(vector, name, [(i, (i + shift) % count) for i in range(count)])  52.3 us
    ppermute x47, waiting for transfers between devices, gather_axis(): lax.ppermute(vector, name, [(i, (i + shift) % count) for i in range(count)])  41.2 us
    psum x1, blocking collectives, local(): lax.psum(local_sums, 'col')[None]  5.65 us
  transfers between devices with their start and end apart: 47, of which 23 were waited for; matrix products, arithmetic and copies ran while one was open for 2% of the time, Pallas kernels for 0%

profile of v13, /device:TPU:0, one launch (start us, length us, event | category | flops | bytes accessed | tf_op | source)
XLA Modules:
  0.0 231.1 jit_solution(13111167349990472979)
XLA Ops:
  2.0 2.5 %collective-permute-start = (f32[296,12]{0,1:T(8,128)S(1)}, f32[296,12]{0,1:T(8,128)S(1)}, u32[]{:S(2)}, u32[]{:S(2)}) collective-permute-start(f32[296,12]{0,1:T(8,128)S(1)} %pad_maximum_fusion.4), channel_id=1, source_target_pairs={{0,3},{1,0},{2,1},{3,2},{4,7},{5,4},{6,5},{7,6},{8,11},{9,8},{10,9... | collective-permute-start | bytes 42632 | tf_op jit(solution)/shard_map/ppermute | solution.py:395
  11.0 4.6 %collective-permute-start.3 = (f32[1184,12]{0,1:T(8,128)S(1)}, f32[1184,12]{0,1:T(8,128)S(1)}, u32[]{:S(2)}, u32[]{:S(2)}) collective-permute-start(f32[1184,12]{0,1:T(8,128)S(1)} %reshape.195), channel_id=1, source_target_pairs={{0,28},{4,0},{8,4},{12,8},{16,12},{20,16},{24,20},{28,24},{1,29},{... | collective-permute-start | bytes 170504 | tf_op jit(solution)/shard_map/ppermute | solution.py:395
  16.0 3.0 %collective-permute-start.6 = (f32[1184,12]{0,1:T(8,128)S(1)}, f32[1184,12]{0,1:T(8,128)S(1)}, u32[]{:S(2)}, u32[]{:S(2)}) collective-permute-start(f32[1184,12]{0,1:T(8,128)S(1)} %reshape.195), channel_id=1, source_target_pairs={{0,16},{4,20},{8,24},{12,28},{16,0},{20,4},{24,8},{28,12},{1,17},{... | collective-permute-start | bytes 170504 | tf_op jit(solution)/shard_map/ppermute | solution.py:395
  22.2 8.8 %collective-permute-done.6 = f32[1184,12]{0,1:T(8,128)S(1)} collective-permute-done((f32[1184,12]{0,1:T(8,128)S(1)}, f32[1184,12]{0,1:T(8,128)S(1)}, u32[]{:S(2)}, u32[]{:S(2)}) %collective-permute-start.6) | collective-permute-done | bytes 56864 | tf_op jit(solution)/shard_map/ppermute | solution.py:395
  31.0 2.6 %collective-permute-done.7 = f32[1184,12]{0,1:T(8,128)S(1)} collective-permute-done((f32[1184,12]{0,1:T(8,128)S(1)}, f32[1184,12]{0,1:T(8,128)S(1)}, u32[]{:S(2)}, u32[]{:S(2)}) %collective-permute-start.7) | collective-permute-done | bytes 56864 | tf_op jit(solution)/shard_map/ppermute | solution.py:395
  36.0 49.6 %shard_map.104 = (f32[296,12]{1,0:T(8,128)}, f32[296,9472]{1,0:T(8,128)}, f32[296,9472]{1,0:T(8,128)}, f32[296,9472]{1,0:T(8,128)}, f32[296,9472]{1,0:T(8,128)}) custom-call(f32[1]{0:T(128)S(6)} %copy.234.wave_ref, f32[296,8]{1,0:T(8,128)} %copy.147.own_ref, f32[4,9472]{1,0:T(4,128)} %get-tuple-element.37.all_ref, f32[12,9472]{1,0:T(8,128)} %pad_maximum_fusion.vec_ref), custom_call_target="tpu_custom_call" | custom-call | flops 420556800 | bytes 45489280 | tf_op jit(solution)/shard_map/pallas_call | solution.py:374
  88.9 2.2 collective-permute-done.11
  97.0 2.4 %collective-permute-start.18 = (f32[1184,8]{0,1:T(8,128)S(1)}, f32[1184,8]{0,1:T(8,128)S(1)}, u32[]{:S(2)}, u32[]{:S(2)}) collective-permute-start(f32[1184,8]{0,1:T(8,128)S(1)} %reshape.197), channel_id=1, source_target_pairs={{0,8},{4,12},{8,16},{12,20},{16,24},{20,28},{24,0},{28,4},{1,9},{5... | collective-permute-start | bytes 113672 | tf_op jit(solution)/shard_map/ppermute | solution.py:395
  99.5 2.0 collective-permute-start.19
  103.0 3.2 %collective-permute-done.19 = f32[1184,8]{0,1:T(8,128)S(1)} collective-permute-done((f32[1184,8]{0,1:T(8,128)S(1)}, f32[1184,8]{0,1:T(8,128)S(1)}, u32[]{:S(2)}, u32[]{:S(2)}) %collective-permute-start.19) | collective-permute-done | bytes 37920 | tf_op jit(solution)/shard_map/ppermute | solution.py:395
  108.1 18.2 %shard_map.105 = f32[296,12]{1,0:T(8,128)} custom-call(f32[1]{0:T(128)S(6)} %copy.234.wave_ref, f32[296,8]{1,0:T(8,128)} %copy.147.own_ref, f32[4,9472]{1,0:T(4,128)} %get-tuple-element.37.all_ref, f32[12,9472]{1,0:T(8,128)} %pad_maximum_fusion.1.vec_ref, f32[296,9472]{1,0:T(8,128)} %get-tuple-element.10.refs_0_, f32[296,9472]{1,0:T(8,128)} %get-tuple-element.11.refs_1_), custom_call_target="tpu_custom_call" | custom-call | flops 89718784 | bytes 23059584 | tf_op jit(solution)/shard_map/pallas_call | solution.py:374
  129.2 2.4 %collective-permute-done.21 = f32[296,8]{0,1:T(8,128)S(1)} collective-permute-done((f32[296,8]{0,1:T(8,128)S(1)}, f32[296,8]{0,1:T(8,128)S(1)}, u32[]{:S(2)}, u32[]{:S(2)}) %collective-permute-start.21) | collective-permute-done | bytes 9504 | tf_op jit(solution)/shard_map/ppermute | solution.py:395
  134.0 2.6 %collective-permute-start.26 = (f32[1184,8]{0,1:T(8,128)S(1)}, f32[1184,8]{0,1:T(8,128)S(1)}, u32[]{:S(2)}, u32[]{:S(2)}) collective-permute-start(f32[1184,8]{0,1:T(8,128)S(1)} %reshape.200), channel_id=1, source_target_pairs={{0,16},{4,20},{8,24},{12,28},{16,0},{20,4},{24,8},{28,12},{1,17},{... | collective-permute-start | bytes 113672 | tf_op jit(solution)/shard_map/ppermute | solution.py:395
  140.0 2.5 %collective-permute-done.27 = f32[1184,8]{0,1:T(8,128)S(1)} collective-permute-done((f32[1184,8]{0,1:T(8,128)S(1)}, f32[1184,8]{0,1:T(8,128)S(1)}, u32[]{:S(2)}, u32[]{:S(2)}) %collective-permute-start.27) | collective-permute-done | bytes 37920 | tf_op jit(solution)/shard_map/ppermute | solution.py:395
  143.1 2.1 collective-permute-done.29
  148.0 18.2 %shard_map.106 = f32[296,12]{1,0:T(8,128)} custom-call(f32[1]{0:T(128)S(6)} %copy.234.wave_ref, f32[296,8]{1,0:T(8,128)} %copy.147.own_ref, f32[4,9472]{1,0:T(4,128)} %get-tuple-element.37.all_ref, f32[12,9472]{1,0:T(8,128)} %pad_maximum_fusion.2.vec_ref, f32[296,9472]{1,0:T(8,128)} %get-tuple-element.10.refs_0_, f32[296,9472]{1,0:T(8,128)} %get-tuple-element.11.refs_1_), custom_call_target="tpu_custom_call" | custom-call | flops 89718784 | bytes 23059584 | tf_op jit(solution)/shard_map/pallas_call | solution.py:374
  169.4 2.2 collective-permute-done.31
  173.2 2.0 collective-permute-start.34
  175.6 2.3 %collective-permute-start.36 = (f32[1184,8]{0,1:T(8,128)S(1)}, f32[1184,8]{0,1:T(8,128)S(1)}, u32[]{:S(2)}, u32[]{:S(2)}) collective-permute-start(f32[1184,8]{0,1:T(8,128)S(1)} %reshape.203), channel_id=1, source_target_pairs={{0,16},{4,20},{8,24},{12,28},{16,0},{20,4},{24,8},{28,12},{1,17},{... | collective-permute-start | bytes 113672 | tf_op jit(solution)/shard_map/ppermute | solution.py:395
  183.9 2.8 %collective-permute-done.39 = f32[1184,8]{0,1:T(8,128)S(1)} collective-permute-done((f32[1184,8]{0,1:T(8,128)S(1)}, f32[1184,8]{0,1:T(8,128)S(1)}, u32[]{:S(2)}, u32[]{:S(2)}) %collective-permute-start.39) | collective-permute-done | bytes 37920 | tf_op jit(solution)/shard_map/ppermute | solution.py:395
  190.8 18.2 %shard_map.107 = f32[296,12]{1,0:T(8,128)} custom-call(f32[1]{0:T(128)S(6)} %copy.234.wave_ref, f32[296,8]{1,0:T(8,128)} %copy.147.own_ref, f32[4,9472]{1,0:T(4,128)} %get-tuple-element.37.all_ref, f32[12,9472]{1,0:T(8,128)} %pad_maximum_fusion.3.vec_ref, f32[296,9472]{1,0:T(8,128)} %get-tuple-element.12.refs_0_, f32[296,9472]{1,0:T(8,128)} %get-tuple-element.13.refs_1_), custom_call_target="tpu_custom_call" | custom-call | flops 89718784 | bytes 23059584 | tf_op jit(solution)/shard_map/pallas_call | solution.py:374
  210.6 5.6 %psum.7 = f32[4,128]{1,0:T(4,128)S(1)} all-reduce(f32[4,128]{1,0:T(4,128)S(1)} %fusion.14), channel_id=1, replica_groups=mesh['row'=8,'col'=4] {'col'}, use_global_device_ids=true, to_apply=%region_13.16 | all-reduce | flops 512 | bytes 4096 | tf_op jit(solution)/shard_map/psum | solution.py:531
  221.9 2.2 collective-permute-start.45
  227.6 2.9 %collective-permute-done.46 = f32[1,4,128]{2,1,0:T(4,128)S(1)} collective-permute-done((f32[1,4,128]{2,1,0:T(4,128)S(1)}, f32[1,4,128]{2,1,0:T(4,128)S(1)}, u32[]{:S(2)}, u32[]{:S(2)}) %collective-permute-start.46) | collective-permute-done | bytes 2080 | tf_op jit(solution)/shard_map/ppermute | solution.py:395
  (249 shorter events, 63.9 us)
Async XLA Ops:
  2.0 7.9 %collective-permute-start = (f32[296,12]{0,1:T(8,128)S(1)}, f32[296,12]{0,1:T(8,128)S(1)}, u32[]{:S(2)}, u32[]{:S(2)}) collective-permute-start(f32[296,12]{0,1:T(8,128)S(1)} %pad_maximum_fusion.4), channel_id=1, source_target_pairs={{0,3},{1,0},{2,1},{3,2},{4,7},{5,4},{6,5},{7,6},{8,11},{9,8},{10,9... | collective-permute-start | bytes 42632 | tf_op jit(solution)/shard_map/ppermute | solution.py:395
  11.0 8.1 %collective-permute-start.3 = (f32[1184,12]{0,1:T(8,128)S(1)}, f32[1184,12]{0,1:T(8,128)S(1)}, u32[]{:S(2)}, u32[]{:S(2)}) collective-permute-start(f32[1184,12]{0,1:T(8,128)S(1)} %reshape.195), channel_id=1, source_target_pairs={{0,28},{4,0},{8,4},{12,8},{16,12},{20,16},{24,20},{28,24},{1,29},{... | collective-permute-start | bytes 170504 | tf_op jit(solution)/shard_map/ppermute | solution.py:395
  15.6 6.0 %collective-permute-start.4 = (f32[1184,12]{0,1:T(8,128)S(1)}, f32[1184,12]{0,1:T(8,128)S(1)}, u32[]{:S(2)}, u32[]{:S(2)}) collective-permute-start(f32[1184,12]{0,1:T(8,128)S(1)} %reshape.195), channel_id=1, source_target_pairs={{0,24},{4,28},{8,0},{12,4},{16,8},{20,12},{24,16},{28,20},{1,25},{... | collective-permute-start | bytes 170504 | tf_op jit(solution)/shard_map/ppermute | solution.py:395
  16.0 6.1 %collective-permute-start.5 = (f32[1184,12]{0,1:T(8,128)S(1)}, f32[1184,12]{0,1:T(8,128)S(1)}, u32[]{:S(2)}, u32[]{:S(2)}) collective-permute-start(f32[1184,12]{0,1:T(8,128)S(1)} %reshape.195), channel_id=1, source_target_pairs={{0,20},{4,24},{8,28},{12,0},{16,4},{20,8},{24,12},{28,16},{1,21},{... | collective-permute-start | bytes 170504 | tf_op jit(solution)/shard_map/ppermute | solution.py:395
  16.0 14.9 %collective-permute-start.6 = (f32[1184,12]{0,1:T(8,128)S(1)}, f32[1184,12]{0,1:T(8,128)S(1)}, u32[]{:S(2)}, u32[]{:S(2)}) collective-permute-start(f32[1184,12]{0,1:T(8,128)S(1)} %reshape.195), channel_id=1, source_target_pairs={{0,16},{4,20},{8,24},{12,28},{16,0},{20,4},{24,8},{28,12},{1,17},{... | collective-permute-start | bytes 170504 | tf_op jit(solution)/shard_map/ppermute | solution.py:395
  19.0 14.6 %collective-permute-start.7 = (f32[1184,12]{0,1:T(8,128)S(1)}, f32[1184,12]{0,1:T(8,128)S(1)}, u32[]{:S(2)}, u32[]{:S(2)}) collective-permute-start(f32[1184,12]{0,1:T(8,128)S(1)} %reshape.195), channel_id=1, source_target_pairs={{0,12},{4,16},{8,20},{12,24},{16,28},{20,0},{24,4},{28,8},{1,13},{... | collective-permute-start | bytes 170504 | tf_op jit(solution)/shard_map/ppermute | solution.py:395
  19.1 14.5 %collective-permute-start.8 = (f32[1184,12]{0,1:T(8,128)S(1)}, f32[1184,12]{0,1:T(8,128)S(1)}, u32[]{:S(2)}, u32[]{:S(2)}) collective-permute-start(f32[1184,12]{0,1:T(8,128)S(1)} %reshape.195), channel_id=1, source_target_pairs={{0,8},{4,12},{8,16},{12,20},{16,24},{20,28},{24,0},{28,4},{1,9},{5... | collective-permute-start | bytes 170504 | tf_op jit(solution)/shard_map/ppermute | solution.py:395
  21.6 12.0 %collective-permute-start.9 = (f32[1184,12]{0,1:T(8,128)S(1)}, f32[1184,12]{0,1:T(8,128)S(1)}, u32[]{:S(2)}, u32[]{:S(2)}) collective-permute-start(f32[1184,12]{0,1:T(8,128)S(1)} %reshape.195), channel_id=1, source_target_pairs={{0,4},{4,8},{8,12},{12,16},{16,20},{20,24},{24,28},{28,0},{1,5},{5... | collective-permute-start | bytes 170504 | tf_op jit(solution)/shard_map/ppermute | solution.py:395
  92.4 7.1 %collective-permute-start.14 = (f32[1184,8]{0,1:T(8,128)S(1)}, f32[1184,8]{0,1:T(8,128)S(1)}, u32[]{:S(2)}, u32[]{:S(2)}) collective-permute-start(f32[1184,8]{0,1:T(8,128)S(1)} %reshape.197), channel_id=1, source_target_pairs={{0,24},{4,28},{8,0},{12,4},{16,8},{20,12},{24,16},{28,20},{1,25},{... | collective-permute-start | bytes 113672 | tf_op jit(solution)/shard_map/ppermute | solution.py:395
  93.7 7.8 %collective-permute-start.15 = (f32[1184,8]{0,1:T(8,128)S(1)}, f32[1184,8]{0,1:T(8,128)S(1)}, u32[]{:S(2)}, u32[]{:S(2)}) collective-permute-start(f32[1184,8]{0,1:T(8,128)S(1)} %reshape.197), channel_id=1, source_target_pairs={{0,20},{4,24},{8,28},{12,0},{16,4},{20,8},{24,12},{28,16},{1,21},{... | collective-permute-start | bytes 113672 | tf_op jit(solution)/shard_map/ppermute | solution.py:395
  95.0 6.5 %collective-permute-start.16 = (f32[1184,8]{0,1:T(8,128)S(1)}, f32[1184,8]{0,1:T(8,128)S(1)}, u32[]{:S(2)}, u32[]{:S(2)}) collective-permute-start(f32[1184,8]{0,1:T(8,128)S(1)} %reshape.197), channel_id=1, source_target_pairs={{0,16},{4,20},{8,24},{12,28},{16,0},{20,4},{24,8},{28,12},{1,17},{... | collective-permute-start | bytes 113672 | tf_op jit(solution)/shard_map/ppermute | solution.py:395
  96.7 6.0 %collective-permute-start.17 = (f32[1184,8]{0,1:T(8,128)S(1)}, f32[1184,8]{0,1:T(8,128)S(1)}, u32[]{:S(2)}, u32[]{:S(2)}) collective-permute-start(f32[1184,8]{0,1:T(8,128)S(1)} %reshape.197), channel_id=1, source_target_pairs={{0,12},{4,16},{8,20},{12,24},{16,28},{20,0},{24,4},{28,8},{1,13},{... | collective-permute-start | bytes 113672 | tf_op jit(solution)/shard_map/ppermute | solution.py:395
  97.0 6.0 %collective-permute-start.18 = (f32[1184,8]{0,1:T(8,128)S(1)}, f32[1184,8]{0,1:T(8,128)S(1)}, u32[]{:S(2)}, u32[]{:S(2)}) collective-permute-start(f32[1184,8]{0,1:T(8,128)S(1)} %reshape.197), channel_id=1, source_target_pairs={{0,8},{4,12},{8,16},{12,20},{16,24},{20,28},{24,0},{28,4},{1,9},{5... | collective-permute-start | bytes 113672 | tf_op jit(solution)/shard_map/ppermute | solution.py:395
  99.5 6.7 %collective-permute-start.19 = (f32[1184,8]{0,1:T(8,128)S(1)}, f32[1184,8]{0,1:T(8,128)S(1)}, u32[]{:S(2)}, u32[]{:S(2)}) collective-permute-start(f32[1184,8]{0,1:T(8,128)S(1)} %reshape.197), channel_id=1, source_target_pairs={{0,4},{4,8},{8,12},{12,16},{16,20},{20,24},{24,28},{28,0},{1,5},{5... | collective-permute-start | bytes 113672 | tf_op jit(solution)/shard_map/ppermute | solution.py:395
  133.9 6.1 %collective-permute-start.25 = (f32[1184,8]{0,1:T(8,128)S(1)}, f32[1184,8]{0,1:T(8,128)S(1)}, u32[]{:S(2)}, u32[]{:S(2)}) collective-permute-start(f32[1184,8]{0,1:T(8,128)S(1)} %reshape.200), channel_id=1, source_target_pairs={{0,20},{4,24},{8,28},{12,0},{16,4},{20,8},{24,12},{28,16},{1,21},{... | collective-permute-start | bytes 113672 | tf_op jit(solution)/shard_map/ppermute | solution.py:395
  137.1 6.0 %collective-permute-start.28 = (f32[1184,8]{0,1:T(8,128)S(1)}, f32[1184,8]{0,1:T(8,128)S(1)}, u32[]{:S(2)}, u32[]{:S(2)}) collective-permute-start(f32[1184,8]{0,1:T(8,128)S(1)} %reshape.200), channel_id=1, source_target_pairs={{0,8},{4,12},{8,16},{12,20},{16,24},{20,28},{24,0},{28,4},{1,9},{5... | collective-permute-start | bytes 113672 | tf_op jit(solution)/shard_map/ppermute | solution.py:395
  138.5 6.7 %collective-permute-start.29 = (f32[1184,8]{0,1:T(8,128)S(1)}, f32[1184,8]{0,1:T(8,128)S(1)}, u32[]{:S(2)}, u32[]{:S(2)}) collective-permute-start(f32[1184,8]{0,1:T(8,128)S(1)} %reshape.200), channel_id=1, source_target_pairs={{0,4},{4,8},{8,12},{12,16},{16,20},{20,24},{24,28},{28,0},{1,5},{5... | collective-permute-start | bytes 113672 | tf_op jit(solution)/shard_map/ppermute | solution.py:395
  173.2 6.7 %collective-permute-start.34 = (f32[1184,8]{0,1:T(8,128)S(1)}, f32[1184,8]{0,1:T(8,128)S(1)}, u32[]{:S(2)}, u32[]{:S(2)}) collective-permute-start(f32[1184,8]{0,1:T(8,128)S(1)} %reshape.203), channel_id=1, source_target_pairs={{0,24},{4,28},{8,0},{12,4},{16,8},{20,12},{24,16},{28,20},{1,25},{... | collective-permute-start | bytes 113672 | tf_op jit(solution)/shard_map/ppermute | solution.py:395
  175.2 6.6 %collective-permute-start.35 = (f32[1184,8]{0,1:T(8,128)S(1)}, f32[1184,8]{0,1:T(8,128)S(1)}, u32[]{:S(2)}, u32[]{:S(2)}) collective-permute-start(f32[1184,8]{0,1:T(8,128)S(1)} %reshape.203), channel_id=1, source_target_pairs={{0,20},{4,24},{8,28},{12,0},{16,4},{20,8},{24,12},{28,16},{1,21},{... | collective-permute-start | bytes 113672 | tf_op jit(solution)/shard_map/ppermute | solution.py:395
  175.6 6.4 %collective-permute-start.36 = (f32[1184,8]{0,1:T(8,128)S(1)}, f32[1184,8]{0,1:T(8,128)S(1)}, u32[]{:S(2)}, u32[]{:S(2)}) collective-permute-start(f32[1184,8]{0,1:T(8,128)S(1)} %reshape.203), channel_id=1, source_target_pairs={{0,16},{4,20},{8,24},{12,28},{16,0},{20,4},{24,8},{28,12},{1,17},{... | collective-permute-start | bytes 113672 | tf_op jit(solution)/shard_map/ppermute | solution.py:395
  179.8 6.9 %collective-permute-start.39 = (f32[1184,8]{0,1:T(8,128)S(1)}, f32[1184,8]{0,1:T(8,128)S(1)}, u32[]{:S(2)}, u32[]{:S(2)}) collective-permute-start(f32[1184,8]{0,1:T(8,128)S(1)} %reshape.203), channel_id=1, source_target_pairs={{0,4},{4,8},{8,12},{12,16},{16,20},{20,24},{24,28},{28,0},{1,5},{5... | collective-permute-start | bytes 113672 | tf_op jit(solution)/shard_map/ppermute | solution.py:395
  217.1 7.1 %collective-permute-start.41 = (f32[1,4,128]{2,1,0:T(4,128)S(1)}, f32[1,4,128]{2,1,0:T(4,128)S(1)}, u32[]{:S(2)}, u32[]{:S(2)}) collective-permute-start(f32[1,4,128]{2,1,0:T(4,128)S(1)} %bitcast.177), channel_id=1, source_target_pairs={{0,24},{4,28},{8,0},{12,4},{16,8},{20,12},{24,16},{28,20},{1,25},{... | collective-permute-start | bytes 6152 | tf_op jit(solution)/shard_map/ppermute | solution.py:395
  218.8 6.4 %collective-permute-start.42 = (f32[1,4,128]{2,1,0:T(4,128)S(1)}, f32[1,4,128]{2,1,0:T(4,128)S(1)}, u32[]{:S(2)}, u32[]{:S(2)}) collective-permute-start(f32[1,4,128]{2,1,0:T(4,128)S(1)} %bitcast.178), channel_id=1, source_target_pairs={{0,20},{4,24},{8,28},{12,0},{16,4},{20,8},{24,12},{28,16},{1,21},{... | collective-permute-start | bytes 6152 | tf_op jit(solution)/shard_map/ppermute | solution.py:395
  224.1 6.3 %collective-permute-start.46 = (f32[1,4,128]{2,1,0:T(4,128)S(1)}, f32[1,4,128]{2,1,0:T(4,128)S(1)}, u32[]{:S(2)}, u32[]{:S(2)}) collective-permute-start(f32[1,4,128]{2,1,0:T(4,128)S(1)} %bitcast.182), channel_id=1, source_target_pairs={{0,4},{4,8},{8,12},{12,16},{16,20},{20,24},{24,28},{28,0},{1,5},{5... | collective-permute-start | bytes 6152 | tf_op jit(solution)/shard_map/ppermute | solution.py:395
  (27 other events, 125.2 us)

commit v14 on v13

--- a/solution.py
+++ b/solution.py
@@ -293,7 +293,7 @@
 
         columns = vec_ref.shape[0]
         zeros = tuple(jnp.zeros((8, width), jnp.float32) for _ in range(columns))
-        sums = lax.fori_loop(0, chunk_count, lane_block, zeros, unroll=6 if stored_in or store_out else 3)
+        sums = lax.fori_loop(0, chunk_count, lane_block, zeros, unroll=9 if stored_in else (6 if store_out else 3))
         lane = lax.broadcasted_iota(jnp.int32, (8, columns), 1)
         result = jnp.zeros((8, columns), jnp.float32)
         for column in range(columns):

time: 232 us -> 230 us (level)
  no operation moved by 1% of the time
where the time goes in v14:
time: 230 us; the launch traced here: 229 us
  Pallas kernels  102 us (44%)
  starting transfers between devices  52.3 us (23%)
  waiting for transfers between devices  41.2 us (18%)
  other arithmetic  15.6 us (7%)
  local copies, waits for them, and re-layouts  8.48 us (4%)
  blocking collectives  5.65 us (2%)
    pallas_call x4, Pallas kernels, panel_call(): pl.pallas_call(functools.partial(panel_kernel, slope_mode, stored_in, sto...  102 us
    ppermute x47, starting transfers between devices, gather_axis(): lax.ppermute(vector, name, [(i, (i + shift) % count) for i in range(count)])  52.3 us
    ppermute x47, waiting for transfers between devices, gather_axis(): lax.ppermute(vector, name, [(i, (i + shift) % count) for i in range(count)])  41.2 us
    psum x1, blocking collectives, local(): lax.psum(local_sums, 'col')[None]  5.65 us
  transfers between devices with their start and end apart: 47, of which 23 were waited for; matrix products, arithmetic and copies ran while one was open for 2% of the time, Pallas kernels for 0%

profile of v14, /device:TPU:0, one launch (start us, length us, event | category | flops | bytes accessed | tf_op | source)
XLA Modules:
  0.0 229.0 jit_solution(16628884018329536934)
XLA Ops:
  2.0 2.5 %collective-permute-start = (f32[296,12]{0,1:T(8,128)S(1)}, f32[296,12]{0,1:T(8,128)S(1)}, u32[]{:S(2)}, u32[]{:S(2)}) collective-permute-start(f32[296,12]{0,1:T(8,128)S(1)} %pad_maximum_fusion.4), channel_id=1, source_target_pairs={{0,3},{1,0},{2,1},{3,2},{4,7},{5,4},{6,5},{7,6},{8,11},{9,8},{10,9... | collective-permute-start | bytes 42632 | tf_op jit(solution)/shard_map/ppermute | solution.py:395
  11.0 4.6 %collective-permute-start.3 = (f32[1184,12]{0,1:T(8,128)S(1)}, f32[1184,12]{0,1:T(8,128)S(1)}, u32[]{:S(2)}, u32[]{:S(2)}) collective-permute-start(f32[1184,12]{0,1:T(8,128)S(1)} %reshape.195), channel_id=1, source_target_pairs={{0,28},{4,0},{8,4},{12,8},{16,12},{20,16},{24,20},{28,24},{1,29},{... | collective-permute-start | bytes 170504 | tf_op jit(solution)/shard_map/ppermute | solution.py:395
  16.0 3.0 %collective-permute-start.6 = (f32[1184,12]{0,1:T(8,128)S(1)}, f32[1184,12]{0,1:T(8,128)S(1)}, u32[]{:S(2)}, u32[]{:S(2)}) collective-permute-start(f32[1184,12]{0,1:T(8,128)S(1)} %reshape.195), channel_id=1, source_target_pairs={{0,16},{4,20},{8,24},{12,28},{16,0},{20,4},{24,8},{28,12},{1,17},{... | collective-permute-start | bytes 170504 | tf_op jit(solution)/shard_map/ppermute | solution.py:395
  22.2 8.8 %collective-permute-done.6 = f32[1184,12]{0,1:T(8,128)S(1)} collective-permute-done((f32[1184,12]{0,1:T(8,128)S(1)}, f32[1184,12]{0,1:T(8,128)S(1)}, u32[]{:S(2)}, u32[]{:S(2)}) %collective-permute-start.6) | collective-permute-done | bytes 56864 | tf_op jit(solution)/shard_map/ppermute | solution.py:395
  31.0 2.6 %collective-permute-done.7 = f32[1184,12]{0,1:T(8,128)S(1)} collective-permute-done((f32[1184,12]{0,1:T(8,128)S(1)}, f32[1184,12]{0,1:T(8,128)S(1)}, u32[]{:S(2)}, u32[]{:S(2)}) %collective-permute-start.7) | collective-permute-done | bytes 56864 | tf_op jit(solution)/shard_map/ppermute | solution.py:395
  36.0 49.6 %shard_map.104 = (f32[296,12]{1,0:T(8,128)}, f32[296,9472]{1,0:T(8,128)}, f32[296,9472]{1,0:T(8,128)}, f32[296,9472]{1,0:T(8,128)}, f32[296,9472]{1,0:T(8,128)}) custom-call(f32[1]{0:T(128)S(6)} %copy.234.wave_ref, f32[296,8]{1,0:T(8,128)} %copy.147.own_ref, f32[4,9472]{1,0:T(4,128)} %get-tuple-element.37.all_ref, f32[12,9472]{1,0:T(8,128)} %pad_maximum_fusion.vec_ref), custom_call_target="tpu_custom_call" | custom-call | flops 420556800 | bytes 45489280 | tf_op jit(solution)/shard_map/pallas_call | solution.py:374
  88.9 2.2 collective-permute-done.11
  97.0 2.4 %collective-permute-start.18 = (f32[1184,8]{0,1:T(8,128)S(1)}, f32[1184,8]{0,1:T(8,128)S(1)}, u32[]{:S(2)}, u32[]{:S(2)}) collective-permute-start(f32[1184,8]{0,1:T(8,128)S(1)} %reshape.197), channel_id=1, source_target_pairs={{0,8},{4,12},{8,16},{12,20},{16,24},{20,28},{24,0},{28,4},{1,9},{5... | collective-permute-start | bytes 113672 | tf_op jit(solution)/shard_map/ppermute | solution.py:395
  99.5 2.0 collective-permute-start.19
  103.0 3.2 %collective-permute-done.19 = f32[1184,8]{0,1:T(8,128)S(1)} collective-permute-done((f32[1184,8]{0,1:T(8,128)S(1)}, f32[1184,8]{0,1:T(8,128)S(1)}, u32[]{:S(2)}, u32[]{:S(2)}) %collective-permute-start.19) | collective-permute-done | bytes 37920 | tf_op jit(solution)/shard_map/ppermute | solution.py:395
  108.1 17.5 %shard_map.105 = f32[296,12]{1,0:T(8,128)} custom-call(f32[1]{0:T(128)S(6)} %copy.234.wave_ref, f32[296,8]{1,0:T(8,128)} %copy.147.own_ref, f32[4,9472]{1,0:T(4,128)} %get-tuple-element.37.all_ref, f32[12,9472]{1,0:T(8,128)} %pad_maximum_fusion.1.vec_ref, f32[296,9472]{1,0:T(8,128)} %get-tuple-element.10.refs_0_, f32[296,9472]{1,0:T(8,128)} %get-tuple-element.11.refs_1_), custom_call_target="tpu_custom_call" | custom-call | flops 89718784 | bytes 23059584 | tf_op jit(solution)/shard_map/pallas_call | solution.py:374
  128.5 2.4 %collective-permute-done.21 = f32[296,8]{0,1:T(8,128)S(1)} collective-permute-done((f32[296,8]{0,1:T(8,128)S(1)}, f32[296,8]{0,1:T(8,128)S(1)}, u32[]{:S(2)}, u32[]{:S(2)}) %collective-permute-start.21) | collective-permute-done | bytes 9504 | tf_op jit(solution)/shard_map/ppermute | solution.py:395
  133.3 2.6 %collective-permute-start.26 = (f32[1184,8]{0,1:T(8,128)S(1)}, f32[1184,8]{0,1:T(8,128)S(1)}, u32[]{:S(2)}, u32[]{:S(2)}) collective-permute-start(f32[1184,8]{0,1:T(8,128)S(1)} %reshape.200), channel_id=1, source_target_pairs={{0,16},{4,20},{8,24},{12,28},{16,0},{20,4},{24,8},{28,12},{1,17},{... | collective-permute-start | bytes 113672 | tf_op jit(solution)/shard_map/ppermute | solution.py:395
  139.2 2.5 %collective-permute-done.27 = f32[1184,8]{0,1:T(8,128)S(1)} collective-permute-done((f32[1184,8]{0,1:T(8,128)S(1)}, f32[1184,8]{0,1:T(8,128)S(1)}, u32[]{:S(2)}, u32[]{:S(2)}) %collective-permute-start.27) | collective-permute-done | bytes 37920 | tf_op jit(solution)/shard_map/ppermute | solution.py:395
  142.4 2.1 collective-permute-done.29
  147.3 17.5 %shard_map.106 = f32[296,12]{1,0:T(8,128)} custom-call(f32[1]{0:T(128)S(6)} %copy.234.wave_ref, f32[296,8]{1,0:T(8,128)} %copy.147.own_ref, f32[4,9472]{1,0:T(4,128)} %get-tuple-element.37.all_ref, f32[12,9472]{1,0:T(8,128)} %pad_maximum_fusion.2.vec_ref, f32[296,9472]{1,0:T(8,128)} %get-tuple-element.10.refs_0_, f32[296,9472]{1,0:T(8,128)} %get-tuple-element.11.refs_1_), custom_call_target="tpu_custom_call" | custom-call | flops 89718784 | bytes 23059584 | tf_op jit(solution)/shard_map/pallas_call | solution.py:374
  167.9 2.2 collective-permute-done.31
  171.7 2.0 collective-permute-start.34
  174.2 2.3 %collective-permute-start.36 = (f32[1184,8]{0,1:T(8,128)S(1)}, f32[1184,8]{0,1:T(8,128)S(1)}, u32[]{:S(2)}, u32[]{:S(2)}) collective-permute-start(f32[1184,8]{0,1:T(8,128)S(1)} %reshape.203), channel_id=1, source_target_pairs={{0,16},{4,20},{8,24},{12,28},{16,0},{20,4},{24,8},{28,12},{1,17},{... | collective-permute-start | bytes 113672 | tf_op jit(solution)/shard_map/ppermute | solution.py:395
  182.5 2.8 %collective-permute-done.39 = f32[1184,8]{0,1:T(8,128)S(1)} collective-permute-done((f32[1184,8]{0,1:T(8,128)S(1)}, f32[1184,8]{0,1:T(8,128)S(1)}, u32[]{:S(2)}, u32[]{:S(2)}) %collective-permute-start.39) | collective-permute-done | bytes 37920 | tf_op jit(solution)/shard_map/ppermute | solution.py:395
  189.4 17.5 %shard_map.107 = f32[296,12]{1,0:T(8,128)} custom-call(f32[1]{0:T(128)S(6)} %copy.234.wave_ref, f32[296,8]{1,0:T(8,128)} %copy.147.own_ref, f32[4,9472]{1,0:T(4,128)} %get-tuple-element.37.all_ref, f32[12,9472]{1,0:T(8,128)} %pad_maximum_fusion.3.vec_ref, f32[296,9472]{1,0:T(8,128)} %get-tuple-element.12.refs_0_, f32[296,9472]{1,0:T(8,128)} %get-tuple-element.13.refs_1_), custom_call_target="tpu_custom_call" | custom-call | flops 89718784 | bytes 23059584 | tf_op jit(solution)/shard_map/pallas_call | solution.py:374
  208.5 5.6 %psum.7 = f32[4,128]{1,0:T(4,128)S(1)} all-reduce(f32[4,128]{1,0:T(4,128)S(1)} %fusion.14), channel_id=1, replica_groups=mesh['row'=8,'col'=4] {'col'}, use_global_device_ids=true, to_apply=%region_13.16 | all-reduce | flops 512 | bytes 4096 | tf_op jit(solution)/shard_map/psum | solution.py:531
  219.8 2.2 collective-permute-start.45
  225.4 2.9 %collective-permute-done.46 = f32[1,4,128]{2,1,0:T(4,128)S(1)} collective-permute-done((f32[1,4,128]{2,1,0:T(4,128)S(1)}, f32[1,4,128]{2,1,0:T(4,128)S(1)}, u32[]{:S(2)}, u32[]{:S(2)}) %collective-permute-start.46) | collective-permute-done | bytes 2080 | tf_op jit(solution)/shard_map/ppermute | solution.py:395
  (249 shorter events, 63.9 us)
Async XLA Ops:
  2.0 7.9 %collective-permute-start = (f32[296,12]{0,1:T(8,128)S(1)}, f32[296,12]{0,1:T(8,128)S(1)}, u32[]{:S(2)}, u32[]{:S(2)}) collective-permute-start(f32[296,12]{0,1:T(8,128)S(1)} %pad_maximum_fusion.4), channel_id=1, source_target_pairs={{0,3},{1,0},{2,1},{3,2},{4,7},{5,4},{6,5},{7,6},{8,11},{9,8},{10,9... | collective-permute-start | bytes 42632 | tf_op jit(solution)/shard_map/ppermute | solution.py:395
  11.0 8.1 %collective-permute-start.3 = (f32[1184,12]{0,1:T(8,128)S(1)}, f32[1184,12]{0,1:T(8,128)S(1)}, u32[]{:S(2)}, u32[]{:S(2)}) collective-permute-start(f32[1184,12]{0,1:T(8,128)S(1)} %reshape.195), channel_id=1, source_target_pairs={{0,28},{4,0},{8,4},{12,8},{16,12},{20,16},{24,20},{28,24},{1,29},{... | collective-permute-start | bytes 170504 | tf_op jit(solution)/shard_map/ppermute | solution.py:395
  15.6 6.0 %collective-permute-start.4 = (f32[1184,12]{0,1:T(8,128)S(1)}, f32[1184,12]{0,1:T(8,128)S(1)}, u32[]{:S(2)}, u32[]{:S(2)}) collective-permute-start(f32[1184,12]{0,1:T(8,128)S(1)} %reshape.195), channel_id=1, source_target_pairs={{0,24},{4,28},{8,0},{12,4},{16,8},{20,12},{24,16},{28,20},{1,25},{... | collective-permute-start | bytes 170504 | tf_op jit(solution)/shard_map/ppermute | solution.py:395
  16.0 6.1 %collective-permute-start.5 = (f32[1184,12]{0,1:T(8,128)S(1)}, f32[1184,12]{0,1:T(8,128)S(1)}, u32[]{:S(2)}, u32[]{:S(2)}) collective-permute-start(f32[1184,12]{0,1:T(8,128)S(1)} %reshape.195), channel_id=1, source_target_pairs={{0,20},{4,24},{8,28},{12,0},{16,4},{20,8},{24,12},{28,16},{1,21},{... | collective-permute-start | bytes 170504 | tf_op jit(solution)/shard_map/ppermute | solution.py:395
  16.0 14.9 %collective-permute-start.6 = (f32[1184,12]{0,1:T(8,128)S(1)}, f32[1184,12]{0,1:T(8,128)S(1)}, u32[]{:S(2)}, u32[]{:S(2)}) collective-permute-start(f32[1184,12]{0,1:T(8,128)S(1)} %reshape.195), channel_id=1, source_target_pairs={{0,16},{4,20},{8,24},{12,28},{16,0},{20,4},{24,8},{28,12},{1,17},{... | collective-permute-start | bytes 170504 | tf_op jit(solution)/shard_map/ppermute | solution.py:395
  19.0 14.6 %collective-permute-start.7 = (f32[1184,12]{0,1:T(8,128)S(1)}, f32[1184,12]{0,1:T(8,128)S(1)}, u32[]{:S(2)}, u32[]{:S(2)}) collective-permute-start(f32[1184,12]{0,1:T(8,128)S(1)} %reshape.195), channel_id=1, source_target_pairs={{0,12},{4,16},{8,20},{12,24},{16,28},{20,0},{24,4},{28,8},{1,13},{... | collective-permute-start | bytes 170504 | tf_op jit(solution)/shard_map/ppermute | solution.py:395
  19.1 14.5 %collective-permute-start.8 = (f32[1184,12]{0,1:T(8,128)S(1)}, f32[1184,12]{0,1:T(8,128)S(1)}, u32[]{:S(2)}, u32[]{:S(2)}) collective-permute-start(f32[1184,12]{0,1:T(8,128)S(1)} %reshape.195), channel_id=1, source_target_pairs={{0,8},{4,12},{8,16},{12,20},{16,24},{20,28},{24,0},{28,4},{1,9},{5... | collective-permute-start | bytes 170504 | tf_op jit(solution)/shard_map/ppermute | solution.py:395
  21.6 12.0 %collective-permute-start.9 = (f32[1184,12]{0,1:T(8,128)S(1)}, f32[1184,12]{0,1:T(8,128)S(1)}, u32[]{:S(2)}, u32[]{:S(2)}) collective-permute-start(f32[1184,12]{0,1:T(8,128)S(1)} %reshape.195), channel_id=1, source_target_pairs={{0,4},{4,8},{8,12},{12,16},{16,20},{20,24},{24,28},{28,0},{1,5},{5... | collective-permute-start | bytes 170504 | tf_op jit(solution)/shard_map/ppermute | solution.py:395
  92.4 7.1 %collective-permute-start.14 = (f32[1184,8]{0,1:T(8,128)S(1)}, f32[1184,8]{0,1:T(8,128)S(1)}, u32[]{:S(2)}, u32[]{:S(2)}) collective-permute-start(f32[1184,8]{0,1:T(8,128)S(1)} %reshape.197), channel_id=1, source_target_pairs={{0,24},{4,28},{8,0},{12,4},{16,8},{20,12},{24,16},{28,20},{1,25},{... | collective-permute-start | bytes 113672 | tf_op jit(solution)/shard_map/ppermute | solution.py:395
  93.7 7.8 %collective-permute-start.15 = (f32[1184,8]{0,1:T(8,128)S(1)}, f32[1184,8]{0,1:T(8,128)S(1)}, u32[]{:S(2)}, u32[]{:S(2)}) collective-permute-start(f32[1184,8]{0,1:T(8,128)S(1)} %reshape.197), channel_id=1, source_target_pairs={{0,20},{4,24},{8,28},{12,0},{16,4},{20,8},{24,12},{28,16},{1,21},{... | collective-permute-start | bytes 113672 | tf_op jit(solution)/shard_map/ppermute | solution.py:395
  95.0 6.5 %collective-permute-start.16 = (f32[1184,8]{0,1:T(8,128)S(1)}, f32[1184,8]{0,1:T(8,128)S(1)}, u32[]{:S(2)}, u32[]{:S(2)}) collective-permute-start(f32[1184,8]{0,1:T(8,128)S(1)} %reshape.197), channel_id=1, source_target_pairs={{0,16},{4,20},{8,24},{12,28},{16,0},{20,4},{24,8},{28,12},{1,17},{... | collective-permute-start | bytes 113672 | tf_op jit(solution)/shard_map/ppermute | solution.py:395
  96.7 6.0 %collective-permute-start.17 = (f32[1184,8]{0,1:T(8,128)S(1)}, f32[1184,8]{0,1:T(8,128)S(1)}, u32[]{:S(2)}, u32[]{:S(2)}) collective-permute-start(f32[1184,8]{0,1:T(8,128)S(1)} %reshape.197), channel_id=1, source_target_pairs={{0,12},{4,16},{8,20},{12,24},{16,28},{20,0},{24,4},{28,8},{1,13},{... | collective-permute-start | bytes 113672 | tf_op jit(solution)/shard_map/ppermute | solution.py:395
  97.0 6.0 %collective-permute-start.18 = (f32[1184,8]{0,1:T(8,128)S(1)}, f32[1184,8]{0,1:T(8,128)S(1)}, u32[]{:S(2)}, u32[]{:S(2)}) collective-permute-start(f32[1184,8]{0,1:T(8,128)S(1)} %reshape.197), channel_id=1, source_target_pairs={{0,8},{4,12},{8,16},{12,20},{16,24},{20,28},{24,0},{28,4},{1,9},{5... | collective-permute-start | bytes 113672 | tf_op jit(solution)/shard_map/ppermute | solution.py:395
  99.5 6.7 %collective-permute-start.19 = (f32[1184,8]{0,1:T(8,128)S(1)}, f32[1184,8]{0,1:T(8,128)S(1)}, u32[]{:S(2)}, u32[]{:S(2)}) collective-permute-start(f32[1184,8]{0,1:T(8,128)S(1)} %reshape.197), channel_id=1, source_target_pairs={{0,4},{4,8},{8,12},{12,16},{16,20},{20,24},{24,28},{28,0},{1,5},{5... | collective-permute-start | bytes 113672 | tf_op jit(solution)/shard_map/ppermute | solution.py:395
  133.2 6.1 %collective-permute-start.25 = (f32[1184,8]{0,1:T(8,128)S(1)}, f32[1184,8]{0,1:T(8,128)S(1)}, u32[]{:S(2)}, u32[]{:S(2)}) collective-permute-start(f32[1184,8]{0,1:T(8,128)S(1)} %reshape.200), channel_id=1, source_target_pairs={{0,20},{4,24},{8,28},{12,0},{16,4},{20,8},{24,12},{28,16},{1,21},{... | collective-permute-start | bytes 113672 | tf_op jit(solution)/shard_map/ppermute | solution.py:395
  136.4 6.0 %collective-permute-start.28 = (f32[1184,8]{0,1:T(8,128)S(1)}, f32[1184,8]{0,1:T(8,128)S(1)}, u32[]{:S(2)}, u32[]{:S(2)}) collective-permute-start(f32[1184,8]{0,1:T(8,128)S(1)} %reshape.200), channel_id=1, source_target_pairs={{0,8},{4,12},{8,16},{12,20},{16,24},{20,28},{24,0},{28,4},{1,9},{5... | collective-permute-start | bytes 113672 | tf_op jit(solution)/shard_map/ppermute | solution.py:395
  137.7 6.7 %collective-permute-start.29 = (f32[1184,8]{0,1:T(8,128)S(1)}, f32[1184,8]{0,1:T(8,128)S(1)}, u32[]{:S(2)}, u32[]{:S(2)}) collective-permute-start(f32[1184,8]{0,1:T(8,128)S(1)} %reshape.200), channel_id=1, source_target_pairs={{0,4},{4,8},{8,12},{12,16},{16,20},{20,24},{24,28},{28,0},{1,5},{5... | collective-permute-start | bytes 113672 | tf_op jit(solution)/shard_map/ppermute | solution.py:395
  171.7 6.7 %collective-permute-start.34 = (f32[1184,8]{0,1:T(8,128)S(1)}, f32[1184,8]{0,1:T(8,128)S(1)}, u32[]{:S(2)}, u32[]{:S(2)}) collective-permute-start(f32[1184,8]{0,1:T(8,128)S(1)} %reshape.203), channel_id=1, source_target_pairs={{0,24},{4,28},{8,0},{12,4},{16,8},{20,12},{24,16},{28,20},{1,25},{... | collective-permute-start | bytes 113672 | tf_op jit(solution)/shard_map/ppermute | solution.py:395
  173.7 6.6 %collective-permute-start.35 = (f32[1184,8]{0,1:T(8,128)S(1)}, f32[1184,8]{0,1:T(8,128)S(1)}, u32[]{:S(2)}, u32[]{:S(2)}) collective-permute-start(f32[1184,8]{0,1:T(8,128)S(1)} %reshape.203), channel_id=1, source_target_pairs={{0,20},{4,24},{8,28},{12,0},{16,4},{20,8},{24,12},{28,16},{1,21},{... | collective-permute-start | bytes 113672 | tf_op jit(solution)/shard_map/ppermute | solution.py:395
  174.2 6.4 %collective-permute-start.36 = (f32[1184,8]{0,1:T(8,128)S(1)}, f32[1184,8]{0,1:T(8,128)S(1)}, u32[]{:S(2)}, u32[]{:S(2)}) collective-permute-start(f32[1184,8]{0,1:T(8,128)S(1)} %reshape.203), channel_id=1, source_target_pairs={{0,16},{4,20},{8,24},{12,28},{16,0},{20,4},{24,8},{28,12},{1,17},{... | collective-permute-start | bytes 113672 | tf_op jit(solution)/shard_map/ppermute | solution.py:395
  178.4 6.9 %collective-permute-start.39 = (f32[1184,8]{0,1:T(8,128)S(1)}, f32[1184,8]{0,1:T(8,128)S(1)}, u32[]{:S(2)}, u32[]{:S(2)}) collective-permute-start(f32[1184,8]{0,1:T(8,128)S(1)} %reshape.203), channel_id=1, source_target_pairs={{0,4},{4,8},{8,12},{12,16},{16,20},{20,24},{24,28},{28,0},{1,5},{5... | collective-permute-start | bytes 113672 | tf_op jit(solution)/shard_map/ppermute | solution.py:395
  214.9 7.1 %collective-permute-start.41 = (f32[1,4,128]{2,1,0:T(4,128)S(1)}, f32[1,4,128]{2,1,0:T(4,128)S(1)}, u32[]{:S(2)}, u32[]{:S(2)}) collective-permute-start(f32[1,4,128]{2,1,0:T(4,128)S(1)} %bitcast.177), channel_id=1, source_target_pairs={{0,24},{4,28},{8,0},{12,4},{16,8},{20,12},{24,16},{28,20},{1,25},{... | collective-permute-start | bytes 6152 | tf_op jit(solution)/shard_map/ppermute | solution.py:395
  216.7 6.4 %collective-permute-start.42 = (f32[1,4,128]{2,1,0:T(4,128)S(1)}, f32[1,4,128]{2,1,0:T(4,128)S(1)}, u32[]{:S(2)}, u32[]{:S(2)}) collective-permute-start(f32[1,4,128]{2,1,0:T(4,128)S(1)} %bitcast.178), channel_id=1, source_target_pairs={{0,20},{4,24},{8,28},{12,0},{16,4},{20,8},{24,12},{28,16},{1,21},{... | collective-permute-start | bytes 6152 | tf_op jit(solution)/shard_map/ppermute | solution.py:395
  222.0 6.3 %collective-permute-start.46 = (f32[1,4,128]{2,1,0:T(4,128)S(1)}, f32[1,4,128]{2,1,0:T(4,128)S(1)}, u32[]{:S(2)}, u32[]{:S(2)}) collective-permute-start(f32[1,4,128]{2,1,0:T(4,128)S(1)} %bitcast.182), channel_id=1, source_target_pairs={{0,4},{4,8},{8,12},{12,16},{16,20},{20,24},{24,28},{28,0},{1,5},{5... | collective-permute-start | bytes 6152 | tf_op jit(solution)/shard_map/ppermute | solution.py:395
  (27 other events, 124.5 us)

commit v15 on v14

--- a/solution.py
+++ b/solution.py
@@ -293,7 +293,7 @@
 
         columns = vec_ref.shape[0]
         zeros = tuple(jnp.zeros((8, width), jnp.float32) for _ in range(columns))
-        sums = lax.fori_loop(0, chunk_count, lane_block, zeros, unroll=9 if stored_in else (6 if store_out else 3))
+        sums = lax.fori_loop(0, chunk_count, lane_block, zeros, unroll=12 if stored_in else (6 if store_out else 3))
         lane = lax.broadcasted_iota(jnp.int32, (8, columns), 1)
         result = jnp.zeros((8, columns), jnp.float32)
         for column in range(columns):

time: 230 us -> 229 us (level)
  no operation moved by 1% of the time
where the time goes in v15:
time: 229 us
  Pallas kernels  102 us (45%)
  starting transfers between devices  52.3 us (23%)
  waiting for transfers between devices  41.2 us (18%)
  other arithmetic  15.6 us (7%)
  local copies, waits for them, and re-layouts  8.48 us (4%)
  blocking collectives  5.65 us (2%)
    pallas_call x4, Pallas kernels, panel_call(): pl.pallas_call(functools.partial(panel_kernel, slope_mode, stored_in, sto...  102 us
    ppermute x47, starting transfers between devices, gather_axis(): lax.ppermute(vector, name, [(i, (i + shift) % count) for i in range(count)])  52.3 us
    ppermute x47, waiting for transfers between devices, gather_axis(): lax.ppermute(vector, name, [(i, (i + shift) % count) for i in range(count)])  41.2 us
    psum x1, blocking collectives, local(): lax.psum(local_sums, 'col')[None]  5.65 us
  transfers between devices with their start and end apart: 47, of which 23 were waited for; matrix products, arithmetic and copies ran while one was open for 2% of the time, Pallas kernels for 0%

profile of v15, /device:TPU:0, one launch (start us, length us, event | category | flops | bytes accessed | tf_op | source)
XLA Modules:
  0.0 228.6 jit_solution(115137733731087314)
XLA Ops:
  2.0 2.5 %collective-permute-start = (f32[296,12]{0,1:T(8,128)S(1)}, f32[296,12]{0,1:T(8,128)S(1)}, u32[]{:S(2)}, u32[]{:S(2)}) collective-permute-start(f32[296,12]{0,1:T(8,128)S(1)} %pad_maximum_fusion.4), channel_id=1, source_target_pairs={{0,3},{1,0},{2,1},{3,2},{4,7},{5,4},{6,5},{7,6},{8,11},{9,8},{10,9... | collective-permute-start | bytes 42632 | tf_op jit(solution)/shard_map/ppermute | solution.py:395
  11.0 4.6 %collective-permute-start.3 = (f32[1184,12]{0,1:T(8,128)S(1)}, f32[1184,12]{0,1:T(8,128)S(1)}, u32[]{:S(2)}, u32[]{:S(2)}) collective-permute-start(f32[1184,12]{0,1:T(8,128)S(1)} %reshape.195), channel_id=1, source_target_pairs={{0,28},{4,0},{8,4},{12,8},{16,12},{20,16},{24,20},{28,24},{1,29},{... | collective-permute-start | bytes 170504 | tf_op jit(solution)/shard_map/ppermute | solution.py:395
  16.0 3.0 %collective-permute-start.6 = (f32[1184,12]{0,1:T(8,128)S(1)}, f32[1184,12]{0,1:T(8,128)S(1)}, u32[]{:S(2)}, u32[]{:S(2)}) collective-permute-start(f32[1184,12]{0,1:T(8,128)S(1)} %reshape.195), channel_id=1, source_target_pairs={{0,16},{4,20},{8,24},{12,28},{16,0},{20,4},{24,8},{28,12},{1,17},{... | collective-permute-start | bytes 170504 | tf_op jit(solution)/shard_map/ppermute | solution.py:395
  22.2 8.8 %collective-permute-done.6 = f32[1184,12]{0,1:T(8,128)S(1)} collective-permute-done((f32[1184,12]{0,1:T(8,128)S(1)}, f32[1184,12]{0,1:T(8,128)S(1)}, u32[]{:S(2)}, u32[]{:S(2)}) %collective-permute-start.6) | collective-permute-done | bytes 56864 | tf_op jit(solution)/shard_map/ppermute | solution.py:395
  31.0 2.6 %collective-permute-done.7 = f32[1184,12]{0,1:T(8,128)S(1)} collective-permute-done((f32[1184,12]{0,1:T(8,128)S(1)}, f32[1184,12]{0,1:T(8,128)S(1)}, u32[]{:S(2)}, u32[]{:S(2)}) %collective-permute-start.7) | collective-permute-done | bytes 56864 | tf_op jit(solution)/shard_map/ppermute | solution.py:395
  36.0 49.6 %shard_map.104 = (f32[296,12]{1,0:T(8,128)}, f32[296,9472]{1,0:T(8,128)}, f32[296,9472]{1,0:T(8,128)}, f32[296,9472]{1,0:T(8,128)}, f32[296,9472]{1,0:T(8,128)}) custom-call(f32[1]{0:T(128)S(6)} %copy.234.wave_ref, f32[296,8]{1,0:T(8,128)} %copy.147.own_ref, f32[4,9472]{1,0:T(4,128)} %get-tuple-element.37.all_ref, f32[12,9472]{1,0:T(8,128)} %pad_maximum_fusion.vec_ref), custom_call_target="tpu_custom_call" | custom-call | flops 420556800 | bytes 45489280 | tf_op jit(solution)/shard_map/pallas_call | solution.py:374
  88.9 2.2 collective-permute-done.11
  97.0 2.4 %collective-permute-start.18 = (f32[1184,8]{0,1:T(8,128)S(1)}, f32[1184,8]{0,1:T(8,128)S(1)}, u32[]{:S(2)}, u32[]{:S(2)}) collective-permute-start(f32[1184,8]{0,1:T(8,128)S(1)} %reshape.197), channel_id=1, source_target_pairs={{0,8},{4,12},{8,16},{12,20},{16,24},{20,28},{24,0},{28,4},{1,9},{5... | collective-permute-start | bytes 113672 | tf_op jit(solution)/shard_map/ppermute | solution.py:395
  99.5 2.0 collective-permute-start.19
  103.0 3.2 %collective-permute-done.19 = f32[1184,8]{0,1:T(8,128)S(1)} collective-permute-done((f32[1184,8]{0,1:T(8,128)S(1)}, f32[1184,8]{0,1:T(8,128)S(1)}, u32[]{:S(2)}, u32[]{:S(2)}) %collective-permute-start.19) | collective-permute-done | bytes 37920 | tf_op jit(solution)/shard_map/ppermute | solution.py:395
  108.1 17.4 %shard_map.105 = f32[296,12]{1,0:T(8,128)} custom-call(f32[1]{0:T(128)S(6)} %copy.234.wave_ref, f32[296,8]{1,0:T(8,128)} %copy.147.own_ref, f32[4,9472]{1,0:T(4,128)} %get-tuple-element.37.all_ref, f32[12,9472]{1,0:T(8,128)} %pad_maximum_fusion.1.vec_ref, f32[296,9472]{1,0:T(8,128)} %get-tuple-element.10.refs_0_, f32[296,9472]{1,0:T(8,128)} %get-tuple-element.11.refs_1_), custom_call_target="tpu_custom_call" | custom-call | flops 89718784 | bytes 23059584 | tf_op jit(solution)/shard_map/pallas_call | solution.py:374
  128.4 2.4 %collective-permute-done.21 = f32[296,8]{0,1:T(8,128)S(1)} collective-permute-done((f32[296,8]{0,1:T(8,128)S(1)}, f32[296,8]{0,1:T(8,128)S(1)}, u32[]{:S(2)}, u32[]{:S(2)}) %collective-permute-start.21) | collective-permute-done | bytes 9504 | tf_op jit(solution)/shard_map/ppermute | solution.py:395
  133.1 2.6 %collective-permute-start.26 = (f32[1184,8]{0,1:T(8,128)S(1)}, f32[1184,8]{0,1:T(8,128)S(1)}, u32[]{:S(2)}, u32[]{:S(2)}) collective-permute-start(f32[1184,8]{0,1:T(8,128)S(1)} %reshape.200), channel_id=1, source_target_pairs={{0,16},{4,20},{8,24},{12,28},{16,0},{20,4},{24,8},{28,12},{1,17},{... | collective-permute-start | bytes 113672 | tf_op jit(solution)/shard_map/ppermute | solution.py:395
  139.1 2.5 %collective-permute-done.27 = f32[1184,8]{0,1:T(8,128)S(1)} collective-permute-done((f32[1184,8]{0,1:T(8,128)S(1)}, f32[1184,8]{0,1:T(8,128)S(1)}, u32[]{:S(2)}, u32[]{:S(2)}) %collective-permute-start.27) | collective-permute-done | bytes 37920 | tf_op jit(solution)/shard_map/ppermute | solution.py:395
  142.3 2.1 collective-permute-done.29
  147.2 17.4 %shard_map.106 = f32[296,12]{1,0:T(8,128)} custom-call(f32[1]{0:T(128)S(6)} %copy.234.wave_ref, f32[296,8]{1,0:T(8,128)} %copy.147.own_ref, f32[4,9472]{1,0:T(4,128)} %get-tuple-element.37.all_ref, f32[12,9472]{1,0:T(8,128)} %pad_maximum_fusion.2.vec_ref, f32[296,9472]{1,0:T(8,128)} %get-tuple-element.10.refs_0_, f32[296,9472]{1,0:T(8,128)} %get-tuple-element.11.refs_1_), custom_call_target="tpu_custom_call" | custom-call | flops 89718784 | bytes 23059584 | tf_op jit(solution)/shard_map/pallas_call | solution.py:374
  167.7 2.2 collective-permute-done.31
  171.5 2.0 collective-permute-start.34
  173.9 2.3 %collective-permute-start.36 = (f32[1184,8]{0,1:T(8,128)S(1)}, f32[1184,8]{0,1:T(8,128)S(1)}, u32[]{:S(2)}, u32[]{:S(2)}) collective-permute-start(f32[1184,8]{0,1:T(8,128)S(1)} %reshape.203), channel_id=1, source_target_pairs={{0,16},{4,20},{8,24},{12,28},{16,0},{20,4},{24,8},{28,12},{1,17},{... | collective-permute-start | bytes 113672 | tf_op jit(solution)/shard_map/ppermute | solution.py:395
  182.2 2.8 %collective-permute-done.39 = f32[1184,8]{0,1:T(8,128)S(1)} collective-permute-done((f32[1184,8]{0,1:T(8,128)S(1)}, f32[1184,8]{0,1:T(8,128)S(1)}, u32[]{:S(2)}, u32[]{:S(2)}) %collective-permute-start.39) | collective-permute-done | bytes 37920 | tf_op jit(solution)/shard_map/ppermute | solution.py:395
  189.1 17.4 %shard_map.107 = f32[296,12]{1,0:T(8,128)} custom-call(f32[1]{0:T(128)S(6)} %copy.234.wave_ref, f32[296,8]{1,0:T(8,128)} %copy.147.own_ref, f32[4,9472]{1,0:T(4,128)} %get-tuple-element.37.all_ref, f32[12,9472]{1,0:T(8,128)} %pad_maximum_fusion.3.vec_ref, f32[296,9472]{1,0:T(8,128)} %get-tuple-element.12.refs_0_, f32[296,9472]{1,0:T(8,128)} %get-tuple-element.13.refs_1_), custom_call_target="tpu_custom_call" | custom-call | flops 89718784 | bytes 23059584 | tf_op jit(solution)/shard_map/pallas_call | solution.py:374
  208.1 5.6 %psum.7 = f32[4,128]{1,0:T(4,128)S(1)} all-reduce(f32[4,128]{1,0:T(4,128)S(1)} %fusion.14), channel_id=1, replica_groups=mesh['row'=8,'col'=4] {'col'}, use_global_device_ids=true, to_apply=%region_13.16 | all-reduce | flops 512 | bytes 4096 | tf_op jit(solution)/shard_map/psum | solution.py:531
  219.4 2.2 collective-permute-start.45
  225.0 2.9 %collective-permute-done.46 = f32[1,4,128]{2,1,0:T(4,128)S(1)} collective-permute-done((f32[1,4,128]{2,1,0:T(4,128)S(1)}, f32[1,4,128]{2,1,0:T(4,128)S(1)}, u32[]{:S(2)}, u32[]{:S(2)}) %collective-permute-start.46) | collective-permute-done | bytes 2080 | tf_op jit(solution)/shard_map/ppermute | solution.py:395
  (249 shorter events, 63.9 us)
Async XLA Ops:
  2.0 7.9 %collective-permute-start = (f32[296,12]{0,1:T(8,128)S(1)}, f32[296,12]{0,1:T(8,128)S(1)}, u32[]{:S(2)}, u32[]{:S(2)}) collective-permute-start(f32[296,12]{0,1:T(8,128)S(1)} %pad_maximum_fusion.4), channel_id=1, source_target_pairs={{0,3},{1,0},{2,1},{3,2},{4,7},{5,4},{6,5},{7,6},{8,11},{9,8},{10,9... | collective-permute-start | bytes 42632 | tf_op jit(solution)/shard_map/ppermute | solution.py:395
  11.0 8.1 %collective-permute-start.3 = (f32[1184,12]{0,1:T(8,128)S(1)}, f32[1184,12]{0,1:T(8,128)S(1)}, u32[]{:S(2)}, u32[]{:S(2)}) collective-permute-start(f32[1184,12]{0,1:T(8,128)S(1)} %reshape.195), channel_id=1, source_target_pairs={{0,28},{4,0},{8,4},{12,8},{16,12},{20,16},{24,20},{28,24},{1,29},{... | collective-permute-start | bytes 170504 | tf_op jit(solution)/shard_map/ppermute | solution.py:395
  15.6 6.0 %collective-permute-start.4 = (f32[1184,12]{0,1:T(8,128)S(1)}, f32[1184,12]{0,1:T(8,128)S(1)}, u32[]{:S(2)}, u32[]{:S(2)}) collective-permute-start(f32[1184,12]{0,1:T(8,128)S(1)} %reshape.195), channel_id=1, source_target_pairs={{0,24},{4,28},{8,0},{12,4},{16,8},{20,12},{24,16},{28,20},{1,25},{... | collective-permute-start | bytes 170504 | tf_op jit(solution)/shard_map/ppermute | solution.py:395
  16.0 6.1 %collective-permute-start.5 = (f32[1184,12]{0,1:T(8,128)S(1)}, f32[1184,12]{0,1:T(8,128)S(1)}, u32[]{:S(2)}, u32[]{:S(2)}) collective-permute-start(f32[1184,12]{0,1:T(8,128)S(1)} %reshape.195), channel_id=1, source_target_pairs={{0,20},{4,24},{8,28},{12,0},{16,4},{20,8},{24,12},{28,16},{1,21},{... | collective-permute-start | bytes 170504 | tf_op jit(solution)/shard_map/ppermute | solution.py:395
  16.0 14.9 %collective-permute-start.6 = (f32[1184,12]{0,1:T(8,128)S(1)}, f32[1184,12]{0,1:T(8,128)S(1)}, u32[]{:S(2)}, u32[]{:S(2)}) collective-permute-start(f32[1184,12]{0,1:T(8,128)S(1)} %reshape.195), channel_id=1, source_target_pairs={{0,16},{4,20},{8,24},{12,28},{16,0},{20,4},{24,8},{28,12},{1,17},{... | collective-permute-start | bytes 170504 | tf_op jit(solution)/shard_map/ppermute | solution.py:395
  19.0 14.6 %collective-permute-start.7 = (f32[1184,12]{0,1:T(8,128)S(1)}, f32[1184,12]{0,1:T(8,128)S(1)}, u32[]{:S(2)}, u32[]{:S(2)}) collective-permute-start(f32[1184,12]{0,1:T(8,128)S(1)} %reshape.195), channel_id=1, source_target_pairs={{0,12},{4,16},{8,20},{12,24},{16,28},{20,0},{24,4},{28,8},{1,13},{... | collective-permute-start | bytes 170504 | tf_op jit(solution)/shard_map/ppermute | solution.py:395
  19.1 14.5 %collective-permute-start.8 = (f32[1184,12]{0,1:T(8,128)S(1)}, f32[1184,12]{0,1:T(8,128)S(1)}, u32[]{:S(2)}, u32[]{:S(2)}) collective-permute-start(f32[1184,12]{0,1:T(8,128)S(1)} %reshape.195), channel_id=1, source_target_pairs={{0,8},{4,12},{8,16},{12,20},{16,24},{20,28},{24,0},{28,4},{1,9},{5... | collective-permute-start | bytes 170504 | tf_op jit(solution)/shard_map/ppermute | solution.py:395
  21.6 12.0 %collective-permute-start.9 = (f32[1184,12]{0,1:T(8,128)S(1)}, f32[1184,12]{0,1:T(8,128)S(1)}, u32[]{:S(2)}, u32[]{:S(2)}) collective-permute-start(f32[1184,12]{0,1:T(8,128)S(1)} %reshape.195), channel_id=1, source_target_pairs={{0,4},{4,8},{8,12},{12,16},{16,20},{20,24},{24,28},{28,0},{1,5},{5... | collective-permute-start | bytes 170504 | tf_op jit(solution)/shard_map/ppermute | solution.py:395
  92.4 7.1 %collective-permute-start.14 = (f32[1184,8]{0,1:T(8,128)S(1)}, f32[1184,8]{0,1:T(8,128)S(1)}, u32[]{:S(2)}, u32[]{:S(2)}) collective-permute-start(f32[1184,8]{0,1:T(8,128)S(1)} %reshape.197), channel_id=1, source_target_pairs={{0,24},{4,28},{8,0},{12,4},{16,8},{20,12},{24,16},{28,20},{1,25},{... | collective-permute-start | bytes 113672 | tf_op jit(solution)/shard_map/ppermute | solution.py:395
  93.7 7.8 %collective-permute-start.15 = (f32[1184,8]{0,1:T(8,128)S(1)}, f32[1184,8]{0,1:T(8,128)S(1)}, u32[]{:S(2)}, u32[]{:S(2)}) collective-permute-start(f32[1184,8]{0,1:T(8,128)S(1)} %reshape.197), channel_id=1, source_target_pairs={{0,20},{4,24},{8,28},{12,0},{16,4},{20,8},{24,12},{28,16},{1,21},{... | collective-permute-start | bytes 113672 | tf_op jit(solution)/shard_map/ppermute | solution.py:395
  95.0 6.5 %collective-permute-start.16 = (f32[1184,8]{0,1:T(8,128)S(1)}, f32[1184,8]{0,1:T(8,128)S(1)}, u32[]{:S(2)}, u32[]{:S(2)}) collective-permute-start(f32[1184,8]{0,1:T(8,128)S(1)} %reshape.197), channel_id=1, source_target_pairs={{0,16},{4,20},{8,24},{12,28},{16,0},{20,4},{24,8},{28,12},{1,17},{... | collective-permute-start | bytes 113672 | tf_op jit(solution)/shard_map/ppermute | solution.py:395
  96.7 6.0 %collective-permute-start.17 = (f32[1184,8]{0,1:T(8,128)S(1)}, f32[1184,8]{0,1:T(8,128)S(1)}, u32[]{:S(2)}, u32[]{:S(2)}) collective-permute-start(f32[1184,8]{0,1:T(8,128)S(1)} %reshape.197), channel_id=1, source_target_pairs={{0,12},{4,16},{8,20},{12,24},{16,28},{20,0},{24,4},{28,8},{1,13},{... | collective-permute-start | bytes 113672 | tf_op jit(solution)/shard_map/ppermute | solution.py:395
  97.0 6.0 %collective-permute-start.18 = (f32[1184,8]{0,1:T(8,128)S(1)}, f32[1184,8]{0,1:T(8,128)S(1)}, u32[]{:S(2)}, u32[]{:S(2)}) collective-permute-start(f32[1184,8]{0,1:T(8,128)S(1)} %reshape.197), channel_id=1, source_target_pairs={{0,8},{4,12},{8,16},{12,20},{16,24},{20,28},{24,0},{28,4},{1,9},{5... | collective-permute-start | bytes 113672 | tf_op jit(solution)/shard_map/ppermute | solution.py:395
  99.5 6.7 %collective-permute-start.19 = (f32[1184,8]{0,1:T(8,128)S(1)}, f32[1184,8]{0,1:T(8,128)S(1)}, u32[]{:S(2)}, u32[]{:S(2)}) collective-permute-start(f32[1184,8]{0,1:T(8,128)S(1)} %reshape.197), channel_id=1, source_target_pairs={{0,4},{4,8},{8,12},{12,16},{16,20},{20,24},{24,28},{28,0},{1,5},{5... | collective-permute-start | bytes 113672 | tf_op jit(solution)/shard_map/ppermute | solution.py:395
  133.0 6.1 %collective-permute-start.25 = (f32[1184,8]{0,1:T(8,128)S(1)}, f32[1184,8]{0,1:T(8,128)S(1)}, u32[]{:S(2)}, u32[]{:S(2)}) collective-permute-start(f32[1184,8]{0,1:T(8,128)S(1)} %reshape.200), channel_id=1, source_target_pairs={{0,20},{4,24},{8,28},{12,0},{16,4},{20,8},{24,12},{28,16},{1,21},{... | collective-permute-start | bytes 113672 | tf_op jit(solution)/shard_map/ppermute | solution.py:395
  136.3 6.0 %collective-permute-start.28 = (f32[1184,8]{0,1:T(8,128)S(1)}, f32[1184,8]{0,1:T(8,128)S(1)}, u32[]{:S(2)}, u32[]{:S(2)}) collective-permute-start(f32[1184,8]{0,1:T(8,128)S(1)} %reshape.200), channel_id=1, source_target_pairs={{0,8},{4,12},{8,16},{12,20},{16,24},{20,28},{24,0},{28,4},{1,9},{5... | collective-permute-start | bytes 113672 | tf_op jit(solution)/shard_map/ppermute | solution.py:395
  137.6 6.7 %collective-permute-start.29 = (f32[1184,8]{0,1:T(8,128)S(1)}, f32[1184,8]{0,1:T(8,128)S(1)}, u32[]{:S(2)}, u32[]{:S(2)}) collective-permute-start(f32[1184,8]{0,1:T(8,128)S(1)} %reshape.200), channel_id=1, source_target_pairs={{0,4},{4,8},{8,12},{12,16},{16,20},{20,24},{24,28},{28,0},{1,5},{5... | collective-permute-start | bytes 113672 | tf_op jit(solution)/shard_map/ppermute | solution.py:395
  171.5 6.7 %collective-permute-start.34 = (f32[1184,8]{0,1:T(8,128)S(1)}, f32[1184,8]{0,1:T(8,128)S(1)}, u32[]{:S(2)}, u32[]{:S(2)}) collective-permute-start(f32[1184,8]{0,1:T(8,128)S(1)} %reshape.203), channel_id=1, source_target_pairs={{0,24},{4,28},{8,0},{12,4},{16,8},{20,12},{24,16},{28,20},{1,25},{... | collective-permute-start | bytes 113672 | tf_op jit(solution)/shard_map/ppermute | solution.py:395
  173.5 6.6 %collective-permute-start.35 = (f32[1184,8]{0,1:T(8,128)S(1)}, f32[1184,8]{0,1:T(8,128)S(1)}, u32[]{:S(2)}, u32[]{:S(2)}) collective-permute-start(f32[1184,8]{0,1:T(8,128)S(1)} %reshape.203), channel_id=1, source_target_pairs={{0,20},{4,24},{8,28},{12,0},{16,4},{20,8},{24,12},{28,16},{1,21},{... | collective-permute-start | bytes 113672 | tf_op jit(solution)/shard_map/ppermute | solution.py:395
  173.9 6.4 %collective-permute-start.36 = (f32[1184,8]{0,1:T(8,128)S(1)}, f32[1184,8]{0,1:T(8,128)S(1)}, u32[]{:S(2)}, u32[]{:S(2)}) collective-permute-start(f32[1184,8]{0,1:T(8,128)S(1)} %reshape.203), channel_id=1, source_target_pairs={{0,16},{4,20},{8,24},{12,28},{16,0},{20,4},{24,8},{28,12},{1,17},{... | collective-permute-start | bytes 113672 | tf_op jit(solution)/shard_map/ppermute | solution.py:395
  178.1 6.9 %collective-permute-start.39 = (f32[1184,8]{0,1:T(8,128)S(1)}, f32[1184,8]{0,1:T(8,128)S(1)}, u32[]{:S(2)}, u32[]{:S(2)}) collective-permute-start(f32[1184,8]{0,1:T(8,128)S(1)} %reshape.203), channel_id=1, source_target_pairs={{0,4},{4,8},{8,12},{12,16},{16,20},{20,24},{24,28},{28,0},{1,5},{5... | collective-permute-start | bytes 113672 | tf_op jit(solution)/shard_map/ppermute | solution.py:395
  214.5 7.1 %collective-permute-start.41 = (f32[1,4,128]{2,1,0:T(4,128)S(1)}, f32[1,4,128]{2,1,0:T(4,128)S(1)}, u32[]{:S(2)}, u32[]{:S(2)}) collective-permute-start(f32[1,4,128]{2,1,0:T(4,128)S(1)} %bitcast.177), channel_id=1, source_target_pairs={{0,24},{4,28},{8,0},{12,4},{16,8},{20,12},{24,16},{28,20},{1,25},{... | collective-permute-start | bytes 6152 | tf_op jit(solution)/shard_map/ppermute | solution.py:395
  216.3 6.4 %collective-permute-start.42 = (f32[1,4,128]{2,1,0:T(4,128)S(1)}, f32[1,4,128]{2,1,0:T(4,128)S(1)}, u32[]{:S(2)}, u32[]{:S(2)}) collective-permute-start(f32[1,4,128]{2,1,0:T(4,128)S(1)} %bitcast.178), channel_id=1, source_target_pairs={{0,20},{4,24},{8,28},{12,0},{16,4},{20,8},{24,12},{28,16},{1,21},{... | collective-permute-start | bytes 6152 | tf_op jit(solution)/shard_map/ppermute | solution.py:395
  221.6 6.3 %collective-permute-start.46 = (f32[1,4,128]{2,1,0:T(4,128)S(1)}, f32[1,4,128]{2,1,0:T(4,128)S(1)}, u32[]{:S(2)}, u32[]{:S(2)}) collective-permute-start(f32[1,4,128]{2,1,0:T(4,128)S(1)} %bitcast.182), channel_id=1, source_target_pairs={{0,4},{4,8},{8,12},{12,16},{16,20},{20,24},{24,28},{28,0},{1,5},{5... | collective-permute-start | bytes 6152 | tf_op jit(solution)/shard_map/ppermute | solution.py:395
  (27 other events, 124.4 us)
